TPU v7x, 512 devices: a whole 4x8x8 slice. The times are simulated.
512 devices in a mesh: box: 512 (over y, x, z, core).
Axes of the slice: x: 4, y: 8, z: 8, core: 2. Of those that a mesh axis runs over, the one named last changes fastest.
Arguments:
- positions: float32 [3, 131072], P(None, 'box'), may hold values from -1 to 1
- leaf_centers: float32 [3, 2048], P(None, 'box'), may hold values from -1 to 1
- atom_counts: int32 [2048], P('box'), may hold values from 32 to 64
- features: bfloat16 [131072, 128], P('box'), may hold values from -6 to 6
- msg_weight: bfloat16 [128, 128], replicated, may hold values from -0.5 to 0.5
- trans_weight: float32 [35, 35], replicated, may hold values from -0.03125 to 0.03125
- read_weight: float32 [128], replicated, may hold values from -0.5 to 0.5
- pair_target: int32 [55296], P('box'), may hold values from 0 to 3
- pair_source: int32 [55296], P('box'), may hold values from 0 to 11
- pair_live: int32 [55296], P('box'), may hold values 0 or 1
- far_list: int32 [64, 32], replicated, may hold values from 0 to 63, as said below
Outputs:
- atom_energy: float32 [131072], P('box')
- forces: float32 [3, 131072], P(None, 'box')
- grad_msg: float32 [128, 128], replicated
- grad_trans: float32 [35, 35], replicated
- grad_read: float32 [128], replicated
Inputs may be any that keep to these rules, and one draw needn't show every extreme that they name: `far_list`: each row names 32 different level-two boxes, none of them the row's own box.
All inputs are finite; a program needn't handle non-finite values. No bound on the sum of `pair_live` on one device may be relied on, other than what follows from the above.
Results may differ from a plain program's by a relative error of at most 0.0047.
Values may be sent and summed in bfloat16 or wider, within the bound.
No kernel may reach another device: no remote copies, remote signals or barrier semaphores. Data moves between devices by JAX's collectives and lax.ppermute only.
A program may use at most 64 MiB of HBM per device.

v0:
```python
import jax
import jax.numpy as jnp
from jax import lax
from jax.sharding import PartitionSpec as P

LEAF_ATOMS = 64
PAIR_LEAF = 27


PRECISE = lax.Precision.HIGHEST
GAMMA = 3.0
NEAR_SCALE = 0.3
REL_SCALE = 0.5
EXPONENTS = [
    (power_x, power_y, degree - power_x - power_y)
    for degree in range(5)
    for power_x in range(degree, -1, -1)
    for power_y in range(degree - power_x, -1, -1)
]


def extended(block, sides, width):
    for axis, dim in sides:
        count = lax.axis_size(axis)
        forward = [(i, i + 1) for i in range(count - 1)]
        backward = [(target, source) for source, target in forward]
        low = lax.ppermute(
            lax.slice_in_dim(block, block.shape[dim] - width, None, axis=dim), axis, forward
        )
        high = lax.ppermute(lax.slice_in_dim(block, 0, width, axis=dim), axis, backward)
        block = jnp.concatenate([low, block, high], axis=dim)
    return block


def passed_along(block, axis, distance):
    devices = range(lax.axis_size(axis))
    route = [(i - distance, i) for i in devices if i - distance in devices]
    return lax.ppermute(block, axis, route)


def monomials(relative):
    powers = []
    for axis_id in range(3):
        coords = relative[axis_id]
        stacked = [jnp.ones_like(coords), coords]
        for degree in range(2, 5):
            stacked.append(stacked[-1] * coords)
        powers.append(stacked)
    return jnp.stack(
        [powers[0][ex_a] * powers[1][ex_b] * powers[2][ex_c] for ex_a, ex_b, ex_c in EXPONENTS]
    )


def near_field(pos_own, pos_ext, hid_ext, targets, sources, alive):
    leaves = pos_own.shape[1] // LEAF_ATOMS
    channels = hid_ext.shape[0]
    own_leaf = pos_own.reshape(3, leaves, LEAF_ATOMS)
    ext_leaf = pos_ext.reshape(3, 3 * leaves, LEAF_ATOMS)
    feat_leaf = hid_ext.reshape(channels, 3 * leaves, LEAF_ATOMS)
    leaf_ids = jnp.arange(leaves, dtype=jnp.int32)
    blocks = (
        targets.reshape(-1, PAIR_LEAF),
        sources.reshape(-1, PAIR_LEAF),
        alive.reshape(-1, PAIR_LEAF),
    )

    def one_block(accumulated, pair_block):
        tgt_ids, src_ids, live_ids = pair_block
        near_pos = own_leaf[:, tgt_ids]
        far_pos = ext_leaf[:, src_ids]
        dist_sq = jnp.zeros((tgt_ids.shape[0], LEAF_ATOMS, LEAF_ATOMS), jnp.float32)
        for axis_id in range(3):
            offset_ax = near_pos[axis_id][:, :, None] - far_pos[axis_id][:, None, :]
            dist_sq = dist_sq + offset_ax * offset_ax
        kernel = (
            NEAR_SCALE * jnp.exp(-GAMMA * dist_sq) * live_ids.astype(jnp.float32)[:, None, None]
        ).astype(jnp.bfloat16)
        source_feat = feat_leaf[:, src_ids].astype(jnp.bfloat16)
        contrib = jnp.einsum(
            "pij,cpj->pic", kernel, source_feat, preferred_element_type=jnp.float32
        )
        onehot = (tgt_ids[None, :] == leaf_ids[:, None]).astype(jnp.float32)
        return (accumulated + jnp.einsum("tp,pic->tic", onehot, contrib, precision=PRECISE), None)

    initial = jnp.zeros((leaves, LEAF_ATOMS, channels), jnp.float32)
    accumulated, unused = lax.scan(jax.checkpoint(one_block), initial, blocks)
    return accumulated.reshape(leaves * LEAF_ATOMS, channels)


def group_sums(moment):
    groups = lax.axis_size("box") // 8
    position = lax.axis_index("box")
    group_id = position // 8
    onehot = (jnp.arange(groups, dtype=jnp.int32) == group_id).astype(jnp.float32)
    placed = onehot[:, None, None] * moment[None]
    return lax.psum(placed, "box")


def on_device(
    positions,
    leaf_centers,
    atom_counts,
    features,
    msg_weight,
    trans_weight,
    read_weight,
    pair_target,
    pair_source,
    pair_live,
    far_list,
):
    atom_num = positions.shape[1]
    groups = lax.axis_size("box") // 8
    group_id = lax.axis_index("box") // 8
    slot_ids = jnp.arange(LEAF_ATOMS, dtype=jnp.int32)
    mask_f = (slot_ids[None, :] < atom_counts[:, None]).astype(jnp.float32).reshape(atom_num)
    hidden_t = (
        jnp.einsum("ic,ai->ca", msg_weight, features, preferred_element_type=jnp.float32)
        * mask_f[None, :]
    )
    pos_ext = extended(positions, (("box", 1),), atom_num)
    hid_ext = extended(hidden_t.astype(jnp.bfloat16), (("box", 1),), atom_num).astype(jnp.float32)

    def near_part(own, ext, feat_ext):
        return near_field(own, ext, feat_ext, pair_target, pair_source, pair_live)

    near_val, near_back = jax.vjp(near_part, positions, pos_ext, hid_ext)
    centers = jnp.repeat(leaf_centers, LEAF_ATOMS, axis=1)

    def far_basis(coords):
        return monomials((coords - centers) * REL_SCALE)

    basis_val, basis_back = jax.vjp(far_basis, positions)
    moment = jnp.einsum("ka,ca->kc", basis_val, hidden_t, precision=PRECISE)
    group_tab = group_sums(moment)
    counts_mat = jnp.sum(
        (far_list[:, :, None] == jnp.arange(groups, dtype=jnp.int32)[None, None, :]).astype(
            jnp.float32
        ),
        axis=1,
    )
    row_weights = lax.dynamic_index_in_dim(counts_mat, group_id, 0, keepdims=False)
    gathered = jnp.einsum("j,jkc->kc", row_weights, group_tab, precision=PRECISE)
    local_exp = jnp.dot(trans_weight, gathered, precision=PRECISE)
    potential = jnp.einsum("ka,kc->ac", basis_val, local_exp, precision=PRECISE)
    pre_act = near_val + potential
    sigma = jax.nn.sigmoid(pre_act)
    activ = pre_act * sigma
    atom_energy = mask_f * jnp.dot(activ, read_weight, precision=PRECISE)
    d_pre = mask_f[:, None] * read_weight[None, :] * (sigma + pre_act * sigma * (1.0 - sigma))
    grad_read_part = jnp.dot(mask_f, activ, precision=PRECISE)
    d_local = jnp.dot(basis_val, d_pre, precision=PRECISE)
    d_basis = jnp.einsum("kc,ac->ka", local_exp, d_pre, precision=PRECISE)
    grad_trans_part = jnp.einsum("kc,qc->kq", d_local, gathered, precision=PRECISE)
    d_gathered = jnp.dot(trans_weight.T, d_local, precision=PRECISE)
    d_group_tab = group_sums(d_gathered)
    col_weights = lax.dynamic_index_in_dim(counts_mat, group_id, 1, keepdims=False)
    d_moment = jnp.einsum("b,bkc->kc", col_weights, d_group_tab, precision=PRECISE)
    d_basis = d_basis + jnp.dot(d_moment, hidden_t, precision=PRECISE)
    d_hidden_far = jnp.einsum("ka,kc->ca", basis_val, d_moment, precision=PRECISE)
    (d_far_pos,) = basis_back(d_basis)
    d_own, d_ext, d_feat_ext = near_back(d_pre)
    low_pos, low_feat = passed_along((d_ext[:, :atom_num], d_feat_ext[:, :atom_num]), "box", -1)
    high_pos, high_feat = (
        passed_along(d_ext[:, 2 * atom_num :].astype(jnp.bfloat16), "box", 1).astype(jnp.float32),
        passed_along(d_feat_ext[:, 2 * atom_num :].astype(jnp.bfloat16), "box", 1).astype(
            jnp.float32
        ),
    )
    d_hidden_t = (
        d_feat_ext[:, atom_num : 2 * atom_num] + low_feat + high_feat + d_hidden_far
    ) * mask_f[None, :]
    grad_msg_part = jnp.einsum(
        "ai,ca->ic", features.astype(jnp.float32), d_hidden_t, precision=PRECISE
    )
    grad_msg, grad_trans, grad_read = lax.psum(
        (grad_msg_part, grad_trans_part, grad_read_part), "box"
    )
    forces = -(d_own + d_ext[:, atom_num : 2 * atom_num] + low_pos + high_pos + d_far_pos)
    return (atom_energy, forces, grad_msg, grad_trans, grad_read)


def solution(mesh):
    return jax.shard_map(
        on_device,
        mesh=mesh,
        in_specs=(
            P(None, "box"),
            P(None, "box"),
            P("box"),
            P("box", None),
            P(),
            P(),
            P(),
            P("box"),
            P("box"),
            P("box"),
            P(),
        ),
        out_specs=(P("box"), P(None, "box"), P(), P(), P()),
        check_vma=False,
    )
```

profile of v0, /device:TPU:1, one launch (start us, length us, event | category | flops | bytes accessed | tf_op | source)
XLA Modules:
  0.0 912.9 jit_solution(6828085566158842293)
XLA Ops:
  7.2 0.7 iota_compare_fusion.2
  8.1 1.0 fusion.132
  9.0 5.4 collective-permute-start.2
  14.4 4.7 collective-permute-start.3
  19.1 1.9 collective-permute-start
  21.0 2.4 collective-permute-start.1
  23.4 0.8 broadcast_in_dim.77
  24.2 0.7 subtract_multiply_fusion.3
  25.5 1.2 broadcast_multiply_fusion.2
  28.4 18.3 %while.33 = (s32[]{:T(128)}, f32[4,64,128]{2,0,1:T(4,128)S(1)}, s32[4,27]{1,0:T(4,128)S(1)}, f32[3,4,64]{2,0,1:T(4,128)S(1)}, s32[4,27]{1,0:T(4,128)S(1)}, /*ind...) while((s32[]{:T(128)}, f32[4,64,128]{2,0,1:T(4,128)S(1)}, ...), condition=%wide.region_1.2_spmd.clone, body=%wide.region_0.1_spmd.clone.sunk | while | flops 40212804 | bytes 3658959 | solution.py:86
  29.8 0.6 gather_fusion.3
  30.5 1.4 fusion.191
  31.9 1.1 convolution_add_fusion.4
  34.4 0.6 gather_fusion.3
  35.1 1.4 fusion.191
  36.5 1.1 convolution_add_fusion.4
  39.0 0.6 gather_fusion.3
  39.6 1.4 fusion.191
  41.0 1.1 convolution_add_fusion.4
  43.5 0.6 gather_fusion.3
  44.2 1.4 fusion.191
  45.6 1.1 convolution_add_fusion.4
  46.8 262.2 %all-reduce.14.cloned.1.call-done = f32[64,35,128]{2,1,0:T(8,128)} async-done(((f32[64,35,128]{2,1,0:T(8,128)}), f32[64,35,128]{2,1,0:T(8,128)}) %all-reduce.14.cloned.1.call-update) | async-done | bytes 1146896 | tf_op jit(solution)/shard_map/psum | solution.py:96
  309.0 2.1 fusion.69
  312.5 50.5 %while.32 = (s32[]{:T(128)}, f32[3,4,64]{2,0,1:T(4,128)S(1)}, f32[3,12,64]{2,0,1:T(4,128)S(1)}, f32[128,12,64]{0,2,1:T(8,128)S(1)}, f32[4,64,128]{2,0,1:T(4,128)...) while((s32[]{:T(128)}, f32[3,4,64]{2,0,1:T(4,128)S(1)}, ...), condition=%wide.region_14.15_spmd.clone, body=%wide.region_4.14_spmd.clone.sunk | while | flops 71802528 | bytes 7040317 | solution.py:86
  312.5 0.7 fusion.181
  314.6 1.8 fusion.183
  316.4 2.2 scatter_fusion.2
  318.7 0.6 gather_fusion.2
  319.3 2.0 fusion.182
  321.5 1.7 scatter_fusion.1
  323.3 1.7 scatter_fusion
  325.1 0.7 fusion.181
  327.3 1.8 fusion.183
  329.1 2.2 scatter_fusion.2
  331.3 0.6 gather_fusion.2
  332.0 2.0 fusion.182
  334.1 1.7 scatter_fusion.1
  336.0 1.7 scatter_fusion
  337.8 0.7 fusion.181
  339.9 1.8 fusion.183
  341.7 2.2 scatter_fusion.2
  343.9 0.6 gather_fusion.2
  344.6 2.0 fusion.182
  346.7 1.7 scatter_fusion.1
  348.6 1.7 scatter_fusion
  350.4 0.7 fusion.181
  352.5 1.8 fusion.183
  354.3 2.2 scatter_fusion.2
  356.6 0.6 gather_fusion.2
  357.2 2.0 fusion.182
  359.3 1.7 scatter_fusion.1
  361.2 1.7 scatter_fusion
  363.1 1.2 broadcast_multiply_fusion.1
  364.5 2.3 collective-permute-start.6
  367.0 3.3 collective-permute-start.7
  370.3 1.9 collective-permute-start.4
  372.2 3.6 collective-permute-start.5
  376.2 108.9 %all-reduce.9 = (f32[35,35]{1,0:T(8,128)}, f32[128]{0:T(128)}) all-reduce(f32[35,35]{1,0:T(8,128)S(1)} %fusion.83, f32[128]{0:T(128)S(1)} %convolution_bitcast_fusion.2), channel_id=1, replica_groups=mesh['box'=512] {'box'}, use_global_device_ids=true, to_apply=%region_17.18 | all-reduce | flops 1353 | bytes 10824 | tf_op jit(solution)/shard_map/psum | solution.py:176
  486.2 152.5 %all-reduce.16.cloned.1.call-done = f32[64,35,128]{2,1,0:T(8,128)} async-done(((f32[64,35,128]{2,1,0:T(8,128)}), f32[64,35,128]{2,1,0:T(8,128)}) %all-reduce.16.cloned.1.call-update) | async-done | bytes 1146896 | tf_op jit(solution)/shard_map/psum | solution.py:96
  638.7 2.1 fusion.67
  641.4 0.8 convolution_bitcast_fusion
  642.9 261.8 %all-reduce.18.cloned.1.call-done = f32[128,128]{0,1:T(8,128)} async-done(((f32[128,128]{0,1:T(8,128)}), f32[128,128]{0,1:T(8,128)}) %all-reduce.18.cloned.1.call-update) | async-done | bytes 65552 | tf_op jit(solution)/shard_map/psum | solution.py:176
  904.8 1.6 copy.101
  (268 shorter events, 18.0 us)
Async XLA Ops:
  7.2 0.9 copy-start
  7.2 301.8 %all-reduce.14.cloned.1.call-start = ((), (), s32[]{:S(2)}) async-start(), calls=%async_computation | async-start | bytes 2621440 | tf_op jit(solution)/shard_map/psum | solution.py:96
  9.0 19.1 %collective-permute-start.2 = (bf16[128,256]{1,0:T(8,128)(2,1)S(1)}, bf16[128,256]{1,0:T(8,128)(2,1)S(1)}, u32[]{:S(2)}, u32[]{:S(2)}) collective-permute-start(bf16[128,256]{1,0:T(8,128)(2,1)S(1)} %get-tuple-element.573), channel_id=1, source_target_pairs={{0,1},{1,2},{2,3},{3,4},{4,5},{5,6},{6,7},{7,8},{8,9},{9,10},{10,1... | collective-permute-start | bytes 196616 | tf_op jit(solution)/shard_map/ppermute | solution.py:27
  14.4 13.9 %collective-permute-start.3 = (bf16[128,256]{1,0:T(8,128)(2,1)S(1)}, bf16[128,256]{1,0:T(8,128)(2,1)S(1)}, u32[]{:S(2)}, u32[]{:S(2)}) collective-permute-start(bf16[128,256]{1,0:T(8,128)(2,1)S(1)} %get-tuple-element.573), channel_id=1, source_target_pairs={{1,0},{2,1},{3,2},{4,3},{5,4},{6,5},{7,6},{8,7},{9,8},{10,9},{11,1... | collective-permute-start | bytes 196616 | tf_op jit(solution)/shard_map/ppermute | solution.py:30
  19.1 8.9 collective-permute-start
  21.0 7.0 collective-permute-start.1
  25.4 1.4 copy-start.3
  25.4 2.0 copy-start.1
  25.4 2.1 copy-start.4
  25.4 2.2 copy-start.5
  25.5 2.3 copy-start.6
  26.7 612.0 %all-reduce.16.cloned.1.call-start = ((), (), s32[]{:S(2)}) async-start(), calls=%async_computation.1 | async-start | bytes 2621440 | tf_op jit(solution)/shard_map/psum | solution.py:96
  46.7 264.4 %copy-start.2 = (f32[35,35]{1,0:T(8,128)S(1)}, f32[35,35]{1,0:T(8,128)}, u32[]{:S(2)}) copy-start(f32[35,35]{1,0:T(8,128)} %param.20) | copy-start | bytes 14704
  46.7 264.5 %copy-start.7 = (f32[128]{0:T(128)S(1)}, f32[128]{0:T(128)}, u32[]{:S(2)}) copy-start(f32[128]{0:T(128)} %param.21) | copy-start | bytes 1540
  364.4 540.4 %all-reduce.18.cloned.1.call-start = ((), (), s32[]{:S(2)}) async-start(), calls=%async_computation.2 | async-start | bytes 131072 | tf_op jit(solution)/shard_map/psum | solution.py:176
  364.5 276.9 %collective-permute-start.6 = (f32[128,256]{1,0:T(8,128)S(1)}, f32[128,256]{1,0:T(8,128)S(1)}, u32[]{:S(2)}, u32[]{:S(2)}) collective-permute-start(f32[128,256]{1,0:T(8,128)S(1)} %copy.120), channel_id=1, source_target_pairs={{1,0},{2,1},{3,2},{4,3},{5,4},{6,5},{7,6},{8,7},{9,8},{10,9},{11,1... | collective-permute-start | bytes 393224 | tf_op jit(solution)/shard_map/ppermute | solution.py:38
  367.0 274.4 %collective-permute-start.7 = (bf16[128,256]{1,0:T(8,128)(2,1)S(1)}, bf16[128,256]{1,0:T(8,128)(2,1)S(1)}, u32[]{:S(2)}, u32[]{:S(2)}) collective-permute-start(bf16[128,256]{1,0:T(8,128)(2,1)S(1)} %copy.121), channel_id=1, source_target_pairs={{0,1},{1,2},{2,3},{3,4},{4,5},{5,6},{6,7},{7,8},{8,9},{9,10},{10,1... | collective-permute-start | bytes 196616 | tf_op jit(solution)/shard_map/ppermute | solution.py:38
  370.3 272.0 %collective-permute-start.4 = (f32[3,256]{1,0:T(4,128)S(1)}, f32[3,256]{1,0:T(4,128)S(1)}, u32[]{:S(2)}, u32[]{:S(2)}) collective-permute-start(f32[3,256]{1,0:T(4,128)S(1)} %slice.151), channel_id=1, source_target_pairs={{1,0},{2,1},{3,2},{4,3},{5,4},{6,5},{7,6},{8,7},{9,8},{10,9},{11,1... | collective-permute-start | bytes 9224 | tf_op jit(solution)/shard_map/ppermute | solution.py:38
  372.2 270.1 %collective-permute-start.5 = (bf16[3,256]{1,0:T(4,128)(2,1)S(1)}, bf16[3,256]{1,0:T(4,128)(2,1)S(1)}, u32[]{:S(2)}, u32[]{:S(2)}) collective-permute-start(bf16[3,256]{1,0:T(4,128)(2,1)S(1)} %slice.228), channel_id=1, source_target_pairs={{0,1},{1,2},{2,3},{3,4},{4,5},{5,6},{6,7},{7,8},{8,9},{9,10},{10,1... | collective-permute-start | bytes 4616 | tf_op jit(solution)/shard_map/ppermute | solution.py:38
Sparse Core Ops, SparseCore 0:
  26.8 282.1 all-reduce.13
  364.5 274.1 all-reduce.15
  644.3 260.4 all-reduce.17
where the time goes:
time: 913 us
  waiting for transfers between devices  677 us (74%)
  blocking collectives  109 us (12%)
  matrix products  36.4 us (4%)
  other arithmetic  29.2 us (3%)
  starting transfers between devices  25.6 us (3%)
  local copies, waits for them, and re-layouts  20.2 us (2%)
  between operations  14.3 us (2%)
    psum x2, waiting for transfers between devices, group_sums(): return lax.psum(placed, 'box')  415 us
    psum x1, waiting for transfers between devices, on_device(): lax.psum((grad_msg_part, grad_trans_part, grad_read_part), 'box')  262 us
    psum x1, blocking collectives, on_device(): lax.psum((grad_msg_part, grad_trans_part, grad_read_part), 'box')  109 us
    dot_general x12, matrix products, one_block(): jnp.einsum('pij,cpj->pic', kernel, source_feat, preferred_element_type=jn...  20.6 us
  transfers between devices with their start and end apart: 11, of which 3 were waited for; matrix products, arithmetic and copies ran while one was open for 3% of the time, Pallas kernels for 0%

commit v1 on v0

--- a/solution.py
+++ b/solution.py
@@ -1,10 +1,11 @@
 import jax
 import jax.numpy as jnp
 from jax import lax
-from jax.sharding import PartitionSpec as P
+from jax.sharding import Mesh, PartitionSpec as P
 
 LEAF_ATOMS = 64
 PAIR_LEAF = 27
+BOX = ("grp", "sub")
 
 
 PRECISE = lax.Precision.HIGHEST
@@ -87,15 +88,6 @@
     return accumulated.reshape(leaves * LEAF_ATOMS, channels)
 
 
-def group_sums(moment):
-    groups = lax.axis_size("box") // 8
-    position = lax.axis_index("box")
-    group_id = position // 8
-    onehot = (jnp.arange(groups, dtype=jnp.int32) == group_id).astype(jnp.float32)
-    placed = onehot[:, None, None] * moment[None]
-    return lax.psum(placed, "box")
-
-
 def on_device(
     positions,
     leaf_centers,
@@ -110,16 +102,16 @@
     far_list,
 ):
     atom_num = positions.shape[1]
-    groups = lax.axis_size("box") // 8
-    group_id = lax.axis_index("box") // 8
+    groups = lax.axis_size("grp")
+    group_id = lax.axis_index("grp")
     slot_ids = jnp.arange(LEAF_ATOMS, dtype=jnp.int32)
     mask_f = (slot_ids[None, :] < atom_counts[:, None]).astype(jnp.float32).reshape(atom_num)
     hidden_t = (
         jnp.einsum("ic,ai->ca", msg_weight, features, preferred_element_type=jnp.float32)
         * mask_f[None, :]
     )
-    pos_ext = extended(positions, (("box", 1),), atom_num)
-    hid_ext = extended(hidden_t.astype(jnp.bfloat16), (("box", 1),), atom_num).astype(jnp.float32)
+    pos_ext = extended(positions, ((BOX, 1),), atom_num)
+    hid_ext = extended(hidden_t.astype(jnp.bfloat16), ((BOX, 1),), atom_num).astype(jnp.float32)
 
     def near_part(own, ext, feat_ext):
         return near_field(own, ext, feat_ext, pair_target, pair_source, pair_live)
@@ -132,7 +124,6 @@
 
     basis_val, basis_back = jax.vjp(far_basis, positions)
     moment = jnp.einsum("ka,ca->kc", basis_val, hidden_t, precision=PRECISE)
-    group_tab = group_sums(moment)
     counts_mat = jnp.sum(
         (far_list[:, :, None] == jnp.arange(groups, dtype=jnp.int32)[None, None, :]).astype(
             jnp.float32
@@ -140,8 +131,12 @@
         axis=1,
     )
     row_weights = lax.dynamic_index_in_dim(counts_mat, group_id, 0, keepdims=False)
-    gathered = jnp.einsum("j,jkc->kc", row_weights, group_tab, precision=PRECISE)
-    local_exp = jnp.dot(trans_weight, gathered, precision=PRECISE)
+    col_weights = lax.dynamic_index_in_dim(counts_mat, group_id, 1, keepdims=False)
+    moment_part = lax.psum_scatter(moment, "sub", scatter_dimension=1, tiled=True)
+    moment_tab = lax.all_gather(moment_part, "grp", axis=0)
+    gathered_part = jnp.einsum("j,jkc->kc", row_weights, moment_tab, precision=PRECISE)
+    local_part = jnp.dot(trans_weight, gathered_part, precision=PRECISE)
+    local_exp = lax.all_gather(local_part, "sub", axis=1, tiled=True)
     potential = jnp.einsum("ka,kc->ac", basis_val, local_exp, precision=PRECISE)
     pre_act = near_val + potential
     sigma = jax.nn.sigmoid(pre_act)
@@ -151,19 +146,20 @@
     grad_read_part = jnp.dot(mask_f, activ, precision=PRECISE)
     d_local = jnp.dot(basis_val, d_pre, precision=PRECISE)
     d_basis = jnp.einsum("kc,ac->ka", local_exp, d_pre, precision=PRECISE)
-    grad_trans_part = jnp.einsum("kc,qc->kq", d_local, gathered, precision=PRECISE)
-    d_gathered = jnp.dot(trans_weight.T, d_local, precision=PRECISE)
-    d_group_tab = group_sums(d_gathered)
-    col_weights = lax.dynamic_index_in_dim(counts_mat, group_id, 1, keepdims=False)
-    d_moment = jnp.einsum("b,bkc->kc", col_weights, d_group_tab, precision=PRECISE)
+    d_local_part = lax.psum_scatter(d_local, "sub", scatter_dimension=1, tiled=True)
+    grad_trans_part = jnp.einsum("kc,qc->kq", d_local_part, gathered_part, precision=PRECISE)
+    d_gathered_part = jnp.dot(trans_weight.T, d_local_part, precision=PRECISE)
+    d_tab = lax.all_gather(d_gathered_part, "grp", axis=0)
+    d_moment_part = jnp.einsum("b,bkc->kc", col_weights, d_tab, precision=PRECISE)
+    d_moment = lax.all_gather(d_moment_part, "sub", axis=1, tiled=True)
     d_basis = d_basis + jnp.dot(d_moment, hidden_t, precision=PRECISE)
     d_hidden_far = jnp.einsum("ka,kc->ca", basis_val, d_moment, precision=PRECISE)
     (d_far_pos,) = basis_back(d_basis)
     d_own, d_ext, d_feat_ext = near_back(d_pre)
-    low_pos, low_feat = passed_along((d_ext[:, :atom_num], d_feat_ext[:, :atom_num]), "box", -1)
+    low_pos, low_feat = passed_along((d_ext[:, :atom_num], d_feat_ext[:, :atom_num]), BOX, -1)
     high_pos, high_feat = (
-        passed_along(d_ext[:, 2 * atom_num :].astype(jnp.bfloat16), "box", 1).astype(jnp.float32),
-        passed_along(d_feat_ext[:, 2 * atom_num :].astype(jnp.bfloat16), "box", 1).astype(
+        passed_along(d_ext[:, 2 * atom_num :].astype(jnp.bfloat16), BOX, 1).astype(jnp.float32),
+        passed_along(d_feat_ext[:, 2 * atom_num :].astype(jnp.bfloat16), BOX, 1).astype(
             jnp.float32
         ),
     )
@@ -174,29 +170,30 @@
         "ai,ca->ic", features.astype(jnp.float32), d_hidden_t, precision=PRECISE
     )
     grad_msg, grad_trans, grad_read = lax.psum(
-        (grad_msg_part, grad_trans_part, grad_read_part), "box"
+        (grad_msg_part, grad_trans_part, grad_read_part), BOX
     )
     forces = -(d_own + d_ext[:, atom_num : 2 * atom_num] + low_pos + high_pos + d_far_pos)
     return (atom_energy, forces, grad_msg, grad_trans, grad_read)
 
 
 def solution(mesh):
+    split = Mesh(mesh.devices.reshape(-1, 8), ("grp", "sub"))
     return jax.shard_map(
         on_device,
-        mesh=mesh,
+        mesh=split,
         in_specs=(
-            P(None, "box"),
-            P(None, "box"),
-            P("box"),
-            P("box", None),
+            P(None, BOX),
+            P(None, BOX),
+            P(BOX),
+            P(BOX, None),
             P(),
             P(),
             P(),
-            P("box"),
-            P("box"),
-            P("box"),
+            P(BOX),
+            P(BOX),
+            P(BOX),
             P(),
         ),
-        out_specs=(P("box"), P(None, "box"), P(), P(), P()),
+        out_specs=(P(BOX), P(None, BOX), P(), P(), P()),
         check_vma=False,
     )

time: 913 us -> 909 us (level)
  waiting for transfers between devices: 677 us -> 206 us
  blocking collectives: 109 us -> 578 us
    psum x3 -> x1, waiting for transfers between devices: 677 us -> 164 us  [on_device(): lax.psum((grad_msg_part, grad_trans_part, grad_read_part), BOX)]
    all_gather x0 -> x4, blocking collectives: none -> 474 us  [the longest x1 198 us: on_device(): moment_tab = lax.all_gather(moment_part, 'grp', axis=0)]
    reduce_scatter x0 -> x2, waiting for transfers between devices: none -> 42.6 us  [the longest x1 42.5 us: on_device(): lax.psum_scatter(moment, 'sub', scatter_dimension=1, tiled=True)]
  transfers between devices with their start and end apart: 11 -> 11, of which waited for: 3 -> 2; matrix products, arithmetic and copies ran while one was open for 3% -> 7% of each run, Pallas kernels for 0% -> 0%
where the time goes in v1:
time: 909 us; the launch traced here: 908 us
  blocking collectives  578 us (64%)
  waiting for transfers between devices  206 us (23%)
  matrix products  34.5 us (4%)
  other arithmetic  27 us (3%)
  starting transfers between devices  25.7 us (3%)
  local copies, waits for them, and re-layouts  20.9 us (2%)
  between operations  14.2 us (2%)
    all_gather x1, blocking collectives, on_device(): moment_tab = lax.all_gather(moment_part, 'grp', axis=0)  198 us
    all_gather x1, blocking collectives, on_device(): d_tab = lax.all_gather(d_gathered_part, 'grp', axis=0)  189 us
    psum x1, waiting for transfers between devices, on_device(): lax.psum((grad_msg_part, grad_trans_part, grad_read_part), BOX)  164 us
    psum x1, blocking collectives, on_device(): lax.psum((grad_msg_part, grad_trans_part, grad_read_part), BOX)  104 us
    all_gather x1, blocking collectives, on_device(): d_moment = lax.all_gather(d_moment_part, 'sub', axis=1, tiled=True)  44.5 us
    all_gather x1, blocking collectives, on_device(): local_exp = lax.all_gather(local_part, 'sub', axis=1, tiled=True)  42.8 us
    reduce_scatter x1, waiting for transfers between devices, on_device(): lax.psum_scatter(moment, 'sub', scatter_dimension=1, tiled=True)  42.5 us
    dot_general x12, matrix products, one_block(): jnp.einsum('pij,cpj->pic', kernel, source_feat, preferred_element_type=jn...  20.6 us
  transfers between devices with their start and end apart: 11, of which 2 were waited for; matrix products, arithmetic and copies ran while one was open for 7% of the time, Pallas kernels for 0%

profile of v1, /device:TPU:1, one launch (start us, length us, event | category | flops | bytes accessed | tf_op | source)
XLA Modules:
  0.0 908.0 jit_solution(2307941957308536601)
XLA Ops:
  7.3 8.7 collective-permute-start.1
  16.0 1.9 collective-permute-start
  18.0 0.7 iota_compare_fusion.2
  18.8 1.0 fusion.113
  19.7 2.4 collective-permute-start.3
  22.1 3.2 collective-permute-start.2
  25.3 0.8 broadcast_in_dim.73
  26.2 0.7 subtract_multiply_fusion.3
  27.0 0.9 fusion.114
  28.0 0.8 copy.112
  30.1 42.5 %reduce-scatter.3.cloned.1.call-done = f32[35,16]{0,1:T(8,128)} async-done(((f32[35,128]{0,1:T(8,128)}), f32[35,16]{0,1:T(8,128)}) %reduce-scatter.3.cloned.1.call-update) | async-done | bytes 2256 | tf_op jit(solution)/shard_map/reduce_scatter | solution.py:135
  72.6 197.6 %all-gather.2 = f32[64,35,16]{1,2,0:T(8,128)S(1)} all-gather(f32[1,35,16]{1,2,0:T(8,128)} %bitcast.213), channel_id=2, replica_groups=mesh['grp'=64,'sub'=8] {'grp'}, dimensions={0}, use_global_device_ids=true | all-gather | bytes 145600 | tf_op jit(solution)/shard_map/all_gather | solution.py:136
  270.6 42.8 %all_gather.20 = f32[35,128]{0,1:T(8,128)S(1)} all-gather(f32[35,16]{0,1:T(8,128)S(1)} %convolution_bitcast_fusion.2), channel_id=1, replica_groups=mesh['grp'=64,'sub'=8] {'sub'}, dimensions={1}, use_global_device_ids=true | all-gather | bytes 20160 | tf_op jit(solution)/shard_map/all_gather | solution.py:139
  313.6 18.3 %while.33 = (s32[]{:T(128)}, f32[4,64,128]{2,0,1:T(4,128)S(1)}, s32[4,27]{1,0:T(4,128)S(1)}, f32[3,4,64]{2,0,1:T(4,128)S(1)}, s32[4,27]{1,0:T(4,128)S(1)}, /*ind...) while((s32[]{:T(128)}, f32[4,64,128]{2,0,1:T(4,128)S(1)}, ...), condition=%wide.region_1.2_spmd.clone, body=%wide.region_0.1_spmd.clone.sunk | while | flops 40212804 | bytes 3658967 | solution.py:87
  315.1 0.6 gather_fusion.3
  315.7 1.4 fusion.178
  317.1 1.1 convolution_add_fusion.4
  319.6 0.6 gather_fusion.3
  320.3 1.4 fusion.178
  321.6 1.1 convolution_add_fusion.4
  324.2 0.6 gather_fusion.3
  324.9 1.4 fusion.178
  326.2 1.1 convolution_add_fusion.4
  328.8 0.6 gather_fusion.3
  329.4 1.4 fusion.178
  330.8 1.1 convolution_add_fusion.4
  332.7 1.0 fusion.116
  334.7 50.5 %while.32 = (s32[]{:T(128)}, f32[3,4,64]{2,0,1:T(4,128)S(1)}, f32[3,12,64]{2,0,1:T(4,128)S(1)}, f32[128,12,64]{0,2,1:T(8,128)S(1)}, f32[4,64,128]{2,0,1:T(4,128)...) while((s32[]{:T(128)}, f32[3,4,64]{2,0,1:T(4,128)S(1)}, ...), condition=%wide.region_14.15_spmd.clone, body=%wide.region_4.14_spmd.clone.sunk | while | flops 71802528 | bytes 7040317 | solution.py:87
  336.2 0.6 gather_fusion.2
  336.9 0.7 fusion.168
  337.6 2.0 fusion.169
  339.7 1.7 scatter_fusion
  341.6 1.7 scatter_fusion.1
  343.3 1.8 fusion.170
  345.1 2.2 scatter_fusion.2
  349.5 0.7 fusion.168
  350.2 2.0 fusion.169
  352.3 1.7 scatter_fusion
  354.2 1.7 scatter_fusion.1
  355.9 1.8 fusion.170
  357.7 2.2 scatter_fusion.2
  362.1 0.7 fusion.168
  362.8 2.0 fusion.169
  364.9 1.7 scatter_fusion
  366.8 1.7 scatter_fusion.1
  368.6 1.8 fusion.170
  370.4 2.2 scatter_fusion.2
  374.7 0.7 fusion.168
  375.5 2.0 fusion.169
  377.6 1.7 scatter_fusion
  379.5 1.7 scatter_fusion.1
  381.2 1.8 fusion.170
  383.0 2.2 scatter_fusion.2
  385.7 1.9 collective-permute-start.5
  387.6 2.4 collective-permute-start.4
  390.2 3.2 collective-permute-start.7
  393.5 1.9 collective-permute-start.6
  395.5 0.9 convolution_bitcast_fusion.1
  396.4 188.7 %all-gather.3 = f32[64,35,16]{1,2,0:T(8,128)S(1)} all-gather(f32[1,35,16]{1,2,0:T(8,128)S(1)} %convolution_bitcast_fusion.1), channel_id=3, replica_groups=mesh['grp'=64,'sub'=8] {'grp'}, dimensions={0}, use_global_device_ids=true | all-gather | bytes 145600 | tf_op jit(solution)/shard_map/all_gather | solution.py:152
  585.2 44.5 %all_gather.23 = f32[35,128]{0,1:T(8,128)S(1)} all-gather(f32[35,16]{0,1:T(8,128)S(1)} %multiply_reduce_fusion), channel_id=1, replica_groups=mesh['grp'=64,'sub'=8] {'sub'}, dimensions={1}, use_global_device_ids=true | all-gather | bytes 20160 | tf_op jit(solution)/shard_map/all_gather | solution.py:154
  630.6 0.8 convolution_bitcast_fusion
  632.1 104.3 %all-reduce.9 = (f32[35,35]{1,0:T(8,128)}, f32[128]{0:T(128)}) all-reduce(f32[35,35]{1,0:T(8,128)S(1)} %fusion.118, f32[128]{0:T(128)S(1)} %convolution_bitcast_fusion.3), channel_id=1, replica_groups=mesh['grp'=64,'sub'=8] {'grp','sub'}, use_global_device_ids=true, to_apply=%region_17.18 | all-reduce | flops 1353 | bytes 10824 | tf_op jit(solution)/shard_map/psum | solution.py:172
  736.4 163.5 %all-reduce.12.cloned.1.call-done = f32[128,128]{0,1:T(8,128)} async-done(((f32[128,128]{0,1:T(8,128)}), f32[128,128]{0,1:T(8,128)}) %all-reduce.12.cloned.1.call-update) | async-done | bytes 65552 | tf_op jit(solution)/shard_map/psum | solution.py:172
  899.9 1.6 copy.121
  (270 shorter events, 19.5 us)
Async XLA Ops:
  7.2 11.6 %copy-start = (bf16[256,128]{1,0:T(8,128)(2,1)S(1)}, bf16[256,128]{1,0:T(8,128)(2,1)}, u32[]{:S(2)}) copy-start(bf16[256,128]{1,0:T(8,128)(2,1)} %param.18) | copy-start | bytes 196612
  7.2 22.1 %copy-start.2 = (f32[3,256]{1,0:T(4,128)S(1)}, f32[3,256]{1,0:T(4,128)}, u32[]{:S(2)}) copy-start(f32[3,256]{1,0:T(4,128)} %param.15) | copy-start | bytes 9220
  7.2 22.3 %copy-start.4 = (s32[108]{0:T(128)S(1)}, s32[108]{0:T(128)}, u32[]{:S(2)}) copy-start(s32[108]{0:T(128)} %param.22) | copy-start | bytes 1300
  7.2 22.4 %copy-start.5 = (s32[108]{0:T(128)S(1)}, s32[108]{0:T(128)}, u32[]{:S(2)}) copy-start(s32[108]{0:T(128)} %param.23) | copy-start | bytes 1300
  7.2 22.5 %copy-start.6 = (s32[108]{0:T(128)S(1)}, s32[108]{0:T(128)}, u32[]{:S(2)}) copy-start(s32[108]{0:T(128)} %param.24) | copy-start | bytes 1300
  7.2 65.4 %reduce-scatter.3.cloned.1.call-start = ((), (), s32[]{:S(2)}) async-start(), calls=%async_computation.2 | async-start | bytes 73728 | tf_op jit(solution)/shard_map/reduce_scatter | solution.py:135
  7.3 22.7 %collective-permute-start.1 = (f32[3,256]{1,0:T(4,128)}, f32[3,256]{1,0:T(4,128)S(1)}, u32[]{:S(2)}, u32[]{:S(2)}) collective-permute-start(f32[3,256]{1,0:T(4,128)} %param.15), channel_id=1, source_target_pairs={{1,0},{2,1},{3,2},{4,3},{5,4},{6,5},{7,6},{8,7},{9,8},{10,9},{11,1... | collective-permute-start | bytes 9224 | tf_op jit(solution)/shard_map/ppermute | solution.py:31
  16.0 13.9 %collective-permute-start = (f32[3,256]{1,0:T(4,128)}, f32[3,256]{1,0:T(4,128)S(1)}, u32[]{:S(2)}, u32[]{:S(2)}) collective-permute-start(f32[3,256]{1,0:T(4,128)} %param.15), channel_id=1, source_target_pairs={{0,1},{1,2},{2,3},{3,4},{4,5},{5,6},{6,7},{7,8},{8,9},{9,10},{10,1... | collective-permute-start | bytes 9224 | tf_op jit(solution)/shard_map/ppermute | solution.py:28
  19.7 293.6 %collective-permute-start.3 = (bf16[128,256]{1,0:T(8,128)(2,1)S(1)}, bf16[128,256]{1,0:T(8,128)(2,1)S(1)}, u32[]{:S(2)}, u32[]{:S(2)}) collective-permute-start(bf16[128,256]{1,0:T(8,128)(2,1)S(1)} %get-tuple-element.597), channel_id=1, source_target_pairs={{1,0},{2,1},{3,2},{4,3},{5,4},{6,5},{7,6},{8,7},{9,8},{10,9},{11,1... | collective-permute-start | bytes 196616 | tf_op jit(solution)/shard_map/ppermute | solution.py:31
  22.1 291.3 %collective-permute-start.2 = (bf16[128,256]{1,0:T(8,128)(2,1)S(1)}, bf16[128,256]{1,0:T(8,128)(2,1)S(1)}, u32[]{:S(2)}, u32[]{:S(2)}) collective-permute-start(bf16[128,256]{1,0:T(8,128)(2,1)S(1)} %get-tuple-element.597), channel_id=1, source_target_pairs={{0,1},{1,2},{2,3},{3,4},{4,5},{5,6},{6,7},{7,8},{8,9},{9,10},{10,1... | collective-permute-start | bytes 196616 | tf_op jit(solution)/shard_map/ppermute | solution.py:28
  27.0 243.4 %copy-start.1 = (f32[35,35]{1,0:T(8,128)S(1)}, f32[35,35]{1,0:T(8,128)}, u32[]{:S(2)}) copy-start(f32[35,35]{1,0:T(8,128)} %param.20) | copy-start | bytes 14704
  28.0 367.5 %reduce-scatter.5.cloned.1.call-start = ((), (), s32[]{:S(2)}) async-start(), calls=%async_computation.3 | async-start | bytes 73728 | tf_op jit(solution)/shard_map/reduce_scatter | solution.py:149
  313.6 18.4 %copy-start.7 = (f32[128]{0:T(128)S(1)}, f32[128]{0:T(128)}, u32[]{:S(2)}) copy-start(f32[128]{0:T(128)} %param.21) | copy-start | bytes 1540
  334.5 565.4 %all-reduce.12.cloned.1.call-start = ((), (), s32[]{:S(2)}) async-start(), calls=%async_computation.4 | async-start | bytes 131072 | tf_op jit(solution)/shard_map/psum | solution.py:172
  385.7 245.8 %collective-permute-start.5 = (bf16[3,256]{1,0:T(4,128)(2,1)S(1)}, bf16[3,256]{1,0:T(4,128)(2,1)S(1)}, u32[]{:S(2)}, u32[]{:S(2)}) collective-permute-start(bf16[3,256]{1,0:T(4,128)(2,1)S(1)} %slice.228), channel_id=1, source_target_pairs={{0,1},{1,2},{2,3},{3,4},{4,5},{5,6},{6,7},{7,8},{8,9},{9,10},{10,1... | collective-permute-start | bytes 4616 | tf_op jit(solution)/shard_map/ppermute | solution.py:39
  387.6 243.9 %collective-permute-start.4 = (f32[3,256]{1,0:T(4,128)S(1)}, f32[3,256]{1,0:T(4,128)S(1)}, u32[]{:S(2)}, u32[]{:S(2)}) collective-permute-start(f32[3,256]{1,0:T(4,128)S(1)} %slice.151), channel_id=1, source_target_pairs={{1,0},{2,1},{3,2},{4,3},{5,4},{6,5},{7,6},{8,7},{9,8},{10,9},{11,1... | collective-permute-start | bytes 9224 | tf_op jit(solution)/shard_map/ppermute | solution.py:39
  390.2 240.4 %collective-permute-start.7 = (bf16[128,256]{1,0:T(8,128)(2,1)S(1)}, bf16[128,256]{1,0:T(8,128)(2,1)S(1)}, u32[]{:S(2)}, u32[]{:S(2)}) collective-permute-start(bf16[128,256]{1,0:T(8,128)(2,1)S(1)} %copy.145), channel_id=1, source_target_pairs={{0,1},{1,2},{2,3},{3,4},{4,5},{5,6},{6,7},{7,8},{8,9},{9,10},{10,1... | collective-permute-start | bytes 196616 | tf_op jit(solution)/shard_map/ppermute | solution.py:39
  393.5 237.1 %collective-permute-start.6 = (f32[128,256]{1,0:T(8,128)S(1)}, f32[128,256]{1,0:T(8,128)S(1)}, u32[]{:S(2)}, u32[]{:S(2)}) collective-permute-start(f32[128,256]{1,0:T(8,128)S(1)} %copy.144), channel_id=1, source_target_pairs={{1,0},{2,1},{3,2},{4,3},{5,4},{6,5},{7,6},{8,7},{9,8},{10,9},{11,1... | collective-permute-start | bytes 393224 | tf_op jit(solution)/shard_map/ppermute | solution.py:39
  395.5 234.9 %copy-start.3 = (f32[35,16]{0,1:T(8,128)S(1)}, f32[35,16]{0,1:T(8,128)}, u32[]{:S(2)}) copy-start(f32[35,16]{0,1:T(8,128)} %reduce-scatter.5.cloned.1.call-done) | copy-start | bytes 6724
Sparse Core Ops, SparseCore 0:
  28.1 44.5 reduce-scatter.2
  334.7 26.8 reduce-scatter.4
  631.6 268.2 all-reduce.11

commit v2 on v0

--- a/solution.py
+++ b/solution.py
@@ -87,13 +87,38 @@
     return accumulated.reshape(leaves * LEAF_ATOMS, channels)
 
 
-def group_sums(moment):
-    groups = lax.axis_size("box") // 8
-    position = lax.axis_index("box")
-    group_id = position // 8
-    onehot = (jnp.arange(groups, dtype=jnp.int32) == group_id).astype(jnp.float32)
-    placed = onehot[:, None, None] * moment[None]
-    return lax.psum(placed, "box")
+def xor_swap(block, bit):
+    count = lax.axis_size("box")
+    return lax.ppermute(block, "box", [(i, i ^ (1 << bit)) for i in range(count)])
+
+
+def tree_sum(block, bits):
+    for bit in bits:
+        block = block + xor_swap(block, bit)
+    return block
+
+
+def split_sum(block, index, bits):
+    for bit in bits:
+        half = block.shape[1] // 2
+        lower, upper = block[:, :half], block[:, half:]
+        up = ((index >> bit) & 1) == 1
+        keep = jnp.where(up, upper, lower)
+        send = jnp.where(up, lower, upper)
+        block = keep + xor_swap(send, bit)
+    return block
+
+
+def tree_gather(block, index, bits, axis):
+    for bit in bits:
+        other = xor_swap(block, bit)
+        up = ((index >> bit) & 1) == 1
+        block = jnp.where(
+            up,
+            jnp.concatenate([other, block], axis=axis),
+            jnp.concatenate([block, other], axis=axis),
+        )
+    return block
 
 
 def on_device(
@@ -110,8 +135,12 @@
     far_list,
 ):
     atom_num = positions.shape[1]
+    all_bits = lax.axis_size("box").bit_length() - 1
+    sub_bits = tuple(range(3))
+    grp_bits = tuple(range(3, all_bits))
+    index = lax.axis_index("box")
     groups = lax.axis_size("box") // 8
-    group_id = lax.axis_index("box") // 8
+    group_id = index // 8
     slot_ids = jnp.arange(LEAF_ATOMS, dtype=jnp.int32)
     mask_f = (slot_ids[None, :] < atom_counts[:, None]).astype(jnp.float32).reshape(atom_num)
     hidden_t = (
@@ -132,7 +161,6 @@
 
     basis_val, basis_back = jax.vjp(far_basis, positions)
     moment = jnp.einsum("ka,ca->kc", basis_val, hidden_t, precision=PRECISE)
-    group_tab = group_sums(moment)
     counts_mat = jnp.sum(
         (far_list[:, :, None] == jnp.arange(groups, dtype=jnp.int32)[None, None, :]).astype(
             jnp.float32
@@ -140,8 +168,12 @@
         axis=1,
     )
     row_weights = lax.dynamic_index_in_dim(counts_mat, group_id, 0, keepdims=False)
-    gathered = jnp.einsum("j,jkc->kc", row_weights, group_tab, precision=PRECISE)
-    local_exp = jnp.dot(trans_weight, gathered, precision=PRECISE)
+    col_weights = lax.dynamic_index_in_dim(counts_mat, group_id, 1, keepdims=False)
+    moment_part = split_sum(moment, index, sub_bits[::-1])
+    moment_tab = tree_gather(moment_part[None], index, grp_bits, 0)
+    gathered_part = jnp.einsum("j,jkc->kc", row_weights, moment_tab, precision=PRECISE)
+    local_part = jnp.dot(trans_weight, gathered_part, precision=PRECISE)
+    local_exp = tree_gather(local_part, index, sub_bits, 1)
     potential = jnp.einsum("ka,kc->ac", basis_val, local_exp, precision=PRECISE)
     pre_act = near_val + potential
     sigma = jax.nn.sigmoid(pre_act)
@@ -151,11 +183,12 @@
     grad_read_part = jnp.dot(mask_f, activ, precision=PRECISE)
     d_local = jnp.dot(basis_val, d_pre, precision=PRECISE)
     d_basis = jnp.einsum("kc,ac->ka", local_exp, d_pre, precision=PRECISE)
-    grad_trans_part = jnp.einsum("kc,qc->kq", d_local, gathered, precision=PRECISE)
-    d_gathered = jnp.dot(trans_weight.T, d_local, precision=PRECISE)
-    d_group_tab = group_sums(d_gathered)
-    col_weights = lax.dynamic_index_in_dim(counts_mat, group_id, 1, keepdims=False)
-    d_moment = jnp.einsum("b,bkc->kc", col_weights, d_group_tab, precision=PRECISE)
+    d_local_part = split_sum(d_local, index, sub_bits[::-1])
+    grad_trans_part = jnp.einsum("kc,qc->kq", d_local_part, gathered_part, precision=PRECISE)
+    d_gathered_part = jnp.dot(trans_weight.T, d_local_part, precision=PRECISE)
+    d_tab = tree_gather(d_gathered_part[None], index, grp_bits, 0)
+    d_moment_part = jnp.einsum("b,bkc->kc", col_weights, d_tab, precision=PRECISE)
+    d_moment = tree_gather(d_moment_part, index, sub_bits, 1)
     d_basis = d_basis + jnp.dot(d_moment, hidden_t, precision=PRECISE)
     d_hidden_far = jnp.einsum("ka,kc->ca", basis_val, d_moment, precision=PRECISE)
     (d_far_pos,) = basis_back(d_basis)
@@ -173,9 +206,14 @@
     grad_msg_part = jnp.einsum(
         "ai,ca->ic", features.astype(jnp.float32), d_hidden_t, precision=PRECISE
     )
-    grad_msg, grad_trans, grad_read = lax.psum(
-        (grad_msg_part, grad_trans_part, grad_read_part), "box"
-    )
+    flat = jnp.concatenate(
+        [grad_msg_part.reshape(-1), grad_trans_part.reshape(-1), grad_read_part.reshape(-1)]
+    )
+    flat = tree_sum(flat, tuple(range(all_bits)))
+    msg_size, trans_size = grad_msg_part.size, grad_trans_part.size
+    grad_msg = flat[:msg_size].reshape(grad_msg_part.shape)
+    grad_trans = flat[msg_size : msg_size + trans_size].reshape(grad_trans_part.shape)
+    grad_read = flat[msg_size + trans_size :]
     forces = -(d_own + d_ext[:, atom_num : 2 * atom_num] + low_pos + high_pos + d_far_pos)
     return (atom_energy, forces, grad_msg, grad_trans, grad_read)
 

time: 913 us -> 332 us (0.36)
  the two profiles are of different devices: /device:TPU:1 before, /device:TPU:16 now
where the time goes in v2:
time: 332 us; the launch traced here: 331 us
  starting transfers between devices  154 us (46%)
  waiting for transfers between devices  88.8 us (27%)
  matrix products  34.2 us (10%)
  other arithmetic  28.3 us (9%)
  local copies, waits for them, and re-layouts  22.2 us (7%)
    ppermute x33, starting transfers between devices, xor_swap(): return lax.ppermute(block, 'box', [(i, i ^ 1 << bit) for i in range(count)])  118 us
    ppermute x33, waiting for transfers between devices, xor_swap(): return lax.ppermute(block, 'box', [(i, i ^ 1 << bit) for i in range(count)])  88.8 us
    dot_general x12, matrix products, one_block(): jnp.einsum('pij,cpj->pic', kernel, source_feat, preferred_element_type=jn...  20.6 us
    ppermute x4, starting transfers between devices, passed_along(): return lax.ppermute(block, axis, route)  19.6 us
    ppermute x2, starting transfers between devices, extended(): lax.ppermute(lax.slice_in_dim(block, 0, width, axis=dim), axis, backward)  12.9 us
    scatter-add x4, other arithmetic, one_block(): source_feat = feat_leaf[:, src_ids].astype(jnp.bfloat16)  8.98 us
    dot_general x8, matrix products, one_block(): jnp.einsum('tp,pic->tic', onehot, contrib, precision=PRECISE)  7.35 us
    scatter-add x4, other arithmetic, one_block(): near_pos = own_leaf[:, tgt_ids]  6.99 us
  transfers between devices with their start and end apart: 41, of which 28 were waited for; matrix products, arithmetic and copies ran while one was open for 23% of the time, Pallas kernels for 0%

profile of v2, /device:TPU:16, one launch (start us, length us, event | category | flops | bytes accessed | tf_op | source)
XLA Modules:
  0.0 331.1 jit_solution(627876919737552414)
XLA Ops:
  4.6 6.1 %collective-permute-start.4 = (f32[35,64]{1,0:T(8,128)S(1)}, f32[35,64]{1,0:T(8,128)S(1)}, u32[]{:S(2)}, u32[]{:S(2)}) collective-permute-start(f32[35,64]{1,0:T(8,128)S(1)} %slice_select_fusion.5), channel_id=1, source_target_pairs={{0,4},{1,5},{2,6},{3,7},{4,0},{5,1},{6,2},{7,3},{8,12},{9,13},{10,... | collective-permute-start | bytes 26888 | tf_op jit(solution)/shard_map/ppermute | solution.py:92
  12.6 4.3 %collective-permute-start.5 = (f32[35,32]{1,0:T(8,128)S(1)}, f32[35,32]{1,0:T(8,128)S(1)}, u32[]{:S(2)}, u32[]{:S(2)}) collective-permute-start(f32[35,32]{1,0:T(8,128)S(1)} %slice_select_fusion.4), channel_id=1, source_target_pairs={{0,2},{1,3},{2,0},{3,1},{4,6},{5,7},{6,4},{7,5},{8,10},{9,11},{10,... | collective-permute-start | bytes 13448 | tf_op jit(solution)/shard_map/ppermute | solution.py:92
  21.9 9.3 %collective-permute-start.7 = (f32[1,35,16]{2,1,0:T(8,128)S(1)}, f32[1,35,16]{2,1,0:T(8,128)S(1)}, u32[]{:S(2)}, u32[]{:S(2)}) collective-permute-start(f32[1,35,16]{2,1,0:T(8,128)S(1)} %add_bitcast_fusion.2), channel_id=1, source_target_pairs={{0,8},{1,9},{2,10},{3,11},{4,12},{5,13},{6,14},{7,15},{8,0},{9,1},... | collective-permute-start | bytes 6728 | tf_op jit(solution)/shard_map/ppermute | solution.py:92
  33.0 3.4 %collective-permute-start.8 = (f32[2,35,16]{1,2,0:T(8,128)S(1)}, f32[2,35,16]{1,2,0:T(8,128)S(1)}, u32[]{:S(2)}, u32[]{:S(2)}) collective-permute-start(f32[2,35,16]{1,2,0:T(8,128)S(1)} %maximum_select_fusion.14), channel_id=1, source_target_pairs={{0,16},{1,17},{2,18},{3,19},{4,20},{5,21},{6,22},{7,23},{8,24},{9,... | collective-permute-start | bytes 13448 | tf_op jit(solution)/shard_map/ppermute | solution.py:92
  36.4 2.2 collective-permute-done.8
  38.7 4.9 %collective-permute-start.9 = (f32[4,35,16]{1,2,0:T(8,128)S(1)}, f32[4,35,16]{1,2,0:T(8,128)S(1)}, u32[]{:S(2)}, u32[]{:S(2)}) collective-permute-start(f32[4,35,16]{1,2,0:T(8,128)S(1)} %maximum_select_fusion.8), channel_id=1, source_target_pairs={{0,32},{1,33},{2,34},{3,35},{4,36},{5,37},{6,38},{7,39},{8,40},{9,... | collective-permute-start | bytes 26888 | tf_op jit(solution)/shard_map/ppermute | solution.py:92
  43.6 2.4 collective-permute-done.9
  46.0 3.5 %collective-permute-start.10 = (f32[8,35,16]{1,2,0:T(8,128)S(1)}, f32[8,35,16]{1,2,0:T(8,128)S(1)}, u32[]{:S(2)}, u32[]{:S(2)}) collective-permute-start(f32[8,35,16]{1,2,0:T(8,128)S(1)} %maximum_select_fusion.6), channel_id=1, source_target_pairs={{0,64},{1,65},{2,66},{3,67},{4,68},{5,69},{6,70},{7,71},{8,72},{9,... | collective-permute-start | bytes 53768 | tf_op jit(solution)/shard_map/ppermute | solution.py:92
  49.5 2.7 collective-permute-done.10
  52.1 4.5 %collective-permute-start.11 = (f32[16,35,16]{1,2,0:T(8,128)S(1)}, f32[16,35,16]{1,2,0:T(8,128)S(1)}, u32[]{:S(2)}, u32[]{:S(2)}) collective-permute-start(f32[16,35,16]{1,2,0:T(8,128)S(1)} %maximum_select_fusion.4), channel_id=1, source_target_pairs={{0,128},{1,129},{2,130},{3,131},{4,132},{5,133},{6,134},{7,135},{8... | collective-permute-start | bytes 107528 | tf_op jit(solution)/shard_map/ppermute | solution.py:92
  56.7 5.0 %collective-permute-start.1 = (f32[3,256]{1,0:T(4,128)S(1)}, f32[3,256]{1,0:T(4,128)S(1)}, u32[]{:S(2)}, u32[]{:S(2)}) collective-permute-start(f32[3,256]{1,0:T(4,128)S(1)} %copy-done.2), channel_id=1, source_target_pairs={{1,0},{2,1},{3,2},{4,3},{5,4},{6,5},{7,6},{8,7},{9,8},{10,9},{11,1... | collective-permute-start | bytes 9224 | tf_op jit(solution)/shard_map/ppermute | solution.py:30
  61.7 1.9 collective-permute-start
  63.6 7.9 %collective-permute-start.3 = (bf16[128,256]{1,0:T(8,128)(2,1)S(1)}, bf16[128,256]{1,0:T(8,128)(2,1)S(1)}, u32[]{:S(2)}, u32[]{:S(2)}) collective-permute-start(bf16[128,256]{1,0:T(8,128)(2,1)S(1)} %get-tuple-element.565), channel_id=1, source_target_pairs={{1,0},{2,1},{3,2},{4,3},{5,4},{6,5},{7,6},{8,7},{9,8},{10,9},{11,1... | collective-permute-start | bytes 196616 | tf_op jit(solution)/shard_map/ppermute | solution.py:30
  71.5 1.9 collective-permute-start.2
  74.1 5.0 %collective-permute-start.12 = (f32[32,35,16]{1,2,0:T(8,128)S(1)}, f32[32,35,16]{1,2,0:T(8,128)S(1)}, u32[]{:S(2)}, u32[]{:S(2)}) collective-permute-start(f32[32,35,16]{1,2,0:T(8,128)S(1)} %maximum_select_fusion.2), channel_id=1, source_target_pairs={{0,256},{1,257},{2,258},{3,259},{4,260},{5,261},{6,262},{7,263},{8... | collective-permute-start | bytes 215048 | tf_op jit(solution)/shard_map/ppermute | solution.py:92
  79.7 7.3 %collective-permute-done.12 = f32[32,35,16]{1,2,0:T(8,128)S(1)} collective-permute-done((f32[32,35,16]{1,2,0:T(8,128)S(1)}, f32[32,35,16]{1,2,0:T(8,128)S(1)}, u32[]{:S(2)}, u32[]{:S(2)}) %collective-permute-start.12) | collective-permute-done | bytes 71712 | tf_op jit(solution)/shard_map/ppermute | solution.py:92
  88.8 1.9 collective-permute-start.13
  91.9 2.4 collective-permute-start.14
  94.3 3.2 collective-permute-done.14
  97.5 2.9 collective-permute-start.15
  100.5 18.3 %while.33 = (s32[]{:T(128)}, f32[4,64,128]{2,0,1:T(4,128)S(1)}, s32[4,27]{1,0:T(4,128)S(1)}, f32[3,4,64]{2,0,1:T(4,128)S(1)}, s32[4,27]{1,0:T(4,128)S(1)}, /*ind...) while((s32[]{:T(128)}, f32[4,64,128]{2,0,1:T(4,128)S(1)}, ...), condition=%wide.region_1.2_spmd.clone, body=%wide.region_0.1_spmd.clone.sunk | while | flops 40212804 | bytes 3658967 | solution.py:86
  119.7 3.8 %collective-permute-start.18 = (f32[35,64]{1,0:T(8,128)S(1)}, f32[35,64]{1,0:T(8,128)S(1)}, u32[]{:S(2)}, u32[]{:S(2)}) collective-permute-start(f32[35,64]{1,0:T(8,128)S(1)} %slice_select_fusion.2), channel_id=1, source_target_pairs={{0,4},{1,5},{2,6},{3,7},{4,0},{5,1},{6,2},{7,3},{8,12},{9,13},{10,... | collective-permute-start | bytes 26888 | tf_op jit(solution)/shard_map/ppermute | solution.py:92
  123.5 2.8 collective-permute-done.18
  126.4 3.9 %collective-permute-start.19 = (f32[35,32]{1,0:T(8,128)S(1)}, f32[35,32]{1,0:T(8,128)S(1)}, u32[]{:S(2)}, u32[]{:S(2)}) collective-permute-start(f32[35,32]{1,0:T(8,128)S(1)} %slice_select_fusion.1), channel_id=1, source_target_pairs={{0,2},{1,3},{2,0},{3,1},{4,6},{5,7},{6,4},{7,5},{8,10},{9,11},{10,... | collective-permute-start | bytes 13448 | tf_op jit(solution)/shard_map/ppermute | solution.py:92
  135.6 7.0 %collective-permute-start.21 = (f32[1,35,16]{1,2,0:T(8,128)S(1)}, f32[1,35,16]{1,2,0:T(8,128)S(1)}, u32[]{:S(2)}, u32[]{:S(2)}) collective-permute-start(f32[1,35,16]{1,2,0:T(8,128)S(1)} %convolution_bitcast_fusion.1), channel_id=1, source_target_pairs={{0,8},{1,9},{2,10},{3,11},{4,12},{5,13},{6,14},{7,15},{8,0},{9,1},... | collective-permute-start | bytes 6728 | tf_op jit(solution)/shard_map/ppermute | solution.py:92
  142.6 2.5 collective-permute-done.21
  145.1 3.4 %collective-permute-start.22 = (f32[2,35,16]{1,2,0:T(8,128)S(1)}, f32[2,35,16]{1,2,0:T(8,128)S(1)}, u32[]{:S(2)}, u32[]{:S(2)}) collective-permute-start(f32[2,35,16]{1,2,0:T(8,128)S(1)} %maximum_select_fusion.16), channel_id=1, source_target_pairs={{0,16},{1,17},{2,18},{3,19},{4,20},{5,21},{6,22},{7,23},{8,24},{9,... | collective-permute-start | bytes 13448 | tf_op jit(solution)/shard_map/ppermute | solution.py:92
  148.5 2.2 collective-permute-done.22
  150.7 4.9 %collective-permute-start.23 = (f32[4,35,16]{1,2,0:T(8,128)S(1)}, f32[4,35,16]{1,2,0:T(8,128)S(1)}, u32[]{:S(2)}, u32[]{:S(2)}) collective-permute-start(f32[4,35,16]{1,2,0:T(8,128)S(1)} %maximum_select_fusion.10), channel_id=1, source_target_pairs={{0,32},{1,33},{2,34},{3,35},{4,36},{5,37},{6,38},{7,39},{8,40},{9,... | collective-permute-start | bytes 26888 | tf_op jit(solution)/shard_map/ppermute | solution.py:92
  155.6 2.4 collective-permute-done.23
  158.0 2.6 collective-permute-start.24
  160.6 3.6 %collective-permute-done.24 = f32[8,35,16]{1,2,0:T(8,128)S(1)} collective-permute-done((f32[8,35,16]{1,2,0:T(8,128)S(1)}, f32[8,35,16]{1,2,0:T(8,128)S(1)}, u32[]{:S(2)}, u32[]{:S(2)}) %collective-permute-start.24) | collective-permute-done | bytes 17952 | tf_op jit(solution)/shard_map/ppermute | solution.py:92
  164.2 4.7 %collective-permute-start.25 = (f32[16,35,16]{1,2,0:T(8,128)S(1)}, f32[16,35,16]{1,2,0:T(8,128)S(1)}, u32[]{:S(2)}, u32[]{:S(2)}) collective-permute-start(f32[16,35,16]{1,2,0:T(8,128)S(1)} %maximum_select_fusion.5), channel_id=1, source_target_pairs={{0,128},{1,129},{2,130},{3,131},{4,132},{5,133},{6,134},{7,135},{8... | collective-permute-start | bytes 107528 | tf_op jit(solution)/shard_map/ppermute | solution.py:92
  169.2 2.8 collective-permute-done.25
  172.1 8.2 %collective-permute-start.26 = (f32[32,35,16]{1,2,0:T(8,128)S(1)}, f32[32,35,16]{1,2,0:T(8,128)S(1)}, u32[]{:S(2)}, u32[]{:S(2)}) collective-permute-start(f32[32,35,16]{1,2,0:T(8,128)S(1)} %maximum_select_fusion.3), channel_id=1, source_target_pairs={{0,256},{1,257},{2,258},{3,259},{4,260},{5,261},{6,262},{7,263},{8... | collective-permute-start | bytes 215048 | tf_op jit(solution)/shard_map/ppermute | solution.py:92
  180.4 50.5 %while.32 = (s32[]{:T(128)}, f32[3,4,64]{2,0,1:T(4,128)S(1)}, f32[3,12,64]{2,0,1:T(4,128)S(1)}, f32[128,12,64]{0,2,1:T(8,128)S(1)}, f32[4,64,128]{2,0,1:T(4,128)...) while((s32[]{:T(128)}, f32[3,4,64]{2,0,1:T(4,128)S(1)}, ...), condition=%wide.region_13.14_spmd.clone, body=%wide.region_3.13_spmd.clone.sunk | while | flops 71802528 | bytes 7040317 | solution.py:86
  183.2 2.0 fusion.177
  190.7 2.2 scatter_fusion.2
  195.8 2.0 fusion.177
  203.3 2.2 scatter_fusion.2
  208.4 2.0 fusion.177
  216.0 2.2 scatter_fusion.2
  221.0 2.0 fusion.177
  228.6 2.2 scatter_fusion.2
  232.7 1.9 collective-permute-start.27
  235.8 3.9 %collective-permute-start.28 = (f32[35,32]{0,1:T(8,128)S(1)}, f32[35,32]{0,1:T(8,128)S(1)}, u32[]{:S(2)}, u32[]{:S(2)}) collective-permute-start(f32[35,32]{0,1:T(8,128)S(1)} %maximum_select_fusion.17), channel_id=1, source_target_pairs={{0,2},{1,3},{2,0},{3,1},{4,6},{5,7},{6,4},{7,5},{8,10},{9,11},{10,... | collective-permute-start | bytes 13448 | tf_op jit(solution)/shard_map/ppermute | solution.py:92
  240.2 1.9 collective-permute-start.31
  242.2 7.9 %collective-permute-start.30 = (f32[128,256]{1,0:T(8,128)S(1)}, f32[128,256]{1,0:T(8,128)S(1)}, u32[]{:S(2)}, u32[]{:S(2)}) collective-permute-start(f32[128,256]{1,0:T(8,128)S(1)} %copy.202), channel_id=1, source_target_pairs={{1,0},{2,1},{3,2},{4,3},{5,4},{6,5},{7,6},{8,7},{9,8},{10,9},{11,1... | collective-permute-start | bytes 393224 | tf_op jit(solution)/shard_map/ppermute | solution.py:38
  250.1 1.9 collective-permute-start.29
  252.4 4.4 %collective-permute-done.29 = f32[35,64]{0,1:T(8,128)S(1)} collective-permute-done((f32[35,64]{0,1:T(8,128)S(1)}, f32[35,64]{0,1:T(8,128)S(1)}, u32[]{:S(2)}, u32[]{:S(2)}) %collective-permute-start.29) | collective-permute-done | bytes 8992 | tf_op jit(solution)/shard_map/ppermute | solution.py:92
  260.9 1.9 collective-permute-start.33
  263.0 4.1 %collective-permute-done.33 = f32[17737]{0:T(1024)S(1)} collective-permute-done((f32[17737]{0:T(1024)S(1)}, f32[17737]{0:T(1024)S(1)}, u32[]{:S(2)}, u32[]{:S(2)}) %collective-permute-start.33) | collective-permute-done | bytes 70980 | tf_op jit(solution)/shard_map/ppermute | solution.py:92
  267.1 2.2 collective-permute-start.34
  272.0 7.9 %collective-permute-start.16 = (f32[3,256]{1,0:T(4,128)S(1)}, f32[3,256]{1,0:T(4,128)S(1)}, u32[]{:S(2)}, u32[]{:S(2)}) collective-permute-start(f32[3,256]{1,0:T(4,128)S(1)} %slice.217), channel_id=1, source_target_pairs={{1,0},{2,1},{3,2},{4,3},{5,4},{6,5},{7,6},{8,7},{9,8},{10,9},{11,1... | collective-permute-start | bytes 9224 | tf_op jit(solution)/shard_map/ppermute | solution.py:38
  279.9 1.9 collective-permute-start.35
  282.0 8.0 %collective-permute-done.35 = f32[17737]{0:T(1024)S(1)} collective-permute-done((f32[17737]{0:T(1024)S(1)}, f32[17737]{0:T(1024)S(1)}, u32[]{:S(2)}, u32[]{:S(2)}) %collective-permute-start.35) | collective-permute-done | bytes 70980 | tf_op jit(solution)/shard_map/ppermute | solution.py:92
  290.0 1.9 collective-permute-start.36
  292.3 4.0 %collective-permute-done.36 = f32[17737]{0:T(1024)S(1)} collective-permute-done((f32[17737]{0:T(1024)S(1)}, f32[17737]{0:T(1024)S(1)}, u32[]{:S(2)}, u32[]{:S(2)}) %collective-permute-start.36) | collective-permute-done | bytes 70980 | tf_op jit(solution)/shard_map/ppermute | solution.py:92
  298.3 5.8 %collective-permute-done.37 = f32[17737]{0:T(1024)S(1)} collective-permute-done((f32[17737]{0:T(1024)S(1)}, f32[17737]{0:T(1024)S(1)}, u32[]{:S(2)}, u32[]{:S(2)}) %collective-permute-start.37) | collective-permute-done | bytes 70980 | tf_op jit(solution)/shard_map/ppermute | solution.py:92
  306.0 4.9 %collective-permute-done.38 = f32[17737]{0:T(1024)S(1)} collective-permute-done((f32[17737]{0:T(1024)S(1)}, f32[17737]{0:T(1024)S(1)}, u32[]{:S(2)}, u32[]{:S(2)}) %collective-permute-start.38) | collective-permute-done | bytes 70980 | tf_op jit(solution)/shard_map/ppermute | solution.py:92
  310.9 1.9 collective-permute-start.39
  312.9 5.3 %collective-permute-done.39 = f32[17737]{0:T(1024)S(1)} collective-permute-done((f32[17737]{0:T(1024)S(1)}, f32[17737]{0:T(1024)S(1)}, u32[]{:S(2)}, u32[]{:S(2)}) %collective-permute-start.39) | collective-permute-done | bytes 70980 | tf_op jit(solution)/shard_map/ppermute | solution.py:92
  318.2 4.2 %collective-permute-start.40 = (f32[17737]{0:T(1024)S(1)}, f32[17737]{0:T(1024)S(1)}, u32[]{:S(2)}, u32[]{:S(2)}) collective-permute-start(f32[17737]{0:T(1024)S(1)} %add.223), channel_id=1, source_target_pairs={{0,256},{1,257},{2,258},{3,259},{4,260},{5,261},{6,262},{7,263},{8... | collective-permute-start | bytes 212852 | tf_op jit(solution)/shard_map/ppermute | solution.py:92
  323.1 6.1 %collective-permute-done.40 = f32[17737]{0:T(1024)S(1)} collective-permute-done((f32[17737]{0:T(1024)S(1)}, f32[17737]{0:T(1024)S(1)}, u32[]{:S(2)}, u32[]{:S(2)}) %collective-permute-start.40) | collective-permute-done | bytes 70980 | tf_op jit(solution)/shard_map/ppermute | solution.py:92
  (374 shorter events, 91.6 us)
Async XLA Ops:
  0.6 2.5 copy-start
  0.6 56.0 %copy-start.2 = (f32[3,256]{1,0:T(4,128)S(1)}, f32[3,256]{1,0:T(4,128)}, u32[]{:S(2)}) copy-start(f32[3,256]{1,0:T(4,128)} %param.15) | copy-start | bytes 9220
  3.1 70.6 %copy-start.4 = (s32[108]{0:T(128)S(1)}, s32[108]{0:T(128)}, u32[]{:S(2)}) copy-start(s32[108]{0:T(128)} %param.22) | copy-start | bytes 1300
  3.1 70.6 %copy-start.5 = (s32[108]{0:T(128)S(1)}, s32[108]{0:T(128)}, u32[]{:S(2)}) copy-start(s32[108]{0:T(128)} %param.23) | copy-start | bytes 1300
  3.1 70.7 %copy-start.6 = (s32[108]{0:T(128)S(1)}, s32[108]{0:T(128)}, u32[]{:S(2)}) copy-start(s32[108]{0:T(128)} %param.24) | copy-start | bytes 1300
  3.1 70.8 %copy-start.3 = (s32[64,32]{0,1:T(8,128)S(1)}, s32[64,32]{0,1:T(8,128)}, u32[]{:S(2)}) copy-start(s32[64,32]{0,1:T(8,128)} %param.25) | copy-start | bytes 24580
  4.6 7.8 %collective-permute-start.4 = (f32[35,64]{1,0:T(8,128)S(1)}, f32[35,64]{1,0:T(8,128)S(1)}, u32[]{:S(2)}, u32[]{:S(2)}) collective-permute-start(f32[35,64]{1,0:T(8,128)S(1)} %slice_select_fusion.5), channel_id=1, source_target_pairs={{0,4},{1,5},{2,6},{3,7},{4,0},{5,1},{6,2},{7,3},{8,12},{9,13},{10,... | collective-permute-start | bytes 26888 | tf_op jit(solution)/shard_map/ppermute | solution.py:92
  12.6 6.0 %collective-permute-start.5 = (f32[35,32]{1,0:T(8,128)S(1)}, f32[35,32]{1,0:T(8,128)S(1)}, u32[]{:S(2)}, u32[]{:S(2)}) collective-permute-start(f32[35,32]{1,0:T(8,128)S(1)} %slice_select_fusion.4), channel_id=1, source_target_pairs={{0,2},{1,3},{2,0},{3,1},{4,6},{5,7},{6,4},{7,5},{8,10},{9,11},{10,... | collective-permute-start | bytes 13448 | tf_op jit(solution)/shard_map/ppermute | solution.py:92
  18.8 3.1 collective-permute-start.6
  21.9 11.0 %collective-permute-start.7 = (f32[1,35,16]{2,1,0:T(8,128)S(1)}, f32[1,35,16]{2,1,0:T(8,128)S(1)}, u32[]{:S(2)}, u32[]{:S(2)}) collective-permute-start(f32[1,35,16]{2,1,0:T(8,128)S(1)} %add_bitcast_fusion.2), channel_id=1, source_target_pairs={{0,8},{1,9},{2,10},{3,11},{4,12},{5,13},{6,14},{7,15},{8,0},{9,1},... | collective-permute-start | bytes 6728 | tf_op jit(solution)/shard_map/ppermute | solution.py:92
  33.0 5.6 %collective-permute-start.8 = (f32[2,35,16]{1,2,0:T(8,128)S(1)}, f32[2,35,16]{1,2,0:T(8,128)S(1)}, u32[]{:S(2)}, u32[]{:S(2)}) collective-permute-start(f32[2,35,16]{1,2,0:T(8,128)S(1)} %maximum_select_fusion.14), channel_id=1, source_target_pairs={{0,16},{1,17},{2,18},{3,19},{4,20},{5,21},{6,22},{7,23},{8,24},{9,... | collective-permute-start | bytes 13448 | tf_op jit(solution)/shard_map/ppermute | solution.py:92
  38.7 7.3 %collective-permute-start.9 = (f32[4,35,16]{1,2,0:T(8,128)S(1)}, f32[4,35,16]{1,2,0:T(8,128)S(1)}, u32[]{:S(2)}, u32[]{:S(2)}) collective-permute-start(f32[4,35,16]{1,2,0:T(8,128)S(1)} %maximum_select_fusion.8), channel_id=1, source_target_pairs={{0,32},{1,33},{2,34},{3,35},{4,36},{5,37},{6,38},{7,39},{8,40},{9,... | collective-permute-start | bytes 26888 | tf_op jit(solution)/shard_map/ppermute | solution.py:92
  46.0 6.2 %collective-permute-start.10 = (f32[8,35,16]{1,2,0:T(8,128)S(1)}, f32[8,35,16]{1,2,0:T(8,128)S(1)}, u32[]{:S(2)}, u32[]{:S(2)}) collective-permute-start(f32[8,35,16]{1,2,0:T(8,128)S(1)} %maximum_select_fusion.6), channel_id=1, source_target_pairs={{0,64},{1,65},{2,66},{3,67},{4,68},{5,69},{6,70},{7,71},{8,72},{9,... | collective-permute-start | bytes 53768 | tf_op jit(solution)/shard_map/ppermute | solution.py:92
  52.1 21.9 %collective-permute-start.11 = (f32[16,35,16]{1,2,0:T(8,128)S(1)}, f32[16,35,16]{1,2,0:T(8,128)S(1)}, u32[]{:S(2)}, u32[]{:S(2)}) collective-permute-start(f32[16,35,16]{1,2,0:T(8,128)S(1)} %maximum_select_fusion.4), channel_id=1, source_target_pairs={{0,128},{1,129},{2,130},{3,131},{4,132},{5,133},{6,134},{7,135},{8... | collective-permute-start | bytes 107528 | tf_op jit(solution)/shard_map/ppermute | solution.py:92
  56.7 34.1 %collective-permute-start.1 = (f32[3,256]{1,0:T(4,128)S(1)}, f32[3,256]{1,0:T(4,128)S(1)}, u32[]{:S(2)}, u32[]{:S(2)}) collective-permute-start(f32[3,256]{1,0:T(4,128)S(1)} %copy-done.2), channel_id=1, source_target_pairs={{1,0},{2,1},{3,2},{4,3},{5,4},{6,5},{7,6},{8,7},{9,8},{10,9},{11,1... | collective-permute-start | bytes 9224 | tf_op jit(solution)/shard_map/ppermute | solution.py:30
  61.7 29.0 %collective-permute-start = (f32[3,256]{1,0:T(4,128)S(1)}, f32[3,256]{1,0:T(4,128)S(1)}, u32[]{:S(2)}, u32[]{:S(2)}) collective-permute-start(f32[3,256]{1,0:T(4,128)S(1)} %copy-done.2), channel_id=1, source_target_pairs={{0,1},{1,2},{2,3},{3,4},{4,5},{5,6},{6,7},{7,8},{8,9},{9,10},{10,1... | collective-permute-start | bytes 9224 | tf_op jit(solution)/shard_map/ppermute | solution.py:27
  63.6 27.2 %collective-permute-start.3 = (bf16[128,256]{1,0:T(8,128)(2,1)S(1)}, bf16[128,256]{1,0:T(8,128)(2,1)S(1)}, u32[]{:S(2)}, u32[]{:S(2)}) collective-permute-start(bf16[128,256]{1,0:T(8,128)(2,1)S(1)} %get-tuple-element.565), channel_id=1, source_target_pairs={{1,0},{2,1},{3,2},{4,3},{5,4},{6,5},{7,6},{8,7},{9,8},{10,9},{11,1... | collective-permute-start | bytes 196616 | tf_op jit(solution)/shard_map/ppermute | solution.py:30
  71.5 19.5 %collective-permute-start.2 = (bf16[128,256]{1,0:T(8,128)(2,1)S(1)}, bf16[128,256]{1,0:T(8,128)(2,1)S(1)}, u32[]{:S(2)}, u32[]{:S(2)}) collective-permute-start(bf16[128,256]{1,0:T(8,128)(2,1)S(1)} %get-tuple-element.565), channel_id=1, source_target_pairs={{0,1},{1,2},{2,3},{3,4},{4,5},{5,6},{6,7},{7,8},{8,9},{9,10},{10,1... | collective-permute-start | bytes 196616 | tf_op jit(solution)/shard_map/ppermute | solution.py:27
  74.1 12.9 %collective-permute-start.12 = (f32[32,35,16]{1,2,0:T(8,128)S(1)}, f32[32,35,16]{1,2,0:T(8,128)S(1)}, u32[]{:S(2)}, u32[]{:S(2)}) collective-permute-start(f32[32,35,16]{1,2,0:T(8,128)S(1)} %maximum_select_fusion.2), channel_id=1, source_target_pairs={{0,256},{1,257},{2,258},{3,259},{4,260},{5,261},{6,262},{7,263},{8... | collective-permute-start | bytes 215048 | tf_op jit(solution)/shard_map/ppermute | solution.py:92
  79.7 8.9 %copy-start.1 = (f32[35,35]{1,0:T(8,128)S(1)}, f32[35,35]{1,0:T(8,128)}, u32[]{:S(2)}) copy-start(f32[35,35]{1,0:T(8,128)} %param.20) | copy-start | bytes 14704
  88.8 3.1 collective-permute-start.13
  91.9 5.6 %collective-permute-start.14 = (f32[35,32]{0,1:T(8,128)S(1)}, f32[35,32]{0,1:T(8,128)S(1)}, u32[]{:S(2)}, u32[]{:S(2)}) collective-permute-start(f32[35,32]{0,1:T(8,128)S(1)} %maximum_select_fusion.15), channel_id=1, source_target_pairs={{0,2},{1,3},{2,0},{3,1},{4,6},{5,7},{6,4},{7,5},{8,10},{9,11},{10,... | collective-permute-start | bytes 13448 | tf_op jit(solution)/shard_map/ppermute | solution.py:92
  97.5 21.4 %collective-permute-start.15 = (f32[35,64]{0,1:T(8,128)S(1)}, f32[35,64]{0,1:T(8,128)S(1)}, u32[]{:S(2)}, u32[]{:S(2)}) collective-permute-start(f32[35,64]{0,1:T(8,128)S(1)} %maximum_select_fusion.9), channel_id=1, source_target_pairs={{0,4},{1,5},{2,6},{3,7},{4,0},{5,1},{6,2},{7,3},{8,12},{9,13},{10,... | collective-permute-start | bytes 26888 | tf_op jit(solution)/shard_map/ppermute | solution.py:92
  100.5 18.5 %copy-start.7 = (f32[128]{0:T(128)S(1)}, f32[128]{0:T(128)}, u32[]{:S(2)}) copy-start(f32[128]{0:T(128)} %param.21) | copy-start | bytes 1540
  119.7 6.6 %collective-permute-start.18 = (f32[35,64]{1,0:T(8,128)S(1)}, f32[35,64]{1,0:T(8,128)S(1)}, u32[]{:S(2)}, u32[]{:S(2)}) collective-permute-start(f32[35,64]{1,0:T(8,128)S(1)} %slice_select_fusion.2), channel_id=1, source_target_pairs={{0,4},{1,5},{2,6},{3,7},{4,0},{5,1},{6,2},{7,3},{8,12},{9,13},{10,... | collective-permute-start | bytes 26888 | tf_op jit(solution)/shard_map/ppermute | solution.py:92
  126.4 5.7 %collective-permute-start.19 = (f32[35,32]{1,0:T(8,128)S(1)}, f32[35,32]{1,0:T(8,128)S(1)}, u32[]{:S(2)}, u32[]{:S(2)}) collective-permute-start(f32[35,32]{1,0:T(8,128)S(1)} %slice_select_fusion.1), channel_id=1, source_target_pairs={{0,2},{1,3},{2,0},{3,1},{4,6},{5,7},{6,4},{7,5},{8,10},{9,11},{10,... | collective-permute-start | bytes 13448 | tf_op jit(solution)/shard_map/ppermute | solution.py:92
  132.3 3.1 collective-permute-start.20
  135.6 9.5 %collective-permute-start.21 = (f32[1,35,16]{1,2,0:T(8,128)S(1)}, f32[1,35,16]{1,2,0:T(8,128)S(1)}, u32[]{:S(2)}, u32[]{:S(2)}) collective-permute-start(f32[1,35,16]{1,2,0:T(8,128)S(1)} %convolution_bitcast_fusion.1), channel_id=1, source_target_pairs={{0,8},{1,9},{2,10},{3,11},{4,12},{5,13},{6,14},{7,15},{8,0},{9,1},... | collective-permute-start | bytes 6728 | tf_op jit(solution)/shard_map/ppermute | solution.py:92
  145.1 5.6 %collective-permute-start.22 = (f32[2,35,16]{1,2,0:T(8,128)S(1)}, f32[2,35,16]{1,2,0:T(8,128)S(1)}, u32[]{:S(2)}, u32[]{:S(2)}) collective-permute-start(f32[2,35,16]{1,2,0:T(8,128)S(1)} %maximum_select_fusion.16), channel_id=1, source_target_pairs={{0,16},{1,17},{2,18},{3,19},{4,20},{5,21},{6,22},{7,23},{8,24},{9,... | collective-permute-start | bytes 13448 | tf_op jit(solution)/shard_map/ppermute | solution.py:92
  150.7 7.3 %collective-permute-start.23 = (f32[4,35,16]{1,2,0:T(8,128)S(1)}, f32[4,35,16]{1,2,0:T(8,128)S(1)}, u32[]{:S(2)}, u32[]{:S(2)}) collective-permute-start(f32[4,35,16]{1,2,0:T(8,128)S(1)} %maximum_select_fusion.10), channel_id=1, source_target_pairs={{0,32},{1,33},{2,34},{3,35},{4,36},{5,37},{6,38},{7,39},{8,40},{9,... | collective-permute-start | bytes 26888 | tf_op jit(solution)/shard_map/ppermute | solution.py:92
  158.0 6.2 %collective-permute-start.24 = (f32[8,35,16]{1,2,0:T(8,128)S(1)}, f32[8,35,16]{1,2,0:T(8,128)S(1)}, u32[]{:S(2)}, u32[]{:S(2)}) collective-permute-start(f32[8,35,16]{1,2,0:T(8,128)S(1)} %maximum_select_fusion.7), channel_id=1, source_target_pairs={{0,64},{1,65},{2,66},{3,67},{4,68},{5,69},{6,70},{7,71},{8,72},{9,... | collective-permute-start | bytes 53768 | tf_op jit(solution)/shard_map/ppermute | solution.py:92
  164.2 7.8 %collective-permute-start.25 = (f32[16,35,16]{1,2,0:T(8,128)S(1)}, f32[16,35,16]{1,2,0:T(8,128)S(1)}, u32[]{:S(2)}, u32[]{:S(2)}) collective-permute-start(f32[16,35,16]{1,2,0:T(8,128)S(1)} %maximum_select_fusion.5), channel_id=1, source_target_pairs={{0,128},{1,129},{2,130},{3,131},{4,132},{5,133},{6,134},{7,135},{8... | collective-permute-start | bytes 107528 | tf_op jit(solution)/shard_map/ppermute | solution.py:92
  172.1 59.0 %collective-permute-start.26 = (f32[32,35,16]{1,2,0:T(8,128)S(1)}, f32[32,35,16]{1,2,0:T(8,128)S(1)}, u32[]{:S(2)}, u32[]{:S(2)}) collective-permute-start(f32[32,35,16]{1,2,0:T(8,128)S(1)} %maximum_select_fusion.3), channel_id=1, source_target_pairs={{0,256},{1,257},{2,258},{3,259},{4,260},{5,261},{6,262},{7,263},{8... | collective-permute-start | bytes 215048 | tf_op jit(solution)/shard_map/ppermute | solution.py:92
  232.7 3.1 collective-permute-start.27
  235.8 14.2 %collective-permute-start.28 = (f32[35,32]{0,1:T(8,128)S(1)}, f32[35,32]{0,1:T(8,128)S(1)}, u32[]{:S(2)}, u32[]{:S(2)}) collective-permute-start(f32[35,32]{0,1:T(8,128)S(1)} %maximum_select_fusion.17), channel_id=1, source_target_pairs={{0,2},{1,3},{2,0},{3,1},{4,6},{5,7},{6,4},{7,5},{8,10},{9,11},{10,... | collective-permute-start | bytes 13448 | tf_op jit(solution)/shard_map/ppermute | solution.py:92
  240.2 17.1 %collective-permute-start.31 = (bf16[128,256]{1,0:T(8,128)(2,1)S(1)}, bf16[128,256]{1,0:T(8,128)(2,1)S(1)}, u32[]{:S(2)}, u32[]{:S(2)}) collective-permute-start(bf16[128,256]{1,0:T(8,128)(2,1)S(1)} %copy.203), channel_id=1, source_target_pairs={{0,1},{1,2},{2,3},{3,4},{4,5},{5,6},{6,7},{7,8},{8,9},{9,10},{10,1... | collective-permute-start | bytes 196616 | tf_op jit(solution)/shard_map/ppermute | solution.py:38
  242.2 15.1 %collective-permute-start.30 = (f32[128,256]{1,0:T(8,128)S(1)}, f32[128,256]{1,0:T(8,128)S(1)}, u32[]{:S(2)}, u32[]{:S(2)}) collective-permute-start(f32[128,256]{1,0:T(8,128)S(1)} %copy.202), channel_id=1, source_target_pairs={{1,0},{2,1},{3,2},{4,3},{5,4},{6,5},{7,6},{8,7},{9,8},{10,9},{11,1... | collective-permute-start | bytes 393224 | tf_op jit(solution)/shard_map/ppermute | solution.py:38
  250.1 6.7 %collective-permute-start.29 = (f32[35,64]{0,1:T(8,128)S(1)}, f32[35,64]{0,1:T(8,128)S(1)}, u32[]{:S(2)}, u32[]{:S(2)}) collective-permute-start(f32[35,64]{0,1:T(8,128)S(1)} %maximum_select_fusion.11), channel_id=1, source_target_pairs={{0,4},{1,5},{2,6},{3,7},{4,0},{5,1},{6,2},{7,3},{8,12},{9,13},{10,... | collective-permute-start | bytes 26888 | tf_op jit(solution)/shard_map/ppermute | solution.py:92
  257.7 3.2 collective-permute-start.32
  260.9 6.2 %collective-permute-start.33 = (f32[17737]{0:T(1024)S(1)}, f32[17737]{0:T(1024)S(1)}, u32[]{:S(2)}, u32[]{:S(2)}) collective-permute-start(f32[17737]{0:T(1024)S(1)} %add.216), channel_id=1, source_target_pairs={{0,2},{1,3},{2,0},{3,1},{4,6},{5,7},{6,4},{7,5},{8,10},{9,11},{10,... | collective-permute-start | bytes 212852 | tf_op jit(solution)/shard_map/ppermute | solution.py:92
  267.1 12.7 %collective-permute-start.34 = (f32[17737]{0:T(1024)S(1)}, f32[17737]{0:T(1024)S(1)}, u32[]{:S(2)}, u32[]{:S(2)}) collective-permute-start(f32[17737]{0:T(1024)S(1)} %add.217), channel_id=1, source_target_pairs={{0,4},{1,5},{2,6},{3,7},{4,0},{5,1},{6,2},{7,3},{8,12},{9,13},{10,... | collective-permute-start | bytes 212852 | tf_op jit(solution)/shard_map/ppermute | solution.py:92
  270.0 52.4 %collective-permute-start.17 = (bf16[3,256]{1,0:T(4,128)(2,1)S(1)}, bf16[3,256]{1,0:T(4,128)(2,1)S(1)}, u32[]{:S(2)}, u32[]{:S(2)}) collective-permute-start(bf16[3,256]{1,0:T(4,128)(2,1)S(1)} %slice.328), channel_id=1, source_target_pairs={{0,1},{1,2},{2,3},{3,4},{4,5},{5,6},{6,7},{7,8},{8,9},{9,10},{10,1... | collective-permute-start | bytes 4616 | tf_op jit(solution)/shard_map/ppermute | solution.py:38
  272.0 50.5 %collective-permute-start.16 = (f32[3,256]{1,0:T(4,128)S(1)}, f32[3,256]{1,0:T(4,128)S(1)}, u32[]{:S(2)}, u32[]{:S(2)}) collective-permute-start(f32[3,256]{1,0:T(4,128)S(1)} %slice.217), channel_id=1, source_target_pairs={{1,0},{2,1},{3,2},{4,3},{5,4},{6,5},{7,6},{8,7},{9,8},{10,9},{11,1... | collective-permute-start | bytes 9224 | tf_op jit(solution)/shard_map/ppermute | solution.py:38
  279.9 10.2 %collective-permute-start.35 = (f32[17737]{0:T(1024)S(1)}, f32[17737]{0:T(1024)S(1)}, u32[]{:S(2)}, u32[]{:S(2)}) collective-permute-start(f32[17737]{0:T(1024)S(1)} %add.218), channel_id=1, source_target_pairs={{0,8},{1,9},{2,10},{3,11},{4,12},{5,13},{6,14},{7,15},{8,0},{9,1},... | collective-permute-start | bytes 212852 | tf_op jit(solution)/shard_map/ppermute | solution.py:92
  290.0 6.2 %collective-permute-start.36 = (f32[17737]{0:T(1024)S(1)}, f32[17737]{0:T(1024)S(1)}, u32[]{:S(2)}, u32[]{:S(2)}) collective-permute-start(f32[17737]{0:T(1024)S(1)} %add.219), channel_id=1, source_target_pairs={{0,16},{1,17},{2,18},{3,19},{4,20},{5,21},{6,22},{7,23},{8,24},{9,... | collective-permute-start | bytes 212852 | tf_op jit(solution)/shard_map/ppermute | solution.py:92
  296.3 7.8 %collective-permute-start.37 = (f32[17737]{0:T(1024)S(1)}, f32[17737]{0:T(1024)S(1)}, u32[]{:S(2)}, u32[]{:S(2)}) collective-permute-start(f32[17737]{0:T(1024)S(1)} %add.220), channel_id=1, source_target_pairs={{0,32},{1,33},{2,34},{3,35},{4,36},{5,37},{6,38},{7,39},{8,40},{9,... | collective-permute-start | bytes 212852 | tf_op jit(solution)/shard_map/ppermute | solution.py:92
  304.1 6.9 %collective-permute-start.38 = (f32[17737]{0:T(1024)S(1)}, f32[17737]{0:T(1024)S(1)}, u32[]{:S(2)}, u32[]{:S(2)}) collective-permute-start(f32[17737]{0:T(1024)S(1)} %add.221), channel_id=1, source_target_pairs={{0,64},{1,65},{2,66},{3,67},{4,68},{5,69},{6,70},{7,71},{8,72},{9,... | collective-permute-start | bytes 212852 | tf_op jit(solution)/shard_map/ppermute | solution.py:92
  310.9 7.2 %collective-permute-start.39 = (f32[17737]{0:T(1024)S(1)}, f32[17737]{0:T(1024)S(1)}, u32[]{:S(2)}, u32[]{:S(2)}) collective-permute-start(f32[17737]{0:T(1024)S(1)} %add.222), channel_id=1, source_target_pairs={{0,128},{1,129},{2,130},{3,131},{4,132},{5,133},{6,134},{7,135},{8... | collective-permute-start | bytes 212852 | tf_op jit(solution)/shard_map/ppermute | solution.py:92
  318.2 10.9 %collective-permute-start.40 = (f32[17737]{0:T(1024)S(1)}, f32[17737]{0:T(1024)S(1)}, u32[]{:S(2)}, u32[]{:S(2)}) collective-permute-start(f32[17737]{0:T(1024)S(1)} %add.223), channel_id=1, source_target_pairs={{0,256},{1,257},{2,258},{3,259},{4,260},{5,261},{6,262},{7,263},{8... | collective-permute-start | bytes 212852 | tf_op jit(solution)/shard_map/ppermute | solution.py:92

commit v3 on v2

--- a/solution.py
+++ b/solution.py
@@ -100,13 +100,26 @@
 
 def split_sum(block, index, bits):
     for bit in bits:
-        half = block.shape[1] // 2
-        lower, upper = block[:, :half], block[:, half:]
+        half = block.shape[-1] // 2
+        lower, upper = block[..., :half], block[..., half:]
         up = ((index >> bit) & 1) == 1
         keep = jnp.where(up, upper, lower)
         send = jnp.where(up, lower, upper)
         block = keep + xor_swap(send, bit)
     return block
+
+
+def tree_gather_sum(block, extra, index, bits, axis):
+    for bit in bits:
+        other, other_extra = xor_swap((block, extra), bit)
+        up = ((index >> bit) & 1) == 1
+        block = jnp.where(
+            up,
+            jnp.concatenate([other, block], axis=axis),
+            jnp.concatenate([block, other], axis=axis),
+        )
+        extra = extra + other_extra
+    return block, extra
 
 
 def tree_gather(block, index, bits, axis):
@@ -161,6 +174,8 @@
 
     basis_val, basis_back = jax.vjp(far_basis, positions)
     moment = jnp.einsum("ka,ca->kc", basis_val, hidden_t, precision=PRECISE)
+    masked_feat = features.astype(jnp.float32) * mask_f[:, None]
+    feat_basis = jnp.einsum("ka,ai->ki", basis_val, masked_feat, precision=PRECISE)
     counts_mat = jnp.sum(
         (far_list[:, :, None] == jnp.arange(groups, dtype=jnp.int32)[None, None, :]).astype(
             jnp.float32
@@ -169,11 +184,13 @@
     )
     row_weights = lax.dynamic_index_in_dim(counts_mat, group_id, 0, keepdims=False)
     col_weights = lax.dynamic_index_in_dim(counts_mat, group_id, 1, keepdims=False)
-    moment_part = split_sum(moment, index, sub_bits[::-1])
+    moment_part = split_sum(jnp.stack([moment, feat_basis]), index, sub_bits[::-1])
     moment_tab = tree_gather(moment_part[None], index, grp_bits, 0)
-    gathered_part = jnp.einsum("j,jkc->kc", row_weights, moment_tab, precision=PRECISE)
+    mixed_part = jnp.einsum("j,jnkc->nkc", row_weights, moment_tab, precision=PRECISE)
+    gathered_part = mixed_part[0]
     local_part = jnp.dot(trans_weight, gathered_part, precision=PRECISE)
-    local_exp = tree_gather(local_part, index, sub_bits, 1)
+    both = tree_gather(jnp.stack([local_part, mixed_part[1]]), index, sub_bits, 2)
+    local_exp, feat_mixed = both[0], both[1]
     potential = jnp.einsum("ka,kc->ac", basis_val, local_exp, precision=PRECISE)
     pre_act = near_val + potential
     sigma = jax.nn.sigmoid(pre_act)
@@ -186,12 +203,14 @@
     d_local_part = split_sum(d_local, index, sub_bits[::-1])
     grad_trans_part = jnp.einsum("kc,qc->kq", d_local_part, gathered_part, precision=PRECISE)
     d_gathered_part = jnp.dot(trans_weight.T, d_local_part, precision=PRECISE)
-    d_tab = tree_gather(d_gathered_part[None], index, grp_bits, 0)
-    d_moment_part = jnp.einsum("b,bkc->kc", col_weights, d_tab, precision=PRECISE)
-    d_moment = tree_gather(d_moment_part, index, sub_bits, 1)
-    d_basis = d_basis + jnp.dot(d_moment, hidden_t, precision=PRECISE)
-    d_hidden_far = jnp.einsum("ka,kc->ca", basis_val, d_moment, precision=PRECISE)
-    (d_far_pos,) = basis_back(d_basis)
+    slice_width = d_gathered_part.shape[1]
+    far_msg_part = jnp.einsum("ki,kc->ic", feat_mixed, d_gathered_part, precision=PRECISE)
+    far_msg = lax.dynamic_update_slice_in_dim(
+        jnp.zeros((far_msg_part.shape[0], slice_width * 8), jnp.float32),
+        far_msg_part,
+        (index % 8) * slice_width,
+        axis=1,
+    )
     d_own, d_ext, d_feat_ext = near_back(d_pre)
     low_pos, low_feat = passed_along((d_ext[:, :atom_num], d_feat_ext[:, :atom_num]), "box", -1)
     high_pos, high_feat = (
@@ -200,16 +219,18 @@
             jnp.float32
         ),
     )
-    d_hidden_t = (
-        d_feat_ext[:, atom_num : 2 * atom_num] + low_feat + high_feat + d_hidden_far
-    ) * mask_f[None, :]
-    grad_msg_part = jnp.einsum(
-        "ai,ca->ic", features.astype(jnp.float32), d_hidden_t, precision=PRECISE
+    d_hidden_near = d_feat_ext[:, atom_num : 2 * atom_num] + low_feat + high_feat
+    grad_msg_part = (
+        jnp.einsum("ai,ca->ic", masked_feat, d_hidden_near, precision=PRECISE) + far_msg
     )
     flat = jnp.concatenate(
         [grad_msg_part.reshape(-1), grad_trans_part.reshape(-1), grad_read_part.reshape(-1)]
     )
-    flat = tree_sum(flat, tuple(range(all_bits)))
+    d_tab, flat = tree_gather_sum(d_gathered_part[None], flat, index, grp_bits, 0)
+    d_moment_part = jnp.einsum("b,bkc->kc", col_weights, d_tab, precision=PRECISE)
+    d_moment, flat = tree_gather_sum(d_moment_part, flat, index, sub_bits, 1)
+    d_basis = d_basis + jnp.dot(d_moment, hidden_t, precision=PRECISE)
+    (d_far_pos,) = basis_back(d_basis)
     msg_size, trans_size = grad_msg_part.size, grad_trans_part.size
     grad_msg = flat[:msg_size].reshape(grad_msg_part.shape)
     grad_trans = flat[msg_size : msg_size + trans_size].reshape(grad_trans_part.shape)

time: 332 us -> 350 us (1.054)
  the two profiles are of different devices: /device:TPU:16 before, /device:TPU:1 now
where the time goes in v3:
time: 350 us; the launch traced here: 347 us
  starting transfers between devices  176 us (50%)
  waiting for transfers between devices  82.3 us (24%)
  matrix products  35.1 us (10%)
  other arithmetic  28.8 us (8%)
  local copies, waits for them, and re-layouts  22 us (6%)
    ppermute x33, starting transfers between devices, xor_swap(): return lax.ppermute(block, 'box', [(i, i ^ 1 << bit) for i in range(count)])  150 us
    ppermute x33, waiting for transfers between devices, xor_swap(): return lax.ppermute(block, 'box', [(i, i ^ 1 << bit) for i in range(count)])  82.3 us
    dot_general x12, matrix products, one_block(): jnp.einsum('pij,cpj->pic', kernel, source_feat, preferred_element_type=jn...  20.6 us
    ppermute x4, starting transfers between devices, passed_along(): return lax.ppermute(block, axis, route)  12.3 us
    scatter-add x4, other arithmetic, one_block(): source_feat = feat_leaf[:, src_ids].astype(jnp.bfloat16)  8.98 us
    dot_general x8, matrix products, one_block(): jnp.einsum('tp,pic->tic', onehot, contrib, precision=PRECISE)  7.34 us
  transfers between devices with their start and end apart: 41, of which 25 were waited for; matrix products, arithmetic and copies ran while one was open for 22% of the time, Pallas kernels for 0%

profile of v3, /device:TPU:1, one launch (start us, length us, event | category | flops | bytes accessed | tf_op | source)
XLA Modules:
  0.0 347.0 jit_solution(11532547847061009532)
XLA Ops:
  5.7 6.6 %collective-permute-start.4 = (f32[2,35,64]{2,1,0:T(8,128)S(1)}, f32[2,35,64]{2,1,0:T(8,128)S(1)}, u32[]{:S(2)}, u32[]{:S(2)}) collective-permute-start(f32[2,35,64]{2,1,0:T(8,128)S(1)} %fusion.78), channel_id=1, source_target_pairs={{0,4},{1,5},{2,6},{3,7},{4,0},{5,1},{6,2},{7,3},{8,12},{9,13},{10,... | collective-permute-start | bytes 53768 | tf_op jit(solution)/shard_map/ppermute | solution.py:92
  13.9 4.0 %collective-permute-start.5 = (f32[2,35,32]{2,1,0:T(8,128)S(1)}, f32[2,35,32]{2,1,0:T(8,128)S(1)}, u32[]{:S(2)}, u32[]{:S(2)}) collective-permute-start(f32[2,35,32]{2,1,0:T(8,128)S(1)} %slice_select_fusion.1), channel_id=1, source_target_pairs={{0,2},{1,3},{2,0},{3,1},{4,6},{5,7},{6,4},{7,5},{8,10},{9,11},{10,... | collective-permute-start | bytes 26888 | tf_op jit(solution)/shard_map/ppermute | solution.py:92
  19.4 8.0 %collective-permute-start.6 = (f32[2,35,16]{2,1,0:T(8,128)S(1)}, f32[2,35,16]{2,1,0:T(8,128)S(1)}, u32[]{:S(2)}, u32[]{:S(2)}) collective-permute-start(f32[2,35,16]{2,1,0:T(8,128)S(1)} %slice_select_fusion), channel_id=1, source_target_pairs={{0,1},{1,0},{2,3},{3,2},{4,5},{5,4},{6,7},{7,6},{8,9},{9,8},{10,11... | collective-permute-start | bytes 13448 | tf_op jit(solution)/shard_map/ppermute | solution.py:92
  28.4 5.5 %collective-permute-start.7 = (f32[1,2,35,16]{3,2,1,0:T(8,128)S(1)}, f32[1,2,35,16]{3,2,1,0:T(8,128)S(1)}, u32[]{:S(2)}, u32[]{:S(2)}) collective-permute-start(f32[1,2,35,16]{3,2,1,0:T(8,128)S(1)} %add_bitcast_fusion.2), channel_id=1, source_target_pairs={{0,8},{1,9},{2,10},{3,11},{4,12},{5,13},{6,14},{7,15},{8,0},{9,1},... | collective-permute-start | bytes 13448 | tf_op jit(solution)/shard_map/ppermute | solution.py:92
  34.0 3.1 collective-permute-done.7
  37.1 1.9 collective-permute-start.8
  39.0 2.7 collective-permute-done.8
  41.8 3.0 collective-permute-start.9
  44.8 3.5 %collective-permute-done.9 = f32[4,2,35,16]{2,3,1,0:T(8,128)S(1)} collective-permute-done((f32[4,2,35,16]{2,3,1,0:T(8,128)S(1)}, f32[4,2,35,16]{2,3,1,0:T(8,128)S(1)}, u32[]{:S(2)}, u32[]{:S(2)}) %collective-permute-start.9) | collective-permute-done | bytes 17952 | tf_op jit(solution)/shard_map/ppermute | solution.py:92
  48.3 1.9 collective-permute-start.10
  50.3 3.7 %collective-permute-done.10 = f32[8,2,35,16]{2,3,1,0:T(8,128)S(1)} collective-permute-done((f32[8,2,35,16]{2,3,1,0:T(8,128)S(1)}, f32[8,2,35,16]{2,3,1,0:T(8,128)S(1)}, u32[]{:S(2)}, u32[]{:S(2)}) %collective-permute-start.10) | collective-permute-done | bytes 35872 | tf_op jit(solution)/shard_map/ppermute | solution.py:92
  54.0 2.6 collective-permute-start.11
  56.6 11.5 %collective-permute-done.11 = f32[16,2,35,16]{2,3,1,0:T(8,128)S(1)} collective-permute-done((f32[16,2,35,16]{2,3,1,0:T(8,128)S(1)}, f32[16,2,35,16]{2,3,1,0:T(8,128)S(1)}, u32[]{:S(2)}, u32[]{:S(2)}) %collective-permute-start.11) | collective-permute-done | bytes 71712 | tf_op jit(solution)/shard_map/ppermute | solution.py:92
  68.2 6.2 %collective-permute-start.12 = (f32[32,2,35,16]{2,3,1,0:T(8,128)S(1)}, f32[32,2,35,16]{2,3,1,0:T(8,128)S(1)}, u32[]{:S(2)}, u32[]{:S(2)}) collective-permute-start(f32[32,2,35,16]{2,3,1,0:T(8,128)S(1)} %maximum_select_fusion.1), channel_id=1, source_target_pairs={{0,256},{1,257},{2,258},{3,259},{4,260},{5,261},{6,262},{7,263},{8... | collective-permute-start | bytes 430088 | tf_op jit(solution)/shard_map/ppermute | solution.py:92
  74.3 4.9 %collective-permute-start.1 = (f32[3,256]{1,0:T(4,128)S(1)}, f32[3,256]{1,0:T(4,128)S(1)}, u32[]{:S(2)}, u32[]{:S(2)}) collective-permute-start(f32[3,256]{1,0:T(4,128)S(1)} %copy-done.3), channel_id=1, source_target_pairs={{1,0},{2,1},{3,2},{4,3},{5,4},{6,5},{7,6},{8,7},{9,8},{10,9},{11,1... | collective-permute-start | bytes 9224 | tf_op jit(solution)/shard_map/ppermute | solution.py:30
  79.2 2.7 collective-permute-start
  81.9 1.9 collective-permute-start.3
  83.9 3.6 %collective-permute-start.2 = (bf16[128,256]{1,0:T(8,128)(2,1)S(1)}, bf16[128,256]{1,0:T(8,128)(2,1)S(1)}, u32[]{:S(2)}, u32[]{:S(2)}) collective-permute-start(bf16[128,256]{1,0:T(8,128)(2,1)S(1)} %get-tuple-element.565), channel_id=1, source_target_pairs={{0,1},{1,2},{2,3},{3,4},{4,5},{5,6},{6,7},{7,8},{8,9},{9,10},{10,1... | collective-permute-start | bytes 196616 | tf_op jit(solution)/shard_map/ppermute | solution.py:27
  89.0 9.1 %collective-permute-done.12 = f32[32,2,35,16]{2,3,1,0:T(8,128)S(1)} collective-permute-done((f32[32,2,35,16]{2,3,1,0:T(8,128)S(1)}, f32[32,2,35,16]{2,3,1,0:T(8,128)S(1)}, u32[]{:S(2)}, u32[]{:S(2)}) %collective-permute-start.12) | collective-permute-done | bytes 143392 | tf_op jit(solution)/shard_map/ppermute | solution.py:92
  99.0 2.2 fusion.67
  101.4 3.5 %collective-permute-start.13 = (f32[2,35,16]{1,2,0:T(8,128)S(1)}, f32[2,35,16]{1,2,0:T(8,128)S(1)}, u32[]{:S(2)}, u32[]{:S(2)}) collective-permute-start(f32[2,35,16]{1,2,0:T(8,128)S(1)} %pad_maximum_fusion.1), channel_id=1, source_target_pairs={{0,1},{1,0},{2,3},{3,2},{4,5},{5,4},{6,7},{7,6},{8,9},{9,8},{10,11... | collective-permute-start | bytes 13448 | tf_op jit(solution)/shard_map/ppermute | solution.py:92
  107.7 2.7 collective-permute-done.14
  110.4 4.6 %collective-permute-start.15 = (f32[2,35,64]{1,2,0:T(8,128)S(1)}, f32[2,35,64]{1,2,0:T(8,128)S(1)}, u32[]{:S(2)}, u32[]{:S(2)}) collective-permute-start(f32[2,35,64]{1,2,0:T(8,128)S(1)} %maximum_select_fusion.8), channel_id=1, source_target_pairs={{0,4},{1,5},{2,6},{3,7},{4,0},{5,1},{6,2},{7,3},{8,12},{9,13},{10,... | collective-permute-start | bytes 53768 | tf_op jit(solution)/shard_map/ppermute | solution.py:92
  115.0 18.3 %while.33 = (s32[]{:T(128)}, f32[4,64,128]{2,0,1:T(4,128)S(1)}, s32[4,27]{1,0:T(4,128)S(1)}, f32[3,4,64]{2,0,1:T(4,128)S(1)}, s32[4,27]{1,0:T(4,128)S(1)}, /*ind...) while((s32[]{:T(128)}, f32[4,64,128]{2,0,1:T(4,128)S(1)}, ...), condition=%wide.region_1.2_spmd.clone, body=%wide.region_0.1_spmd.clone.sunk | while | flops 40212804 | bytes 3658967 | solution.py:86
  136.4 3.5 %collective-permute-done.18 = f32[35,64]{1,0:T(8,128)S(1)} collective-permute-done((f32[35,64]{1,0:T(8,128)S(1)}, f32[35,64]{1,0:T(8,128)S(1)}, u32[]{:S(2)}, u32[]{:S(2)}) %collective-permute-start.18) | collective-permute-done | bytes 8992 | tf_op jit(solution)/shard_map/ppermute | solution.py:92
  141.9 2.6 collective-permute-done.19
  144.7 6.0 %collective-permute-start.20 = (f32[35,16]{1,0:T(8,128)S(1)}, f32[35,16]{1,0:T(8,128)S(1)}, u32[]{:S(2)}, u32[]{:S(2)}) collective-permute-start(f32[35,16]{1,0:T(8,128)S(1)} %slice_select_fusion.2), channel_id=1, source_target_pairs={{0,1},{1,0},{2,3},{3,2},{4,5},{5,4},{6,7},{7,6},{8,9},{9,8},{10,11... | collective-permute-start | bytes 6728 | tf_op jit(solution)/shard_map/ppermute | solution.py:92
  151.8 6.6 %collective-permute-start.21 = (f32[1,35,16]{1,2,0:T(8,128)S(1)}, f32[1,35,16]{1,2,0:T(8,128)S(1)}, u32[]{:S(2)}, u32[]{:S(2)}) collective-permute-start(f32[1,35,16]{1,2,0:T(8,128)S(1)} %bitcast.242), channel_id=1, source_target_pairs={{0,8},{1,9},{2,10},{3,11},{4,12},{5,13},{6,14},{7,15},{8,0},{9,1},... | collective-permute-start | bytes 6728 | tf_op jit(solution)/shard_map/ppermute | solution.py:92
  160.1 3.2 collective-permute-start.22
  163.4 50.5 %while.32 = (s32[]{:T(128)}, f32[3,4,64]{2,0,1:T(4,128)S(1)}, f32[3,12,64]{2,0,1:T(4,128)S(1)}, f32[128,12,64]{0,2,1:T(8,128)S(1)}, f32[4,64,128]{2,0,1:T(4,128)...) while((s32[]{:T(128)}, f32[3,4,64]{2,0,1:T(4,128)S(1)}, ...), condition=%wide.region_13.14_spmd.clone, body=%wide.region_3.13_spmd.clone.sunk | while | flops 71802528 | bytes 7040317 | solution.py:86
  166.2 2.0 fusion.183
  173.8 2.2 scatter_fusion.2
  178.8 2.0 fusion.183
  186.4 2.2 scatter_fusion.2
  191.5 2.0 fusion.183
  199.0 2.2 scatter_fusion.2
  204.1 2.0 fusion.183
  211.6 2.2 scatter_fusion.2
  213.9 4.3 %collective-permute-start.23 = (f32[4,35,16]{1,2,0:T(8,128)S(1)}, f32[4,35,16]{1,2,0:T(8,128)S(1)}, u32[]{:S(2)}, u32[]{:S(2)}) collective-permute-start(f32[4,35,16]{1,2,0:T(8,128)S(1)} %maximum_select_fusion.13), channel_id=1, source_target_pairs={{0,32},{1,33},{2,34},{3,35},{4,36},{5,37},{6,38},{7,39},{8,40},{9,... | collective-permute-start | bytes 26888 | tf_op jit(solution)/shard_map/ppermute | solution.py:92
  218.6 3.6 %collective-permute-start.31 = (bf16[128,256]{0,1:T(8,128)(2,1)S(1)}, bf16[128,256]{0,1:T(8,128)(2,1)S(1)}, u32[]{:S(2)}, u32[]{:S(2)}) collective-permute-start(bf16[128,256]{0,1:T(8,128)(2,1)S(1)} %slice.362), channel_id=1, source_target_pairs={{0,1},{1,2},{2,3},{3,4},{4,5},{5,6},{6,7},{7,8},{8,9},{9,10},{10,1... | collective-permute-start | bytes 196616 | tf_op jit(solution)/shard_map/ppermute | solution.py:38
  222.2 1.9 collective-permute-start.30
  224.1 14.8 %collective-permute-start.24 = (f32[8,35,16]{1,2,0:T(8,128)S(1)}, f32[8,35,16]{1,2,0:T(8,128)S(1)}, u32[]{:S(2)}, u32[]{:S(2)}) collective-permute-start(f32[8,35,16]{1,2,0:T(8,128)S(1)} %maximum_select_fusion.9), channel_id=1, source_target_pairs={{0,64},{1,65},{2,66},{3,67},{4,68},{5,69},{6,70},{7,71},{8,72},{9,... | collective-permute-start | bytes 53768 | tf_op jit(solution)/shard_map/ppermute | solution.py:92
  240.6 5.1 %collective-permute-start.25 = (f32[16,35,16]{1,2,0:T(8,128)S(1)}, f32[16,35,16]{1,2,0:T(8,128)S(1)}, u32[]{:S(2)}, u32[]{:S(2)}) collective-permute-start(f32[16,35,16]{1,2,0:T(8,128)S(1)} %maximum_select_fusion.6), channel_id=1, source_target_pairs={{0,128},{1,129},{2,130},{3,131},{4,132},{5,133},{6,134},{7,135},{8... | collective-permute-start | bytes 107528 | tf_op jit(solution)/shard_map/ppermute | solution.py:92
  246.0 2.2 collective-permute-done.25
  248.3 1.9 collective-permute-start.26
  250.7 10.0 %collective-permute-done.26 = f32[32,35,16]{1,2,0:T(8,128)S(1)} collective-permute-done((f32[32,35,16]{1,2,0:T(8,128)S(1)}, f32[32,35,16]{1,2,0:T(8,128)S(1)}, u32[]{:S(2)}, u32[]{:S(2)}) %collective-permute-start.26) | collective-permute-done | bytes 71712 | tf_op jit(solution)/shard_map/ppermute | solution.py:92
  261.0 10.6 %collective-permute-start.27 = (f32[35,16]{1,0:T(8,128)S(1)}, f32[35,16]{1,0:T(8,128)S(1)}, u32[]{:S(2)}, u32[]{:S(2)}) collective-permute-start(f32[35,16]{1,0:T(8,128)S(1)} %copy.148), channel_id=1, source_target_pairs={{0,1},{1,0},{2,3},{3,2},{4,5},{5,4},{6,7},{7,6},{8,9},{9,8},{10,11... | collective-permute-start | bytes 6728 | tf_op jit(solution)/shard_map/ppermute | solution.py:92
  273.9 7.8 %collective-permute-start.28 = (f32[35,32]{1,0:T(8,128)S(1)}, f32[35,32]{1,0:T(8,128)S(1)}, u32[]{:S(2)}, u32[]{:S(2)}) collective-permute-start(f32[35,32]{1,0:T(8,128)S(1)} %maximum_select_fusion.14), channel_id=1, source_target_pairs={{0,2},{1,3},{2,0},{3,1},{4,6},{5,7},{6,4},{7,5},{8,10},{9,11},{10,... | collective-permute-start | bytes 13448 | tf_op jit(solution)/shard_map/ppermute | solution.py:92
  281.7 1.9 collective-permute-start.33
  283.9 3.0 collective-permute-done.33
  286.8 2.5 collective-permute-start.34
  289.5 2.4 collective-permute-start.29
  293.5 4.1 %collective-permute-start.35 = (f32[17737]{0:T(1024)S(1)}, f32[17737]{0:T(1024)S(1)}, u32[]{:S(2)}, u32[]{:S(2)}) collective-permute-start(f32[17737]{0:T(1024)S(1)} %add.228), channel_id=1, source_target_pairs={{0,64},{1,65},{2,66},{3,67},{4,68},{5,69},{6,70},{7,71},{8,72},{9,... | collective-permute-start | bytes 212852 | tf_op jit(solution)/shard_map/ppermute | solution.py:92
  298.4 4.9 %collective-permute-start.17 = (bf16[3,256]{1,0:T(4,128)(2,1)S(1)}, bf16[3,256]{1,0:T(4,128)(2,1)S(1)}, u32[]{:S(2)}, u32[]{:S(2)}) collective-permute-start(bf16[3,256]{1,0:T(4,128)(2,1)S(1)} %slice.363), channel_id=1, source_target_pairs={{0,1},{1,2},{2,3},{3,4},{4,5},{5,6},{6,7},{7,8},{8,9},{9,10},{10,1... | collective-permute-start | bytes 4616 | tf_op jit(solution)/shard_map/ppermute | solution.py:38
  303.3 1.9 collective-permute-start.16
  305.2 5.6 %collective-permute-start.36 = (f32[17737]{0:T(1024)S(1)}, f32[17737]{0:T(1024)S(1)}, u32[]{:S(2)}, u32[]{:S(2)}) collective-permute-start(f32[17737]{0:T(1024)S(1)} %add.229), channel_id=1, source_target_pairs={{0,128},{1,129},{2,130},{3,131},{4,132},{5,133},{6,134},{7,135},{8... | collective-permute-start | bytes 212852 | tf_op jit(solution)/shard_map/ppermute | solution.py:92
  311.1 2.2 collective-permute-done.36
  313.4 4.1 %collective-permute-start.37 = (f32[17737]{0:T(1024)S(1)}, f32[17737]{0:T(1024)S(1)}, u32[]{:S(2)}, u32[]{:S(2)}) collective-permute-start(f32[17737]{0:T(1024)S(1)} %add.230), channel_id=1, source_target_pairs={{0,256},{1,257},{2,258},{3,259},{4,260},{5,261},{6,262},{7,263},{8... | collective-permute-start | bytes 212852 | tf_op jit(solution)/shard_map/ppermute | solution.py:92
  317.6 4.9 %collective-permute-done.37 = f32[17737]{0:T(1024)S(1)} collective-permute-done((f32[17737]{0:T(1024)S(1)}, f32[17737]{0:T(1024)S(1)}, u32[]{:S(2)}, u32[]{:S(2)}) %collective-permute-start.37) | collective-permute-done | bytes 70980 | tf_op jit(solution)/shard_map/ppermute | solution.py:92
  322.5 9.7 %collective-permute-start.38 = (f32[17737]{0:T(1024)S(1)}, f32[17737]{0:T(1024)S(1)}, u32[]{:S(2)}, u32[]{:S(2)}) collective-permute-start(f32[17737]{0:T(1024)S(1)} %add.231), channel_id=1, source_target_pairs={{0,1},{1,0},{2,3},{3,2},{4,5},{5,4},{6,7},{7,6},{8,9},{9,8},{10,11... | collective-permute-start | bytes 212852 | tf_op jit(solution)/shard_map/ppermute | solution.py:92
  333.2 1.9 collective-permute-start.39
  335.1 3.1 collective-permute-done.39
  338.3 1.9 collective-permute-start.40
  340.8 4.2 %collective-permute-done.40 = f32[17737]{0:T(1024)S(1)} collective-permute-done((f32[17737]{0:T(1024)S(1)}, f32[17737]{0:T(1024)S(1)}, u32[]{:S(2)}, u32[]{:S(2)}) %collective-permute-start.40) | collective-permute-done | bytes 70980 | tf_op jit(solution)/shard_map/ppermute | solution.py:92
  (374 shorter events, 84.6 us)
Async XLA Ops:
  0.6 3.7 %copy-start = (bf16[128,128]{1,0:T(8,128)(2,1)S(1)}, bf16[128,128]{1,0:T(8,128)(2,1)}, u32[]{:S(2)}) copy-start(bf16[128,128]{1,0:T(8,128)(2,1)} %param.19) | copy-start | bytes 98308
  5.7 8.0 %collective-permute-start.4 = (f32[2,35,64]{2,1,0:T(8,128)S(1)}, f32[2,35,64]{2,1,0:T(8,128)S(1)}, u32[]{:S(2)}, u32[]{:S(2)}) collective-permute-start(f32[2,35,64]{2,1,0:T(8,128)S(1)} %fusion.78), channel_id=1, source_target_pairs={{0,4},{1,5},{2,6},{3,7},{4,0},{5,1},{6,2},{7,3},{8,12},{9,13},{10,... | collective-permute-start | bytes 53768 | tf_op jit(solution)/shard_map/ppermute | solution.py:92
  13.9 5.4 %collective-permute-start.5 = (f32[2,35,32]{2,1,0:T(8,128)S(1)}, f32[2,35,32]{2,1,0:T(8,128)S(1)}, u32[]{:S(2)}, u32[]{:S(2)}) collective-permute-start(f32[2,35,32]{2,1,0:T(8,128)S(1)} %slice_select_fusion.1), channel_id=1, source_target_pairs={{0,2},{1,3},{2,0},{3,1},{4,6},{5,7},{6,4},{7,5},{8,10},{9,11},{10,... | collective-permute-start | bytes 26888 | tf_op jit(solution)/shard_map/ppermute | solution.py:92
  19.4 8.9 %collective-permute-start.6 = (f32[2,35,16]{2,1,0:T(8,128)S(1)}, f32[2,35,16]{2,1,0:T(8,128)S(1)}, u32[]{:S(2)}, u32[]{:S(2)}) collective-permute-start(f32[2,35,16]{2,1,0:T(8,128)S(1)} %slice_select_fusion), channel_id=1, source_target_pairs={{0,1},{1,0},{2,3},{3,2},{4,5},{5,4},{6,7},{7,6},{8,9},{9,8},{10,11... | collective-permute-start | bytes 13448 | tf_op jit(solution)/shard_map/ppermute | solution.py:92
  28.4 8.6 %collective-permute-start.7 = (f32[1,2,35,16]{3,2,1,0:T(8,128)S(1)}, f32[1,2,35,16]{3,2,1,0:T(8,128)S(1)}, u32[]{:S(2)}, u32[]{:S(2)}) collective-permute-start(f32[1,2,35,16]{3,2,1,0:T(8,128)S(1)} %add_bitcast_fusion.2), channel_id=1, source_target_pairs={{0,8},{1,9},{2,10},{3,11},{4,12},{5,13},{6,14},{7,15},{8,0},{9,1},... | collective-permute-start | bytes 13448 | tf_op jit(solution)/shard_map/ppermute | solution.py:92
  37.1 4.7 %collective-permute-start.8 = (f32[2,2,35,16]{2,3,1,0:T(8,128)S(1)}, f32[2,2,35,16]{2,3,1,0:T(8,128)S(1)}, u32[]{:S(2)}, u32[]{:S(2)}) collective-permute-start(f32[2,2,35,16]{2,3,1,0:T(8,128)S(1)} %maximum_select_fusion.11), channel_id=1, source_target_pairs={{0,16},{1,17},{2,18},{3,19},{4,20},{5,21},{6,22},{7,23},{8,24},{9,... | collective-permute-start | bytes 26888 | tf_op jit(solution)/shard_map/ppermute | solution.py:92
  41.8 6.5 %collective-permute-start.9 = (f32[4,2,35,16]{2,3,1,0:T(8,128)S(1)}, f32[4,2,35,16]{2,3,1,0:T(8,128)S(1)}, u32[]{:S(2)}, u32[]{:S(2)}) collective-permute-start(f32[4,2,35,16]{2,3,1,0:T(8,128)S(1)} %maximum_select_fusion.7), channel_id=1, source_target_pairs={{0,32},{1,33},{2,34},{3,35},{4,36},{5,37},{6,38},{7,39},{8,40},{9,... | collective-permute-start | bytes 53768 | tf_op jit(solution)/shard_map/ppermute | solution.py:92
  44.8 29.6 %copy-start.3 = (f32[3,256]{1,0:T(4,128)S(1)}, f32[3,256]{1,0:T(4,128)}, u32[]{:S(2)}) copy-start(f32[3,256]{1,0:T(4,128)} %param.15) | copy-start | bytes 9220
  48.3 5.7 %collective-permute-start.10 = (f32[8,2,35,16]{2,3,1,0:T(8,128)S(1)}, f32[8,2,35,16]{2,3,1,0:T(8,128)S(1)}, u32[]{:S(2)}, u32[]{:S(2)}) collective-permute-start(f32[8,2,35,16]{2,3,1,0:T(8,128)S(1)} %maximum_select_fusion.5), channel_id=1, source_target_pairs={{0,64},{1,65},{2,66},{3,67},{4,68},{5,69},{6,70},{7,71},{8,72},{9,... | collective-permute-start | bytes 107528 | tf_op jit(solution)/shard_map/ppermute | solution.py:92
  50.2 37.5 %copy-start.5 = (s32[108]{0:T(128)S(1)}, s32[108]{0:T(128)}, u32[]{:S(2)}) copy-start(s32[108]{0:T(128)} %param.22) | copy-start | bytes 1300
  50.2 37.6 %copy-start.6 = (s32[108]{0:T(128)S(1)}, s32[108]{0:T(128)}, u32[]{:S(2)}) copy-start(s32[108]{0:T(128)} %param.23) | copy-start | bytes 1300
  50.3 37.7 %copy-start.7 = (s32[108]{0:T(128)S(1)}, s32[108]{0:T(128)}, u32[]{:S(2)}) copy-start(s32[108]{0:T(128)} %param.24) | copy-start | bytes 1300
  50.3 37.7 %copy-start.4 = (s32[64,32]{0,1:T(8,128)S(1)}, s32[64,32]{0,1:T(8,128)}, u32[]{:S(2)}) copy-start(s32[64,32]{0,1:T(8,128)} %param.25) | copy-start | bytes 24580
  54.0 14.0 %collective-permute-start.11 = (f32[16,2,35,16]{2,3,1,0:T(8,128)S(1)}, f32[16,2,35,16]{2,3,1,0:T(8,128)S(1)}, u32[]{:S(2)}, u32[]{:S(2)}) collective-permute-start(f32[16,2,35,16]{2,3,1,0:T(8,128)S(1)} %maximum_select_fusion.3), channel_id=1, source_target_pairs={{0,128},{1,129},{2,130},{3,131},{4,132},{5,133},{6,134},{7,135},{8... | collective-permute-start | bytes 215048 | tf_op jit(solution)/shard_map/ppermute | solution.py:92
  68.2 29.9 %collective-permute-start.12 = (f32[32,2,35,16]{2,3,1,0:T(8,128)S(1)}, f32[32,2,35,16]{2,3,1,0:T(8,128)S(1)}, u32[]{:S(2)}, u32[]{:S(2)}) collective-permute-start(f32[32,2,35,16]{2,3,1,0:T(8,128)S(1)} %maximum_select_fusion.1), channel_id=1, source_target_pairs={{0,256},{1,257},{2,258},{3,259},{4,260},{5,261},{6,262},{7,263},{8... | collective-permute-start | bytes 430088 | tf_op jit(solution)/shard_map/ppermute | solution.py:92
  74.3 30.6 %collective-permute-start.1 = (f32[3,256]{1,0:T(4,128)S(1)}, f32[3,256]{1,0:T(4,128)S(1)}, u32[]{:S(2)}, u32[]{:S(2)}) collective-permute-start(f32[3,256]{1,0:T(4,128)S(1)} %copy-done.3), channel_id=1, source_target_pairs={{1,0},{2,1},{3,2},{4,3},{5,4},{6,5},{7,6},{8,7},{9,8},{10,9},{11,1... | collective-permute-start | bytes 9224 | tf_op jit(solution)/shard_map/ppermute | solution.py:30
  79.2 25.7 %collective-permute-start = (f32[3,256]{1,0:T(4,128)S(1)}, f32[3,256]{1,0:T(4,128)S(1)}, u32[]{:S(2)}, u32[]{:S(2)}) collective-permute-start(f32[3,256]{1,0:T(4,128)S(1)} %copy-done.3), channel_id=1, source_target_pairs={{0,1},{1,2},{2,3},{3,4},{4,5},{5,6},{6,7},{7,8},{8,9},{9,10},{10,1... | collective-permute-start | bytes 9224 | tf_op jit(solution)/shard_map/ppermute | solution.py:27
  81.9 23.1 %collective-permute-start.3 = (bf16[128,256]{1,0:T(8,128)(2,1)S(1)}, bf16[128,256]{1,0:T(8,128)(2,1)S(1)}, u32[]{:S(2)}, u32[]{:S(2)}) collective-permute-start(bf16[128,256]{1,0:T(8,128)(2,1)S(1)} %get-tuple-element.565), channel_id=1, source_target_pairs={{1,0},{2,1},{3,2},{4,3},{5,4},{6,5},{7,6},{8,7},{9,8},{10,9},{11,1... | collective-permute-start | bytes 196616 | tf_op jit(solution)/shard_map/ppermute | solution.py:30
  83.9 21.3 %collective-permute-start.2 = (bf16[128,256]{1,0:T(8,128)(2,1)S(1)}, bf16[128,256]{1,0:T(8,128)(2,1)S(1)}, u32[]{:S(2)}, u32[]{:S(2)}) collective-permute-start(bf16[128,256]{1,0:T(8,128)(2,1)S(1)} %get-tuple-element.565), channel_id=1, source_target_pairs={{0,1},{1,2},{2,3},{3,4},{4,5},{5,6},{6,7},{7,8},{8,9},{9,10},{10,1... | collective-permute-start | bytes 196616 | tf_op jit(solution)/shard_map/ppermute | solution.py:27
  98.6 2.6 copy-start.2
  101.4 4.3 %collective-permute-start.13 = (f32[2,35,16]{1,2,0:T(8,128)S(1)}, f32[2,35,16]{1,2,0:T(8,128)S(1)}, u32[]{:S(2)}, u32[]{:S(2)}) collective-permute-start(f32[2,35,16]{1,2,0:T(8,128)S(1)} %pad_maximum_fusion.1), channel_id=1, source_target_pairs={{0,1},{1,0},{2,3},{3,2},{4,5},{5,4},{6,7},{7,6},{8,9},{9,8},{10,11... | collective-permute-start | bytes 13448 | tf_op jit(solution)/shard_map/ppermute | solution.py:92
  105.7 4.6 %collective-permute-start.14 = (f32[2,35,32]{1,2,0:T(8,128)S(1)}, f32[2,35,32]{1,2,0:T(8,128)S(1)}, u32[]{:S(2)}, u32[]{:S(2)}) collective-permute-start(f32[2,35,32]{1,2,0:T(8,128)S(1)} %maximum_select_fusion.12), channel_id=1, source_target_pairs={{0,2},{1,3},{2,0},{3,1},{4,6},{5,7},{6,4},{7,5},{8,10},{9,11},{10,... | collective-permute-start | bytes 26888 | tf_op jit(solution)/shard_map/ppermute | solution.py:92
  110.4 23.1 %collective-permute-start.15 = (f32[2,35,64]{1,2,0:T(8,128)S(1)}, f32[2,35,64]{1,2,0:T(8,128)S(1)}, u32[]{:S(2)}, u32[]{:S(2)}) collective-permute-start(f32[2,35,64]{1,2,0:T(8,128)S(1)} %maximum_select_fusion.8), channel_id=1, source_target_pairs={{0,4},{1,5},{2,6},{3,7},{4,0},{5,1},{6,2},{7,3},{8,12},{9,13},{10,... | collective-permute-start | bytes 53768 | tf_op jit(solution)/shard_map/ppermute | solution.py:92
  115.0 18.7 %copy-start.8 = (f32[128]{0:T(128)S(1)}, f32[128]{0:T(128)}, u32[]{:S(2)}) copy-start(f32[128]{0:T(128)} %param.21) | copy-start | bytes 1540
  134.4 5.4 %collective-permute-start.18 = (f32[35,64]{1,0:T(8,128)S(1)}, f32[35,64]{1,0:T(8,128)S(1)}, u32[]{:S(2)}, u32[]{:S(2)}) collective-permute-start(f32[35,64]{1,0:T(8,128)S(1)} %slice_select_fusion.4), channel_id=1, source_target_pairs={{0,4},{1,5},{2,6},{3,7},{4,0},{5,1},{6,2},{7,3},{8,12},{9,13},{10,... | collective-permute-start | bytes 26888 | tf_op jit(solution)/shard_map/ppermute | solution.py:92
  140.0 4.5 %collective-permute-start.19 = (f32[35,32]{1,0:T(8,128)S(1)}, f32[35,32]{1,0:T(8,128)S(1)}, u32[]{:S(2)}, u32[]{:S(2)}) collective-permute-start(f32[35,32]{1,0:T(8,128)S(1)} %slice_select_fusion.3), channel_id=1, source_target_pairs={{0,2},{1,3},{2,0},{3,1},{4,6},{5,7},{6,4},{7,5},{8,10},{9,11},{10,... | collective-permute-start | bytes 13448 | tf_op jit(solution)/shard_map/ppermute | solution.py:92
  144.7 6.8 %collective-permute-start.20 = (f32[35,16]{1,0:T(8,128)S(1)}, f32[35,16]{1,0:T(8,128)S(1)}, u32[]{:S(2)}, u32[]{:S(2)}) collective-permute-start(f32[35,16]{1,0:T(8,128)S(1)} %slice_select_fusion.2), channel_id=1, source_target_pairs={{0,1},{1,0},{2,3},{3,2},{4,5},{5,4},{6,7},{7,6},{8,9},{9,8},{10,11... | collective-permute-start | bytes 6728 | tf_op jit(solution)/shard_map/ppermute | solution.py:92
  151.8 8.3 %collective-permute-start.21 = (f32[1,35,16]{1,2,0:T(8,128)S(1)}, f32[1,35,16]{1,2,0:T(8,128)S(1)}, u32[]{:S(2)}, u32[]{:S(2)}) collective-permute-start(f32[1,35,16]{1,2,0:T(8,128)S(1)} %bitcast.242), channel_id=1, source_target_pairs={{0,8},{1,9},{2,10},{3,11},{4,12},{5,13},{6,14},{7,15},{8,0},{9,1},... | collective-permute-start | bytes 6728 | tf_op jit(solution)/shard_map/ppermute | solution.py:92
  160.1 53.8 %collective-permute-start.22 = (f32[2,35,16]{1,2,0:T(8,128)S(1)}, f32[2,35,16]{1,2,0:T(8,128)S(1)}, u32[]{:S(2)}, u32[]{:S(2)}) collective-permute-start(f32[2,35,16]{1,2,0:T(8,128)S(1)} %maximum_select_fusion.18), channel_id=1, source_target_pairs={{0,16},{1,17},{2,18},{3,19},{4,20},{5,21},{6,22},{7,23},{8,24},{9,... | collective-permute-start | bytes 13448 | tf_op jit(solution)/shard_map/ppermute | solution.py:92
  213.9 10.2 %collective-permute-start.23 = (f32[4,35,16]{1,2,0:T(8,128)S(1)}, f32[4,35,16]{1,2,0:T(8,128)S(1)}, u32[]{:S(2)}, u32[]{:S(2)}) collective-permute-start(f32[4,35,16]{1,2,0:T(8,128)S(1)} %maximum_select_fusion.13), channel_id=1, source_target_pairs={{0,32},{1,33},{2,34},{3,35},{4,36},{5,37},{6,38},{7,39},{8,40},{9,... | collective-permute-start | bytes 26888 | tf_op jit(solution)/shard_map/ppermute | solution.py:92
  218.5 31.7 %copy-start.1 = (bf16[256,128]{1,0:T(8,128)(2,1)S(1)}, bf16[256,128]{1,0:T(8,128)(2,1)}, u32[]{:S(2)}) copy-start(bf16[256,128]{1,0:T(8,128)(2,1)} %param.18) | copy-start | bytes 196612
  218.6 31.6 %collective-permute-start.31 = (bf16[128,256]{0,1:T(8,128)(2,1)S(1)}, bf16[128,256]{0,1:T(8,128)(2,1)S(1)}, u32[]{:S(2)}, u32[]{:S(2)}) collective-permute-start(bf16[128,256]{0,1:T(8,128)(2,1)S(1)} %slice.362), channel_id=1, source_target_pairs={{0,1},{1,2},{2,3},{3,4},{4,5},{5,6},{6,7},{7,8},{8,9},{9,10},{10,1... | collective-permute-start | bytes 196616 | tf_op jit(solution)/shard_map/ppermute | solution.py:38
  222.2 28.1 %collective-permute-start.30 = (f32[128,256]{0,1:T(8,128)S(1)}, f32[128,256]{0,1:T(8,128)S(1)}, u32[]{:S(2)}, u32[]{:S(2)}) collective-permute-start(f32[128,256]{0,1:T(8,128)S(1)} %slice.245), channel_id=1, source_target_pairs={{1,0},{2,1},{3,2},{4,3},{5,4},{6,5},{7,6},{8,7},{9,8},{10,9},{11,1... | collective-permute-start | bytes 393224 | tf_op jit(solution)/shard_map/ppermute | solution.py:38
  224.1 16.5 %collective-permute-start.24 = (f32[8,35,16]{1,2,0:T(8,128)S(1)}, f32[8,35,16]{1,2,0:T(8,128)S(1)}, u32[]{:S(2)}, u32[]{:S(2)}) collective-permute-start(f32[8,35,16]{1,2,0:T(8,128)S(1)} %maximum_select_fusion.9), channel_id=1, source_target_pairs={{0,64},{1,65},{2,66},{3,67},{4,68},{5,69},{6,70},{7,71},{8,72},{9,... | collective-permute-start | bytes 53768 | tf_op jit(solution)/shard_map/ppermute | solution.py:92
  240.6 7.6 %collective-permute-start.25 = (f32[16,35,16]{1,2,0:T(8,128)S(1)}, f32[16,35,16]{1,2,0:T(8,128)S(1)}, u32[]{:S(2)}, u32[]{:S(2)}) collective-permute-start(f32[16,35,16]{1,2,0:T(8,128)S(1)} %maximum_select_fusion.6), channel_id=1, source_target_pairs={{0,128},{1,129},{2,130},{3,131},{4,132},{5,133},{6,134},{7,135},{8... | collective-permute-start | bytes 107528 | tf_op jit(solution)/shard_map/ppermute | solution.py:92
  248.3 12.4 %collective-permute-start.26 = (f32[32,35,16]{1,2,0:T(8,128)S(1)}, f32[32,35,16]{1,2,0:T(8,128)S(1)}, u32[]{:S(2)}, u32[]{:S(2)}) collective-permute-start(f32[32,35,16]{1,2,0:T(8,128)S(1)} %maximum_select_fusion.4), channel_id=1, source_target_pairs={{0,256},{1,257},{2,258},{3,259},{4,260},{5,261},{6,262},{7,263},{8... | collective-permute-start | bytes 215048 | tf_op jit(solution)/shard_map/ppermute | solution.py:92
  261.0 12.8 %collective-permute-start.27 = (f32[35,16]{1,0:T(8,128)S(1)}, f32[35,16]{1,0:T(8,128)S(1)}, u32[]{:S(2)}, u32[]{:S(2)}) collective-permute-start(f32[35,16]{1,0:T(8,128)S(1)} %copy.148), channel_id=1, source_target_pairs={{0,1},{1,0},{2,3},{3,2},{4,5},{5,4},{6,7},{7,6},{8,9},{9,8},{10,11... | collective-permute-start | bytes 6728 | tf_op jit(solution)/shard_map/ppermute | solution.py:92
  271.9 9.9 %collective-permute-start.32 = (f32[17737]{0:T(1024)S(1)}, f32[17737]{0:T(1024)S(1)}, u32[]{:S(2)}, u32[]{:S(2)}) collective-permute-start(f32[17737]{0:T(1024)S(1)} %concatenate.165), channel_id=1, source_target_pairs={{0,8},{1,9},{2,10},{3,11},{4,12},{5,13},{6,14},{7,15},{8,0},{9,1},... | collective-permute-start | bytes 212852 | tf_op jit(solution)/shard_map/ppermute | solution.py:92
  273.9 15.5 %collective-permute-start.28 = (f32[35,32]{1,0:T(8,128)S(1)}, f32[35,32]{1,0:T(8,128)S(1)}, u32[]{:S(2)}, u32[]{:S(2)}) collective-permute-start(f32[35,32]{1,0:T(8,128)S(1)} %maximum_select_fusion.14), channel_id=1, source_target_pairs={{0,2},{1,3},{2,0},{3,1},{4,6},{5,7},{6,4},{7,5},{8,10},{9,11},{10,... | collective-permute-start | bytes 13448 | tf_op jit(solution)/shard_map/ppermute | solution.py:92
  281.7 5.1 %collective-permute-start.33 = (f32[17737]{0:T(1024)S(1)}, f32[17737]{0:T(1024)S(1)}, u32[]{:S(2)}, u32[]{:S(2)}) collective-permute-start(f32[17737]{0:T(1024)S(1)} %add.226), channel_id=1, source_target_pairs={{0,16},{1,17},{2,18},{3,19},{4,20},{5,21},{6,22},{7,23},{8,24},{9,... | collective-permute-start | bytes 212852 | tf_op jit(solution)/shard_map/ppermute | solution.py:92
  286.8 6.6 %collective-permute-start.34 = (f32[17737]{0:T(1024)S(1)}, f32[17737]{0:T(1024)S(1)}, u32[]{:S(2)}, u32[]{:S(2)}) collective-permute-start(f32[17737]{0:T(1024)S(1)} %add.227), channel_id=1, source_target_pairs={{0,32},{1,33},{2,34},{3,35},{4,36},{5,37},{6,38},{7,39},{8,40},{9,... | collective-permute-start | bytes 212852 | tf_op jit(solution)/shard_map/ppermute | solution.py:92
  289.5 21.4 %collective-permute-start.29 = (f32[35,64]{1,0:T(8,128)S(1)}, f32[35,64]{1,0:T(8,128)S(1)}, u32[]{:S(2)}, u32[]{:S(2)}) collective-permute-start(f32[35,64]{1,0:T(8,128)S(1)} %maximum_select_fusion.15), channel_id=1, source_target_pairs={{0,4},{1,5},{2,6},{3,7},{4,0},{5,1},{6,2},{7,3},{8,12},{9,13},{10,... | collective-permute-start | bytes 26888 | tf_op jit(solution)/shard_map/ppermute | solution.py:92
  293.5 11.7 %collective-permute-start.35 = (f32[17737]{0:T(1024)S(1)}, f32[17737]{0:T(1024)S(1)}, u32[]{:S(2)}, u32[]{:S(2)}) collective-permute-start(f32[17737]{0:T(1024)S(1)} %add.228), channel_id=1, source_target_pairs={{0,64},{1,65},{2,66},{3,67},{4,68},{5,69},{6,70},{7,71},{8,72},{9,... | collective-permute-start | bytes 212852 | tf_op jit(solution)/shard_map/ppermute | solution.py:92
  298.4 41.8 %collective-permute-start.17 = (bf16[3,256]{1,0:T(4,128)(2,1)S(1)}, bf16[3,256]{1,0:T(4,128)(2,1)S(1)}, u32[]{:S(2)}, u32[]{:S(2)}) collective-permute-start(bf16[3,256]{1,0:T(4,128)(2,1)S(1)} %slice.363), channel_id=1, source_target_pairs={{0,1},{1,2},{2,3},{3,4},{4,5},{5,6},{6,7},{7,8},{8,9},{9,10},{10,1... | collective-permute-start | bytes 4616 | tf_op jit(solution)/shard_map/ppermute | solution.py:38
  303.3 36.9 %collective-permute-start.16 = (f32[3,256]{1,0:T(4,128)S(1)}, f32[3,256]{1,0:T(4,128)S(1)}, u32[]{:S(2)}, u32[]{:S(2)}) collective-permute-start(f32[3,256]{1,0:T(4,128)S(1)} %slice.236), channel_id=1, source_target_pairs={{1,0},{2,1},{3,2},{4,3},{5,4},{6,5},{7,6},{8,7},{9,8},{10,9},{11,1... | collective-permute-start | bytes 9224 | tf_op jit(solution)/shard_map/ppermute | solution.py:38
  305.2 8.1 %collective-permute-start.36 = (f32[17737]{0:T(1024)S(1)}, f32[17737]{0:T(1024)S(1)}, u32[]{:S(2)}, u32[]{:S(2)}) collective-permute-start(f32[17737]{0:T(1024)S(1)} %add.229), channel_id=1, source_target_pairs={{0,128},{1,129},{2,130},{3,131},{4,132},{5,133},{6,134},{7,135},{8... | collective-permute-start | bytes 212852 | tf_op jit(solution)/shard_map/ppermute | solution.py:92
  313.4 9.1 %collective-permute-start.37 = (f32[17737]{0:T(1024)S(1)}, f32[17737]{0:T(1024)S(1)}, u32[]{:S(2)}, u32[]{:S(2)}) collective-permute-start(f32[17737]{0:T(1024)S(1)} %add.230), channel_id=1, source_target_pairs={{0,256},{1,257},{2,258},{3,259},{4,260},{5,261},{6,262},{7,263},{8... | collective-permute-start | bytes 212852 | tf_op jit(solution)/shard_map/ppermute | solution.py:92
  322.5 10.6 %collective-permute-start.38 = (f32[17737]{0:T(1024)S(1)}, f32[17737]{0:T(1024)S(1)}, u32[]{:S(2)}, u32[]{:S(2)}) collective-permute-start(f32[17737]{0:T(1024)S(1)} %add.231), channel_id=1, source_target_pairs={{0,1},{1,0},{2,3},{3,2},{4,5},{5,4},{6,7},{7,6},{8,9},{9,8},{10,11... | collective-permute-start | bytes 212852 | tf_op jit(solution)/shard_map/ppermute | solution.py:92
  333.2 5.1 %collective-permute-start.39 = (f32[17737]{0:T(1024)S(1)}, f32[17737]{0:T(1024)S(1)}, u32[]{:S(2)}, u32[]{:S(2)}) collective-permute-start(f32[17737]{0:T(1024)S(1)} %add.232), channel_id=1, source_target_pairs={{0,2},{1,3},{2,0},{3,1},{4,6},{5,7},{6,4},{7,5},{8,10},{9,11},{10,... | collective-permute-start | bytes 212852 | tf_op jit(solution)/shard_map/ppermute | solution.py:92
  338.3 6.8 %collective-permute-start.40 = (f32[17737]{0:T(1024)S(1)}, f32[17737]{0:T(1024)S(1)}, u32[]{:S(2)}, u32[]{:S(2)}) collective-permute-start(f32[17737]{0:T(1024)S(1)} %add.233), channel_id=1, source_target_pairs={{0,4},{1,5},{2,6},{3,7},{4,0},{5,1},{6,2},{7,3},{8,12},{9,13},{10,... | collective-permute-start | bytes 212852 | tf_op jit(solution)/shard_map/ppermute | solution.py:92

commit v4 on v3

--- a/solution.py
+++ b/solution.py
@@ -111,7 +111,9 @@
 
 def tree_gather_sum(block, extra, index, bits, axis):
     for bit in bits:
-        other, other_extra = xor_swap((block, extra), bit)
+        packed = xor_swap(jnp.concatenate([block.reshape(-1), extra]), bit)
+        other = packed[: block.size].reshape(block.shape)
+        other_extra = packed[block.size :]
         up = ((index >> bit) & 1) == 1
         block = jnp.where(
             up,

time: 350 us -> 300 us (0.86)
  starting transfers between devices: 176 us -> 135 us
  waiting for transfers between devices: 82.3 us -> 65.9 us
  local copies, waits for them, and re-layouts: 22 us -> 25.8 us
    ppermute x33 -> x24, starting transfers between devices: 150 us -> 108 us  [xor_swap(): return lax.ppermute(block, 'box', [(i, i ^ 1 << bit) for i in range(count)])]
    ppermute x33 -> x24, waiting for transfers between devices: 82.3 us -> 65 us  [xor_swap(): return lax.ppermute(block, 'box', [(i, i ^ 1 << bit) for i in range(count)])]
  transfers between devices with their start and end apart: 41 -> 32, of which waited for: 25 -> 23; matrix products, arithmetic and copies ran while one was open for 22% -> 26% of each run, Pallas kernels for 0% -> 0%
where the time goes in v4:
time: 300 us; the launch traced here: 295 us
  starting transfers between devices  135 us (45%)
  waiting for transfers between devices  65.9 us (22%)
  matrix products  35.1 us (12%)
  other arithmetic  29.7 us (10%)
  local copies, waits for them, and re-layouts  25.8 us (9%)
    ppermute x24, starting transfers between devices, xor_swap(): return lax.ppermute(block, 'box', [(i, i ^ 1 << bit) for i in range(count)])  108 us
    ppermute x24, waiting for transfers between devices, xor_swap(): return lax.ppermute(block, 'box', [(i, i ^ 1 << bit) for i in range(count)])  65 us
    dot_general x12, matrix products, one_block(): jnp.einsum('pij,cpj->pic', kernel, source_feat, preferred_element_type=jn...  20.6 us
    ppermute x4, starting transfers between devices, passed_along(): return lax.ppermute(block, axis, route)  14.7 us
    scatter-add x4, other arithmetic, one_block(): source_feat = feat_leaf[:, src_ids].astype(jnp.bfloat16)  8.98 us
    dot_general x8, matrix products, one_block(): jnp.einsum('tp,pic->tic', onehot, contrib, precision=PRECISE)  7.35 us
    scatter-add x4, other arithmetic, one_block(): near_pos = own_leaf[:, tgt_ids]  6.98 us
    scatter-add x4, other arithmetic, one_block(): far_pos = ext_leaf[:, src_ids]  6.9 us
  transfers between devices with their start and end apart: 32, of which 23 were waited for; matrix products, arithmetic and copies ran while one was open for 26% of the time, Pallas kernels for 0%

profile of v4, /device:TPU:1, one launch (start us, length us, event | category | flops | bytes accessed | tf_op | source)
XLA Modules:
  0.0 295.2 jit_solution(17796240981899970953)
XLA Ops:
  5.7 6.6 %collective-permute-start.4 = (f32[2,35,64]{2,1,0:T(8,128)S(1)}, f32[2,35,64]{2,1,0:T(8,128)S(1)}, u32[]{:S(2)}, u32[]{:S(2)}) collective-permute-start(f32[2,35,64]{2,1,0:T(8,128)S(1)} %fusion.78), channel_id=1, source_target_pairs={{0,4},{1,5},{2,6},{3,7},{4,0},{5,1},{6,2},{7,3},{8,12},{9,13},{10,... | collective-permute-start | bytes 53768 | tf_op jit(solution)/shard_map/ppermute | solution.py:92
  13.9 4.0 %collective-permute-start.5 = (f32[2,35,32]{2,1,0:T(8,128)S(1)}, f32[2,35,32]{2,1,0:T(8,128)S(1)}, u32[]{:S(2)}, u32[]{:S(2)}) collective-permute-start(f32[2,35,32]{2,1,0:T(8,128)S(1)} %slice_select_fusion.1), channel_id=1, source_target_pairs={{0,2},{1,3},{2,0},{3,1},{4,6},{5,7},{6,4},{7,5},{8,10},{9,11},{10,... | collective-permute-start | bytes 26888 | tf_op jit(solution)/shard_map/ppermute | solution.py:92
  19.4 8.0 %collective-permute-start.6 = (f32[2,35,16]{2,1,0:T(8,128)S(1)}, f32[2,35,16]{2,1,0:T(8,128)S(1)}, u32[]{:S(2)}, u32[]{:S(2)}) collective-permute-start(f32[2,35,16]{2,1,0:T(8,128)S(1)} %slice_select_fusion), channel_id=1, source_target_pairs={{0,1},{1,0},{2,3},{3,2},{4,5},{5,4},{6,7},{7,6},{8,9},{9,8},{10,11... | collective-permute-start | bytes 13448 | tf_op jit(solution)/shard_map/ppermute | solution.py:92
  28.4 5.5 %collective-permute-start.7 = (f32[1,2,35,16]{3,2,1,0:T(8,128)S(1)}, f32[1,2,35,16]{3,2,1,0:T(8,128)S(1)}, u32[]{:S(2)}, u32[]{:S(2)}) collective-permute-start(f32[1,2,35,16]{3,2,1,0:T(8,128)S(1)} %add_bitcast_fusion.2), channel_id=1, source_target_pairs={{0,8},{1,9},{2,10},{3,11},{4,12},{5,13},{6,14},{7,15},{8,0},{9,1},... | collective-permute-start | bytes 13448 | tf_op jit(solution)/shard_map/ppermute | solution.py:92
  34.0 3.1 %collective-permute-done.7 = f32[1,2,35,16]{3,2,1,0:T(8,128)S(1)} collective-permute-done((f32[1,2,35,16]{3,2,1,0:T(8,128)S(1)}, f32[1,2,35,16]{3,2,1,0:T(8,128)S(1)}, u32[]{:S(2)}, u32[]{:S(2)}) %collective-permute-start.7) | collective-permute-done | bytes 4512 | tf_op jit(solution)/shard_map/ppermute | solution.py:92
  37.1 1.9 collective-permute-start.8
  39.0 2.7 collective-permute-done.8
  41.8 3.0 %collective-permute-start.9 = (f32[4,2,35,16]{2,3,1,0:T(8,128)S(1)}, f32[4,2,35,16]{2,3,1,0:T(8,128)S(1)}, u32[]{:S(2)}, u32[]{:S(2)}) collective-permute-start(f32[4,2,35,16]{2,3,1,0:T(8,128)S(1)} %maximum_select_fusion.7), channel_id=1, source_target_pairs={{0,32},{1,33},{2,34},{3,35},{4,36},{5,37},{6,38},{7,39},{8,40},{9,... | collective-permute-start | bytes 53768 | tf_op jit(solution)/shard_map/ppermute | solution.py:92
  44.8 3.5 %collective-permute-done.9 = f32[4,2,35,16]{2,3,1,0:T(8,128)S(1)} collective-permute-done((f32[4,2,35,16]{2,3,1,0:T(8,128)S(1)}, f32[4,2,35,16]{2,3,1,0:T(8,128)S(1)}, u32[]{:S(2)}, u32[]{:S(2)}) %collective-permute-start.9) | collective-permute-done | bytes 17952 | tf_op jit(solution)/shard_map/ppermute | solution.py:92
  48.3 1.9 collective-permute-start.10
  50.3 3.7 %collective-permute-done.10 = f32[8,2,35,16]{2,3,1,0:T(8,128)S(1)} collective-permute-done((f32[8,2,35,16]{2,3,1,0:T(8,128)S(1)}, f32[8,2,35,16]{2,3,1,0:T(8,128)S(1)}, u32[]{:S(2)}, u32[]{:S(2)}) %collective-permute-start.10) | collective-permute-done | bytes 35872 | tf_op jit(solution)/shard_map/ppermute | solution.py:92
  54.0 2.6 collective-permute-start.11
  56.6 11.5 %collective-permute-done.11 = f32[16,2,35,16]{2,3,1,0:T(8,128)S(1)} collective-permute-done((f32[16,2,35,16]{2,3,1,0:T(8,128)S(1)}, f32[16,2,35,16]{2,3,1,0:T(8,128)S(1)}, u32[]{:S(2)}, u32[]{:S(2)}) %collective-permute-start.11) | collective-permute-done | bytes 71712 | tf_op jit(solution)/shard_map/ppermute | solution.py:92
  68.2 6.2 %collective-permute-start.12 = (f32[32,2,35,16]{2,3,1,0:T(8,128)S(1)}, f32[32,2,35,16]{2,3,1,0:T(8,128)S(1)}, u32[]{:S(2)}, u32[]{:S(2)}) collective-permute-start(f32[32,2,35,16]{2,3,1,0:T(8,128)S(1)} %maximum_select_fusion.1), channel_id=1, source_target_pairs={{0,256},{1,257},{2,258},{3,259},{4,260},{5,261},{6,262},{7,263},{8... | collective-permute-start | bytes 430088 | tf_op jit(solution)/shard_map/ppermute | solution.py:92
  74.3 4.9 %collective-permute-start.1 = (f32[3,256]{1,0:T(4,128)S(1)}, f32[3,256]{1,0:T(4,128)S(1)}, u32[]{:S(2)}, u32[]{:S(2)}) collective-permute-start(f32[3,256]{1,0:T(4,128)S(1)} %copy-done.3), channel_id=1, source_target_pairs={{1,0},{2,1},{3,2},{4,3},{5,4},{6,5},{7,6},{8,7},{9,8},{10,9},{11,1... | collective-permute-start | bytes 9224 | tf_op jit(solution)/shard_map/ppermute | solution.py:30
  79.2 2.7 collective-permute-start
  81.9 1.9 collective-permute-start.3
  83.9 3.6 %collective-permute-start.2 = (bf16[128,256]{1,0:T(8,128)(2,1)S(1)}, bf16[128,256]{1,0:T(8,128)(2,1)S(1)}, u32[]{:S(2)}, u32[]{:S(2)}) collective-permute-start(bf16[128,256]{1,0:T(8,128)(2,1)S(1)} %get-tuple-element.565), channel_id=1, source_target_pairs={{0,1},{1,2},{2,3},{3,4},{4,5},{5,6},{6,7},{7,8},{8,9},{9,10},{10,1... | collective-permute-start | bytes 196616 | tf_op jit(solution)/shard_map/ppermute | solution.py:27
  89.0 9.1 %collective-permute-done.12 = f32[32,2,35,16]{2,3,1,0:T(8,128)S(1)} collective-permute-done((f32[32,2,35,16]{2,3,1,0:T(8,128)S(1)}, f32[32,2,35,16]{2,3,1,0:T(8,128)S(1)}, u32[]{:S(2)}, u32[]{:S(2)}) %collective-permute-start.12) | collective-permute-done | bytes 143392 | tf_op jit(solution)/shard_map/ppermute | solution.py:92
  99.0 2.2 fusion.67
  101.4 3.5 %collective-permute-start.13 = (f32[2,35,16]{1,2,0:T(8,128)S(1)}, f32[2,35,16]{1,2,0:T(8,128)S(1)}, u32[]{:S(2)}, u32[]{:S(2)}) collective-permute-start(f32[2,35,16]{1,2,0:T(8,128)S(1)} %pad_maximum_fusion.9), channel_id=1, source_target_pairs={{0,1},{1,0},{2,3},{3,2},{4,5},{5,4},{6,7},{7,6},{8,9},{9,8},{10,11... | collective-permute-start | bytes 13448 | tf_op jit(solution)/shard_map/ppermute | solution.py:92
  105.7 1.9 collective-permute-start.14
  107.7 2.7 collective-permute-done.14
  110.4 4.6 %collective-permute-start.15 = (f32[2,35,64]{1,2,0:T(8,128)S(1)}, f32[2,35,64]{1,2,0:T(8,128)S(1)}, u32[]{:S(2)}, u32[]{:S(2)}) collective-permute-start(f32[2,35,64]{1,2,0:T(8,128)S(1)} %maximum_select_fusion.8), channel_id=1, source_target_pairs={{0,4},{1,5},{2,6},{3,7},{4,0},{5,1},{6,2},{7,3},{8,12},{9,13},{10,... | collective-permute-start | bytes 53768 | tf_op jit(solution)/shard_map/ppermute | solution.py:92
  115.0 18.3 %while.33 = (s32[]{:T(128)}, f32[4,64,128]{2,0,1:T(4,128)S(1)}, s32[4,27]{1,0:T(4,128)S(1)}, f32[3,4,64]{2,0,1:T(4,128)S(1)}, s32[4,27]{1,0:T(4,128)S(1)}, /*ind...) while((s32[]{:T(128)}, f32[4,64,128]{2,0,1:T(4,128)S(1)}, ...), condition=%wide.region_1.2_spmd.clone, body=%wide.region_0.1_spmd.clone.sunk | while | flops 40212804 | bytes 3658967 | solution.py:86
  134.4 1.9 collective-permute-start.18
  136.5 3.3 %collective-permute-done.18 = f32[35,64]{1,0:T(8,128)S(1)} collective-permute-done((f32[35,64]{1,0:T(8,128)S(1)}, f32[35,64]{1,0:T(8,128)S(1)}, u32[]{:S(2)}, u32[]{:S(2)}) %collective-permute-start.18) | collective-permute-done | bytes 8992 | tf_op jit(solution)/shard_map/ppermute | solution.py:92
  140.0 2.1 collective-permute-start.19
  142.2 50.5 %while.32 = (s32[]{:T(128)}, f32[3,4,64]{2,0,1:T(4,128)S(1)}, f32[3,12,64]{2,0,1:T(4,128)S(1)}, f32[128,12,64]{0,2,1:T(8,128)S(1)}, f32[4,64,128]{2,0,1:T(4,128)...) while((s32[]{:T(128)}, f32[3,4,64]{2,0,1:T(4,128)S(1)}, ...), condition=%wide.region_13.14_spmd.clone, body=%wide.region_3.13_spmd.clone.sunk | while | flops 71802528 | bytes 7040317 | solution.py:86
  145.0 2.0 fusion.183
  147.1 1.7 scatter_fusion
  150.8 1.8 fusion.184
  152.5 2.2 scatter_fusion.2
  157.6 2.0 fusion.183
  163.4 1.8 fusion.184
  165.2 2.2 scatter_fusion.2
  170.3 2.0 fusion.183
  172.4 1.7 scatter_fusion
  176.0 1.8 fusion.184
  177.8 2.2 scatter_fusion.2
  182.9 2.0 fusion.183
  188.6 1.8 fusion.184
  190.4 2.2 scatter_fusion.2
  192.7 6.4 %collective-permute-start.22 = (bf16[128,256]{0,1:T(8,128)(2,1)S(1)}, bf16[128,256]{0,1:T(8,128)(2,1)S(1)}, u32[]{:S(2)}, u32[]{:S(2)}) collective-permute-start(bf16[128,256]{0,1:T(8,128)(2,1)S(1)} %slice.461), channel_id=1, source_target_pairs={{0,1},{1,2},{2,3},{3,4},{4,5},{5,6},{6,7},{7,8},{8,9},{9,10},{10,1... | collective-permute-start | bytes 196616 | tf_op jit(solution)/shard_map/ppermute | solution.py:38
  199.2 1.9 collective-permute-start.21
  201.3 1.9 collective-permute-start.20
  206.3 7.1 %collective-permute-start.23 = (f32[18297]{0:T(1024)S(1)}, f32[18297]{0:T(1024)S(1)}, u32[]{:S(2)}, u32[]{:S(2)}) collective-permute-start(f32[18297]{0:T(1024)S(1)} %concatenate.175), channel_id=1, source_target_pairs={{0,8},{1,9},{2,10},{3,11},{4,12},{5,13},{6,14},{7,15},{8,0},{9,1},... | collective-permute-start | bytes 219572 | tf_op jit(solution)/shard_map/ppermute | solution.py:92
  213.5 2.4 collective-permute-done.23
  216.5 5.9 %collective-permute-start.24 = (f32[18857]{0:T(1024)S(1)}, f32[18857]{0:T(1024)S(1)}, u32[]{:S(2)}, u32[]{:S(2)}) collective-permute-start(f32[18857]{0:T(1024)S(1)} %pad_maximum_fusion.5), channel_id=1, source_target_pairs={{0,16},{1,17},{2,18},{3,19},{4,20},{5,21},{6,22},{7,23},{8,24},{9,... | collective-permute-start | bytes 226292 | tf_op jit(solution)/shard_map/ppermute | solution.py:92
  222.5 1.8 collective-permute-done.24
  224.8 4.9 %collective-permute-start.25 = (f32[19977]{0:T(1024)S(1)}, f32[19977]{0:T(1024)S(1)}, u32[]{:S(2)}, u32[]{:S(2)}) collective-permute-start(f32[19977]{0:T(1024)S(1)} %pad_maximum_fusion.3), channel_id=1, source_target_pairs={{0,32},{1,33},{2,34},{3,35},{4,36},{5,37},{6,38},{7,39},{8,40},{9,... | collective-permute-start | bytes 239732 | tf_op jit(solution)/shard_map/ppermute | solution.py:92
  229.7 1.8 collective-permute-done.25
  232.1 12.8 %collective-permute-start.26 = (f32[22217]{0:T(1024)S(1)}, f32[22217]{0:T(1024)S(1)}, u32[]{:S(2)}, u32[]{:S(2)}) collective-permute-start(f32[22217]{0:T(1024)S(1)} %pad_maximum_fusion.2), channel_id=1, source_target_pairs={{0,64},{1,65},{2,66},{3,67},{4,68},{5,69},{6,70},{7,71},{8,72},{9,... | collective-permute-start | bytes 266612 | tf_op jit(solution)/shard_map/ppermute | solution.py:92
  244.9 1.9 collective-permute-done.26
  247.5 5.5 %collective-permute-start.27 = (f32[26697]{0:T(1024)S(1)}, f32[26697]{0:T(1024)S(1)}, u32[]{:S(2)}, u32[]{:S(2)}) collective-permute-start(f32[26697]{0:T(1024)S(1)} %pad_maximum_fusion.1), channel_id=1, source_target_pairs={{0,128},{1,129},{2,130},{3,131},{4,132},{5,133},{6,134},{7,135},{8... | collective-permute-start | bytes 320372 | tf_op jit(solution)/shard_map/ppermute | solution.py:92
  252.9 2.1 collective-permute-done.27
  256.0 4.4 %collective-permute-start.28 = (f32[35657]{0:T(1024)S(1)}, f32[35657]{0:T(1024)S(1)}, u32[]{:S(2)}, u32[]{:S(2)}) collective-permute-start(f32[35657]{0:T(1024)S(1)} %pad_maximum_fusion), channel_id=1, source_target_pairs={{0,256},{1,257},{2,258},{3,259},{4,260},{5,261},{6,262},{7,263},{8... | collective-permute-start | bytes 427892 | tf_op jit(solution)/shard_map/ppermute | solution.py:92
  260.6 6.4 %collective-permute-done.28 = f32[35657]{0:T(1024)S(1)} collective-permute-done((f32[35657]{0:T(1024)S(1)}, f32[35657]{0:T(1024)S(1)}, u32[]{:S(2)}, u32[]{:S(2)}) %collective-permute-start.28) | collective-permute-done | bytes 142660 | tf_op jit(solution)/shard_map/ppermute | solution.py:92
  268.0 6.8 %collective-permute-start.29 = (f32[18297]{0:T(1024)S(1)}, f32[18297]{0:T(1024)S(1)}, u32[]{:S(2)}, u32[]{:S(2)}) collective-permute-start(f32[18297]{0:T(1024)S(1)} %pad_maximum_fusion.7), channel_id=1, source_target_pairs={{0,1},{1,0},{2,3},{3,2},{4,5},{5,4},{6,7},{7,6},{8,9},{9,8},{10,11... | collective-permute-start | bytes 219572 | tf_op jit(solution)/shard_map/ppermute | solution.py:92
  276.1 1.9 collective-permute-start.30
  278.3 3.3 %collective-permute-done.30 = f32[18857]{0:T(1024)S(1)} collective-permute-done((f32[18857]{0:T(1024)S(1)}, f32[18857]{0:T(1024)S(1)}, u32[]{:S(2)}, u32[]{:S(2)}) %collective-permute-start.30) | collective-permute-done | bytes 75460 | tf_op jit(solution)/shard_map/ppermute | solution.py:92
  282.0 2.5 collective-permute-start.31
  285.2 4.4 %collective-permute-start.17 = (bf16[3,256]{1,0:T(4,128)(2,1)S(1)}, bf16[3,256]{1,0:T(4,128)(2,1)S(1)}, u32[]{:S(2)}, u32[]{:S(2)}) collective-permute-start(bf16[3,256]{1,0:T(4,128)(2,1)S(1)} %slice.462), channel_id=1, source_target_pairs={{0,1},{1,2},{2,3},{3,4},{4,5},{5,6},{6,7},{7,8},{8,9},{9,10},{10,1... | collective-permute-start | bytes 4616 | tf_op jit(solution)/shard_map/ppermute | solution.py:38
  289.7 1.9 collective-permute-start.16
  (404 shorter events, 67.4 us)
Async XLA Ops:
  0.6 3.7 %copy-start = (bf16[128,128]{1,0:T(8,128)(2,1)S(1)}, bf16[128,128]{1,0:T(8,128)(2,1)}, u32[]{:S(2)}) copy-start(bf16[128,128]{1,0:T(8,128)(2,1)} %param.19) | copy-start | bytes 98308
  5.7 8.0 %collective-permute-start.4 = (f32[2,35,64]{2,1,0:T(8,128)S(1)}, f32[2,35,64]{2,1,0:T(8,128)S(1)}, u32[]{:S(2)}, u32[]{:S(2)}) collective-permute-start(f32[2,35,64]{2,1,0:T(8,128)S(1)} %fusion.78), channel_id=1, source_target_pairs={{0,4},{1,5},{2,6},{3,7},{4,0},{5,1},{6,2},{7,3},{8,12},{9,13},{10,... | collective-permute-start | bytes 53768 | tf_op jit(solution)/shard_map/ppermute | solution.py:92
  13.9 5.4 %collective-permute-start.5 = (f32[2,35,32]{2,1,0:T(8,128)S(1)}, f32[2,35,32]{2,1,0:T(8,128)S(1)}, u32[]{:S(2)}, u32[]{:S(2)}) collective-permute-start(f32[2,35,32]{2,1,0:T(8,128)S(1)} %slice_select_fusion.1), channel_id=1, source_target_pairs={{0,2},{1,3},{2,0},{3,1},{4,6},{5,7},{6,4},{7,5},{8,10},{9,11},{10,... | collective-permute-start | bytes 26888 | tf_op jit(solution)/shard_map/ppermute | solution.py:92
  19.4 8.9 %collective-permute-start.6 = (f32[2,35,16]{2,1,0:T(8,128)S(1)}, f32[2,35,16]{2,1,0:T(8,128)S(1)}, u32[]{:S(2)}, u32[]{:S(2)}) collective-permute-start(f32[2,35,16]{2,1,0:T(8,128)S(1)} %slice_select_fusion), channel_id=1, source_target_pairs={{0,1},{1,0},{2,3},{3,2},{4,5},{5,4},{6,7},{7,6},{8,9},{9,8},{10,11... | collective-permute-start | bytes 13448 | tf_op jit(solution)/shard_map/ppermute | solution.py:92
  28.4 8.6 %collective-permute-start.7 = (f32[1,2,35,16]{3,2,1,0:T(8,128)S(1)}, f32[1,2,35,16]{3,2,1,0:T(8,128)S(1)}, u32[]{:S(2)}, u32[]{:S(2)}) collective-permute-start(f32[1,2,35,16]{3,2,1,0:T(8,128)S(1)} %add_bitcast_fusion.2), channel_id=1, source_target_pairs={{0,8},{1,9},{2,10},{3,11},{4,12},{5,13},{6,14},{7,15},{8,0},{9,1},... | collective-permute-start | bytes 13448 | tf_op jit(solution)/shard_map/ppermute | solution.py:92
  37.1 4.7 %collective-permute-start.8 = (f32[2,2,35,16]{2,3,1,0:T(8,128)S(1)}, f32[2,2,35,16]{2,3,1,0:T(8,128)S(1)}, u32[]{:S(2)}, u32[]{:S(2)}) collective-permute-start(f32[2,2,35,16]{2,3,1,0:T(8,128)S(1)} %maximum_select_fusion.11), channel_id=1, source_target_pairs={{0,16},{1,17},{2,18},{3,19},{4,20},{5,21},{6,22},{7,23},{8,24},{9,... | collective-permute-start | bytes 26888 | tf_op jit(solution)/shard_map/ppermute | solution.py:92
  41.8 6.5 %collective-permute-start.9 = (f32[4,2,35,16]{2,3,1,0:T(8,128)S(1)}, f32[4,2,35,16]{2,3,1,0:T(8,128)S(1)}, u32[]{:S(2)}, u32[]{:S(2)}) collective-permute-start(f32[4,2,35,16]{2,3,1,0:T(8,128)S(1)} %maximum_select_fusion.7), channel_id=1, source_target_pairs={{0,32},{1,33},{2,34},{3,35},{4,36},{5,37},{6,38},{7,39},{8,40},{9,... | collective-permute-start | bytes 53768 | tf_op jit(solution)/shard_map/ppermute | solution.py:92
  44.8 29.6 %copy-start.3 = (f32[3,256]{1,0:T(4,128)S(1)}, f32[3,256]{1,0:T(4,128)}, u32[]{:S(2)}) copy-start(f32[3,256]{1,0:T(4,128)} %param.15) | copy-start | bytes 9220
  48.3 5.7 %collective-permute-start.10 = (f32[8,2,35,16]{2,3,1,0:T(8,128)S(1)}, f32[8,2,35,16]{2,3,1,0:T(8,128)S(1)}, u32[]{:S(2)}, u32[]{:S(2)}) collective-permute-start(f32[8,2,35,16]{2,3,1,0:T(8,128)S(1)} %maximum_select_fusion.5), channel_id=1, source_target_pairs={{0,64},{1,65},{2,66},{3,67},{4,68},{5,69},{6,70},{7,71},{8,72},{9,... | collective-permute-start | bytes 107528 | tf_op jit(solution)/shard_map/ppermute | solution.py:92
  50.2 37.5 %copy-start.5 = (s32[108]{0:T(128)S(1)}, s32[108]{0:T(128)}, u32[]{:S(2)}) copy-start(s32[108]{0:T(128)} %param.22) | copy-start | bytes 1300
  50.2 37.6 %copy-start.6 = (s32[108]{0:T(128)S(1)}, s32[108]{0:T(128)}, u32[]{:S(2)}) copy-start(s32[108]{0:T(128)} %param.23) | copy-start | bytes 1300
  50.3 37.7 %copy-start.7 = (s32[108]{0:T(128)S(1)}, s32[108]{0:T(128)}, u32[]{:S(2)}) copy-start(s32[108]{0:T(128)} %param.24) | copy-start | bytes 1300
  50.3 37.7 %copy-start.4 = (s32[64,32]{0,1:T(8,128)S(1)}, s32[64,32]{0,1:T(8,128)}, u32[]{:S(2)}) copy-start(s32[64,32]{0,1:T(8,128)} %param.25) | copy-start | bytes 24580
  54.0 14.0 %collective-permute-start.11 = (f32[16,2,35,16]{2,3,1,0:T(8,128)S(1)}, f32[16,2,35,16]{2,3,1,0:T(8,128)S(1)}, u32[]{:S(2)}, u32[]{:S(2)}) collective-permute-start(f32[16,2,35,16]{2,3,1,0:T(8,128)S(1)} %maximum_select_fusion.3), channel_id=1, source_target_pairs={{0,128},{1,129},{2,130},{3,131},{4,132},{5,133},{6,134},{7,135},{8... | collective-permute-start | bytes 215048 | tf_op jit(solution)/shard_map/ppermute | solution.py:92
  68.2 29.9 %collective-permute-start.12 = (f32[32,2,35,16]{2,3,1,0:T(8,128)S(1)}, f32[32,2,35,16]{2,3,1,0:T(8,128)S(1)}, u32[]{:S(2)}, u32[]{:S(2)}) collective-permute-start(f32[32,2,35,16]{2,3,1,0:T(8,128)S(1)} %maximum_select_fusion.1), channel_id=1, source_target_pairs={{0,256},{1,257},{2,258},{3,259},{4,260},{5,261},{6,262},{7,263},{8... | collective-permute-start | bytes 430088 | tf_op jit(solution)/shard_map/ppermute | solution.py:92
  74.3 30.6 %collective-permute-start.1 = (f32[3,256]{1,0:T(4,128)S(1)}, f32[3,256]{1,0:T(4,128)S(1)}, u32[]{:S(2)}, u32[]{:S(2)}) collective-permute-start(f32[3,256]{1,0:T(4,128)S(1)} %copy-done.3), channel_id=1, source_target_pairs={{1,0},{2,1},{3,2},{4,3},{5,4},{6,5},{7,6},{8,7},{9,8},{10,9},{11,1... | collective-permute-start | bytes 9224 | tf_op jit(solution)/shard_map/ppermute | solution.py:30
  79.2 25.7 %collective-permute-start = (f32[3,256]{1,0:T(4,128)S(1)}, f32[3,256]{1,0:T(4,128)S(1)}, u32[]{:S(2)}, u32[]{:S(2)}) collective-permute-start(f32[3,256]{1,0:T(4,128)S(1)} %copy-done.3), channel_id=1, source_target_pairs={{0,1},{1,2},{2,3},{3,4},{4,5},{5,6},{6,7},{7,8},{8,9},{9,10},{10,1... | collective-permute-start | bytes 9224 | tf_op jit(solution)/shard_map/ppermute | solution.py:27
  81.9 23.1 %collective-permute-start.3 = (bf16[128,256]{1,0:T(8,128)(2,1)S(1)}, bf16[128,256]{1,0:T(8,128)(2,1)S(1)}, u32[]{:S(2)}, u32[]{:S(2)}) collective-permute-start(bf16[128,256]{1,0:T(8,128)(2,1)S(1)} %get-tuple-element.565), channel_id=1, source_target_pairs={{1,0},{2,1},{3,2},{4,3},{5,4},{6,5},{7,6},{8,7},{9,8},{10,9},{11,1... | collective-permute-start | bytes 196616 | tf_op jit(solution)/shard_map/ppermute | solution.py:30
  83.9 21.3 %collective-permute-start.2 = (bf16[128,256]{1,0:T(8,128)(2,1)S(1)}, bf16[128,256]{1,0:T(8,128)(2,1)S(1)}, u32[]{:S(2)}, u32[]{:S(2)}) collective-permute-start(bf16[128,256]{1,0:T(8,128)(2,1)S(1)} %get-tuple-element.565), channel_id=1, source_target_pairs={{0,1},{1,2},{2,3},{3,4},{4,5},{5,6},{6,7},{7,8},{8,9},{9,10},{10,1... | collective-permute-start | bytes 196616 | tf_op jit(solution)/shard_map/ppermute | solution.py:27
  98.6 2.6 copy-start.2
  101.4 4.3 %collective-permute-start.13 = (f32[2,35,16]{1,2,0:T(8,128)S(1)}, f32[2,35,16]{1,2,0:T(8,128)S(1)}, u32[]{:S(2)}, u32[]{:S(2)}) collective-permute-start(f32[2,35,16]{1,2,0:T(8,128)S(1)} %pad_maximum_fusion.9), channel_id=1, source_target_pairs={{0,1},{1,0},{2,3},{3,2},{4,5},{5,4},{6,7},{7,6},{8,9},{9,8},{10,11... | collective-permute-start | bytes 13448 | tf_op jit(solution)/shard_map/ppermute | solution.py:92
  105.7 4.6 %collective-permute-start.14 = (f32[2,35,32]{1,2,0:T(8,128)S(1)}, f32[2,35,32]{1,2,0:T(8,128)S(1)}, u32[]{:S(2)}, u32[]{:S(2)}) collective-permute-start(f32[2,35,32]{1,2,0:T(8,128)S(1)} %maximum_select_fusion.12), channel_id=1, source_target_pairs={{0,2},{1,3},{2,0},{3,1},{4,6},{5,7},{6,4},{7,5},{8,10},{9,11},{10,... | collective-permute-start | bytes 26888 | tf_op jit(solution)/shard_map/ppermute | solution.py:92
  110.4 23.1 %collective-permute-start.15 = (f32[2,35,64]{1,2,0:T(8,128)S(1)}, f32[2,35,64]{1,2,0:T(8,128)S(1)}, u32[]{:S(2)}, u32[]{:S(2)}) collective-permute-start(f32[2,35,64]{1,2,0:T(8,128)S(1)} %maximum_select_fusion.8), channel_id=1, source_target_pairs={{0,4},{1,5},{2,6},{3,7},{4,0},{5,1},{6,2},{7,3},{8,12},{9,13},{10,... | collective-permute-start | bytes 53768 | tf_op jit(solution)/shard_map/ppermute | solution.py:92
  115.0 18.7 %copy-start.8 = (f32[128]{0:T(128)S(1)}, f32[128]{0:T(128)}, u32[]{:S(2)}) copy-start(f32[128]{0:T(128)} %param.21) | copy-start | bytes 1540
  134.4 5.4 %collective-permute-start.18 = (f32[35,64]{1,0:T(8,128)S(1)}, f32[35,64]{1,0:T(8,128)S(1)}, u32[]{:S(2)}, u32[]{:S(2)}) collective-permute-start(f32[35,64]{1,0:T(8,128)S(1)} %slice_select_fusion.4), channel_id=1, source_target_pairs={{0,4},{1,5},{2,6},{3,7},{4,0},{5,1},{6,2},{7,3},{8,12},{9,13},{10,... | collective-permute-start | bytes 26888 | tf_op jit(solution)/shard_map/ppermute | solution.py:92
  140.0 61.1 %collective-permute-start.19 = (f32[35,32]{1,0:T(8,128)S(1)}, f32[35,32]{1,0:T(8,128)S(1)}, u32[]{:S(2)}, u32[]{:S(2)}) collective-permute-start(f32[35,32]{1,0:T(8,128)S(1)} %slice_select_fusion.3), channel_id=1, source_target_pairs={{0,2},{1,3},{2,0},{3,1},{4,6},{5,7},{6,4},{7,5},{8,10},{9,11},{10,... | collective-permute-start | bytes 13448 | tf_op jit(solution)/shard_map/ppermute | solution.py:92
  192.7 12.8 %copy-start.1 = (bf16[256,128]{1,0:T(8,128)(2,1)S(1)}, bf16[256,128]{1,0:T(8,128)(2,1)}, u32[]{:S(2)}) copy-start(bf16[256,128]{1,0:T(8,128)(2,1)} %param.18) | copy-start | bytes 196612
  192.7 12.4 %collective-permute-start.22 = (bf16[128,256]{0,1:T(8,128)(2,1)S(1)}, bf16[128,256]{0,1:T(8,128)(2,1)S(1)}, u32[]{:S(2)}, u32[]{:S(2)}) collective-permute-start(bf16[128,256]{0,1:T(8,128)(2,1)S(1)} %slice.461), channel_id=1, source_target_pairs={{0,1},{1,2},{2,3},{3,4},{4,5},{5,6},{6,7},{7,8},{8,9},{9,10},{10,1... | collective-permute-start | bytes 196616 | tf_op jit(solution)/shard_map/ppermute | solution.py:38
  199.2 6.3 %collective-permute-start.21 = (f32[128,256]{0,1:T(8,128)S(1)}, f32[128,256]{0,1:T(8,128)S(1)}, u32[]{:S(2)}, u32[]{:S(2)}) collective-permute-start(f32[128,256]{0,1:T(8,128)S(1)} %slice.317), channel_id=1, source_target_pairs={{1,0},{2,1},{3,2},{4,3},{5,4},{6,5},{7,6},{8,7},{9,8},{10,9},{11,1... | collective-permute-start | bytes 393224 | tf_op jit(solution)/shard_map/ppermute | solution.py:38
  201.3 3.1 %collective-permute-start.20 = (f32[35,16]{1,0:T(8,128)S(1)}, f32[35,16]{1,0:T(8,128)S(1)}, u32[]{:S(2)}, u32[]{:S(2)}) collective-permute-start(f32[35,16]{1,0:T(8,128)S(1)} %slice_select_fusion.2), channel_id=1, source_target_pairs={{0,1},{1,0},{2,3},{3,2},{4,5},{5,4},{6,7},{7,6},{8,9},{9,8},{10,11... | collective-permute-start | bytes 6728 | tf_op jit(solution)/shard_map/ppermute | solution.py:92
  206.3 9.7 %collective-permute-start.23 = (f32[18297]{0:T(1024)S(1)}, f32[18297]{0:T(1024)S(1)}, u32[]{:S(2)}, u32[]{:S(2)}) collective-permute-start(f32[18297]{0:T(1024)S(1)} %concatenate.175), channel_id=1, source_target_pairs={{0,8},{1,9},{2,10},{3,11},{4,12},{5,13},{6,14},{7,15},{8,0},{9,1},... | collective-permute-start | bytes 219572 | tf_op jit(solution)/shard_map/ppermute | solution.py:92
  216.5 7.7 %collective-permute-start.24 = (f32[18857]{0:T(1024)S(1)}, f32[18857]{0:T(1024)S(1)}, u32[]{:S(2)}, u32[]{:S(2)}) collective-permute-start(f32[18857]{0:T(1024)S(1)} %pad_maximum_fusion.5), channel_id=1, source_target_pairs={{0,16},{1,17},{2,18},{3,19},{4,20},{5,21},{6,22},{7,23},{8,24},{9,... | collective-permute-start | bytes 226292 | tf_op jit(solution)/shard_map/ppermute | solution.py:92
  224.8 6.7 %collective-permute-start.25 = (f32[19977]{0:T(1024)S(1)}, f32[19977]{0:T(1024)S(1)}, u32[]{:S(2)}, u32[]{:S(2)}) collective-permute-start(f32[19977]{0:T(1024)S(1)} %pad_maximum_fusion.3), channel_id=1, source_target_pairs={{0,32},{1,33},{2,34},{3,35},{4,36},{5,37},{6,38},{7,39},{8,40},{9,... | collective-permute-start | bytes 239732 | tf_op jit(solution)/shard_map/ppermute | solution.py:92
  232.1 14.8 %collective-permute-start.26 = (f32[22217]{0:T(1024)S(1)}, f32[22217]{0:T(1024)S(1)}, u32[]{:S(2)}, u32[]{:S(2)}) collective-permute-start(f32[22217]{0:T(1024)S(1)} %pad_maximum_fusion.2), channel_id=1, source_target_pairs={{0,64},{1,65},{2,66},{3,67},{4,68},{5,69},{6,70},{7,71},{8,72},{9,... | collective-permute-start | bytes 266612 | tf_op jit(solution)/shard_map/ppermute | solution.py:92
  247.5 7.6 %collective-permute-start.27 = (f32[26697]{0:T(1024)S(1)}, f32[26697]{0:T(1024)S(1)}, u32[]{:S(2)}, u32[]{:S(2)}) collective-permute-start(f32[26697]{0:T(1024)S(1)} %pad_maximum_fusion.1), channel_id=1, source_target_pairs={{0,128},{1,129},{2,130},{3,131},{4,132},{5,133},{6,134},{7,135},{8... | collective-permute-start | bytes 320372 | tf_op jit(solution)/shard_map/ppermute | solution.py:92
  256.0 11.0 %collective-permute-start.28 = (f32[35657]{0:T(1024)S(1)}, f32[35657]{0:T(1024)S(1)}, u32[]{:S(2)}, u32[]{:S(2)}) collective-permute-start(f32[35657]{0:T(1024)S(1)} %pad_maximum_fusion), channel_id=1, source_target_pairs={{0,256},{1,257},{2,258},{3,259},{4,260},{5,261},{6,262},{7,263},{8... | collective-permute-start | bytes 427892 | tf_op jit(solution)/shard_map/ppermute | solution.py:92
  268.0 7.7 %collective-permute-start.29 = (f32[18297]{0:T(1024)S(1)}, f32[18297]{0:T(1024)S(1)}, u32[]{:S(2)}, u32[]{:S(2)}) collective-permute-start(f32[18297]{0:T(1024)S(1)} %pad_maximum_fusion.7), channel_id=1, source_target_pairs={{0,1},{1,0},{2,3},{3,2},{4,5},{5,4},{6,7},{7,6},{8,9},{9,8},{10,11... | collective-permute-start | bytes 219572 | tf_op jit(solution)/shard_map/ppermute | solution.py:92
  276.1 5.5 %collective-permute-start.30 = (f32[18857]{0:T(1024)S(1)}, f32[18857]{0:T(1024)S(1)}, u32[]{:S(2)}, u32[]{:S(2)}) collective-permute-start(f32[18857]{0:T(1024)S(1)} %pad_maximum_fusion.6), channel_id=1, source_target_pairs={{0,2},{1,3},{2,0},{3,1},{4,6},{5,7},{6,4},{7,5},{8,10},{9,11},{10,... | collective-permute-start | bytes 226292 | tf_op jit(solution)/shard_map/ppermute | solution.py:92
  282.0 9.6 %collective-permute-start.31 = (f32[19977]{0:T(1024)S(1)}, f32[19977]{0:T(1024)S(1)}, u32[]{:S(2)}, u32[]{:S(2)}) collective-permute-start(f32[19977]{0:T(1024)S(1)} %pad_maximum_fusion.4), channel_id=1, source_target_pairs={{0,4},{1,5},{2,6},{3,7},{4,0},{5,1},{6,2},{7,3},{8,12},{9,13},{10,... | collective-permute-start | bytes 239732 | tf_op jit(solution)/shard_map/ppermute | solution.py:92
  285.2 8.9 %collective-permute-start.17 = (bf16[3,256]{1,0:T(4,128)(2,1)S(1)}, bf16[3,256]{1,0:T(4,128)(2,1)S(1)}, u32[]{:S(2)}, u32[]{:S(2)}) collective-permute-start(bf16[3,256]{1,0:T(4,128)(2,1)S(1)} %slice.462), channel_id=1, source_target_pairs={{0,1},{1,2},{2,3},{3,4},{4,5},{5,6},{6,7},{7,8},{8,9},{9,10},{10,1... | collective-permute-start | bytes 4616 | tf_op jit(solution)/shard_map/ppermute | solution.py:38
  289.7 4.9 %collective-permute-start.16 = (f32[3,256]{1,0:T(4,128)S(1)}, f32[3,256]{1,0:T(4,128)S(1)}, u32[]{:S(2)}, u32[]{:S(2)}) collective-permute-start(f32[3,256]{1,0:T(4,128)S(1)} %slice.308), channel_id=1, source_target_pairs={{1,0},{2,1},{3,2},{4,3},{5,4},{6,5},{7,6},{8,7},{9,8},{10,9},{11,1... | collective-permute-start | bytes 9224 | tf_op jit(solution)/shard_map/ppermute | solution.py:38

commit v5 on v4

--- a/solution.py
+++ b/solution.py
@@ -57,33 +57,26 @@
     own_leaf = pos_own.reshape(3, leaves, LEAF_ATOMS)
     ext_leaf = pos_ext.reshape(3, 3 * leaves, LEAF_ATOMS)
     feat_leaf = hid_ext.reshape(channels, 3 * leaves, LEAF_ATOMS)
-    leaf_ids = jnp.arange(leaves, dtype=jnp.int32)
-    blocks = (
-        targets.reshape(-1, PAIR_LEAF),
-        sources.reshape(-1, PAIR_LEAF),
-        alive.reshape(-1, PAIR_LEAF),
-    )
-
-    def one_block(accumulated, pair_block):
-        tgt_ids, src_ids, live_ids = pair_block
-        near_pos = own_leaf[:, tgt_ids]
-        far_pos = ext_leaf[:, src_ids]
-        dist_sq = jnp.zeros((tgt_ids.shape[0], LEAF_ATOMS, LEAF_ATOMS), jnp.float32)
-        for axis_id in range(3):
-            offset_ax = near_pos[axis_id][:, :, None] - far_pos[axis_id][:, None, :]
-            dist_sq = dist_sq + offset_ax * offset_ax
-        kernel = (
-            NEAR_SCALE * jnp.exp(-GAMMA * dist_sq) * live_ids.astype(jnp.float32)[:, None, None]
-        ).astype(jnp.bfloat16)
-        source_feat = feat_leaf[:, src_ids].astype(jnp.bfloat16)
-        contrib = jnp.einsum(
-            "pij,cpj->pic", kernel, source_feat, preferred_element_type=jnp.float32
-        )
-        onehot = (tgt_ids[None, :] == leaf_ids[:, None]).astype(jnp.float32)
-        return (accumulated + jnp.einsum("tp,pic->tic", onehot, contrib, precision=PRECISE), None)
-
-    initial = jnp.zeros((leaves, LEAF_ATOMS, channels), jnp.float32)
-    accumulated, unused = lax.scan(jax.checkpoint(one_block), initial, blocks)
+    tgt_hot = (targets[:, None] == jnp.arange(leaves, dtype=jnp.int32)[None, :]).astype(
+        jnp.float32
+    )
+    src_hot = (sources[:, None] == jnp.arange(3 * leaves, dtype=jnp.int32)[None, :]).astype(
+        jnp.float32
+    )
+    near_pos = jnp.einsum("pt,xti->xpi", tgt_hot, own_leaf, precision=PRECISE)
+    far_pos = jnp.einsum("ps,xsj->xpj", src_hot, ext_leaf, precision=PRECISE)
+    dist_sq = jnp.zeros((targets.shape[0], LEAF_ATOMS, LEAF_ATOMS), jnp.float32)
+    for axis_id in range(3):
+        offset_ax = near_pos[axis_id][:, :, None] - far_pos[axis_id][:, None, :]
+        dist_sq = dist_sq + offset_ax * offset_ax
+    kernel = (
+        NEAR_SCALE * jnp.exp(-GAMMA * dist_sq) * alive.astype(jnp.float32)[:, None, None]
+    ).astype(jnp.bfloat16)
+    source_feat = jnp.einsum("ps,csj->pjc", src_hot, feat_leaf, precision=PRECISE).astype(
+        jnp.bfloat16
+    )
+    contrib = jnp.einsum("pij,pjc->pic", kernel, source_feat, preferred_element_type=jnp.float32)
+    accumulated = jnp.einsum("pt,pic->tic", tgt_hot, contrib, precision=PRECISE)
     return accumulated.reshape(leaves * LEAF_ATOMS, channels)
 
 

time: 300 us -> 259 us (0.86)
  the two profiles are of different devices: /device:TPU:1 before, /device:TPU:2 now
where the time goes in v5:
time: 259 us; the launch traced here: 258 us
  starting transfers between devices  118 us (46%)
  waiting for transfers between devices  82.4 us (32%)
  matrix products  36.4 us (14%)
  local copies, waits for them, and re-layouts  11.7 us (5%)
  other arithmetic  7.55 us (3%)
    ppermute x24, starting transfers between devices, xor_swap(): return lax.ppermute(block, 'box', [(i, i ^ 1 << bit) for i in range(count)])  91.1 us
    ppermute x24, waiting for transfers between devices, xor_swap(): return lax.ppermute(block, 'box', [(i, i ^ 1 << bit) for i in range(count)])  80.5 us
    dot_general x3, matrix products, near_field(): jnp.einsum('pij,pjc->pic', kernel, source_feat, preferred_element_type=jn...  20.8 us
    ppermute x2, starting transfers between devices, extended(): lax.ppermute(lax.slice_in_dim(block, 0, width, axis=dim), axis, backward)  11.8 us
    ppermute x4, starting transfers between devices, passed_along(): return lax.ppermute(block, axis, route)  11.6 us
  transfers between devices with their start and end apart: 32, of which 19 were waited for; matrix products, arithmetic and copies ran while one was open for 15% of the time, Pallas kernels for 0%

profile of v5, /device:TPU:2, one launch (start us, length us, event | category | flops | bytes accessed | tf_op | source)
XLA Modules:
  0.0 257.9 jit_solution(7755961024024973578)
XLA Ops:
  0.7 0.8 broadcast_in_dim.12
  2.2 0.7 iota_compare_fusion.3
  3.1 1.0 fusion.129
  4.3 1.1 convolution_bitcast_fusion.3
  5.7 6.1 %collective-permute-start.4 = (f32[2,35,64]{2,1,0:T(8,128)S(1)}, f32[2,35,64]{2,1,0:T(8,128)S(1)}, u32[]{:S(2)}, u32[]{:S(2)}) collective-permute-start(f32[2,35,64]{2,1,0:T(8,128)S(1)} %fusion.57), channel_id=1, source_target_pairs={{0,4},{1,5},{2,6},{3,7},{4,0},{5,1},{6,2},{7,3},{8,12},{9,13},{10,... | collective-permute-start | bytes 53768 | tf_op jit(solution)/shard_map/ppermute | solution.py:85
  11.8 2.0 collective-permute-done.4
  13.9 4.3 %collective-permute-start.5 = (f32[2,35,32]{2,1,0:T(8,128)S(1)}, f32[2,35,32]{2,1,0:T(8,128)S(1)}, u32[]{:S(2)}, u32[]{:S(2)}) collective-permute-start(f32[2,35,32]{2,1,0:T(8,128)S(1)} %slice_select_fusion.1), channel_id=1, source_target_pairs={{0,2},{1,3},{2,0},{3,1},{4,6},{5,7},{6,4},{7,5},{8,10},{9,11},{10,... | collective-permute-start | bytes 26888 | tf_op jit(solution)/shard_map/ppermute | solution.py:85
  18.2 6.0 %collective-permute-start.3 = (bf16[128,256]{1,0:T(8,128)(2,1)S(1)}, bf16[128,256]{1,0:T(8,128)(2,1)S(1)}, u32[]{:S(2)}, u32[]{:S(2)}) collective-permute-start(bf16[128,256]{1,0:T(8,128)(2,1)S(1)} %get-tuple-element.56), channel_id=1, source_target_pairs={{1,0},{2,1},{3,2},{4,3},{5,4},{6,5},{7,6},{8,7},{9,8},{10,9},{11,1... | collective-permute-start | bytes 196616 | tf_op jit(solution)/shard_map/ppermute | solution.py:30
  24.2 1.9 collective-permute-start.2
  26.2 5.8 %collective-permute-start.1 = (f32[3,256]{1,0:T(4,128)}, f32[3,256]{1,0:T(4,128)S(1)}, u32[]{:S(2)}, u32[]{:S(2)}) collective-permute-start(f32[3,256]{1,0:T(4,128)} %param.11), channel_id=1, source_target_pairs={{1,0},{2,1},{3,2},{4,3},{5,4},{6,5},{7,6},{8,7},{9,8},{10,9},{11,1... | collective-permute-start | bytes 9224 | tf_op jit(solution)/shard_map/ppermute | solution.py:30
  31.9 1.9 collective-permute-start
  33.8 0.8 reshape.208
  34.8 1.9 collective-permute-start.6
  36.7 0.9 convolution_bitcast_fusion.1
  38.0 3.8 %collective-permute-start.7 = (f32[1,2,35,16]{3,2,1,0:T(8,128)S(1)}, f32[1,2,35,16]{3,2,1,0:T(8,128)S(1)}, u32[]{:S(2)}, u32[]{:S(2)}) collective-permute-start(f32[1,2,35,16]{3,2,1,0:T(8,128)S(1)} %add_bitcast_fusion), channel_id=1, source_target_pairs={{0,8},{1,9},{2,10},{3,11},{4,12},{5,13},{6,14},{7,15},{8,0},{9,1},... | collective-permute-start | bytes 13448 | tf_op jit(solution)/shard_map/ppermute | solution.py:85
  41.8 6.4 %collective-permute-done.7 = f32[1,2,35,16]{3,2,1,0:T(8,128)S(1)} collective-permute-done((f32[1,2,35,16]{3,2,1,0:T(8,128)S(1)}, f32[1,2,35,16]{3,2,1,0:T(8,128)S(1)}, u32[]{:S(2)}, u32[]{:S(2)}) %collective-permute-start.7) | collective-permute-done | bytes 4512 | tf_op jit(solution)/shard_map/ppermute | solution.py:85
  48.3 1.9 collective-permute-start.8
  50.9 0.8 copy.175
  51.7 2.4 collective-permute-done.8
  54.1 4.1 %collective-permute-start.9 = (f32[4,2,35,16]{2,3,1,0:T(8,128)S(1)}, f32[4,2,35,16]{2,3,1,0:T(8,128)S(1)}, u32[]{:S(2)}, u32[]{:S(2)}) collective-permute-start(f32[4,2,35,16]{2,3,1,0:T(8,128)S(1)} %maximum_select_fusion.7), channel_id=1, source_target_pairs={{0,32},{1,33},{2,34},{3,35},{4,36},{5,37},{6,38},{7,39},{8,40},{9,... | collective-permute-start | bytes 53768 | tf_op jit(solution)/shard_map/ppermute | solution.py:85
  59.1 2.7 %collective-permute-done.9 = f32[4,2,35,16]{2,3,1,0:T(8,128)S(1)} collective-permute-done((f32[4,2,35,16]{2,3,1,0:T(8,128)S(1)}, f32[4,2,35,16]{2,3,1,0:T(8,128)S(1)}, u32[]{:S(2)}, u32[]{:S(2)}) %collective-permute-start.9) | collective-permute-done | bytes 17952 | tf_op jit(solution)/shard_map/ppermute | solution.py:85
  61.8 5.8 %collective-permute-start.10 = (f32[8,2,35,16]{2,3,1,0:T(8,128)S(1)}, f32[8,2,35,16]{2,3,1,0:T(8,128)S(1)}, u32[]{:S(2)}, u32[]{:S(2)}) collective-permute-start(f32[8,2,35,16]{2,3,1,0:T(8,128)S(1)} %maximum_select_fusion.5), channel_id=1, source_target_pairs={{0,64},{1,65},{2,66},{3,67},{4,68},{5,69},{6,70},{7,71},{8,72},{9,... | collective-permute-start | bytes 107528 | tf_op jit(solution)/shard_map/ppermute | solution.py:85
  68.4 2.1 collective-permute-done.10
  70.6 4.9 %collective-permute-start.11 = (f32[16,2,35,16]{2,3,1,0:T(8,128)S(1)}, f32[16,2,35,16]{2,3,1,0:T(8,128)S(1)}, u32[]{:S(2)}, u32[]{:S(2)}) collective-permute-start(f32[16,2,35,16]{2,3,1,0:T(8,128)S(1)} %maximum_select_fusion.3), channel_id=1, source_target_pairs={{0,128},{1,129},{2,130},{3,131},{4,132},{5,133},{6,134},{7,135},{8... | collective-permute-start | bytes 215048 | tf_op jit(solution)/shard_map/ppermute | solution.py:85
  75.8 7.9 %collective-permute-done.11 = f32[16,2,35,16]{2,3,1,0:T(8,128)S(1)} collective-permute-done((f32[16,2,35,16]{2,3,1,0:T(8,128)S(1)}, f32[16,2,35,16]{2,3,1,0:T(8,128)S(1)}, u32[]{:S(2)}, u32[]{:S(2)}) %collective-permute-start.11) | collective-permute-done | bytes 71712 | tf_op jit(solution)/shard_map/ppermute | solution.py:85
  83.8 8.8 %collective-permute-start.12 = (f32[32,2,35,16]{2,3,1,0:T(8,128)S(1)}, f32[32,2,35,16]{2,3,1,0:T(8,128)S(1)}, u32[]{:S(2)}, u32[]{:S(2)}) collective-permute-start(f32[32,2,35,16]{2,3,1,0:T(8,128)S(1)} %maximum_select_fusion.1), channel_id=1, source_target_pairs={{0,256},{1,257},{2,258},{3,259},{4,260},{5,261},{6,262},{7,263},{8... | collective-permute-start | bytes 430088 | tf_op jit(solution)/shard_map/ppermute | solution.py:85
  93.6 20.4 %collective-permute-done.12 = f32[32,2,35,16]{2,3,1,0:T(8,128)S(1)} collective-permute-done((f32[32,2,35,16]{2,3,1,0:T(8,128)S(1)}, f32[32,2,35,16]{2,3,1,0:T(8,128)S(1)}, u32[]{:S(2)}, u32[]{:S(2)}) %collective-permute-start.12) | collective-permute-done | bytes 143392 | tf_op jit(solution)/shard_map/ppermute | solution.py:85
  114.9 2.2 fusion.31
  117.3 1.9 collective-permute-start.13
  120.4 1.9 collective-permute-start.14
  122.4 6.9 %fusion.26 = f32[108,64,128]{2,1,0:T(8,128)S(1)} fusion(bf16[108,64,128]{2,0,1:T(8,128)(2,1)S(1)} %convert_bitcast_fusion, f32[108]{0:T(128)S(1)} %broadcast_multiply_fusion, f32[108,64]{1,0:T(8,128)S(1)} %copy.169, f32[108,64]{1,0:T(8,128)S(1)} %copy.168, f32[108,64]{1,0:T(8,128)S(1)} %copy.167, f32[108,64]{1,0:T(8,128)S(1)} %copy.166, ...), kind=kOutput, calls=%fused_computation.32 | convolution fusion | flops 118112256 | bytes 5474736 | tf_op jit(solution)/shard_map/jvp(pij,pjc->pic)/dot_general | solution.py:78
  129.3 5.5 %collective-permute-start.15 = (f32[2,35,64]{1,2,0:T(8,128)S(1)}, f32[2,35,64]{1,2,0:T(8,128)S(1)}, u32[]{:S(2)}, u32[]{:S(2)}) collective-permute-start(f32[2,35,64]{1,2,0:T(8,128)S(1)} %maximum_select_fusion.8), channel_id=1, source_target_pairs={{0,4},{1,5},{2,6},{3,7},{4,0},{5,1},{6,2},{7,3},{8,12},{9,13},{10,... | collective-permute-start | bytes 53768 | tf_op jit(solution)/shard_map/ppermute | solution.py:85
  134.8 3.3 %fusion = f32[4,64,128]{2,0,1:T(4,128)S(1)} fusion(f32[108,64,128]{2,1,0:T(8,128)S(1)} %fusion.26, s32[108]{0:T(128)S(1)} %copy-done.5), kind=kOutput, calls=%fused_computation.6 | convolution fusion | flops 42467760 | bytes 3670448 | tf_op jit(solution)/shard_map/jvp(pt,pic->tic)/dot_general | solution.py:79
  139.1 1.7 fusion.51
  140.9 3.4 %collective-permute-start.18 = (f32[35,64]{1,0:T(8,128)S(1)}, f32[35,64]{1,0:T(8,128)S(1)}, u32[]{:S(2)}, u32[]{:S(2)}) collective-permute-start(f32[35,64]{1,0:T(8,128)S(1)} %slice_select_fusion.4), channel_id=1, source_target_pairs={{0,4},{1,5},{2,6},{3,7},{4,0},{5,1},{6,2},{7,3},{8,12},{9,13},{10,... | collective-permute-start | bytes 26888 | tf_op jit(solution)/shard_map/ppermute | solution.py:85
  144.3 6.0 %convert_bitcast_fusion.1 = bf16[128,64,108]{0,1,2:T(8,128)(2,1)S(1)} fusion(bf16[108,64,128]{2,0,1:T(8,128)(2,1)S(1)} %fusion.51, f32[108]{0:T(128)S(1)} %broadcast_multiply_fusion, f32[108,64]{1,0:T(8,128)S(1)} %copy.169, f32[108,64]{1,0:T(8,128)S(1)} %copy.168, f32[108,64]{1,0:T(8,128)S(1)} %copy.167, f32[108,64]{1,0:T(8,128)S(1)} %copy.166, ...), kind=kOutput, calls=%fused_computation.30 | convolution fusion | flops 118112256 | bytes 3705264 | tf_op jit(solution)/shard_map/transpose(jvp(pij,pjc->pic))/dot_general | solution.py:78
  150.5 2.6 %collective-permute-start.19 = (f32[35,32]{1,0:T(8,128)S(1)}, f32[35,32]{1,0:T(8,128)S(1)}, u32[]{:S(2)}, u32[]{:S(2)}) collective-permute-start(f32[35,32]{1,0:T(8,128)S(1)} %slice_select_fusion.3), channel_id=1, source_target_pairs={{0,2},{1,3},{2,0},{3,1},{4,6},{5,7},{6,4},{7,5},{8,10},{9,11},{10,... | collective-permute-start | bytes 13448 | tf_op jit(solution)/shard_map/ppermute | solution.py:85
  153.1 1.0 fusion.28
  154.4 5.9 %collective-permute-start.21 = (f32[128,256]{0,1:T(8,128)S(1)}, f32[128,256]{0,1:T(8,128)S(1)}, u32[]{:S(2)}, u32[]{:S(2)}) collective-permute-start(f32[128,256]{0,1:T(8,128)S(1)} %slice.239), channel_id=1, source_target_pairs={{1,0},{2,1},{3,2},{4,3},{5,4},{6,5},{7,6},{8,7},{9,8},{10,9},{11,1... | collective-permute-start | bytes 393224 | tf_op jit(solution)/shard_map/ppermute | solution.py:38
  160.2 1.9 collective-permute-start.22
  162.3 1.9 collective-permute-start.20
  164.4 1.0 collective-permute-done.20
  166.1 1.8 collective-permute-done.22
  168.7 2.6 %collective-permute-start.23 = (f32[18297]{0:T(1024)S(1)}, f32[18297]{0:T(1024)S(1)}, u32[]{:S(2)}, u32[]{:S(2)}) collective-permute-start(f32[18297]{0:T(1024)S(1)} %concatenate.165), channel_id=1, source_target_pairs={{0,8},{1,9},{2,10},{3,11},{4,12},{5,13},{6,14},{7,15},{8,0},{9,1},... | collective-permute-start | bytes 219572 | tf_op jit(solution)/shard_map/ppermute | solution.py:85
  171.6 7.4 %collective-permute-done.23 = f32[18297]{0:T(1024)S(1)} collective-permute-done((f32[18297]{0:T(1024)S(1)}, f32[18297]{0:T(1024)S(1)}, u32[]{:S(2)}, u32[]{:S(2)}) %collective-permute-start.23) | collective-permute-done | bytes 73220 | tf_op jit(solution)/shard_map/ppermute | solution.py:85
  179.6 1.9 collective-permute-start.24
  181.5 8.0 %fusion.14 = (f32[108,64]{1,0:T(8,128)S(1)}, f32[108,64]{1,0:T(8,128)S(1)}, f32[108,64]{1,0:T(8,128)S(1)}, f32[108,64]{1,0:T(8,128)S(1)}, f32[108,64]{1,0:T(8,128)S(1)}, /*index=5*/f32[108,64]{1,0:T(8,128)S(1)}) fusion(f32[108,64]{1,0:T(8,128)S(1)} %copy.169, f32[108,64]{1,0:T(8,128)S(1)} %copy.168, f32[108,64]{1,0:T(8,128)S(1)} %copy.165, ...), kind=kOutput, calls=%fused_computation.22 | convolution fusion | flops 124706304 | bytes 3871152 | tf_op jit(solution)/shard_map/transpose(jvp(pij,pjc->pic))/dot_general | solution.py:78
  190.1 5.2 %collective-permute-start.25 = (f32[19977]{0:T(1024)S(1)}, f32[19977]{0:T(1024)S(1)}, u32[]{:S(2)}, u32[]{:S(2)}) collective-permute-start(f32[19977]{0:T(1024)S(1)} %pad_maximum_fusion.4), channel_id=1, source_target_pairs={{0,32},{1,33},{2,34},{3,35},{4,36},{5,37},{6,38},{7,39},{8,40},{9,... | collective-permute-start | bytes 239732 | tf_op jit(solution)/shard_map/ppermute | solution.py:85
  195.4 2.6 collective-permute-done.25
  198.5 7.8 %collective-permute-start.26 = (f32[22217]{0:T(1024)S(1)}, f32[22217]{0:T(1024)S(1)}, u32[]{:S(2)}, u32[]{:S(2)}) collective-permute-start(f32[22217]{0:T(1024)S(1)} %pad_maximum_fusion.3), channel_id=1, source_target_pairs={{0,64},{1,65},{2,66},{3,67},{4,68},{5,69},{6,70},{7,71},{8,72},{9,... | collective-permute-start | bytes 266612 | tf_op jit(solution)/shard_map/ppermute | solution.py:85
  206.5 3.0 %collective-permute-done.26 = f32[22217]{0:T(1024)S(1)} collective-permute-done((f32[22217]{0:T(1024)S(1)}, f32[22217]{0:T(1024)S(1)}, u32[]{:S(2)}, u32[]{:S(2)}) %collective-permute-start.26) | collective-permute-done | bytes 88900 | tf_op jit(solution)/shard_map/ppermute | solution.py:85
  210.2 1.9 collective-permute-start.27
  212.4 9.6 %collective-permute-done.27 = f32[26697]{0:T(1024)S(1)} collective-permute-done((f32[26697]{0:T(1024)S(1)}, f32[26697]{0:T(1024)S(1)}, u32[]{:S(2)}, u32[]{:S(2)}) %collective-permute-start.27) | collective-permute-done | bytes 106820 | tf_op jit(solution)/shard_map/ppermute | solution.py:85
  222.9 5.8 %collective-permute-start.28 = (f32[35657]{0:T(1024)S(1)}, f32[35657]{0:T(1024)S(1)}, u32[]{:S(2)}, u32[]{:S(2)}) collective-permute-start(f32[35657]{0:T(1024)S(1)} %pad_maximum_fusion.1), channel_id=1, source_target_pairs={{0,256},{1,257},{2,258},{3,259},{4,260},{5,261},{6,262},{7,263},{8... | collective-permute-start | bytes 427892 | tf_op jit(solution)/shard_map/ppermute | solution.py:85
  228.7 6.6 %collective-permute-done.28 = f32[35657]{0:T(1024)S(1)} collective-permute-done((f32[35657]{0:T(1024)S(1)}, f32[35657]{0:T(1024)S(1)}, u32[]{:S(2)}, u32[]{:S(2)}) %collective-permute-start.28) | collective-permute-done | bytes 142660 | tf_op jit(solution)/shard_map/ppermute | solution.py:85
  236.3 1.9 collective-permute-start.29
  238.4 1.0 collective-permute-done.29
  239.9 1.9 collective-permute-start.30
  242.5 1.9 collective-permute-start.16
  244.4 1.8 collective-permute-done.30
  246.6 3.1 %collective-permute-start.31 = (f32[19977]{0:T(1024)S(1)}, f32[19977]{0:T(1024)S(1)}, u32[]{:S(2)}, u32[]{:S(2)}) collective-permute-start(f32[19977]{0:T(1024)S(1)} %pad_maximum_fusion.5), channel_id=1, source_target_pairs={{0,4},{1,5},{2,6},{3,7},{4,0},{5,1},{6,2},{7,3},{8,12},{9,13},{10,... | collective-permute-start | bytes 239732 | tf_op jit(solution)/shard_map/ppermute | solution.py:85
  250.0 1.9 collective-permute-start.17
  251.9 2.9 %collective-permute-done.31 = f32[19977]{0:T(1024)S(1)} collective-permute-done((f32[19977]{0:T(1024)S(1)}, f32[19977]{0:T(1024)S(1)}, u32[]{:S(2)}, u32[]{:S(2)}) %collective-permute-start.31) | collective-permute-done | bytes 79940 | tf_op jit(solution)/shard_map/ppermute | solution.py:85
  256.6 0.7 reshape.230
  (194 shorter events, 20.4 us)
Async XLA Ops:
  0.6 2.4 copy-start
  0.6 74.9 %copy-start.4 = (s32[108]{0:T(128)S(1)}, s32[108]{0:T(128)}, u32[]{:S(2)}) copy-start(s32[108]{0:T(128)} %param.19) | copy-start | bytes 1300
  5.7 8.1 %collective-permute-start.4 = (f32[2,35,64]{2,1,0:T(8,128)S(1)}, f32[2,35,64]{2,1,0:T(8,128)S(1)}, u32[]{:S(2)}, u32[]{:S(2)}) collective-permute-start(f32[2,35,64]{2,1,0:T(8,128)S(1)} %fusion.57), channel_id=1, source_target_pairs={{0,4},{1,5},{2,6},{3,7},{4,0},{5,1},{6,2},{7,3},{8,12},{9,13},{10,... | collective-permute-start | bytes 53768 | tf_op jit(solution)/shard_map/ppermute | solution.py:85
  13.9 20.7 %collective-permute-start.5 = (f32[2,35,32]{2,1,0:T(8,128)S(1)}, f32[2,35,32]{2,1,0:T(8,128)S(1)}, u32[]{:S(2)}, u32[]{:S(2)}) collective-permute-start(f32[2,35,32]{2,1,0:T(8,128)S(1)} %slice_select_fusion.1), channel_id=1, source_target_pairs={{0,2},{1,3},{2,0},{3,1},{4,6},{5,7},{6,4},{7,5},{8,10},{9,11},{10,... | collective-permute-start | bytes 26888 | tf_op jit(solution)/shard_map/ppermute | solution.py:85
  18.2 74.7 %collective-permute-start.3 = (bf16[128,256]{1,0:T(8,128)(2,1)S(1)}, bf16[128,256]{1,0:T(8,128)(2,1)S(1)}, u32[]{:S(2)}, u32[]{:S(2)}) collective-permute-start(bf16[128,256]{1,0:T(8,128)(2,1)S(1)} %get-tuple-element.56), channel_id=1, source_target_pairs={{1,0},{2,1},{3,2},{4,3},{5,4},{6,5},{7,6},{8,7},{9,8},{10,9},{11,1... | collective-permute-start | bytes 196616 | tf_op jit(solution)/shard_map/ppermute | solution.py:30
  24.2 68.7 %collective-permute-start.2 = (bf16[128,256]{1,0:T(8,128)(2,1)S(1)}, bf16[128,256]{1,0:T(8,128)(2,1)S(1)}, u32[]{:S(2)}, u32[]{:S(2)}) collective-permute-start(bf16[128,256]{1,0:T(8,128)(2,1)S(1)} %get-tuple-element.56), channel_id=1, source_target_pairs={{0,1},{1,2},{2,3},{3,4},{4,5},{5,6},{6,7},{7,8},{8,9},{9,10},{10,1... | collective-permute-start | bytes 196616 | tf_op jit(solution)/shard_map/ppermute | solution.py:27
  26.2 41.4 %collective-permute-start.1 = (f32[3,256]{1,0:T(4,128)}, f32[3,256]{1,0:T(4,128)S(1)}, u32[]{:S(2)}, u32[]{:S(2)}) collective-permute-start(f32[3,256]{1,0:T(4,128)} %param.11), channel_id=1, source_target_pairs={{1,0},{2,1},{3,2},{4,3},{5,4},{6,5},{7,6},{8,7},{9,8},{10,9},{11,1... | collective-permute-start | bytes 9224 | tf_op jit(solution)/shard_map/ppermute | solution.py:30
  31.9 35.7 %collective-permute-start = (f32[3,256]{1,0:T(4,128)}, f32[3,256]{1,0:T(4,128)S(1)}, u32[]{:S(2)}, u32[]{:S(2)}) collective-permute-start(f32[3,256]{1,0:T(4,128)} %param.11), channel_id=1, source_target_pairs={{0,1},{1,2},{2,3},{3,4},{4,5},{5,6},{6,7},{7,8},{8,9},{9,10},{10,1... | collective-permute-start | bytes 9224 | tf_op jit(solution)/shard_map/ppermute | solution.py:27
  34.8 3.1 %collective-permute-start.6 = (f32[2,35,16]{2,1,0:T(8,128)S(1)}, f32[2,35,16]{2,1,0:T(8,128)S(1)}, u32[]{:S(2)}, u32[]{:S(2)}) collective-permute-start(f32[2,35,16]{2,1,0:T(8,128)S(1)} %slice_select_fusion), channel_id=1, source_target_pairs={{0,1},{1,0},{2,3},{3,2},{4,5},{5,4},{6,7},{7,6},{8,9},{9,8},{10,11... | collective-permute-start | bytes 13448 | tf_op jit(solution)/shard_map/ppermute | solution.py:85
  38.0 10.2 %collective-permute-start.7 = (f32[1,2,35,16]{3,2,1,0:T(8,128)S(1)}, f32[1,2,35,16]{3,2,1,0:T(8,128)S(1)}, u32[]{:S(2)}, u32[]{:S(2)}) collective-permute-start(f32[1,2,35,16]{3,2,1,0:T(8,128)S(1)} %add_bitcast_fusion), channel_id=1, source_target_pairs={{0,8},{1,9},{2,10},{3,11},{4,12},{5,13},{6,14},{7,15},{8,0},{9,1},... | collective-permute-start | bytes 13448 | tf_op jit(solution)/shard_map/ppermute | solution.py:85
  48.3 5.8 %collective-permute-start.8 = (f32[2,2,35,16]{2,3,1,0:T(8,128)S(1)}, f32[2,2,35,16]{2,3,1,0:T(8,128)S(1)}, u32[]{:S(2)}, u32[]{:S(2)}) collective-permute-start(f32[2,2,35,16]{2,3,1,0:T(8,128)S(1)} %maximum_select_fusion.11), channel_id=1, source_target_pairs={{0,16},{1,17},{2,18},{3,19},{4,20},{5,21},{6,22},{7,23},{8,24},{9,... | collective-permute-start | bytes 26888 | tf_op jit(solution)/shard_map/ppermute | solution.py:85
  54.1 7.7 %collective-permute-start.9 = (f32[4,2,35,16]{2,3,1,0:T(8,128)S(1)}, f32[4,2,35,16]{2,3,1,0:T(8,128)S(1)}, u32[]{:S(2)}, u32[]{:S(2)}) collective-permute-start(f32[4,2,35,16]{2,3,1,0:T(8,128)S(1)} %maximum_select_fusion.7), channel_id=1, source_target_pairs={{0,32},{1,33},{2,34},{3,35},{4,36},{5,37},{6,38},{7,39},{8,40},{9,... | collective-permute-start | bytes 53768 | tf_op jit(solution)/shard_map/ppermute | solution.py:85
  61.8 8.7 %collective-permute-start.10 = (f32[8,2,35,16]{2,3,1,0:T(8,128)S(1)}, f32[8,2,35,16]{2,3,1,0:T(8,128)S(1)}, u32[]{:S(2)}, u32[]{:S(2)}) collective-permute-start(f32[8,2,35,16]{2,3,1,0:T(8,128)S(1)} %maximum_select_fusion.5), channel_id=1, source_target_pairs={{0,64},{1,65},{2,66},{3,67},{4,68},{5,69},{6,70},{7,71},{8,72},{9,... | collective-permute-start | bytes 107528 | tf_op jit(solution)/shard_map/ppermute | solution.py:85
  70.5 46.6 %copy-start.3 = (f32[35,35]{1,0:T(8,128)S(1)}, f32[35,35]{1,0:T(8,128)}, u32[]{:S(2)}) copy-start(f32[35,35]{1,0:T(8,128)} %param.16) | copy-start | bytes 14704
  70.6 13.1 %collective-permute-start.11 = (f32[16,2,35,16]{2,3,1,0:T(8,128)S(1)}, f32[16,2,35,16]{2,3,1,0:T(8,128)S(1)}, u32[]{:S(2)}, u32[]{:S(2)}) collective-permute-start(f32[16,2,35,16]{2,3,1,0:T(8,128)S(1)} %maximum_select_fusion.3), channel_id=1, source_target_pairs={{0,128},{1,129},{2,130},{3,131},{4,132},{5,133},{6,134},{7,135},{8... | collective-permute-start | bytes 215048 | tf_op jit(solution)/shard_map/ppermute | solution.py:85
  83.8 30.2 %collective-permute-start.12 = (f32[32,2,35,16]{2,3,1,0:T(8,128)S(1)}, f32[32,2,35,16]{2,3,1,0:T(8,128)S(1)}, u32[]{:S(2)}, u32[]{:S(2)}) collective-permute-start(f32[32,2,35,16]{2,3,1,0:T(8,128)S(1)} %maximum_select_fusion.1), channel_id=1, source_target_pairs={{0,256},{1,257},{2,258},{3,259},{4,260},{5,261},{6,262},{7,263},{8... | collective-permute-start | bytes 430088 | tf_op jit(solution)/shard_map/ppermute | solution.py:85
  117.3 3.1 %collective-permute-start.13 = (f32[2,35,16]{1,2,0:T(8,128)S(1)}, f32[2,35,16]{1,2,0:T(8,128)S(1)}, u32[]{:S(2)}, u32[]{:S(2)}) collective-permute-start(f32[2,35,16]{1,2,0:T(8,128)S(1)} %pad_maximum_fusion.10), channel_id=1, source_target_pairs={{0,1},{1,0},{2,3},{3,2},{4,5},{5,4},{6,7},{7,6},{8,9},{9,8},{10,11... | collective-permute-start | bytes 13448 | tf_op jit(solution)/shard_map/ppermute | solution.py:85
  120.4 14.3 %copy-start.5 = (s32[108]{0:T(128)S(1)}, s32[108]{0:T(128)}, u32[]{:S(2)}) copy-start(s32[108]{0:T(128)} %param.18) | copy-start | bytes 1300
  120.4 8.8 %collective-permute-start.14 = (f32[2,35,32]{1,2,0:T(8,128)S(1)}, f32[2,35,32]{1,2,0:T(8,128)S(1)}, u32[]{:S(2)}, u32[]{:S(2)}) collective-permute-start(f32[2,35,32]{1,2,0:T(8,128)S(1)} %maximum_select_fusion.12), channel_id=1, source_target_pairs={{0,2},{1,3},{2,0},{3,1},{4,6},{5,7},{6,4},{7,5},{8,10},{9,11},{10,... | collective-permute-start | bytes 26888 | tf_op jit(solution)/shard_map/ppermute | solution.py:85
  129.2 9.2 %copy-start.7 = (f32[128]{0:T(128)S(1)}, f32[128]{0:T(128)}, u32[]{:S(2)}) copy-start(f32[128]{0:T(128)} %param.17) | copy-start | bytes 1540
  129.3 8.9 %collective-permute-start.15 = (f32[2,35,64]{1,2,0:T(8,128)S(1)}, f32[2,35,64]{1,2,0:T(8,128)S(1)}, u32[]{:S(2)}, u32[]{:S(2)}) collective-permute-start(f32[2,35,64]{1,2,0:T(8,128)S(1)} %maximum_select_fusion.8), channel_id=1, source_target_pairs={{0,4},{1,5},{2,6},{3,7},{4,0},{5,1},{6,2},{7,3},{8,12},{9,13},{10,... | collective-permute-start | bytes 53768 | tf_op jit(solution)/shard_map/ppermute | solution.py:85
  138.9 25.4 %copy-start.8 = (f32[256,128]{1,0:T(8,128)}, f32[256,128]{1,0:T(8,128)S(1)}, u32[]{:S(2)}) copy-start(f32[256,128]{1,0:T(8,128)S(1)} %get-tuple-element.59) | copy-start | bytes 393220
  140.8 9.5 %copy-start.1 = (bf16[108,64,128]{2,0,1:T(8,128)(2,1)}, bf16[108,64,128]{2,0,1:T(8,128)(2,1)S(1)}, u32[]{:S(2)}) copy-start(bf16[108,64,128]{2,0,1:T(8,128)(2,1)S(1)} %fusion.51) | copy-start | bytes 5308420
  140.9 9.5 %collective-permute-start.18 = (f32[35,64]{1,0:T(8,128)S(1)}, f32[35,64]{1,0:T(8,128)S(1)}, u32[]{:S(2)}, u32[]{:S(2)}) collective-permute-start(f32[35,64]{1,0:T(8,128)S(1)} %slice_select_fusion.4), channel_id=1, source_target_pairs={{0,4},{1,5},{2,6},{3,7},{4,0},{5,1},{6,2},{7,3},{8,12},{9,13},{10,... | collective-permute-start | bytes 26888 | tf_op jit(solution)/shard_map/ppermute | solution.py:85
  150.3 17.6 %copy-start.2 = (bf16[256,128]{1,0:T(8,128)(2,1)S(1)}, bf16[256,128]{1,0:T(8,128)(2,1)}, u32[]{:S(2)}) copy-start(bf16[256,128]{1,0:T(8,128)(2,1)} %param.14) | copy-start | bytes 196612
  150.3 21.0 %copy-start.6 = (s32[108]{0:T(128)S(1)}, s32[108]{0:T(128)}, u32[]{:S(2)}) copy-start(s32[108]{0:T(128)} %param.20) | copy-start | bytes 1300
  150.5 11.6 %collective-permute-start.19 = (f32[35,32]{1,0:T(8,128)S(1)}, f32[35,32]{1,0:T(8,128)S(1)}, u32[]{:S(2)}, u32[]{:S(2)}) collective-permute-start(f32[35,32]{1,0:T(8,128)S(1)} %slice_select_fusion.3), channel_id=1, source_target_pairs={{0,2},{1,3},{2,0},{3,1},{4,6},{5,7},{6,4},{7,5},{8,10},{9,11},{10,... | collective-permute-start | bytes 13448 | tf_op jit(solution)/shard_map/ppermute | solution.py:85
  154.4 13.6 %collective-permute-start.21 = (f32[128,256]{0,1:T(8,128)S(1)}, f32[128,256]{0,1:T(8,128)S(1)}, u32[]{:S(2)}, u32[]{:S(2)}) collective-permute-start(f32[128,256]{0,1:T(8,128)S(1)} %slice.239), channel_id=1, source_target_pairs={{1,0},{2,1},{3,2},{4,3},{5,4},{6,5},{7,6},{8,7},{9,8},{10,9},{11,1... | collective-permute-start | bytes 393224 | tf_op jit(solution)/shard_map/ppermute | solution.py:38
  160.2 7.7 %collective-permute-start.22 = (bf16[128,256]{0,1:T(8,128)(2,1)S(1)}, bf16[128,256]{0,1:T(8,128)(2,1)S(1)}, u32[]{:S(2)}, u32[]{:S(2)}) collective-permute-start(bf16[128,256]{0,1:T(8,128)(2,1)S(1)} %slice.389), channel_id=1, source_target_pairs={{0,1},{1,2},{2,3},{3,4},{4,5},{5,6},{6,7},{7,8},{8,9},{9,10},{10,1... | collective-permute-start | bytes 196616 | tf_op jit(solution)/shard_map/ppermute | solution.py:38
  162.3 3.1 %collective-permute-start.20 = (f32[35,16]{1,0:T(8,128)S(1)}, f32[35,16]{1,0:T(8,128)S(1)}, u32[]{:S(2)}, u32[]{:S(2)}) collective-permute-start(f32[35,16]{1,0:T(8,128)S(1)} %slice_select_fusion.2), channel_id=1, source_target_pairs={{0,1},{1,0},{2,3},{3,2},{4,5},{5,4},{6,7},{7,6},{8,9},{9,8},{10,11... | collective-permute-start | bytes 6728 | tf_op jit(solution)/shard_map/ppermute | solution.py:85
  168.7 10.3 %collective-permute-start.23 = (f32[18297]{0:T(1024)S(1)}, f32[18297]{0:T(1024)S(1)}, u32[]{:S(2)}, u32[]{:S(2)}) collective-permute-start(f32[18297]{0:T(1024)S(1)} %concatenate.165), channel_id=1, source_target_pairs={{0,8},{1,9},{2,10},{3,11},{4,12},{5,13},{6,14},{7,15},{8,0},{9,1},... | collective-permute-start | bytes 219572 | tf_op jit(solution)/shard_map/ppermute | solution.py:85
  179.6 9.9 %collective-permute-start.24 = (f32[18857]{0:T(1024)S(1)}, f32[18857]{0:T(1024)S(1)}, u32[]{:S(2)}, u32[]{:S(2)}) collective-permute-start(f32[18857]{0:T(1024)S(1)} %pad_maximum_fusion.6), channel_id=1, source_target_pairs={{0,16},{1,17},{2,18},{3,19},{4,20},{5,21},{6,22},{7,23},{8,24},{9,... | collective-permute-start | bytes 226292 | tf_op jit(solution)/shard_map/ppermute | solution.py:85
  189.5 22.7 %copy-start.9 = (f32[256,128]{1,0:T(8,128)S(1)}, f32[256,128]{1,0:T(8,128)}, u32[]{:S(2)}) copy-start(f32[256,128]{1,0:T(8,128)} %copy-done.8) | copy-start | bytes 393220
  190.1 7.8 %collective-permute-start.25 = (f32[19977]{0:T(1024)S(1)}, f32[19977]{0:T(1024)S(1)}, u32[]{:S(2)}, u32[]{:S(2)}) collective-permute-start(f32[19977]{0:T(1024)S(1)} %pad_maximum_fusion.4), channel_id=1, source_target_pairs={{0,32},{1,33},{2,34},{3,35},{4,36},{5,37},{6,38},{7,39},{8,40},{9,... | collective-permute-start | bytes 239732 | tf_op jit(solution)/shard_map/ppermute | solution.py:85
  198.5 11.1 %collective-permute-start.26 = (f32[22217]{0:T(1024)S(1)}, f32[22217]{0:T(1024)S(1)}, u32[]{:S(2)}, u32[]{:S(2)}) collective-permute-start(f32[22217]{0:T(1024)S(1)} %pad_maximum_fusion.3), channel_id=1, source_target_pairs={{0,64},{1,65},{2,66},{3,67},{4,68},{5,69},{6,70},{7,71},{8,72},{9,... | collective-permute-start | bytes 266612 | tf_op jit(solution)/shard_map/ppermute | solution.py:85
  210.2 11.7 %collective-permute-start.27 = (f32[26697]{0:T(1024)S(1)}, f32[26697]{0:T(1024)S(1)}, u32[]{:S(2)}, u32[]{:S(2)}) collective-permute-start(f32[26697]{0:T(1024)S(1)} %pad_maximum_fusion.2), channel_id=1, source_target_pairs={{0,128},{1,129},{2,130},{3,131},{4,132},{5,133},{6,134},{7,135},{8... | collective-permute-start | bytes 320372 | tf_op jit(solution)/shard_map/ppermute | solution.py:85
  222.9 12.4 %collective-permute-start.28 = (f32[35657]{0:T(1024)S(1)}, f32[35657]{0:T(1024)S(1)}, u32[]{:S(2)}, u32[]{:S(2)}) collective-permute-start(f32[35657]{0:T(1024)S(1)} %pad_maximum_fusion.1), channel_id=1, source_target_pairs={{0,256},{1,257},{2,258},{3,259},{4,260},{5,261},{6,262},{7,263},{8... | collective-permute-start | bytes 427892 | tf_op jit(solution)/shard_map/ppermute | solution.py:85
  236.3 3.2 %collective-permute-start.29 = (f32[18297]{0:T(1024)S(1)}, f32[18297]{0:T(1024)S(1)}, u32[]{:S(2)}, u32[]{:S(2)}) collective-permute-start(f32[18297]{0:T(1024)S(1)} %pad_maximum_fusion.8), channel_id=1, source_target_pairs={{0,1},{1,0},{2,3},{3,2},{4,5},{5,4},{6,7},{7,6},{8,9},{9,8},{10,11... | collective-permute-start | bytes 219572 | tf_op jit(solution)/shard_map/ppermute | solution.py:85
  239.9 6.3 %collective-permute-start.30 = (f32[18857]{0:T(1024)S(1)}, f32[18857]{0:T(1024)S(1)}, u32[]{:S(2)}, u32[]{:S(2)}) collective-permute-start(f32[18857]{0:T(1024)S(1)} %pad_maximum_fusion.7), channel_id=1, source_target_pairs={{0,2},{1,3},{2,0},{3,1},{4,6},{5,7},{6,4},{7,5},{8,10},{9,11},{10,... | collective-permute-start | bytes 226292 | tf_op jit(solution)/shard_map/ppermute | solution.py:85
  242.5 14.8 %collective-permute-start.16 = (f32[3,256]{1,0:T(4,128)S(1)}, f32[3,256]{1,0:T(4,128)S(1)}, u32[]{:S(2)}, u32[]{:S(2)}) collective-permute-start(f32[3,256]{1,0:T(4,128)S(1)} %slice.230), channel_id=1, source_target_pairs={{1,0},{2,1},{3,2},{4,3},{5,4},{6,5},{7,6},{8,7},{9,8},{10,9},{11,1... | collective-permute-start | bytes 9224 | tf_op jit(solution)/shard_map/ppermute | solution.py:38
  246.6 8.2 %collective-permute-start.31 = (f32[19977]{0:T(1024)S(1)}, f32[19977]{0:T(1024)S(1)}, u32[]{:S(2)}, u32[]{:S(2)}) collective-permute-start(f32[19977]{0:T(1024)S(1)} %pad_maximum_fusion.5), channel_id=1, source_target_pairs={{0,4},{1,5},{2,6},{3,7},{4,0},{5,1},{6,2},{7,3},{8,12},{9,13},{10,... | collective-permute-start | bytes 239732 | tf_op jit(solution)/shard_map/ppermute | solution.py:85
  250.0 7.3 %collective-permute-start.17 = (bf16[3,256]{1,0:T(4,128)(2,1)S(1)}, bf16[3,256]{1,0:T(4,128)(2,1)S(1)}, u32[]{:S(2)}, u32[]{:S(2)}) collective-permute-start(bf16[3,256]{1,0:T(4,128)(2,1)S(1)} %slice.390), channel_id=1, source_target_pairs={{0,1},{1,2},{2,3},{3,4},{4,5},{5,6},{6,7},{7,8},{8,9},{9,10},{10,1... | collective-permute-start | bytes 4616 | tf_op jit(solution)/shard_map/ppermute | solution.py:38

commit v6 on v5

--- a/solution.py
+++ b/solution.py
@@ -85,16 +85,10 @@
     return lax.ppermute(block, "box", [(i, i ^ (1 << bit)) for i in range(count)])
 
 
-def tree_sum(block, bits):
-    for bit in bits:
-        block = block + xor_swap(block, bit)
-    return block
-
-
 def split_sum(block, index, bits):
     for bit in bits:
-        half = block.shape[-1] // 2
-        lower, upper = block[..., :half], block[..., half:]
+        half = block.shape[0] // 2
+        lower, upper = block[:half], block[half:]
         up = ((index >> bit) & 1) == 1
         keep = jnp.where(up, upper, lower)
         send = jnp.where(up, lower, upper)
@@ -102,29 +96,24 @@
     return block
 
 
-def tree_gather_sum(block, extra, index, bits, axis):
+def tree_gather_sum(block, extra, index, bits):
     for bit in bits:
-        packed = xor_swap(jnp.concatenate([block.reshape(-1), extra]), bit)
-        other = packed[: block.size].reshape(block.shape)
-        other_extra = packed[block.size :]
+        packed = xor_swap(jnp.concatenate([block, extra]), bit)
+        other, other_extra = packed[: block.size], packed[block.size :]
         up = ((index >> bit) & 1) == 1
         block = jnp.where(
-            up,
-            jnp.concatenate([other, block], axis=axis),
-            jnp.concatenate([block, other], axis=axis),
+            up, jnp.concatenate([other, block]), jnp.concatenate([block, other])
         )
         extra = extra + other_extra
     return block, extra
 
 
-def tree_gather(block, index, bits, axis):
+def tree_gather(block, index, bits):
     for bit in bits:
         other = xor_swap(block, bit)
         up = ((index >> bit) & 1) == 1
         block = jnp.where(
-            up,
-            jnp.concatenate([other, block], axis=axis),
-            jnp.concatenate([block, other], axis=axis),
+            up, jnp.concatenate([other, block]), jnp.concatenate([block, other])
         )
     return block
 
@@ -155,8 +144,11 @@
         jnp.einsum("ic,ai->ca", msg_weight, features, preferred_element_type=jnp.float32)
         * mask_f[None, :]
     )
-    pos_ext = extended(positions, (("box", 1),), atom_num)
-    hid_ext = extended(hidden_t.astype(jnp.bfloat16), (("box", 1),), atom_num).astype(jnp.float32)
+    own_pack = jnp.concatenate(
+        [positions, hidden_t.astype(jnp.bfloat16).astype(jnp.float32)], axis=0
+    )
+    ext_pack = extended(own_pack, (("box", 1),), atom_num)
+    pos_ext, hid_ext = ext_pack[:3], ext_pack[3:]
 
     def near_part(own, ext, feat_ext):
         return near_field(own, ext, feat_ext, pair_target, pair_source, pair_live)
@@ -179,12 +171,17 @@
     )
     row_weights = lax.dynamic_index_in_dim(counts_mat, group_id, 0, keepdims=False)
     col_weights = lax.dynamic_index_in_dim(counts_mat, group_id, 1, keepdims=False)
-    moment_part = split_sum(jnp.stack([moment, feat_basis]), index, sub_bits[::-1])
-    moment_tab = tree_gather(moment_part[None], index, grp_bits, 0)
+    channels = moment.shape[1]
+    subs = 8
+    width = channels // subs
+    rows = jnp.stack([moment, feat_basis]).reshape(2, -1, subs, width)
+    moment_part = split_sum(rows.transpose(2, 0, 1, 3).reshape(-1), index, sub_bits[::-1])
+    moment_tab = tree_gather(moment_part, index, grp_bits).reshape(groups, 2, -1, width)
     mixed_part = jnp.einsum("j,jnkc->nkc", row_weights, moment_tab, precision=PRECISE)
     gathered_part = mixed_part[0]
     local_part = jnp.dot(trans_weight, gathered_part, precision=PRECISE)
-    both = tree_gather(jnp.stack([local_part, mixed_part[1]]), index, sub_bits, 2)
+    both = tree_gather(jnp.stack([local_part, mixed_part[1]]).reshape(-1), index, sub_bits)
+    both = both.reshape(subs, 2, -1, width).transpose(1, 2, 0, 3).reshape(2, -1, channels)
     local_exp, feat_mixed = both[0], both[1]
     potential = jnp.einsum("ka,kc->ac", basis_val, local_exp, precision=PRECISE)
     pre_act = near_val + potential
@@ -195,7 +192,8 @@
     grad_read_part = jnp.dot(mask_f, activ, precision=PRECISE)
     d_local = jnp.dot(basis_val, d_pre, precision=PRECISE)
     d_basis = jnp.einsum("kc,ac->ka", local_exp, d_pre, precision=PRECISE)
-    d_local_part = split_sum(d_local, index, sub_bits[::-1])
+    d_rows = d_local.reshape(-1, subs, width).transpose(1, 0, 2).reshape(-1)
+    d_local_part = split_sum(d_rows, index, sub_bits[::-1]).reshape(-1, width)
     grad_trans_part = jnp.einsum("kc,qc->kq", d_local_part, gathered_part, precision=PRECISE)
     d_gathered_part = jnp.dot(trans_weight.T, d_local_part, precision=PRECISE)
     slice_width = d_gathered_part.shape[1]
@@ -207,13 +205,11 @@
         axis=1,
     )
     d_own, d_ext, d_feat_ext = near_back(d_pre)
-    low_pos, low_feat = passed_along((d_ext[:, :atom_num], d_feat_ext[:, :atom_num]), "box", -1)
-    high_pos, high_feat = (
-        passed_along(d_ext[:, 2 * atom_num :].astype(jnp.bfloat16), "box", 1).astype(jnp.float32),
-        passed_along(d_feat_ext[:, 2 * atom_num :].astype(jnp.bfloat16), "box", 1).astype(
-            jnp.float32
-        ),
-    )
+    d_pack = jnp.concatenate([d_ext, d_feat_ext], axis=0)
+    low_pack = passed_along(d_pack[:, :atom_num], "box", -1)
+    high_pack = passed_along(d_pack[:, 2 * atom_num :], "box", 1)
+    low_pos, low_feat = low_pack[:3], low_pack[3:]
+    high_pos, high_feat = high_pack[:3], high_pack[3:]
     d_hidden_near = d_feat_ext[:, atom_num : 2 * atom_num] + low_feat + high_feat
     grad_msg_part = (
         jnp.einsum("ai,ca->ic", masked_feat, d_hidden_near, precision=PRECISE) + far_msg
@@ -221,9 +217,11 @@
     flat = jnp.concatenate(
         [grad_msg_part.reshape(-1), grad_trans_part.reshape(-1), grad_read_part.reshape(-1)]
     )
-    d_tab, flat = tree_gather_sum(d_gathered_part[None], flat, index, grp_bits, 0)
+    d_tab, flat = tree_gather_sum(d_gathered_part.reshape(-1), flat, index, grp_bits)
+    d_tab = d_tab.reshape(groups, -1, width)
     d_moment_part = jnp.einsum("b,bkc->kc", col_weights, d_tab, precision=PRECISE)
-    d_moment, flat = tree_gather_sum(d_moment_part, flat, index, sub_bits, 1)
+    d_moment, flat = tree_gather_sum(d_moment_part.reshape(-1), flat, index, sub_bits)
+    d_moment = d_moment.reshape(subs, -1, width).transpose(1, 0, 2).reshape(-1, channels)
     d_basis = d_basis + jnp.dot(d_moment, hidden_t, precision=PRECISE)
     (d_far_pos,) = basis_back(d_basis)
     msg_size, trans_size = grad_msg_part.size, grad_trans_part.size

time: 259 us -> 228 us (0.88)
  the two profiles are of different devices: /device:TPU:2 before, /device:TPU:1 now
where the time goes in v6:
time: 228 us; the launch traced here: 227 us
  starting transfers between devices  128 us (56%)
  matrix products  39.3 us (17%)
  waiting for transfers between devices  35.1 us (15%)
  local copies, waits for them, and re-layouts  13.7 us (6%)
  other arithmetic  8.48 us (4%)
    ppermute x24, starting transfers between devices, xor_swap(): return lax.ppermute(block, 'box', [(i, i ^ 1 << bit) for i in range(count)])  113 us
    ppermute x24, waiting for transfers between devices, xor_swap(): return lax.ppermute(block, 'box', [(i, i ^ 1 << bit) for i in range(count)])  35.1 us
    dot_general x3, matrix products, near_field(): jnp.einsum('pij,pjc->pic', kernel, source_feat, preferred_element_type=jn...  20.2 us
    dot_general x2, matrix products, near_field(): accumulated = jnp.einsum('pt,pic->tic', tgt_hot, contrib, precision=PRECISE)  6.77 us
    ppermute x2, starting transfers between devices, passed_along(): return lax.ppermute(block, axis, route)  6.7 us
    ppermute x1, starting transfers between devices, extended(): lax.ppermute(lax.slice_in_dim(block, 0, width, axis=dim), axis, backward)  5.45 us
  transfers between devices with their start and end apart: 28, of which 16 were waited for; matrix products, arithmetic and copies ran while one was open for 19% of the time, Pallas kernels for 0%

profile of v6, /device:TPU:1, one launch (start us, length us, event | category | flops | bytes accessed | tf_op | source)
XLA Modules:
  0.0 226.9 jit_solution(13145275911440382222)
XLA Ops:
  0.7 0.8 broadcast_in_dim.8
  1.5 0.7 subtract_multiply_fusion.3
  2.2 0.7 iota_compare_fusion.3
  3.2 1.3 fusion.51
  4.5 1.0 convert_convert_fusion
  6.1 6.6 %collective-permute-start.2 = (f32[4480]{0:T(1024)S(1)}, f32[4480]{0:T(1024)S(1)}, u32[]{:S(2)}, u32[]{:S(2)}) collective-permute-start(f32[4480]{0:T(1024)S(1)} %select_n.283), channel_id=1, source_target_pairs={{0,4},{1,5},{2,6},{3,7},{4,0},{5,1},{6,2},{7,3},{8,12},{9,13},{10,... | collective-permute-start | bytes 53768 | tf_op jit(solution)/shard_map/ppermute | solution.py:85
  13.0 0.9 collective-permute-done.2
  14.0 4.0 %collective-permute-start.3 = (f32[2240]{0:T(1024)S(1)}, f32[2240]{0:T(1024)S(1)}, u32[]{:S(2)}, u32[]{:S(2)}) collective-permute-start(f32[2240]{0:T(1024)S(1)} %slice_select_fusion.4), channel_id=1, source_target_pairs={{0,2},{1,3},{2,0},{3,1},{4,6},{5,7},{6,4},{7,5},{8,10},{9,11},{10,... | collective-permute-start | bytes 26888 | tf_op jit(solution)/shard_map/ppermute | solution.py:85
  18.0 0.7 pad_maximum_fusion.6
  18.7 5.5 %collective-permute-start.1 = (f32[131,256]{1,0:T(8,128)S(1)}, f32[131,256]{1,0:T(8,128)S(1)}, u32[]{:S(2)}, u32[]{:S(2)}) collective-permute-start(f32[131,256]{1,0:T(8,128)S(1)} %pad_maximum_fusion.6), channel_id=1, source_target_pairs={{1,0},{2,1},{3,2},{4,3},{5,4},{6,5},{7,6},{8,7},{9,8},{10,9},{11,1... | collective-permute-start | bytes 402440 | tf_op jit(solution)/shard_map/ppermute | solution.py:30
  24.2 3.5 %collective-permute-start = (f32[131,256]{1,0:T(8,128)S(1)}, f32[131,256]{1,0:T(8,128)S(1)}, u32[]{:S(2)}, u32[]{:S(2)}) collective-permute-start(f32[131,256]{1,0:T(8,128)S(1)} %pad_maximum_fusion.6), channel_id=1, source_target_pairs={{0,1},{1,2},{2,3},{3,4},{4,5},{5,6},{6,7},{7,8},{8,9},{9,10},{10,1... | collective-permute-start | bytes 402440 | tf_op jit(solution)/shard_map/ppermute | solution.py:27
  27.7 0.8 reshape.246
  28.6 1.9 collective-permute-start.4
  30.5 0.9 convolution_bitcast_fusion.1
  31.8 5.4 %collective-permute-start.5 = (f32[1120]{0:T(1024)S(1)}, f32[1120]{0:T(1024)S(1)}, u32[]{:S(2)}, u32[]{:S(2)}) collective-permute-start(f32[1120]{0:T(1024)S(1)} %select_add_fusion.2), channel_id=1, source_target_pairs={{0,8},{1,9},{2,10},{3,11},{4,12},{5,13},{6,14},{7,15},{8,0},{9,1},... | collective-permute-start | bytes 13448 | tf_op jit(solution)/shard_map/ppermute | solution.py:85
  37.2 2.9 %collective-permute-done.5 = f32[1120]{0:T(1024)S(1)} collective-permute-done((f32[1120]{0:T(1024)S(1)}, f32[1120]{0:T(1024)S(1)}, u32[]{:S(2)}, u32[]{:S(2)}) %collective-permute-start.5) | collective-permute-done | bytes 4512 | tf_op jit(solution)/shard_map/ppermute | solution.py:85
  40.1 3.5 %collective-permute-start.6 = (f32[2240]{0:T(1024)S(1)}, f32[2240]{0:T(1024)S(1)}, u32[]{:S(2)}, u32[]{:S(2)}) collective-permute-start(f32[2240]{0:T(1024)S(1)} %maximum_select_fusion.22), channel_id=1, source_target_pairs={{0,16},{1,17},{2,18},{3,19},{4,20},{5,21},{6,22},{7,23},{8,24},{9,... | collective-permute-start | bytes 26888 | tf_op jit(solution)/shard_map/ppermute | solution.py:85
  43.7 0.7 broadcast_multiply_fusion
  44.3 0.8 copy.214
  45.2 4.6 %collective-permute-start.7 = (f32[4480]{0:T(1024)S(1)}, f32[4480]{0:T(1024)S(1)}, u32[]{:S(2)}, u32[]{:S(2)}) collective-permute-start(f32[4480]{0:T(1024)S(1)} %maximum_select_fusion.18), channel_id=1, source_target_pairs={{0,32},{1,33},{2,34},{3,35},{4,36},{5,37},{6,38},{7,39},{8,40},{9,... | collective-permute-start | bytes 53768 | tf_op jit(solution)/shard_map/ppermute | solution.py:85
  50.3 0.7 convert_element_type.55
  51.6 4.8 %collective-permute-start.8 = (f32[8960]{0:T(1024)S(1)}, f32[8960]{0:T(1024)S(1)}, u32[]{:S(2)}, u32[]{:S(2)}) collective-permute-start(f32[8960]{0:T(1024)S(1)} %maximum_select_fusion.14), channel_id=1, source_target_pairs={{0,64},{1,65},{2,66},{3,67},{4,68},{5,69},{6,70},{7,71},{8,72},{9,... | collective-permute-start | bytes 107528 | tf_op jit(solution)/shard_map/ppermute | solution.py:85
  56.7 1.1 collective-permute-done.8
  57.7 4.4 %collective-permute-start.9 = (f32[17920]{0:T(1024)S(1)}, f32[17920]{0:T(1024)S(1)}, u32[]{:S(2)}, u32[]{:S(2)}) collective-permute-start(f32[17920]{0:T(1024)S(1)} %maximum_select_fusion.9), channel_id=1, source_target_pairs={{0,128},{1,129},{2,130},{3,131},{4,132},{5,133},{6,134},{7,135},{8... | collective-permute-start | bytes 215048 | tf_op jit(solution)/shard_map/ppermute | solution.py:85
  63.1 1.7 convert_bitcast_fusion
  65.2 6.6 %collective-permute-start.10 = (f32[35840]{0:T(1024)S(1)}, f32[35840]{0:T(1024)S(1)}, u32[]{:S(2)}, u32[]{:S(2)}) collective-permute-start(f32[35840]{0:T(1024)S(1)} %maximum_select_fusion.5), channel_id=1, source_target_pairs={{0,256},{1,257},{2,258},{3,259},{4,260},{5,261},{6,262},{7,263},{8... | collective-permute-start | bytes 430088 | tf_op jit(solution)/shard_map/ppermute | solution.py:85
  71.8 6.5 %fusion.26 = f32[108,64,128]{2,1,0:T(8,128)} fusion(bf16[108,64,128]{2,0,1:T(8,128)(2,1)S(1)} %convert_bitcast_fusion, f32[108]{0:T(128)S(1)} %broadcast_multiply_fusion, f32[108,64]{1,0:T(8,128)S(1)} %copy.208, f32[108,64]{1,0:T(8,128)S(1)} %copy.207, f32[108,64]{1,0:T(8,128)S(1)} %copy.206, f32[108,64]{1,0:T(8,128)S(1)} %copy.205, ...), kind=kOutput, calls=%fused_computation.32 | convolution fusion | flops 118112256 | bytes 5474736 | tf_op jit(solution)/shard_map/jvp(pij,pjc->pic)/dot_general | solution.py:78
  80.9 2.2 fusion.31
  83.5 8.1 %collective-permute-start.11 = (f32[1120]{0:T(1024)S(1)}, f32[1120]{0:T(1024)S(1)}, u32[]{:S(2)}, u32[]{:S(2)}) collective-permute-start(f32[1120]{0:T(1024)S(1)} %reshape.251), channel_id=1, source_target_pairs={{0,1},{1,0},{2,3},{3,2},{4,5},{5,4},{6,7},{7,6},{8,9},{9,8},{10,11... | collective-permute-start | bytes 13448 | tf_op jit(solution)/shard_map/ppermute | solution.py:85
  91.6 5.1 %fusion = f32[4,64,128]{2,0,1:T(4,128)S(1)} fusion(f32[108,64,128]{2,1,0:T(8,128)} %fusion.26, s32[108]{0:T(128)S(1)} %copy-done.13), kind=kOutput, calls=%fused_computation.6 | convolution fusion | flops 42467760 | bytes 3670448 | tf_op jit(solution)/shard_map/jvp(pt,pic->tic)/dot_general | solution.py:79
  96.8 1.9 collective-permute-start.12
  98.9 2.3 %collective-permute-done.12 = f32[2240]{0:T(1024)S(1)} collective-permute-done((f32[2240]{0:T(1024)S(1)}, f32[2240]{0:T(1024)S(1)}, u32[]{:S(2)}, u32[]{:S(2)}) %collective-permute-start.12) | collective-permute-done | bytes 8992 | tf_op jit(solution)/shard_map/ppermute | solution.py:85
  101.3 2.5 %collective-permute-start.13 = (f32[4480]{0:T(1024)S(1)}, f32[4480]{0:T(1024)S(1)}, u32[]{:S(2)}, u32[]{:S(2)}) collective-permute-start(f32[4480]{0:T(1024)S(1)} %maximum_select_fusion.19), channel_id=1, source_target_pairs={{0,4},{1,5},{2,6},{3,7},{4,0},{5,1},{6,2},{7,3},{8,12},{9,13},{10,... | collective-permute-start | bytes 53768 | tf_op jit(solution)/shard_map/ppermute | solution.py:85
  104.0 2.7 %collective-permute-done.13 = f32[4480]{0:T(1024)S(1)} collective-permute-done((f32[4480]{0:T(1024)S(1)}, f32[4480]{0:T(1024)S(1)}, u32[]{:S(2)}, u32[]{:S(2)}) %collective-permute-start.13) | collective-permute-done | bytes 17952 | tf_op jit(solution)/shard_map/ppermute | solution.py:85
  108.0 2.5 %collective-permute-start.16 = (f32[2240]{0:T(1024)S(1)}, f32[2240]{0:T(1024)S(1)}, u32[]{:S(2)}, u32[]{:S(2)}) collective-permute-start(f32[2240]{0:T(1024)S(1)} %select_n.320), channel_id=1, source_target_pairs={{0,4},{1,5},{2,6},{3,7},{4,0},{5,1},{6,2},{7,3},{8,12},{9,13},{10,... | collective-permute-start | bytes 26888 | tf_op jit(solution)/shard_map/ppermute | solution.py:85
  110.6 1.7 fusion.49
  112.3 6.0 %convert_bitcast_fusion.1 = bf16[128,64,108]{0,1,2:T(8,128)(2,1)S(1)} fusion(bf16[108,64,128]{2,0,1:T(8,128)(2,1)S(1)} %fusion.49, f32[108]{0:T(128)S(1)} %broadcast_multiply_fusion, f32[108,64]{1,0:T(8,128)S(1)} %copy-done.9, f32[108,64]{1,0:T(8,128)S(1)} %copy.207, f32[108,64]{1,0:T(8,128)S(1)} %copy-done.11, f32[108,64]{1,0:T(8,128)S(1)} %copy.205, ...), kind=kOutput, calls=%fused_computation.30 | convolution fusion | flops 118112256 | bytes 3705264 | tf_op jit(solution)/shard_map/transpose(jvp(pij,pjc->pic))/dot_general | solution.py:78
  118.3 7.7 %fusion.14 = (f32[108,64]{1,0:T(8,128)S(1)}, f32[108,64]{1,0:T(8,128)S(1)}, f32[108,64]{1,0:T(8,128)S(1)}, f32[108,64]{1,0:T(8,128)S(1)}, f32[108,64]{1,0:T(8,128)S(1)}, /*index=5*/f32[108,64]{1,0:T(8,128)S(1)}) fusion(f32[108,64]{1,0:T(8,128)S(1)} %copy-done.9, f32[108,64]{1,0:T(8,128)S(1)} %copy.207, f32[108,64]{1,0:T(8,128)S(1)} %copy-done.7, ...), kind=kOutput, calls=%fused_computation.22 | convolution fusion | flops 124706304 | bytes 3871152 | tf_op jit(solution)/shard_map/transpose(jvp(pij,pjc->pic))/dot_general | solution.py:78
  126.0 1.0 fusion.28
  128.0 3.4 %collective-permute-start.17 = (f32[1120]{0:T(1024)S(1)}, f32[1120]{0:T(1024)S(1)}, u32[]{:S(2)}, u32[]{:S(2)}) collective-permute-start(f32[1120]{0:T(1024)S(1)} %slice_select_fusion.5), channel_id=1, source_target_pairs={{0,2},{1,3},{2,0},{3,1},{4,6},{5,7},{6,4},{7,5},{8,10},{9,11},{10,... | collective-permute-start | bytes 13448 | tf_op jit(solution)/shard_map/ppermute | solution.py:85
  131.4 4.8 %collective-permute-start.14 = (f32[131,256]{1,0:T(8,128)S(1)}, f32[131,256]{1,0:T(8,128)S(1)}, u32[]{:S(2)}, u32[]{:S(2)}) collective-permute-start(f32[131,256]{1,0:T(8,128)S(1)} %get-tuple-element.17), channel_id=1, source_target_pairs={{1,0},{2,1},{3,2},{4,3},{5,4},{6,5},{7,6},{8,7},{9,8},{10,9},{11,1... | collective-permute-start | bytes 402440 | tf_op jit(solution)/shard_map/ppermute | solution.py:38
  136.2 1.9 collective-permute-start.15
  138.3 2.4 %collective-permute-start.18 = (f32[560]{0:T(1024)S(1)}, f32[560]{0:T(1024)S(1)}, u32[]{:S(2)}, u32[]{:S(2)}) collective-permute-start(f32[560]{0:T(1024)S(1)} %slice_select_fusion.7), channel_id=1, source_target_pairs={{0,1},{1,0},{2,3},{3,2},{4,5},{5,4},{6,7},{7,6},{8,9},{9,8},{10,11... | collective-permute-start | bytes 6728 | tf_op jit(solution)/shard_map/ppermute | solution.py:85
  140.9 0.6 collective-permute-done.18
  143.1 6.4 %collective-permute-start.19 = (f32[18297]{0:T(1024)S(1)}, f32[18297]{0:T(1024)S(1)}, u32[]{:S(2)}, u32[]{:S(2)}) collective-permute-start(f32[18297]{0:T(1024)S(1)} %concatenate.293), channel_id=1, source_target_pairs={{0,8},{1,9},{2,10},{3,11},{4,12},{5,13},{6,14},{7,15},{8,0},{9,1},... | collective-permute-start | bytes 219572 | tf_op jit(solution)/shard_map/ppermute | solution.py:85
  149.8 2.4 %collective-permute-done.19 = f32[18297]{0:T(1024)S(1)} collective-permute-done((f32[18297]{0:T(1024)S(1)}, f32[18297]{0:T(1024)S(1)}, u32[]{:S(2)}, u32[]{:S(2)}) %collective-permute-start.19) | collective-permute-done | bytes 73220 | tf_op jit(solution)/shard_map/ppermute | solution.py:85
  152.5 3.0 %collective-permute-start.20 = (f32[18857]{0:T(1024)S(1)}, f32[18857]{0:T(1024)S(1)}, u32[]{:S(2)}, u32[]{:S(2)}) collective-permute-start(f32[18857]{0:T(1024)S(1)} %pad_maximum_fusion.11), channel_id=1, source_target_pairs={{0,16},{1,17},{2,18},{3,19},{4,20},{5,21},{6,22},{7,23},{8,24},{9,... | collective-permute-start | bytes 226292 | tf_op jit(solution)/shard_map/ppermute | solution.py:85
  155.8 1.8 collective-permute-done.20
  157.9 4.5 %collective-permute-start.21 = (f32[19977]{0:T(1024)S(1)}, f32[19977]{0:T(1024)S(1)}, u32[]{:S(2)}, u32[]{:S(2)}) collective-permute-start(f32[19977]{0:T(1024)S(1)} %pad_maximum_fusion.9), channel_id=1, source_target_pairs={{0,32},{1,33},{2,34},{3,35},{4,36},{5,37},{6,38},{7,39},{8,40},{9,... | collective-permute-start | bytes 239732 | tf_op jit(solution)/shard_map/ppermute | solution.py:85
  162.7 1.9 collective-permute-done.21
  164.8 5.2 %collective-permute-start.22 = (f32[22217]{0:T(1024)S(1)}, f32[22217]{0:T(1024)S(1)}, u32[]{:S(2)}, u32[]{:S(2)}) collective-permute-start(f32[22217]{0:T(1024)S(1)} %pad_maximum_fusion.8), channel_id=1, source_target_pairs={{0,64},{1,65},{2,66},{3,67},{4,68},{5,69},{6,70},{7,71},{8,72},{9,... | collective-permute-start | bytes 266612 | tf_op jit(solution)/shard_map/ppermute | solution.py:85
  170.5 1.3 collective-permute-done.22
  171.9 3.3 %collective-permute-start.23 = (f32[26697]{0:T(1024)S(1)}, f32[26697]{0:T(1024)S(1)}, u32[]{:S(2)}, u32[]{:S(2)}) collective-permute-start(f32[26697]{0:T(1024)S(1)} %pad_maximum_fusion.7), channel_id=1, source_target_pairs={{0,128},{1,129},{2,130},{3,131},{4,132},{5,133},{6,134},{7,135},{8... | collective-permute-start | bytes 320372 | tf_op jit(solution)/shard_map/ppermute | solution.py:85
  175.5 2.8 %collective-permute-done.23 = f32[26697]{0:T(1024)S(1)} collective-permute-done((f32[26697]{0:T(1024)S(1)}, f32[26697]{0:T(1024)S(1)}, u32[]{:S(2)}, u32[]{:S(2)}) %collective-permute-start.23) | collective-permute-done | bytes 106820 | tf_op jit(solution)/shard_map/ppermute | solution.py:85
  178.4 6.6 %collective-permute-start.24 = (f32[35657]{0:T(1024)S(1)}, f32[35657]{0:T(1024)S(1)}, u32[]{:S(2)}, u32[]{:S(2)}) collective-permute-start(f32[35657]{0:T(1024)S(1)} %pad_maximum_fusion.3), channel_id=1, source_target_pairs={{0,256},{1,257},{2,258},{3,259},{4,260},{5,261},{6,262},{7,263},{8... | collective-permute-start | bytes 427892 | tf_op jit(solution)/shard_map/ppermute | solution.py:85
  185.6 3.9 %collective-permute-done.24 = f32[35657]{0:T(1024)S(1)} collective-permute-done((f32[35657]{0:T(1024)S(1)}, f32[35657]{0:T(1024)S(1)}, u32[]{:S(2)}, u32[]{:S(2)}) %collective-permute-start.24) | collective-permute-done | bytes 142660 | tf_op jit(solution)/shard_map/ppermute | solution.py:85
  190.8 17.2 %collective-permute-start.25 = (f32[18297]{0:T(1024)S(1)}, f32[18297]{0:T(1024)S(1)}, u32[]{:S(2)}, u32[]{:S(2)}) collective-permute-start(f32[18297]{0:T(1024)S(1)} %pad_maximum_fusion.13), channel_id=1, source_target_pairs={{0,1},{1,0},{2,3},{3,2},{4,5},{5,4},{6,7},{7,6},{8,9},{9,8},{10,11... | collective-permute-start | bytes 219572 | tf_op jit(solution)/shard_map/ppermute | solution.py:85
  209.3 1.9 collective-permute-start.26
  211.2 3.5 %collective-permute-done.26 = f32[18857]{0:T(1024)S(1)} collective-permute-done((f32[18857]{0:T(1024)S(1)}, f32[18857]{0:T(1024)S(1)}, u32[]{:S(2)}, u32[]{:S(2)}) %collective-permute-start.26) | collective-permute-done | bytes 75460 | tf_op jit(solution)/shard_map/ppermute | solution.py:85
  215.2 1.9 collective-permute-start.27
  217.1 6.5 %collective-permute-done.27 = f32[19977]{0:T(1024)S(1)} collective-permute-done((f32[19977]{0:T(1024)S(1)}, f32[19977]{0:T(1024)S(1)}, u32[]{:S(2)}, u32[]{:S(2)}) %collective-permute-start.27) | collective-permute-done | bytes 79940 | tf_op jit(solution)/shard_map/ppermute | solution.py:85
  224.3 0.6 slice_bitcast_fusion
  225.6 0.7 reshape.263
  226.3 0.6 fusion.62
  (220 shorter events, 18.8 us)
Async XLA Ops:
  0.6 3.9 %copy-start = (bf16[128,128]{1,0:T(8,128)(2,1)S(1)}, bf16[128,128]{1,0:T(8,128)(2,1)}, u32[]{:S(2)}) copy-start(bf16[128,128]{1,0:T(8,128)(2,1)} %param.15) | copy-start | bytes 98308
  0.6 61.9 %copy-start.4 = (f32[3,256]{1,0:T(4,128)S(1)}, f32[3,256]{1,0:T(4,128)}, u32[]{:S(2)}) copy-start(f32[3,256]{1,0:T(4,128)} %param.11) | copy-start | bytes 9220
  5.8 57.0 %copy-start.12 = (s32[108]{0:T(128)S(1)}, s32[108]{0:T(128)}, u32[]{:S(2)}) copy-start(s32[108]{0:T(128)} %param.19) | copy-start | bytes 1300
  6.1 7.8 %collective-permute-start.2 = (f32[4480]{0:T(1024)S(1)}, f32[4480]{0:T(1024)S(1)}, u32[]{:S(2)}, u32[]{:S(2)}) collective-permute-start(f32[4480]{0:T(1024)S(1)} %select_n.283), channel_id=1, source_target_pairs={{0,4},{1,5},{2,6},{3,7},{4,0},{5,1},{6,2},{7,3},{8,12},{9,13},{10,... | collective-permute-start | bytes 53768 | tf_op jit(solution)/shard_map/ppermute | solution.py:85
  14.0 14.5 %collective-permute-start.3 = (f32[2240]{0:T(1024)S(1)}, f32[2240]{0:T(1024)S(1)}, u32[]{:S(2)}, u32[]{:S(2)}) collective-permute-start(f32[2240]{0:T(1024)S(1)} %slice_select_fusion.4), channel_id=1, source_target_pairs={{0,2},{1,3},{2,0},{3,1},{4,6},{5,7},{6,4},{7,5},{8,10},{9,11},{10,... | collective-permute-start | bytes 26888 | tf_op jit(solution)/shard_map/ppermute | solution.py:85
  18.7 43.8 %collective-permute-start.1 = (f32[131,256]{1,0:T(8,128)S(1)}, f32[131,256]{1,0:T(8,128)S(1)}, u32[]{:S(2)}, u32[]{:S(2)}) collective-permute-start(f32[131,256]{1,0:T(8,128)S(1)} %pad_maximum_fusion.6), channel_id=1, source_target_pairs={{1,0},{2,1},{3,2},{4,3},{5,4},{6,5},{7,6},{8,7},{9,8},{10,9},{11,1... | collective-permute-start | bytes 402440 | tf_op jit(solution)/shard_map/ppermute | solution.py:30
  24.2 38.3 %collective-permute-start = (f32[131,256]{1,0:T(8,128)S(1)}, f32[131,256]{1,0:T(8,128)S(1)}, u32[]{:S(2)}, u32[]{:S(2)}) collective-permute-start(f32[131,256]{1,0:T(8,128)S(1)} %pad_maximum_fusion.6), channel_id=1, source_target_pairs={{0,1},{1,2},{2,3},{3,4},{4,5},{5,6},{6,7},{7,8},{8,9},{9,10},{10,1... | collective-permute-start | bytes 402440 | tf_op jit(solution)/shard_map/ppermute | solution.py:27
  28.6 3.1 %collective-permute-start.4 = (f32[1120]{0:T(1024)S(1)}, f32[1120]{0:T(1024)S(1)}, u32[]{:S(2)}, u32[]{:S(2)}) collective-permute-start(f32[1120]{0:T(1024)S(1)} %slice_select_fusion.6), channel_id=1, source_target_pairs={{0,1},{1,0},{2,3},{3,2},{4,5},{5,4},{6,7},{7,6},{8,9},{9,8},{10,11... | collective-permute-start | bytes 13448 | tf_op jit(solution)/shard_map/ppermute | solution.py:85
  31.8 8.3 %collective-permute-start.5 = (f32[1120]{0:T(1024)S(1)}, f32[1120]{0:T(1024)S(1)}, u32[]{:S(2)}, u32[]{:S(2)}) collective-permute-start(f32[1120]{0:T(1024)S(1)} %select_add_fusion.2), channel_id=1, source_target_pairs={{0,8},{1,9},{2,10},{3,11},{4,12},{5,13},{6,14},{7,15},{8,0},{9,1},... | collective-permute-start | bytes 13448 | tf_op jit(solution)/shard_map/ppermute | solution.py:85
  40.1 5.0 %collective-permute-start.6 = (f32[2240]{0:T(1024)S(1)}, f32[2240]{0:T(1024)S(1)}, u32[]{:S(2)}, u32[]{:S(2)}) collective-permute-start(f32[2240]{0:T(1024)S(1)} %maximum_select_fusion.22), channel_id=1, source_target_pairs={{0,16},{1,17},{2,18},{3,19},{4,20},{5,21},{6,22},{7,23},{8,24},{9,... | collective-permute-start | bytes 26888 | tf_op jit(solution)/shard_map/ppermute | solution.py:85
  45.2 6.3 %collective-permute-start.7 = (f32[4480]{0:T(1024)S(1)}, f32[4480]{0:T(1024)S(1)}, u32[]{:S(2)}, u32[]{:S(2)}) collective-permute-start(f32[4480]{0:T(1024)S(1)} %maximum_select_fusion.18), channel_id=1, source_target_pairs={{0,32},{1,33},{2,34},{3,35},{4,36},{5,37},{6,38},{7,39},{8,40},{9,... | collective-permute-start | bytes 53768 | tf_op jit(solution)/shard_map/ppermute | solution.py:85
  51.6 6.2 %collective-permute-start.8 = (f32[8960]{0:T(1024)S(1)}, f32[8960]{0:T(1024)S(1)}, u32[]{:S(2)}, u32[]{:S(2)}) collective-permute-start(f32[8960]{0:T(1024)S(1)} %maximum_select_fusion.14), channel_id=1, source_target_pairs={{0,64},{1,65},{2,66},{3,67},{4,68},{5,69},{6,70},{7,71},{8,72},{9,... | collective-permute-start | bytes 107528 | tf_op jit(solution)/shard_map/ppermute | solution.py:85
  57.7 7.4 %collective-permute-start.9 = (f32[17920]{0:T(1024)S(1)}, f32[17920]{0:T(1024)S(1)}, u32[]{:S(2)}, u32[]{:S(2)}) collective-permute-start(f32[17920]{0:T(1024)S(1)} %maximum_select_fusion.9), channel_id=1, source_target_pairs={{0,128},{1,129},{2,130},{3,131},{4,132},{5,133},{6,134},{7,135},{8... | collective-permute-start | bytes 215048 | tf_op jit(solution)/shard_map/ppermute | solution.py:85
  64.8 7.0 %copy-start.1 = (bf16[108,64,128]{2,0,1:T(8,128)(2,1)}, bf16[108,64,128]{2,0,1:T(8,128)(2,1)S(1)}, u32[]{:S(2)}) copy-start(bf16[108,64,128]{2,0,1:T(8,128)(2,1)S(1)} %convert_bitcast_fusion) | copy-start | bytes 5308420
  64.9 13.4 %copy-start.6 = (f32[108,64]{1,0:T(8,128)}, f32[108,64]{1,0:T(8,128)S(1)}, u32[]{:S(2)}) copy-start(f32[108,64]{1,0:T(8,128)S(1)} %copy.204) | copy-start | bytes 82948
  65.0 6.8 %copy-start.8 = (f32[108,64]{1,0:T(8,128)}, f32[108,64]{1,0:T(8,128)S(1)}, u32[]{:S(2)}) copy-start(f32[108,64]{1,0:T(8,128)S(1)} %copy.208) | copy-start | bytes 82948
  65.1 6.7 %copy-start.10 = (f32[108,64]{1,0:T(8,128)}, f32[108,64]{1,0:T(8,128)S(1)}, u32[]{:S(2)}) copy-start(f32[108,64]{1,0:T(8,128)S(1)} %copy.206) | copy-start | bytes 82948
  65.2 14.3 %collective-permute-start.10 = (f32[35840]{0:T(1024)S(1)}, f32[35840]{0:T(1024)S(1)}, u32[]{:S(2)}, u32[]{:S(2)}) collective-permute-start(f32[35840]{0:T(1024)S(1)} %maximum_select_fusion.5), channel_id=1, source_target_pairs={{0,256},{1,257},{2,258},{3,259},{4,260},{5,261},{6,262},{7,263},{8... | collective-permute-start | bytes 430088 | tf_op jit(solution)/shard_map/ppermute | solution.py:85
  78.9 4.2 %copy-start.5 = (f32[35,35]{1,0:T(8,128)S(1)}, f32[35,35]{1,0:T(8,128)}, u32[]{:S(2)}) copy-start(f32[35,35]{1,0:T(8,128)} %param.16) | copy-start | bytes 14704
  78.9 12.7 %copy-start.13 = (s32[108]{0:T(128)S(1)}, s32[108]{0:T(128)}, u32[]{:S(2)}) copy-start(s32[108]{0:T(128)} %param.18) | copy-start | bytes 1300
  80.9 26.2 %copy-start.14 = (f32[128]{0:T(128)S(1)}, f32[128]{0:T(128)}, u32[]{:S(2)}) copy-start(f32[128]{0:T(128)} %param.17) | copy-start | bytes 1540
  83.5 28.8 %copy-start.7 = (f32[108,64]{1,0:T(8,128)S(1)}, f32[108,64]{1,0:T(8,128)}, u32[]{:S(2)}) copy-start(f32[108,64]{1,0:T(8,128)} %copy-done.6) | copy-start | bytes 82948
  83.5 28.8 %copy-start.9 = (f32[108,64]{1,0:T(8,128)S(1)}, f32[108,64]{1,0:T(8,128)}, u32[]{:S(2)}) copy-start(f32[108,64]{1,0:T(8,128)} %copy-done.8) | copy-start | bytes 82948
  83.5 28.8 %copy-start.11 = (f32[108,64]{1,0:T(8,128)S(1)}, f32[108,64]{1,0:T(8,128)}, u32[]{:S(2)}) copy-start(f32[108,64]{1,0:T(8,128)} %copy-done.10) | copy-start | bytes 82948
  83.5 13.2 %collective-permute-start.11 = (f32[1120]{0:T(1024)S(1)}, f32[1120]{0:T(1024)S(1)}, u32[]{:S(2)}, u32[]{:S(2)}) collective-permute-start(f32[1120]{0:T(1024)S(1)} %reshape.251), channel_id=1, source_target_pairs={{0,1},{1,0},{2,3},{3,2},{4,5},{5,4},{6,7},{7,6},{8,9},{9,8},{10,11... | collective-permute-start | bytes 13448 | tf_op jit(solution)/shard_map/ppermute | solution.py:85
  96.8 4.4 %collective-permute-start.12 = (f32[2240]{0:T(1024)S(1)}, f32[2240]{0:T(1024)S(1)}, u32[]{:S(2)}, u32[]{:S(2)}) collective-permute-start(f32[2240]{0:T(1024)S(1)} %maximum_select_fusion.23), channel_id=1, source_target_pairs={{0,2},{1,3},{2,0},{3,1},{4,6},{5,7},{6,4},{7,5},{8,10},{9,11},{10,... | collective-permute-start | bytes 26888 | tf_op jit(solution)/shard_map/ppermute | solution.py:85
  101.3 5.4 %collective-permute-start.13 = (f32[4480]{0:T(1024)S(1)}, f32[4480]{0:T(1024)S(1)}, u32[]{:S(2)}, u32[]{:S(2)}) collective-permute-start(f32[4480]{0:T(1024)S(1)} %maximum_select_fusion.19), channel_id=1, source_target_pairs={{0,4},{1,5},{2,6},{3,7},{4,0},{5,1},{6,2},{7,3},{8,12},{9,13},{10,... | collective-permute-start | bytes 53768 | tf_op jit(solution)/shard_map/ppermute | solution.py:85
  108.0 19.9 %collective-permute-start.16 = (f32[2240]{0:T(1024)S(1)}, f32[2240]{0:T(1024)S(1)}, u32[]{:S(2)}, u32[]{:S(2)}) collective-permute-start(f32[2240]{0:T(1024)S(1)} %select_n.320), channel_id=1, source_target_pairs={{0,4},{1,5},{2,6},{3,7},{4,0},{5,1},{6,2},{7,3},{8,12},{9,13},{10,... | collective-permute-start | bytes 26888 | tf_op jit(solution)/shard_map/ppermute | solution.py:85
  112.3 6.0 %copy-start.2 = (bf16[108,64,128]{2,0,1:T(8,128)(2,1)S(1)}, bf16[108,64,128]{2,0,1:T(8,128)(2,1)}, u32[]{:S(2)}) copy-start(bf16[108,64,128]{2,0,1:T(8,128)(2,1)} %copy-done.1) | copy-start | bytes 5308420
  126.0 16.3 %copy-start.3 = (bf16[256,128]{1,0:T(8,128)(2,1)S(1)}, bf16[256,128]{1,0:T(8,128)(2,1)}, u32[]{:S(2)}) copy-start(bf16[256,128]{1,0:T(8,128)(2,1)} %param.14) | copy-start | bytes 196612
  128.0 10.1 %collective-permute-start.17 = (f32[1120]{0:T(1024)S(1)}, f32[1120]{0:T(1024)S(1)}, u32[]{:S(2)}, u32[]{:S(2)}) collective-permute-start(f32[1120]{0:T(1024)S(1)} %slice_select_fusion.5), channel_id=1, source_target_pairs={{0,2},{1,3},{2,0},{3,1},{4,6},{5,7},{6,4},{7,5},{8,10},{9,11},{10,... | collective-permute-start | bytes 13448 | tf_op jit(solution)/shard_map/ppermute | solution.py:85
  131.4 10.9 %collective-permute-start.14 = (f32[131,256]{1,0:T(8,128)S(1)}, f32[131,256]{1,0:T(8,128)S(1)}, u32[]{:S(2)}, u32[]{:S(2)}) collective-permute-start(f32[131,256]{1,0:T(8,128)S(1)} %get-tuple-element.17), channel_id=1, source_target_pairs={{1,0},{2,1},{3,2},{4,3},{5,4},{6,5},{7,6},{8,7},{9,8},{10,9},{11,1... | collective-permute-start | bytes 402440 | tf_op jit(solution)/shard_map/ppermute | solution.py:38
  136.2 6.1 %collective-permute-start.15 = (f32[131,256]{1,0:T(8,128)S(1)}, f32[131,256]{1,0:T(8,128)S(1)}, u32[]{:S(2)}, u32[]{:S(2)}) collective-permute-start(f32[131,256]{1,0:T(8,128)S(1)} %get-tuple-element.18), channel_id=1, source_target_pairs={{0,1},{1,2},{2,3},{3,4},{4,5},{5,6},{6,7},{7,8},{8,9},{9,10},{10,1... | collective-permute-start | bytes 402440 | tf_op jit(solution)/shard_map/ppermute | solution.py:38
  138.3 3.2 %collective-permute-start.18 = (f32[560]{0:T(1024)S(1)}, f32[560]{0:T(1024)S(1)}, u32[]{:S(2)}, u32[]{:S(2)}) collective-permute-start(f32[560]{0:T(1024)S(1)} %slice_select_fusion.7), channel_id=1, source_target_pairs={{0,1},{1,0},{2,3},{3,2},{4,5},{5,4},{6,7},{7,6},{8,9},{9,8},{10,11... | collective-permute-start | bytes 6728 | tf_op jit(solution)/shard_map/ppermute | solution.py:85
  143.1 9.1 %collective-permute-start.19 = (f32[18297]{0:T(1024)S(1)}, f32[18297]{0:T(1024)S(1)}, u32[]{:S(2)}, u32[]{:S(2)}) collective-permute-start(f32[18297]{0:T(1024)S(1)} %concatenate.293), channel_id=1, source_target_pairs={{0,8},{1,9},{2,10},{3,11},{4,12},{5,13},{6,14},{7,15},{8,0},{9,1},... | collective-permute-start | bytes 219572 | tf_op jit(solution)/shard_map/ppermute | solution.py:85
  152.5 5.1 %collective-permute-start.20 = (f32[18857]{0:T(1024)S(1)}, f32[18857]{0:T(1024)S(1)}, u32[]{:S(2)}, u32[]{:S(2)}) collective-permute-start(f32[18857]{0:T(1024)S(1)} %pad_maximum_fusion.11), channel_id=1, source_target_pairs={{0,16},{1,17},{2,18},{3,19},{4,20},{5,21},{6,22},{7,23},{8,24},{9,... | collective-permute-start | bytes 226292 | tf_op jit(solution)/shard_map/ppermute | solution.py:85
  157.9 6.7 %collective-permute-start.21 = (f32[19977]{0:T(1024)S(1)}, f32[19977]{0:T(1024)S(1)}, u32[]{:S(2)}, u32[]{:S(2)}) collective-permute-start(f32[19977]{0:T(1024)S(1)} %pad_maximum_fusion.9), channel_id=1, source_target_pairs={{0,32},{1,33},{2,34},{3,35},{4,36},{5,37},{6,38},{7,39},{8,40},{9,... | collective-permute-start | bytes 239732 | tf_op jit(solution)/shard_map/ppermute | solution.py:85
  164.8 7.1 %collective-permute-start.22 = (f32[22217]{0:T(1024)S(1)}, f32[22217]{0:T(1024)S(1)}, u32[]{:S(2)}, u32[]{:S(2)}) collective-permute-start(f32[22217]{0:T(1024)S(1)} %pad_maximum_fusion.8), channel_id=1, source_target_pairs={{0,64},{1,65},{2,66},{3,67},{4,68},{5,69},{6,70},{7,71},{8,72},{9,... | collective-permute-start | bytes 266612 | tf_op jit(solution)/shard_map/ppermute | solution.py:85
  171.9 6.4 %collective-permute-start.23 = (f32[26697]{0:T(1024)S(1)}, f32[26697]{0:T(1024)S(1)}, u32[]{:S(2)}, u32[]{:S(2)}) collective-permute-start(f32[26697]{0:T(1024)S(1)} %pad_maximum_fusion.7), channel_id=1, source_target_pairs={{0,128},{1,129},{2,130},{3,131},{4,132},{5,133},{6,134},{7,135},{8... | collective-permute-start | bytes 320372 | tf_op jit(solution)/shard_map/ppermute | solution.py:85
  178.4 11.2 %collective-permute-start.24 = (f32[35657]{0:T(1024)S(1)}, f32[35657]{0:T(1024)S(1)}, u32[]{:S(2)}, u32[]{:S(2)}) collective-permute-start(f32[35657]{0:T(1024)S(1)} %pad_maximum_fusion.3), channel_id=1, source_target_pairs={{0,256},{1,257},{2,258},{3,259},{4,260},{5,261},{6,262},{7,263},{8... | collective-permute-start | bytes 427892 | tf_op jit(solution)/shard_map/ppermute | solution.py:85
  190.8 18.1 %collective-permute-start.25 = (f32[18297]{0:T(1024)S(1)}, f32[18297]{0:T(1024)S(1)}, u32[]{:S(2)}, u32[]{:S(2)}) collective-permute-start(f32[18297]{0:T(1024)S(1)} %pad_maximum_fusion.13), channel_id=1, source_target_pairs={{0,1},{1,0},{2,3},{3,2},{4,5},{5,4},{6,7},{7,6},{8,9},{9,8},{10,11... | collective-permute-start | bytes 219572 | tf_op jit(solution)/shard_map/ppermute | solution.py:85
  209.3 5.5 %collective-permute-start.26 = (f32[18857]{0:T(1024)S(1)}, f32[18857]{0:T(1024)S(1)}, u32[]{:S(2)}, u32[]{:S(2)}) collective-permute-start(f32[18857]{0:T(1024)S(1)} %pad_maximum_fusion.12), channel_id=1, source_target_pairs={{0,2},{1,3},{2,0},{3,1},{4,6},{5,7},{6,4},{7,5},{8,10},{9,11},{10,... | collective-permute-start | bytes 226292 | tf_op jit(solution)/shard_map/ppermute | solution.py:85
  215.2 8.5 %collective-permute-start.27 = (f32[19977]{0:T(1024)S(1)}, f32[19977]{0:T(1024)S(1)}, u32[]{:S(2)}, u32[]{:S(2)}) collective-permute-start(f32[19977]{0:T(1024)S(1)} %pad_maximum_fusion.10), channel_id=1, source_target_pairs={{0,4},{1,5},{2,6},{3,7},{4,0},{5,1},{6,2},{7,3},{8,12},{9,13},{10,... | collective-permute-start | bytes 239732 | tf_op jit(solution)/shard_map/ppermute | solution.py:85

commit v7 on v6

--- a/solution.py
+++ b/solution.py
@@ -72,11 +72,11 @@
     kernel = (
         NEAR_SCALE * jnp.exp(-GAMMA * dist_sq) * alive.astype(jnp.float32)[:, None, None]
     ).astype(jnp.bfloat16)
-    source_feat = jnp.einsum("ps,csj->pjc", src_hot, feat_leaf, precision=PRECISE).astype(
-        jnp.bfloat16
-    )
+    source_feat = jnp.einsum(
+        "ps,csj->pjc", src_hot, feat_leaf, precision=lax.Precision.DEFAULT
+    ).astype(jnp.bfloat16)
     contrib = jnp.einsum("pij,pjc->pic", kernel, source_feat, preferred_element_type=jnp.float32)
-    accumulated = jnp.einsum("pt,pic->tic", tgt_hot, contrib, precision=PRECISE)
+    accumulated = jnp.einsum("pt,pic->tic", tgt_hot, contrib, precision=lax.Precision.HIGH)
     return accumulated.reshape(leaves * LEAF_ATOMS, channels)
 
 

time: 228 us -> 227 us (level)
  waiting for transfers between devices: 35.1 us -> 37.8 us
    ppermute x24, waiting for transfers between devices: 35.1 us -> 37.7 us  [xor_swap(): return lax.ppermute(block, 'box', [(i, i ^ 1 << bit) for i in range(count)])]
  transfers between devices with their start and end apart: 28 -> 28, of which waited for: 16 -> 16; matrix products, arithmetic and copies ran while one was open for 19% -> 18% of each run, Pallas kernels for 0% -> 0%
where the time goes in v7:
time: 227 us; the launch traced here: 225 us
  starting transfers between devices  127 us (56%)
  waiting for transfers between devices  37.8 us (17%)
  matrix products  37.2 us (16%)
  local copies, waits for them, and re-layouts  13.7 us (6%)
  other arithmetic  8.49 us (4%)
    ppermute x24, starting transfers between devices, xor_swap(): return lax.ppermute(block, 'box', [(i, i ^ 1 << bit) for i in range(count)])  111 us
    ppermute x24, waiting for transfers between devices, xor_swap(): return lax.ppermute(block, 'box', [(i, i ^ 1 << bit) for i in range(count)])  37.7 us
    dot_general x3, matrix products, near_field(): jnp.einsum('pij,pjc->pic', kernel, source_feat, preferred_element_type=jn...  20.2 us
    ppermute x2, starting transfers between devices, passed_along(): return lax.ppermute(block, axis, route)  6.7 us
    dot_general x2, matrix products, near_field(): jnp.einsum('pt,pic->tic', tgt_hot, contrib, precision=lax.Precision.HIGH)  5.65 us
    ppermute x1, starting transfers between devices, extended(): lax.ppermute(lax.slice_in_dim(block, 0, width, axis=dim), axis, backward)  5.46 us
  transfers between devices with their start and end apart: 28, of which 16 were waited for; matrix products, arithmetic and copies ran while one was open for 18% of the time, Pallas kernels for 0%

profile of v7, /device:TPU:1, one launch (start us, length us, event | category | flops | bytes accessed | tf_op | source)
XLA Modules:
  0.0 225.4 jit_solution(11646000885445433444)
XLA Ops:
  0.7 0.8 broadcast_in_dim.8
  1.5 0.7 subtract_multiply_fusion.3
  2.2 0.7 iota_compare_fusion.3
  3.2 1.3 fusion.51
  4.5 1.0 convert_convert_fusion
  6.1 6.6 %collective-permute-start.2 = (f32[4480]{0:T(1024)S(1)}, f32[4480]{0:T(1024)S(1)}, u32[]{:S(2)}, u32[]{:S(2)}) collective-permute-start(f32[4480]{0:T(1024)S(1)} %select_n.283), channel_id=1, source_target_pairs={{0,4},{1,5},{2,6},{3,7},{4,0},{5,1},{6,2},{7,3},{8,12},{9,13},{10,... | collective-permute-start | bytes 53768 | tf_op jit(solution)/shard_map/ppermute | solution.py:85
  13.0 0.9 collective-permute-done.2
  14.0 4.0 %collective-permute-start.3 = (f32[2240]{0:T(1024)S(1)}, f32[2240]{0:T(1024)S(1)}, u32[]{:S(2)}, u32[]{:S(2)}) collective-permute-start(f32[2240]{0:T(1024)S(1)} %slice_select_fusion.4), channel_id=1, source_target_pairs={{0,2},{1,3},{2,0},{3,1},{4,6},{5,7},{6,4},{7,5},{8,10},{9,11},{10,... | collective-permute-start | bytes 26888 | tf_op jit(solution)/shard_map/ppermute | solution.py:85
  18.0 0.7 pad_maximum_fusion.6
  18.7 5.5 %collective-permute-start.1 = (f32[131,256]{1,0:T(8,128)S(1)}, f32[131,256]{1,0:T(8,128)S(1)}, u32[]{:S(2)}, u32[]{:S(2)}) collective-permute-start(f32[131,256]{1,0:T(8,128)S(1)} %pad_maximum_fusion.6), channel_id=1, source_target_pairs={{1,0},{2,1},{3,2},{4,3},{5,4},{6,5},{7,6},{8,7},{9,8},{10,9},{11,1... | collective-permute-start | bytes 402440 | tf_op jit(solution)/shard_map/ppermute | solution.py:30
  24.2 3.5 %collective-permute-start = (f32[131,256]{1,0:T(8,128)S(1)}, f32[131,256]{1,0:T(8,128)S(1)}, u32[]{:S(2)}, u32[]{:S(2)}) collective-permute-start(f32[131,256]{1,0:T(8,128)S(1)} %pad_maximum_fusion.6), channel_id=1, source_target_pairs={{0,1},{1,2},{2,3},{3,4},{4,5},{5,6},{6,7},{7,8},{8,9},{9,10},{10,1... | collective-permute-start | bytes 402440 | tf_op jit(solution)/shard_map/ppermute | solution.py:27
  27.7 0.8 reshape.246
  28.6 1.9 collective-permute-start.4
  30.5 0.9 convolution_bitcast_fusion.1
  31.8 5.4 %collective-permute-start.5 = (f32[1120]{0:T(1024)S(1)}, f32[1120]{0:T(1024)S(1)}, u32[]{:S(2)}, u32[]{:S(2)}) collective-permute-start(f32[1120]{0:T(1024)S(1)} %select_add_fusion.2), channel_id=1, source_target_pairs={{0,8},{1,9},{2,10},{3,11},{4,12},{5,13},{6,14},{7,15},{8,0},{9,1},... | collective-permute-start | bytes 13448 | tf_op jit(solution)/shard_map/ppermute | solution.py:85
  37.2 2.9 %collective-permute-done.5 = f32[1120]{0:T(1024)S(1)} collective-permute-done((f32[1120]{0:T(1024)S(1)}, f32[1120]{0:T(1024)S(1)}, u32[]{:S(2)}, u32[]{:S(2)}) %collective-permute-start.5) | collective-permute-done | bytes 4512 | tf_op jit(solution)/shard_map/ppermute | solution.py:85
  40.1 3.5 %collective-permute-start.6 = (f32[2240]{0:T(1024)S(1)}, f32[2240]{0:T(1024)S(1)}, u32[]{:S(2)}, u32[]{:S(2)}) collective-permute-start(f32[2240]{0:T(1024)S(1)} %maximum_select_fusion.22), channel_id=1, source_target_pairs={{0,16},{1,17},{2,18},{3,19},{4,20},{5,21},{6,22},{7,23},{8,24},{9,... | collective-permute-start | bytes 26888 | tf_op jit(solution)/shard_map/ppermute | solution.py:85
  43.7 0.7 broadcast_multiply_fusion
  44.3 0.8 copy.214
  45.2 4.6 %collective-permute-start.7 = (f32[4480]{0:T(1024)S(1)}, f32[4480]{0:T(1024)S(1)}, u32[]{:S(2)}, u32[]{:S(2)}) collective-permute-start(f32[4480]{0:T(1024)S(1)} %maximum_select_fusion.18), channel_id=1, source_target_pairs={{0,32},{1,33},{2,34},{3,35},{4,36},{5,37},{6,38},{7,39},{8,40},{9,... | collective-permute-start | bytes 53768 | tf_op jit(solution)/shard_map/ppermute | solution.py:85
  50.3 0.7 convert_element_type.55
  51.6 4.8 %collective-permute-start.8 = (f32[8960]{0:T(1024)S(1)}, f32[8960]{0:T(1024)S(1)}, u32[]{:S(2)}, u32[]{:S(2)}) collective-permute-start(f32[8960]{0:T(1024)S(1)} %maximum_select_fusion.14), channel_id=1, source_target_pairs={{0,64},{1,65},{2,66},{3,67},{4,68},{5,69},{6,70},{7,71},{8,72},{9,... | collective-permute-start | bytes 107528 | tf_op jit(solution)/shard_map/ppermute | solution.py:85
  56.7 1.1 collective-permute-done.8
  57.7 4.4 %collective-permute-start.9 = (f32[17920]{0:T(1024)S(1)}, f32[17920]{0:T(1024)S(1)}, u32[]{:S(2)}, u32[]{:S(2)}) collective-permute-start(f32[17920]{0:T(1024)S(1)} %maximum_select_fusion.9), channel_id=1, source_target_pairs={{0,128},{1,129},{2,130},{3,131},{4,132},{5,133},{6,134},{7,135},{8... | collective-permute-start | bytes 215048 | tf_op jit(solution)/shard_map/ppermute | solution.py:85
  63.1 0.7 convert_bitcast_fusion
  64.2 7.2 %collective-permute-start.10 = (f32[35840]{0:T(1024)S(1)}, f32[35840]{0:T(1024)S(1)}, u32[]{:S(2)}, u32[]{:S(2)}) collective-permute-start(f32[35840]{0:T(1024)S(1)} %maximum_select_fusion.5), channel_id=1, source_target_pairs={{0,256},{1,257},{2,258},{3,259},{4,260},{5,261},{6,262},{7,263},{8... | collective-permute-start | bytes 430088 | tf_op jit(solution)/shard_map/ppermute | solution.py:85
  71.4 6.5 %fusion.26 = f32[108,64,128]{2,1,0:T(8,128)} fusion(bf16[108,64,128]{2,0,1:T(8,128)(2,1)S(1)} %convert_bitcast_fusion, f32[108]{0:T(128)S(1)} %broadcast_multiply_fusion, f32[108,64]{1,0:T(8,128)S(1)} %copy.208, f32[108,64]{1,0:T(8,128)S(1)} %copy.207, f32[108,64]{1,0:T(8,128)S(1)} %copy.206, f32[108,64]{1,0:T(8,128)S(1)} %copy.205, ...), kind=kOutput, calls=%fused_computation.32 | convolution fusion | flops 118112256 | bytes 5474736 | tf_op jit(solution)/shard_map/jvp(pij,pjc->pic)/dot_general | solution.py:78
  80.5 2.2 fusion.31
  83.1 8.2 %collective-permute-start.11 = (f32[1120]{0:T(1024)S(1)}, f32[1120]{0:T(1024)S(1)}, u32[]{:S(2)}, u32[]{:S(2)}) collective-permute-start(f32[1120]{0:T(1024)S(1)} %reshape.251), channel_id=1, source_target_pairs={{0,1},{1,0},{2,3},{3,2},{4,5},{5,4},{6,7},{7,6},{8,9},{9,8},{10,11... | collective-permute-start | bytes 13448 | tf_op jit(solution)/shard_map/ppermute | solution.py:85
  91.4 4.4 %fusion = f32[4,64,128]{2,0,1:T(4,128)S(1)} fusion(f32[108,64,128]{2,1,0:T(8,128)} %fusion.26, s32[108]{0:T(128)S(1)} %copy-done.7), kind=kOutput, calls=%fused_computation.6 | convolution fusion | flops 21234096 | bytes 3670448 | tf_op jit(solution)/shard_map/jvp(pt,pic->tic)/dot_general | solution.py:79
  95.9 1.9 collective-permute-start.12
  98.0 2.3 %collective-permute-done.12 = f32[2240]{0:T(1024)S(1)} collective-permute-done((f32[2240]{0:T(1024)S(1)}, f32[2240]{0:T(1024)S(1)}, u32[]{:S(2)}, u32[]{:S(2)}) %collective-permute-start.12) | collective-permute-done | bytes 8992 | tf_op jit(solution)/shard_map/ppermute | solution.py:85
  100.4 2.6 %collective-permute-start.13 = (f32[4480]{0:T(1024)S(1)}, f32[4480]{0:T(1024)S(1)}, u32[]{:S(2)}, u32[]{:S(2)}) collective-permute-start(f32[4480]{0:T(1024)S(1)} %maximum_select_fusion.19), channel_id=1, source_target_pairs={{0,4},{1,5},{2,6},{3,7},{4,0},{5,1},{6,2},{7,3},{8,12},{9,13},{10,... | collective-permute-start | bytes 53768 | tf_op jit(solution)/shard_map/ppermute | solution.py:85
  103.2 2.6 %collective-permute-done.13 = f32[4480]{0:T(1024)S(1)} collective-permute-done((f32[4480]{0:T(1024)S(1)}, f32[4480]{0:T(1024)S(1)}, u32[]{:S(2)}, u32[]{:S(2)}) %collective-permute-start.13) | collective-permute-done | bytes 17952 | tf_op jit(solution)/shard_map/ppermute | solution.py:85
  107.1 2.4 %collective-permute-start.16 = (f32[2240]{0:T(1024)S(1)}, f32[2240]{0:T(1024)S(1)}, u32[]{:S(2)}, u32[]{:S(2)}) collective-permute-start(f32[2240]{0:T(1024)S(1)} %select_n.320), channel_id=1, source_target_pairs={{0,4},{1,5},{2,6},{3,7},{4,0},{5,1},{6,2},{7,3},{8,12},{9,13},{10,... | collective-permute-start | bytes 26888 | tf_op jit(solution)/shard_map/ppermute | solution.py:85
  109.5 1.2 fusion.49
  110.8 6.0 %convert_bitcast_fusion.1 = bf16[128,64,108]{0,1,2:T(8,128)(2,1)S(1)} fusion(bf16[108,64,128]{2,0,1:T(8,128)(2,1)S(1)} %fusion.49, f32[108]{0:T(128)S(1)} %broadcast_multiply_fusion, f32[108,64]{1,0:T(8,128)S(1)} %copy.208, f32[108,64]{1,0:T(8,128)S(1)} %copy.207, f32[108,64]{1,0:T(8,128)S(1)} %copy.206, f32[108,64]{1,0:T(8,128)S(1)} %copy.205, ...), kind=kOutput, calls=%fused_computation.30 | convolution fusion | flops 118112256 | bytes 3705264 | tf_op jit(solution)/shard_map/transpose(jvp(pij,pjc->pic))/dot_general | solution.py:78
  116.8 7.7 %fusion.14 = (f32[108,64]{1,0:T(8,128)S(1)}, f32[108,64]{1,0:T(8,128)S(1)}, f32[108,64]{1,0:T(8,128)S(1)}, f32[108,64]{1,0:T(8,128)S(1)}, f32[108,64]{1,0:T(8,128)S(1)}, /*index=5*/f32[108,64]{1,0:T(8,128)S(1)}) fusion(f32[108,64]{1,0:T(8,128)S(1)} %copy.208, f32[108,64]{1,0:T(8,128)S(1)} %copy.207, f32[108,64]{1,0:T(8,128)S(1)} %copy.204, ...), kind=kOutput, calls=%fused_computation.22 | convolution fusion | flops 124706304 | bytes 3871152 | tf_op jit(solution)/shard_map/transpose(jvp(pij,pjc->pic))/dot_general | solution.py:78
  124.5 1.0 fusion.28
  126.5 3.4 %collective-permute-start.17 = (f32[1120]{0:T(1024)S(1)}, f32[1120]{0:T(1024)S(1)}, u32[]{:S(2)}, u32[]{:S(2)}) collective-permute-start(f32[1120]{0:T(1024)S(1)} %slice_select_fusion.5), channel_id=1, source_target_pairs={{0,2},{1,3},{2,0},{3,1},{4,6},{5,7},{6,4},{7,5},{8,10},{9,11},{10,... | collective-permute-start | bytes 13448 | tf_op jit(solution)/shard_map/ppermute | solution.py:85
  129.9 4.8 %collective-permute-start.14 = (f32[131,256]{1,0:T(8,128)S(1)}, f32[131,256]{1,0:T(8,128)S(1)}, u32[]{:S(2)}, u32[]{:S(2)}) collective-permute-start(f32[131,256]{1,0:T(8,128)S(1)} %get-tuple-element.17), channel_id=1, source_target_pairs={{1,0},{2,1},{3,2},{4,3},{5,4},{6,5},{7,6},{8,7},{9,8},{10,9},{11,1... | collective-permute-start | bytes 402440 | tf_op jit(solution)/shard_map/ppermute | solution.py:38
  134.7 1.9 collective-permute-start.15
  136.8 2.4 %collective-permute-start.18 = (f32[560]{0:T(1024)S(1)}, f32[560]{0:T(1024)S(1)}, u32[]{:S(2)}, u32[]{:S(2)}) collective-permute-start(f32[560]{0:T(1024)S(1)} %slice_select_fusion.7), channel_id=1, source_target_pairs={{0,1},{1,0},{2,3},{3,2},{4,5},{5,4},{6,7},{7,6},{8,9},{9,8},{10,11... | collective-permute-start | bytes 6728 | tf_op jit(solution)/shard_map/ppermute | solution.py:85
  139.4 0.6 collective-permute-done.18
  141.6 6.4 %collective-permute-start.19 = (f32[18297]{0:T(1024)S(1)}, f32[18297]{0:T(1024)S(1)}, u32[]{:S(2)}, u32[]{:S(2)}) collective-permute-start(f32[18297]{0:T(1024)S(1)} %concatenate.293), channel_id=1, source_target_pairs={{0,8},{1,9},{2,10},{3,11},{4,12},{5,13},{6,14},{7,15},{8,0},{9,1},... | collective-permute-start | bytes 219572 | tf_op jit(solution)/shard_map/ppermute | solution.py:85
  148.2 2.5 %collective-permute-done.19 = f32[18297]{0:T(1024)S(1)} collective-permute-done((f32[18297]{0:T(1024)S(1)}, f32[18297]{0:T(1024)S(1)}, u32[]{:S(2)}, u32[]{:S(2)}) %collective-permute-start.19) | collective-permute-done | bytes 73220 | tf_op jit(solution)/shard_map/ppermute | solution.py:85
  151.0 3.1 %collective-permute-start.20 = (f32[18857]{0:T(1024)S(1)}, f32[18857]{0:T(1024)S(1)}, u32[]{:S(2)}, u32[]{:S(2)}) collective-permute-start(f32[18857]{0:T(1024)S(1)} %pad_maximum_fusion.11), channel_id=1, source_target_pairs={{0,16},{1,17},{2,18},{3,19},{4,20},{5,21},{6,22},{7,23},{8,24},{9,... | collective-permute-start | bytes 226292 | tf_op jit(solution)/shard_map/ppermute | solution.py:85
  154.4 1.7 collective-permute-done.20
  156.4 4.6 %collective-permute-start.21 = (f32[19977]{0:T(1024)S(1)}, f32[19977]{0:T(1024)S(1)}, u32[]{:S(2)}, u32[]{:S(2)}) collective-permute-start(f32[19977]{0:T(1024)S(1)} %pad_maximum_fusion.9), channel_id=1, source_target_pairs={{0,32},{1,33},{2,34},{3,35},{4,36},{5,37},{6,38},{7,39},{8,40},{9,... | collective-permute-start | bytes 239732 | tf_op jit(solution)/shard_map/ppermute | solution.py:85
  161.2 1.9 collective-permute-done.21
  163.3 5.3 %collective-permute-start.22 = (f32[22217]{0:T(1024)S(1)}, f32[22217]{0:T(1024)S(1)}, u32[]{:S(2)}, u32[]{:S(2)}) collective-permute-start(f32[22217]{0:T(1024)S(1)} %pad_maximum_fusion.8), channel_id=1, source_target_pairs={{0,64},{1,65},{2,66},{3,67},{4,68},{5,69},{6,70},{7,71},{8,72},{9,... | collective-permute-start | bytes 266612 | tf_op jit(solution)/shard_map/ppermute | solution.py:85
  169.1 1.3 collective-permute-done.22
  170.5 3.2 %collective-permute-start.23 = (f32[26697]{0:T(1024)S(1)}, f32[26697]{0:T(1024)S(1)}, u32[]{:S(2)}, u32[]{:S(2)}) collective-permute-start(f32[26697]{0:T(1024)S(1)} %pad_maximum_fusion.7), channel_id=1, source_target_pairs={{0,128},{1,129},{2,130},{3,131},{4,132},{5,133},{6,134},{7,135},{8... | collective-permute-start | bytes 320372 | tf_op jit(solution)/shard_map/ppermute | solution.py:85
  174.0 2.9 %collective-permute-done.23 = f32[26697]{0:T(1024)S(1)} collective-permute-done((f32[26697]{0:T(1024)S(1)}, f32[26697]{0:T(1024)S(1)}, u32[]{:S(2)}, u32[]{:S(2)}) %collective-permute-start.23) | collective-permute-done | bytes 106820 | tf_op jit(solution)/shard_map/ppermute | solution.py:85
  176.9 4.4 %collective-permute-start.24 = (f32[35657]{0:T(1024)S(1)}, f32[35657]{0:T(1024)S(1)}, u32[]{:S(2)}, u32[]{:S(2)}) collective-permute-start(f32[35657]{0:T(1024)S(1)} %pad_maximum_fusion.3), channel_id=1, source_target_pairs={{0,256},{1,257},{2,258},{3,259},{4,260},{5,261},{6,262},{7,263},{8... | collective-permute-start | bytes 427892 | tf_op jit(solution)/shard_map/ppermute | solution.py:85
  182.0 6.6 %collective-permute-done.24 = f32[35657]{0:T(1024)S(1)} collective-permute-done((f32[35657]{0:T(1024)S(1)}, f32[35657]{0:T(1024)S(1)}, u32[]{:S(2)}, u32[]{:S(2)}) %collective-permute-start.24) | collective-permute-done | bytes 142660 | tf_op jit(solution)/shard_map/ppermute | solution.py:85
  189.8 16.6 %collective-permute-start.25 = (f32[18297]{0:T(1024)S(1)}, f32[18297]{0:T(1024)S(1)}, u32[]{:S(2)}, u32[]{:S(2)}) collective-permute-start(f32[18297]{0:T(1024)S(1)} %pad_maximum_fusion.13), channel_id=1, source_target_pairs={{0,1},{1,0},{2,3},{3,2},{4,5},{5,4},{6,7},{7,6},{8,9},{9,8},{10,11... | collective-permute-start | bytes 219572 | tf_op jit(solution)/shard_map/ppermute | solution.py:85
  207.8 1.9 collective-permute-start.26
  209.7 3.5 %collective-permute-done.26 = f32[18857]{0:T(1024)S(1)} collective-permute-done((f32[18857]{0:T(1024)S(1)}, f32[18857]{0:T(1024)S(1)}, u32[]{:S(2)}, u32[]{:S(2)}) %collective-permute-start.26) | collective-permute-done | bytes 75460 | tf_op jit(solution)/shard_map/ppermute | solution.py:85
  213.7 1.9 collective-permute-start.27
  215.6 6.5 %collective-permute-done.27 = f32[19977]{0:T(1024)S(1)} collective-permute-done((f32[19977]{0:T(1024)S(1)}, f32[19977]{0:T(1024)S(1)}, u32[]{:S(2)}, u32[]{:S(2)}) %collective-permute-start.27) | collective-permute-done | bytes 79940 | tf_op jit(solution)/shard_map/ppermute | solution.py:85
  222.8 0.6 slice_bitcast_fusion
  224.1 0.7 reshape.263
  224.8 0.6 fusion.62
  (208 shorter events, 18.8 us)
Async XLA Ops:
  0.6 3.9 %copy-start = (bf16[128,128]{1,0:T(8,128)(2,1)S(1)}, bf16[128,128]{1,0:T(8,128)(2,1)}, u32[]{:S(2)}) copy-start(bf16[128,128]{1,0:T(8,128)(2,1)} %param.15) | copy-start | bytes 98308
  0.6 61.9 %copy-start.4 = (f32[3,256]{1,0:T(4,128)S(1)}, f32[3,256]{1,0:T(4,128)}, u32[]{:S(2)}) copy-start(f32[3,256]{1,0:T(4,128)} %param.11) | copy-start | bytes 9220
  5.6 57.3 %copy-start.6 = (s32[108]{0:T(128)S(1)}, s32[108]{0:T(128)}, u32[]{:S(2)}) copy-start(s32[108]{0:T(128)} %param.19) | copy-start | bytes 1300
  6.1 7.8 %collective-permute-start.2 = (f32[4480]{0:T(1024)S(1)}, f32[4480]{0:T(1024)S(1)}, u32[]{:S(2)}, u32[]{:S(2)}) collective-permute-start(f32[4480]{0:T(1024)S(1)} %select_n.283), channel_id=1, source_target_pairs={{0,4},{1,5},{2,6},{3,7},{4,0},{5,1},{6,2},{7,3},{8,12},{9,13},{10,... | collective-permute-start | bytes 53768 | tf_op jit(solution)/shard_map/ppermute | solution.py:85
  14.0 14.5 %collective-permute-start.3 = (f32[2240]{0:T(1024)S(1)}, f32[2240]{0:T(1024)S(1)}, u32[]{:S(2)}, u32[]{:S(2)}) collective-permute-start(f32[2240]{0:T(1024)S(1)} %slice_select_fusion.4), channel_id=1, source_target_pairs={{0,2},{1,3},{2,0},{3,1},{4,6},{5,7},{6,4},{7,5},{8,10},{9,11},{10,... | collective-permute-start | bytes 26888 | tf_op jit(solution)/shard_map/ppermute | solution.py:85
  18.7 43.8 %collective-permute-start.1 = (f32[131,256]{1,0:T(8,128)S(1)}, f32[131,256]{1,0:T(8,128)S(1)}, u32[]{:S(2)}, u32[]{:S(2)}) collective-permute-start(f32[131,256]{1,0:T(8,128)S(1)} %pad_maximum_fusion.6), channel_id=1, source_target_pairs={{1,0},{2,1},{3,2},{4,3},{5,4},{6,5},{7,6},{8,7},{9,8},{10,9},{11,1... | collective-permute-start | bytes 402440 | tf_op jit(solution)/shard_map/ppermute | solution.py:30
  24.2 38.3 %collective-permute-start = (f32[131,256]{1,0:T(8,128)S(1)}, f32[131,256]{1,0:T(8,128)S(1)}, u32[]{:S(2)}, u32[]{:S(2)}) collective-permute-start(f32[131,256]{1,0:T(8,128)S(1)} %pad_maximum_fusion.6), channel_id=1, source_target_pairs={{0,1},{1,2},{2,3},{3,4},{4,5},{5,6},{6,7},{7,8},{8,9},{9,10},{10,1... | collective-permute-start | bytes 402440 | tf_op jit(solution)/shard_map/ppermute | solution.py:27
  28.6 3.1 %collective-permute-start.4 = (f32[1120]{0:T(1024)S(1)}, f32[1120]{0:T(1024)S(1)}, u32[]{:S(2)}, u32[]{:S(2)}) collective-permute-start(f32[1120]{0:T(1024)S(1)} %slice_select_fusion.6), channel_id=1, source_target_pairs={{0,1},{1,0},{2,3},{3,2},{4,5},{5,4},{6,7},{7,6},{8,9},{9,8},{10,11... | collective-permute-start | bytes 13448 | tf_op jit(solution)/shard_map/ppermute | solution.py:85
  31.8 8.3 %collective-permute-start.5 = (f32[1120]{0:T(1024)S(1)}, f32[1120]{0:T(1024)S(1)}, u32[]{:S(2)}, u32[]{:S(2)}) collective-permute-start(f32[1120]{0:T(1024)S(1)} %select_add_fusion.2), channel_id=1, source_target_pairs={{0,8},{1,9},{2,10},{3,11},{4,12},{5,13},{6,14},{7,15},{8,0},{9,1},... | collective-permute-start | bytes 13448 | tf_op jit(solution)/shard_map/ppermute | solution.py:85
  40.1 5.0 %collective-permute-start.6 = (f32[2240]{0:T(1024)S(1)}, f32[2240]{0:T(1024)S(1)}, u32[]{:S(2)}, u32[]{:S(2)}) collective-permute-start(f32[2240]{0:T(1024)S(1)} %maximum_select_fusion.22), channel_id=1, source_target_pairs={{0,16},{1,17},{2,18},{3,19},{4,20},{5,21},{6,22},{7,23},{8,24},{9,... | collective-permute-start | bytes 26888 | tf_op jit(solution)/shard_map/ppermute | solution.py:85
  45.2 6.3 %collective-permute-start.7 = (f32[4480]{0:T(1024)S(1)}, f32[4480]{0:T(1024)S(1)}, u32[]{:S(2)}, u32[]{:S(2)}) collective-permute-start(f32[4480]{0:T(1024)S(1)} %maximum_select_fusion.18), channel_id=1, source_target_pairs={{0,32},{1,33},{2,34},{3,35},{4,36},{5,37},{6,38},{7,39},{8,40},{9,... | collective-permute-start | bytes 53768 | tf_op jit(solution)/shard_map/ppermute | solution.py:85
  51.6 6.2 %collective-permute-start.8 = (f32[8960]{0:T(1024)S(1)}, f32[8960]{0:T(1024)S(1)}, u32[]{:S(2)}, u32[]{:S(2)}) collective-permute-start(f32[8960]{0:T(1024)S(1)} %maximum_select_fusion.14), channel_id=1, source_target_pairs={{0,64},{1,65},{2,66},{3,67},{4,68},{5,69},{6,70},{7,71},{8,72},{9,... | collective-permute-start | bytes 107528 | tf_op jit(solution)/shard_map/ppermute | solution.py:85
  57.7 6.4 %collective-permute-start.9 = (f32[17920]{0:T(1024)S(1)}, f32[17920]{0:T(1024)S(1)}, u32[]{:S(2)}, u32[]{:S(2)}) collective-permute-start(f32[17920]{0:T(1024)S(1)} %maximum_select_fusion.9), channel_id=1, source_target_pairs={{0,128},{1,129},{2,130},{3,131},{4,132},{5,133},{6,134},{7,135},{8... | collective-permute-start | bytes 215048 | tf_op jit(solution)/shard_map/ppermute | solution.py:85
  63.8 7.6 %copy-start.1 = (bf16[108,64,128]{2,0,1:T(8,128)(2,1)}, bf16[108,64,128]{2,0,1:T(8,128)(2,1)S(1)}, u32[]{:S(2)}) copy-start(bf16[108,64,128]{2,0,1:T(8,128)(2,1)S(1)} %convert_bitcast_fusion) | copy-start | bytes 5308420
  64.2 14.9 %collective-permute-start.10 = (f32[35840]{0:T(1024)S(1)}, f32[35840]{0:T(1024)S(1)}, u32[]{:S(2)}, u32[]{:S(2)}) collective-permute-start(f32[35840]{0:T(1024)S(1)} %maximum_select_fusion.5), channel_id=1, source_target_pairs={{0,256},{1,257},{2,258},{3,259},{4,260},{5,261},{6,262},{7,263},{8... | collective-permute-start | bytes 430088 | tf_op jit(solution)/shard_map/ppermute | solution.py:85
  78.5 4.2 %copy-start.5 = (f32[35,35]{1,0:T(8,128)S(1)}, f32[35,35]{1,0:T(8,128)}, u32[]{:S(2)}) copy-start(f32[35,35]{1,0:T(8,128)} %param.16) | copy-start | bytes 14704
  78.5 12.8 %copy-start.7 = (s32[108]{0:T(128)S(1)}, s32[108]{0:T(128)}, u32[]{:S(2)}) copy-start(s32[108]{0:T(128)} %param.18) | copy-start | bytes 1300
  80.5 25.6 %copy-start.8 = (f32[128]{0:T(128)S(1)}, f32[128]{0:T(128)}, u32[]{:S(2)}) copy-start(f32[128]{0:T(128)} %param.17) | copy-start | bytes 1540
  83.1 12.7 %collective-permute-start.11 = (f32[1120]{0:T(1024)S(1)}, f32[1120]{0:T(1024)S(1)}, u32[]{:S(2)}, u32[]{:S(2)}) collective-permute-start(f32[1120]{0:T(1024)S(1)} %reshape.251), channel_id=1, source_target_pairs={{0,1},{1,0},{2,3},{3,2},{4,5},{5,4},{6,7},{7,6},{8,9},{9,8},{10,11... | collective-permute-start | bytes 13448 | tf_op jit(solution)/shard_map/ppermute | solution.py:85
  95.9 4.4 %collective-permute-start.12 = (f32[2240]{0:T(1024)S(1)}, f32[2240]{0:T(1024)S(1)}, u32[]{:S(2)}, u32[]{:S(2)}) collective-permute-start(f32[2240]{0:T(1024)S(1)} %maximum_select_fusion.23), channel_id=1, source_target_pairs={{0,2},{1,3},{2,0},{3,1},{4,6},{5,7},{6,4},{7,5},{8,10},{9,11},{10,... | collective-permute-start | bytes 26888 | tf_op jit(solution)/shard_map/ppermute | solution.py:85
  100.4 5.4 %collective-permute-start.13 = (f32[4480]{0:T(1024)S(1)}, f32[4480]{0:T(1024)S(1)}, u32[]{:S(2)}, u32[]{:S(2)}) collective-permute-start(f32[4480]{0:T(1024)S(1)} %maximum_select_fusion.19), channel_id=1, source_target_pairs={{0,4},{1,5},{2,6},{3,7},{4,0},{5,1},{6,2},{7,3},{8,12},{9,13},{10,... | collective-permute-start | bytes 53768 | tf_op jit(solution)/shard_map/ppermute | solution.py:85
  107.1 19.3 %collective-permute-start.16 = (f32[2240]{0:T(1024)S(1)}, f32[2240]{0:T(1024)S(1)}, u32[]{:S(2)}, u32[]{:S(2)}) collective-permute-start(f32[2240]{0:T(1024)S(1)} %select_n.320), channel_id=1, source_target_pairs={{0,4},{1,5},{2,6},{3,7},{4,0},{5,1},{6,2},{7,3},{8,12},{9,13},{10,... | collective-permute-start | bytes 26888 | tf_op jit(solution)/shard_map/ppermute | solution.py:85
  110.8 6.0 %copy-start.2 = (bf16[108,64,128]{2,0,1:T(8,128)(2,1)S(1)}, bf16[108,64,128]{2,0,1:T(8,128)(2,1)}, u32[]{:S(2)}) copy-start(bf16[108,64,128]{2,0,1:T(8,128)(2,1)} %copy-done.1) | copy-start | bytes 5308420
  124.5 16.3 %copy-start.3 = (bf16[256,128]{1,0:T(8,128)(2,1)S(1)}, bf16[256,128]{1,0:T(8,128)(2,1)}, u32[]{:S(2)}) copy-start(bf16[256,128]{1,0:T(8,128)(2,1)} %param.14) | copy-start | bytes 196612
  126.5 10.1 %collective-permute-start.17 = (f32[1120]{0:T(1024)S(1)}, f32[1120]{0:T(1024)S(1)}, u32[]{:S(2)}, u32[]{:S(2)}) collective-permute-start(f32[1120]{0:T(1024)S(1)} %slice_select_fusion.5), channel_id=1, source_target_pairs={{0,2},{1,3},{2,0},{3,1},{4,6},{5,7},{6,4},{7,5},{8,10},{9,11},{10,... | collective-permute-start | bytes 13448 | tf_op jit(solution)/shard_map/ppermute | solution.py:85
  129.9 10.9 %collective-permute-start.14 = (f32[131,256]{1,0:T(8,128)S(1)}, f32[131,256]{1,0:T(8,128)S(1)}, u32[]{:S(2)}, u32[]{:S(2)}) collective-permute-start(f32[131,256]{1,0:T(8,128)S(1)} %get-tuple-element.17), channel_id=1, source_target_pairs={{1,0},{2,1},{3,2},{4,3},{5,4},{6,5},{7,6},{8,7},{9,8},{10,9},{11,1... | collective-permute-start | bytes 402440 | tf_op jit(solution)/shard_map/ppermute | solution.py:38
  134.7 6.1 %collective-permute-start.15 = (f32[131,256]{1,0:T(8,128)S(1)}, f32[131,256]{1,0:T(8,128)S(1)}, u32[]{:S(2)}, u32[]{:S(2)}) collective-permute-start(f32[131,256]{1,0:T(8,128)S(1)} %get-tuple-element.18), channel_id=1, source_target_pairs={{0,1},{1,2},{2,3},{3,4},{4,5},{5,6},{6,7},{7,8},{8,9},{9,10},{10,1... | collective-permute-start | bytes 402440 | tf_op jit(solution)/shard_map/ppermute | solution.py:38
  136.8 3.2 %collective-permute-start.18 = (f32[560]{0:T(1024)S(1)}, f32[560]{0:T(1024)S(1)}, u32[]{:S(2)}, u32[]{:S(2)}) collective-permute-start(f32[560]{0:T(1024)S(1)} %slice_select_fusion.7), channel_id=1, source_target_pairs={{0,1},{1,0},{2,3},{3,2},{4,5},{5,4},{6,7},{7,6},{8,9},{9,8},{10,11... | collective-permute-start | bytes 6728 | tf_op jit(solution)/shard_map/ppermute | solution.py:85
  141.6 9.1 %collective-permute-start.19 = (f32[18297]{0:T(1024)S(1)}, f32[18297]{0:T(1024)S(1)}, u32[]{:S(2)}, u32[]{:S(2)}) collective-permute-start(f32[18297]{0:T(1024)S(1)} %concatenate.293), channel_id=1, source_target_pairs={{0,8},{1,9},{2,10},{3,11},{4,12},{5,13},{6,14},{7,15},{8,0},{9,1},... | collective-permute-start | bytes 219572 | tf_op jit(solution)/shard_map/ppermute | solution.py:85
  151.0 5.1 %collective-permute-start.20 = (f32[18857]{0:T(1024)S(1)}, f32[18857]{0:T(1024)S(1)}, u32[]{:S(2)}, u32[]{:S(2)}) collective-permute-start(f32[18857]{0:T(1024)S(1)} %pad_maximum_fusion.11), channel_id=1, source_target_pairs={{0,16},{1,17},{2,18},{3,19},{4,20},{5,21},{6,22},{7,23},{8,24},{9,... | collective-permute-start | bytes 226292 | tf_op jit(solution)/shard_map/ppermute | solution.py:85
  156.4 6.7 %collective-permute-start.21 = (f32[19977]{0:T(1024)S(1)}, f32[19977]{0:T(1024)S(1)}, u32[]{:S(2)}, u32[]{:S(2)}) collective-permute-start(f32[19977]{0:T(1024)S(1)} %pad_maximum_fusion.9), channel_id=1, source_target_pairs={{0,32},{1,33},{2,34},{3,35},{4,36},{5,37},{6,38},{7,39},{8,40},{9,... | collective-permute-start | bytes 239732 | tf_op jit(solution)/shard_map/ppermute | solution.py:85
  163.3 7.2 %collective-permute-start.22 = (f32[22217]{0:T(1024)S(1)}, f32[22217]{0:T(1024)S(1)}, u32[]{:S(2)}, u32[]{:S(2)}) collective-permute-start(f32[22217]{0:T(1024)S(1)} %pad_maximum_fusion.8), channel_id=1, source_target_pairs={{0,64},{1,65},{2,66},{3,67},{4,68},{5,69},{6,70},{7,71},{8,72},{9,... | collective-permute-start | bytes 266612 | tf_op jit(solution)/shard_map/ppermute | solution.py:85
  170.5 6.4 %collective-permute-start.23 = (f32[26697]{0:T(1024)S(1)}, f32[26697]{0:T(1024)S(1)}, u32[]{:S(2)}, u32[]{:S(2)}) collective-permute-start(f32[26697]{0:T(1024)S(1)} %pad_maximum_fusion.7), channel_id=1, source_target_pairs={{0,128},{1,129},{2,130},{3,131},{4,132},{5,133},{6,134},{7,135},{8... | collective-permute-start | bytes 320372 | tf_op jit(solution)/shard_map/ppermute | solution.py:85
  176.9 11.6 %collective-permute-start.24 = (f32[35657]{0:T(1024)S(1)}, f32[35657]{0:T(1024)S(1)}, u32[]{:S(2)}, u32[]{:S(2)}) collective-permute-start(f32[35657]{0:T(1024)S(1)} %pad_maximum_fusion.3), channel_id=1, source_target_pairs={{0,256},{1,257},{2,258},{3,259},{4,260},{5,261},{6,262},{7,263},{8... | collective-permute-start | bytes 427892 | tf_op jit(solution)/shard_map/ppermute | solution.py:85
  189.8 17.5 %collective-permute-start.25 = (f32[18297]{0:T(1024)S(1)}, f32[18297]{0:T(1024)S(1)}, u32[]{:S(2)}, u32[]{:S(2)}) collective-permute-start(f32[18297]{0:T(1024)S(1)} %pad_maximum_fusion.13), channel_id=1, source_target_pairs={{0,1},{1,0},{2,3},{3,2},{4,5},{5,4},{6,7},{7,6},{8,9},{9,8},{10,11... | collective-permute-start | bytes 219572 | tf_op jit(solution)/shard_map/ppermute | solution.py:85
  207.8 5.5 %collective-permute-start.26 = (f32[18857]{0:T(1024)S(1)}, f32[18857]{0:T(1024)S(1)}, u32[]{:S(2)}, u32[]{:S(2)}) collective-permute-start(f32[18857]{0:T(1024)S(1)} %pad_maximum_fusion.12), channel_id=1, source_target_pairs={{0,2},{1,3},{2,0},{3,1},{4,6},{5,7},{6,4},{7,5},{8,10},{9,11},{10,... | collective-permute-start | bytes 226292 | tf_op jit(solution)/shard_map/ppermute | solution.py:85
  213.7 8.5 %collective-permute-start.27 = (f32[19977]{0:T(1024)S(1)}, f32[19977]{0:T(1024)S(1)}, u32[]{:S(2)}, u32[]{:S(2)}) collective-permute-start(f32[19977]{0:T(1024)S(1)} %pad_maximum_fusion.10), channel_id=1, source_target_pairs={{0,4},{1,5},{2,6},{3,7},{4,0},{5,1},{6,2},{7,3},{8,12},{9,13},{10,... | collective-permute-start | bytes 239732 | tf_op jit(solution)/shard_map/ppermute | solution.py:85

commit v8 on v7

--- a/solution.py
+++ b/solution.py
@@ -144,11 +144,14 @@
         jnp.einsum("ic,ai->ca", msg_weight, features, preferred_element_type=jnp.float32)
         * mask_f[None, :]
     )
+    masked_feat = features.astype(jnp.float32) * mask_f[:, None]
+    channels = hidden_t.shape[0]
     own_pack = jnp.concatenate(
-        [positions, hidden_t.astype(jnp.bfloat16).astype(jnp.float32)], axis=0
+        [positions, hidden_t.astype(jnp.bfloat16).astype(jnp.float32), masked_feat.T], axis=0
     )
     ext_pack = extended(own_pack, (("box", 1),), atom_num)
-    pos_ext, hid_ext = ext_pack[:3], ext_pack[3:]
+    pos_ext, hid_ext = ext_pack[:3], ext_pack[3 : 3 + channels]
+    feat_ext = ext_pack[3 + channels :]
 
     def near_part(own, ext, feat_ext):
         return near_field(own, ext, feat_ext, pair_target, pair_source, pair_live)
@@ -161,7 +164,6 @@
 
     basis_val, basis_back = jax.vjp(far_basis, positions)
     moment = jnp.einsum("ka,ca->kc", basis_val, hidden_t, precision=PRECISE)
-    masked_feat = features.astype(jnp.float32) * mask_f[:, None]
     feat_basis = jnp.einsum("ka,ai->ki", basis_val, masked_feat, precision=PRECISE)
     counts_mat = jnp.sum(
         (far_list[:, :, None] == jnp.arange(groups, dtype=jnp.int32)[None, None, :]).astype(
@@ -171,7 +173,6 @@
     )
     row_weights = lax.dynamic_index_in_dim(counts_mat, group_id, 0, keepdims=False)
     col_weights = lax.dynamic_index_in_dim(counts_mat, group_id, 1, keepdims=False)
-    channels = moment.shape[1]
     subs = 8
     width = channels // subs
     rows = jnp.stack([moment, feat_basis]).reshape(2, -1, subs, width)
@@ -205,14 +206,10 @@
         axis=1,
     )
     d_own, d_ext, d_feat_ext = near_back(d_pre)
-    d_pack = jnp.concatenate([d_ext, d_feat_ext], axis=0)
-    low_pack = passed_along(d_pack[:, :atom_num], "box", -1)
-    high_pack = passed_along(d_pack[:, 2 * atom_num :], "box", 1)
-    low_pos, low_feat = low_pack[:3], low_pack[3:]
-    high_pos, high_feat = high_pack[:3], high_pack[3:]
-    d_hidden_near = d_feat_ext[:, atom_num : 2 * atom_num] + low_feat + high_feat
+    low_pos = passed_along(d_ext[:, :atom_num], "box", -1)
+    high_pos = passed_along(d_ext[:, 2 * atom_num :], "box", 1)
     grad_msg_part = (
-        jnp.einsum("ai,ca->ic", masked_feat, d_hidden_near, precision=PRECISE) + far_msg
+        jnp.einsum("ia,ca->ic", feat_ext, d_feat_ext, precision=PRECISE) + far_msg
     )
     flat = jnp.concatenate(
         [grad_msg_part.reshape(-1), grad_trans_part.reshape(-1), grad_read_part.reshape(-1)]

time: 227 us -> 238 us (1.048)
  local copies, waits for them, and re-layouts: 13.7 us -> 22.1 us
  matrix products: 37.2 us -> 42.8 us
  waiting for transfers between devices: 37.8 us -> 34.3 us
    sub x8, local copies, waits for them, and re-layouts: 0.64 us -> 5.99 us  [near_field(): offset_ax = near_pos[axis_id][:, :, None] - far_pos[axis_id][:, None, :]]
    ppermute x24, waiting for transfers between devices: 37.7 us -> 34.3 us  [xor_swap(): return lax.ppermute(block, 'box', [(i, i ^ 1 << bit) for i in range(count)])]
    dot_general x3, matrix products: 20.2 us -> 23.3 us  [near_field(): jnp.einsum('pij,pjc->pic', kernel, source_feat, preferred_element_type=jn...]
    ppermute x24, starting transfers between devices: 111 us -> 108 us  [xor_swap(): return lax.ppermute(block, 'box', [(i, i ^ 1 << bit) for i in range(count)])]
where the time goes in v8:
time: 238 us; the launch traced here: 234 us
  starting transfers between devices  125 us (53%)
  matrix products  42.8 us (18%)
  waiting for transfers between devices  34.3 us (14%)
  local copies, waits for them, and re-layouts  22.1 us (9%)
  other arithmetic  8.4 us (4%)
    ppermute x24, starting transfers between devices, xor_swap(): return lax.ppermute(block, 'box', [(i, i ^ 1 << bit) for i in range(count)])  108 us
    ppermute x24, waiting for transfers between devices, xor_swap(): return lax.ppermute(block, 'box', [(i, i ^ 1 << bit) for i in range(count)])  34.3 us
    dot_general x3, matrix products, near_field(): jnp.einsum('pij,pjc->pic', kernel, source_feat, preferred_element_type=jn...  23.3 us
    ppermute x2, starting transfers between devices, passed_along(): return lax.ppermute(block, axis, route)  7.8 us
    sub x8, local copies, waits for them, and re-layouts, near_field(): offset_ax = near_pos[axis_id][:, :, None] - far_pos[axis_id][:, None, :]  5.99 us
    dot_general x2, matrix products, near_field(): jnp.einsum('pt,pic->tic', tgt_hot, contrib, precision=lax.Precision.HIGH)  5.65 us
    ppermute x1, starting transfers between devices, extended(): lax.ppermute(lax.slice_in_dim(block, 0, width, axis=dim), axis, backward)  5.44 us
  transfers between devices with their start and end apart: 28, of which 16 were waited for; matrix products, arithmetic and copies ran while one was open for 18% of the time, Pallas kernels for 0%

profile of v8, /device:TPU:1, one launch (start us, length us, event | category | flops | bytes accessed | tf_op | source)
XLA Modules:
  0.0 234.2 jit_solution(4463795545278051228)
XLA Ops:
  0.7 0.8 broadcast_in_dim.8
  3.1 0.9 copy.213
  4.1 1.0 convert_convert_fusion
  6.0 6.6 %collective-permute-start.2 = (f32[4480]{0:T(1024)S(1)}, f32[4480]{0:T(1024)S(1)}, u32[]{:S(2)}, u32[]{:S(2)}) collective-permute-start(f32[4480]{0:T(1024)S(1)} %select_n.283), channel_id=1, source_target_pairs={{0,4},{1,5},{2,6},{3,7},{4,0},{5,1},{6,2},{7,3},{8,12},{9,13},{10,... | collective-permute-start | bytes 53768 | tf_op jit(solution)/shard_map/ppermute | solution.py:85
  13.0 0.9 collective-permute-done.2
  13.9 4.0 %collective-permute-start.3 = (f32[2240]{0:T(1024)S(1)}, f32[2240]{0:T(1024)S(1)}, u32[]{:S(2)}, u32[]{:S(2)}) collective-permute-start(f32[2240]{0:T(1024)S(1)} %slice_select_fusion.4), channel_id=1, source_target_pairs={{0,2},{1,3},{2,0},{3,1},{4,6},{5,7},{6,4},{7,5},{8,10},{9,11},{10,... | collective-permute-start | bytes 26888 | tf_op jit(solution)/shard_map/ppermute | solution.py:85
  18.6 5.4 %collective-permute-start.1 = (f32[259,256]{1,0:T(8,128)S(1)}, f32[259,256]{1,0:T(8,128)S(1)}, u32[]{:S(2)}, u32[]{:S(2)}) collective-permute-start(f32[259,256]{1,0:T(8,128)S(1)} %pad_maximum_fusion.9), channel_id=1, source_target_pairs={{1,0},{2,1},{3,2},{4,3},{5,4},{6,5},{7,6},{8,7},{9,8},{10,9},{11,1... | collective-permute-start | bytes 795656 | tf_op jit(solution)/shard_map/ppermute | solution.py:30
  24.1 3.5 %collective-permute-start = (f32[259,256]{1,0:T(8,128)S(1)}, f32[259,256]{1,0:T(8,128)S(1)}, u32[]{:S(2)}, u32[]{:S(2)}) collective-permute-start(f32[259,256]{1,0:T(8,128)S(1)} %pad_maximum_fusion.9), channel_id=1, source_target_pairs={{0,1},{1,2},{2,3},{3,4},{4,5},{5,6},{6,7},{7,8},{8,9},{9,10},{10,1... | collective-permute-start | bytes 795656 | tf_op jit(solution)/shard_map/ppermute | solution.py:27
  27.6 0.8 reshape.246
  28.6 1.9 collective-permute-start.4
  30.5 0.9 convolution_bitcast_fusion.1
  31.7 5.4 %collective-permute-start.5 = (f32[1120]{0:T(1024)S(1)}, f32[1120]{0:T(1024)S(1)}, u32[]{:S(2)}, u32[]{:S(2)}) collective-permute-start(f32[1120]{0:T(1024)S(1)} %select_add_fusion.2), channel_id=1, source_target_pairs={{0,8},{1,9},{2,10},{3,11},{4,12},{5,13},{6,14},{7,15},{8,0},{9,1},... | collective-permute-start | bytes 13448 | tf_op jit(solution)/shard_map/ppermute | solution.py:85
  37.1 2.8 %collective-permute-done.5 = f32[1120]{0:T(1024)S(1)} collective-permute-done((f32[1120]{0:T(1024)S(1)}, f32[1120]{0:T(1024)S(1)}, u32[]{:S(2)}, u32[]{:S(2)}) %collective-permute-start.5) | collective-permute-done | bytes 4512 | tf_op jit(solution)/shard_map/ppermute | solution.py:85
  40.1 3.5 %collective-permute-start.6 = (f32[2240]{0:T(1024)S(1)}, f32[2240]{0:T(1024)S(1)}, u32[]{:S(2)}, u32[]{:S(2)}) collective-permute-start(f32[2240]{0:T(1024)S(1)} %maximum_select_fusion.22), channel_id=1, source_target_pairs={{0,16},{1,17},{2,18},{3,19},{4,20},{5,21},{6,22},{7,23},{8,24},{9,... | collective-permute-start | bytes 26888 | tf_op jit(solution)/shard_map/ppermute | solution.py:85
  43.7 0.9 collective-permute-done.6
  44.7 4.9 %collective-permute-start.7 = (f32[4480]{0:T(1024)S(1)}, f32[4480]{0:T(1024)S(1)}, u32[]{:S(2)}, u32[]{:S(2)}) collective-permute-start(f32[4480]{0:T(1024)S(1)} %maximum_select_fusion.18), channel_id=1, source_target_pairs={{0,32},{1,33},{2,34},{3,35},{4,36},{5,37},{6,38},{7,39},{8,40},{9,... | collective-permute-start | bytes 53768 | tf_op jit(solution)/shard_map/ppermute | solution.py:85
  53.4 0.8 dynamic-slice_reduce_fusion
  54.6 3.2 %collective-permute-start.8 = (f32[8960]{0:T(1024)S(1)}, f32[8960]{0:T(1024)S(1)}, u32[]{:S(2)}, u32[]{:S(2)}) collective-permute-start(f32[8960]{0:T(1024)S(1)} %maximum_select_fusion.14), channel_id=1, source_target_pairs={{0,64},{1,65},{2,66},{3,67},{4,68},{5,69},{6,70},{7,71},{8,72},{9,... | collective-permute-start | bytes 107528 | tf_op jit(solution)/shard_map/ppermute | solution.py:85
  57.9 1.5 collective-permute-done.8
  59.7 4.2 %collective-permute-start.9 = (f32[17920]{0:T(1024)S(1)}, f32[17920]{0:T(1024)S(1)}, u32[]{:S(2)}, u32[]{:S(2)}) collective-permute-start(f32[17920]{0:T(1024)S(1)} %maximum_select_fusion.9), channel_id=1, source_target_pairs={{0,128},{1,129},{2,130},{3,131},{4,132},{5,133},{6,134},{7,135},{8... | collective-permute-start | bytes 215048 | tf_op jit(solution)/shard_map/ppermute | solution.py:85
  63.9 1.7 collective-permute-done.9
  67.5 8.3 %collective-permute-start.10 = (f32[35840]{0:T(1024)}, f32[35840]{0:T(1024)}, u32[]{:S(2)}, u32[]{:S(2)}) collective-permute-start(f32[35840]{0:T(1024)} %maximum_select_fusion.5), channel_id=1, source_target_pairs={{0,256},{1,257},{2,258},{3,259},{4,260},{5,261},{6,262},{7,263},{8... | collective-permute-start | bytes 430088 | tf_op jit(solution)/shard_map/ppermute | solution.py:85
  75.8 0.8 copy.219
  76.7 1.6 convert_bitcast_fusion
  78.6 0.9 slice_bitcast_fusion.5
  79.5 1.5 copy.218
  82.4 7.9 %fusion.26 = f32[108,64,128]{2,1,0:T(8,128)} fusion(bf16[108,64,128]{2,0,1:T(8,128)(2,1)S(1)} %convert_bitcast_fusion, f32[108]{0:T(128)S(1)} %broadcast_multiply_fusion, f32[108,64]{1,0:T(8,128)} %copy.218, f32[108,64]{1,0:T(8,128)} %copy.217, f32[108,64]{1,0:T(8,128)} %copy.216, f32[108,64]{1,0:T(8,128)} %copy.215, f32[108,64]{1,0:T(8,128)} %copy.214, ...), kind=kOutput, calls=%fused_computation.32 | convolution fusion | flops 118112256 | bytes 5474736 | tf_op jit(solution)/shard_map/jvp(pij,pjc->pic)/dot_general | solution.py:78
  90.4 1.4 concatenate.262
  92.7 2.2 fusion.31
  95.3 7.3 %collective-permute-start.11 = (f32[1120]{0:T(1024)S(1)}, f32[1120]{0:T(1024)S(1)}, u32[]{:S(2)}, u32[]{:S(2)}) collective-permute-start(f32[1120]{0:T(1024)S(1)} %reshape.251), channel_id=1, source_target_pairs={{0,1},{1,0},{2,3},{3,2},{4,5},{5,4},{6,7},{7,6},{8,9},{9,8},{10,11... | collective-permute-start | bytes 13448 | tf_op jit(solution)/shard_map/ppermute | solution.py:85
  102.6 4.4 %fusion = f32[4,64,128]{2,0,1:T(4,128)S(1)} fusion(f32[108,64,128]{2,1,0:T(8,128)} %fusion.26, s32[108]{0:T(128)S(1)} %copy-done.15), kind=kOutput, calls=%fused_computation.6 | convolution fusion | flops 21234096 | bytes 3670448 | tf_op jit(solution)/shard_map/jvp(pt,pic->tic)/dot_general | solution.py:79
  107.5 1.9 collective-permute-start.12
  109.4 2.5 %collective-permute-done.12 = f32[2240]{0:T(1024)S(1)} collective-permute-done((f32[2240]{0:T(1024)S(1)}, f32[2240]{0:T(1024)S(1)}, u32[]{:S(2)}, u32[]{:S(2)}) %collective-permute-start.12) | collective-permute-done | bytes 8992 | tf_op jit(solution)/shard_map/ppermute | solution.py:85
  112.2 4.0 %collective-permute-start.13 = (f32[4480]{0:T(1024)S(1)}, f32[4480]{0:T(1024)S(1)}, u32[]{:S(2)}, u32[]{:S(2)}) collective-permute-start(f32[4480]{0:T(1024)S(1)} %maximum_select_fusion.19), channel_id=1, source_target_pairs={{0,4},{1,5},{2,6},{3,7},{4,0},{5,1},{6,2},{7,3},{8,12},{9,13},{10,... | collective-permute-start | bytes 53768 | tf_op jit(solution)/shard_map/ppermute | solution.py:85
  116.2 1.4 collective-permute-done.13
  117.9 0.9 add_multiply_fusion
  119.4 1.2 fusion.49
  120.8 7.0 %convert_bitcast_fusion.1 = bf16[128,64,108]{0,1,2:T(8,128)(2,1)S(1)} fusion(bf16[108,64,128]{2,0,1:T(8,128)(2,1)S(1)} %fusion.49, f32[108]{0:T(128)S(1)} %copy-done.27, f32[108,64]{1,0:T(8,128)S(1)} %copy-done.8, f32[108,64]{1,0:T(8,128)S(1)} %copy-done.5, f32[108,64]{1,0:T(8,128)S(1)} %copy-done.10, f32[108,64]{1,0:T(8,128)S(1)} %copy-done.6, ...), kind=kOutput, calls=%fused_computation.30 | convolution fusion | flops 118112256 | bytes 3705264 | tf_op jit(solution)/shard_map/transpose(jvp(pij,pjc->pic))/dot_general | solution.py:78
  127.8 8.4 %fusion.14 = (f32[108,64]{1,0:T(8,128)}, f32[108,64]{1,0:T(8,128)S(1)}, f32[108,64]{1,0:T(8,128)S(1)}, f32[108,64]{1,0:T(8,128)}, f32[108,64]{1,0:T(8,128)S(1)}, /*index=5*/f32[108,64]{1,0:T(8,128)}) fusion(f32[108,64]{1,0:T(8,128)S(1)} %copy-done.9, f32[108,64]{1,0:T(8,128)S(1)} %copy-done.5, f32[108,64]{1,0:T(8,128)S(1)} %copy-done.12, ...), kind=kOutput, calls=%fused_computation.22 | convolution fusion | flops 124706304 | bytes 3871152 | tf_op jit(solution)/shard_map/transpose(jvp(pij,pjc->pic))/dot_general | solution.py:78
  136.4 3.8 %collective-permute-start.16 = (f32[2240]{0:T(1024)S(1)}, f32[2240]{0:T(1024)S(1)}, u32[]{:S(2)}, u32[]{:S(2)}) collective-permute-start(f32[2240]{0:T(1024)S(1)} %select_n.320), channel_id=1, source_target_pairs={{0,4},{1,5},{2,6},{3,7},{4,0},{5,1},{6,2},{7,3},{8,12},{9,13},{10,... | collective-permute-start | bytes 26888 | tf_op jit(solution)/shard_map/ppermute | solution.py:85
  140.3 1.0 fusion.28
  141.5 0.8 fusion.34
  142.6 3.4 %collective-permute-start.17 = (f32[1120]{0:T(1024)S(1)}, f32[1120]{0:T(1024)S(1)}, u32[]{:S(2)}, u32[]{:S(2)}) collective-permute-start(f32[1120]{0:T(1024)S(1)} %slice_select_fusion.5), channel_id=1, source_target_pairs={{0,2},{1,3},{2,0},{3,1},{4,6},{5,7},{6,4},{7,5},{8,10},{9,11},{10,... | collective-permute-start | bytes 13448 | tf_op jit(solution)/shard_map/ppermute | solution.py:85
  145.9 1.1 fusion.88
  147.2 5.7 %collective-permute-start.18 = (f32[560]{0:T(1024)S(1)}, f32[560]{0:T(1024)S(1)}, u32[]{:S(2)}, u32[]{:S(2)}) collective-permute-start(f32[560]{0:T(1024)S(1)} %slice_select_fusion.7), channel_id=1, source_target_pairs={{0,1},{1,0},{2,3},{3,2},{4,5},{5,4},{6,7},{7,6},{8,9},{9,8},{10,11... | collective-permute-start | bytes 6728 | tf_op jit(solution)/shard_map/ppermute | solution.py:85
  152.9 1.1 convolution_bitcast_fusion.5
  155.3 6.5 %collective-permute-start.19 = (f32[18297]{0:T(1024)S(1)}, f32[18297]{0:T(1024)S(1)}, u32[]{:S(2)}, u32[]{:S(2)}) collective-permute-start(f32[18297]{0:T(1024)S(1)} %concatenate.289), channel_id=1, source_target_pairs={{0,8},{1,9},{2,10},{3,11},{4,12},{5,13},{6,14},{7,15},{8,0},{9,1},... | collective-permute-start | bytes 219572 | tf_op jit(solution)/shard_map/ppermute | solution.py:85
  161.9 3.1 %collective-permute-done.19 = f32[18297]{0:T(1024)S(1)} collective-permute-done((f32[18297]{0:T(1024)S(1)}, f32[18297]{0:T(1024)S(1)}, u32[]{:S(2)}, u32[]{:S(2)}) %collective-permute-start.19) | collective-permute-done | bytes 73220 | tf_op jit(solution)/shard_map/ppermute | solution.py:85
  165.2 2.5 %collective-permute-start.20 = (f32[18857]{0:T(1024)S(1)}, f32[18857]{0:T(1024)S(1)}, u32[]{:S(2)}, u32[]{:S(2)}) collective-permute-start(f32[18857]{0:T(1024)S(1)} %pad_maximum_fusion.15), channel_id=1, source_target_pairs={{0,16},{1,17},{2,18},{3,19},{4,20},{5,21},{6,22},{7,23},{8,24},{9,... | collective-permute-start | bytes 226292 | tf_op jit(solution)/shard_map/ppermute | solution.py:85
  168.0 2.3 collective-permute-done.20
  170.6 3.5 %collective-permute-start.21 = (f32[19977]{0:T(1024)S(1)}, f32[19977]{0:T(1024)S(1)}, u32[]{:S(2)}, u32[]{:S(2)}) collective-permute-start(f32[19977]{0:T(1024)S(1)} %pad_maximum_fusion.13), channel_id=1, source_target_pairs={{0,32},{1,33},{2,34},{3,35},{4,36},{5,37},{6,38},{7,39},{8,40},{9,... | collective-permute-start | bytes 239732 | tf_op jit(solution)/shard_map/ppermute | solution.py:85
  174.1 3.2 %collective-permute-done.21 = f32[19977]{0:T(1024)S(1)} collective-permute-done((f32[19977]{0:T(1024)S(1)}, f32[19977]{0:T(1024)S(1)}, u32[]{:S(2)}, u32[]{:S(2)}) %collective-permute-start.21) | collective-permute-done | bytes 79940 | tf_op jit(solution)/shard_map/ppermute | solution.py:85
  177.5 2.3 collective-permute-start.22
  180.4 5.9 %collective-permute-start.15 = (f32[3,256]{1,0:T(4,128)S(1)}, f32[3,256]{1,0:T(4,128)S(1)}, u32[]{:S(2)}, u32[]{:S(2)}) collective-permute-start(f32[3,256]{1,0:T(4,128)S(1)} %get-tuple-element.32), channel_id=1, source_target_pairs={{0,1},{1,2},{2,3},{3,4},{4,5},{5,6},{6,7},{7,8},{8,9},{9,10},{10,1... | collective-permute-start | bytes 9224 | tf_op jit(solution)/shard_map/ppermute | solution.py:38
  186.2 1.9 collective-permute-start.14
  188.7 2.5 %collective-permute-start.23 = (f32[26697]{0:T(1024)S(1)}, f32[26697]{0:T(1024)S(1)}, u32[]{:S(2)}, u32[]{:S(2)}) collective-permute-start(f32[26697]{0:T(1024)S(1)} %pad_maximum_fusion.11), channel_id=1, source_target_pairs={{0,128},{1,129},{2,130},{3,131},{4,132},{5,133},{6,134},{7,135},{8... | collective-permute-start | bytes 320372 | tf_op jit(solution)/shard_map/ppermute | solution.py:85
  191.4 3.8 %collective-permute-done.23 = f32[26697]{0:T(1024)S(1)} collective-permute-done((f32[26697]{0:T(1024)S(1)}, f32[26697]{0:T(1024)S(1)}, u32[]{:S(2)}, u32[]{:S(2)}) %collective-permute-start.23) | collective-permute-done | bytes 106820 | tf_op jit(solution)/shard_map/ppermute | solution.py:85
  195.2 4.3 %collective-permute-start.24 = (f32[35657]{0:T(1024)S(1)}, f32[35657]{0:T(1024)S(1)}, u32[]{:S(2)}, u32[]{:S(2)}) collective-permute-start(f32[35657]{0:T(1024)S(1)} %pad_maximum_fusion.10), channel_id=1, source_target_pairs={{0,256},{1,257},{2,258},{3,259},{4,260},{5,261},{6,262},{7,263},{8... | collective-permute-start | bytes 427892 | tf_op jit(solution)/shard_map/ppermute | solution.py:85
  200.1 4.9 %collective-permute-done.24 = f32[35657]{0:T(1024)S(1)} collective-permute-done((f32[35657]{0:T(1024)S(1)}, f32[35657]{0:T(1024)S(1)}, u32[]{:S(2)}, u32[]{:S(2)}) %collective-permute-start.24) | collective-permute-done | bytes 142660 | tf_op jit(solution)/shard_map/ppermute | solution.py:85
  206.2 7.6 %collective-permute-start.25 = (f32[18297]{0:T(1024)S(1)}, f32[18297]{0:T(1024)S(1)}, u32[]{:S(2)}, u32[]{:S(2)}) collective-permute-start(f32[18297]{0:T(1024)S(1)} %pad_maximum_fusion.17), channel_id=1, source_target_pairs={{0,1},{1,0},{2,3},{3,2},{4,5},{5,4},{6,7},{7,6},{8,9},{9,8},{10,11... | collective-permute-start | bytes 219572 | tf_op jit(solution)/shard_map/ppermute | solution.py:85
  215.1 6.9 %collective-permute-start.26 = (f32[18857]{0:T(1024)S(1)}, f32[18857]{0:T(1024)S(1)}, u32[]{:S(2)}, u32[]{:S(2)}) collective-permute-start(f32[18857]{0:T(1024)S(1)} %pad_maximum_fusion.16), channel_id=1, source_target_pairs={{0,2},{1,3},{2,0},{3,1},{4,6},{5,7},{6,4},{7,5},{8,10},{9,11},{10,... | collective-permute-start | bytes 226292 | tf_op jit(solution)/shard_map/ppermute | solution.py:85
  222.1 2.3 %collective-permute-done.26 = f32[18857]{0:T(1024)S(1)} collective-permute-done((f32[18857]{0:T(1024)S(1)}, f32[18857]{0:T(1024)S(1)}, u32[]{:S(2)}, u32[]{:S(2)}) %collective-permute-start.26) | collective-permute-done | bytes 75460 | tf_op jit(solution)/shard_map/ppermute | solution.py:85
  224.9 3.7 %collective-permute-start.27 = (f32[19977]{0:T(1024)S(1)}, f32[19977]{0:T(1024)S(1)}, u32[]{:S(2)}, u32[]{:S(2)}) collective-permute-start(f32[19977]{0:T(1024)S(1)} %pad_maximum_fusion.14), channel_id=1, source_target_pairs={{0,4},{1,5},{2,6},{3,7},{4,0},{5,1},{6,2},{7,3},{8,12},{9,13},{10,... | collective-permute-start | bytes 239732 | tf_op jit(solution)/shard_map/ppermute | solution.py:85
  228.6 2.3 collective-permute-done.27
  (251 shorter events, 26.3 us)
Async XLA Ops:
  0.6 3.4 %copy-start = (bf16[128,128]{1,0:T(8,128)(2,1)S(1)}, bf16[128,128]{1,0:T(8,128)(2,1)}, u32[]{:S(2)}) copy-start(bf16[128,128]{1,0:T(8,128)(2,1)} %param.15) | copy-start | bytes 98308
  0.6 42.9 %copy-start.19 = (s32[108]{0:T(128)S(1)}, s32[108]{0:T(128)}, u32[]{:S(2)}) copy-start(s32[108]{0:T(128)} %param.20) | copy-start | bytes 1300
  0.7 43.0 %copy-start.13 = (s32[64,32]{0,1:T(8,128)S(1)}, s32[64,32]{0,1:T(8,128)}, u32[]{:S(2)}) copy-start(s32[64,32]{0,1:T(8,128)} %param.21) | copy-start | bytes 24580
  3.1 1.0 copy-start.17
  6.0 7.8 %collective-permute-start.2 = (f32[4480]{0:T(1024)S(1)}, f32[4480]{0:T(1024)S(1)}, u32[]{:S(2)}, u32[]{:S(2)}) collective-permute-start(f32[4480]{0:T(1024)S(1)} %select_n.283), channel_id=1, source_target_pairs={{0,4},{1,5},{2,6},{3,7},{4,0},{5,1},{6,2},{7,3},{8,12},{9,13},{10,... | collective-permute-start | bytes 53768 | tf_op jit(solution)/shard_map/ppermute | solution.py:85
  13.9 14.5 %collective-permute-start.3 = (f32[2240]{0:T(1024)S(1)}, f32[2240]{0:T(1024)S(1)}, u32[]{:S(2)}, u32[]{:S(2)}) collective-permute-start(f32[2240]{0:T(1024)S(1)} %slice_select_fusion.4), channel_id=1, source_target_pairs={{0,2},{1,3},{2,0},{3,1},{4,6},{5,7},{6,4},{7,5},{8,10},{9,11},{10,... | collective-permute-start | bytes 26888 | tf_op jit(solution)/shard_map/ppermute | solution.py:85
  18.6 57.1 %collective-permute-start.1 = (f32[259,256]{1,0:T(8,128)S(1)}, f32[259,256]{1,0:T(8,128)S(1)}, u32[]{:S(2)}, u32[]{:S(2)}) collective-permute-start(f32[259,256]{1,0:T(8,128)S(1)} %pad_maximum_fusion.9), channel_id=1, source_target_pairs={{1,0},{2,1},{3,2},{4,3},{5,4},{6,5},{7,6},{8,7},{9,8},{10,9},{11,1... | collective-permute-start | bytes 795656 | tf_op jit(solution)/shard_map/ppermute | solution.py:30
  24.1 51.7 %collective-permute-start = (f32[259,256]{1,0:T(8,128)S(1)}, f32[259,256]{1,0:T(8,128)S(1)}, u32[]{:S(2)}, u32[]{:S(2)}) collective-permute-start(f32[259,256]{1,0:T(8,128)S(1)} %pad_maximum_fusion.9), channel_id=1, source_target_pairs={{0,1},{1,2},{2,3},{3,4},{4,5},{5,6},{6,7},{7,8},{8,9},{9,10},{10,1... | collective-permute-start | bytes 795656 | tf_op jit(solution)/shard_map/ppermute | solution.py:27
  28.6 3.1 %collective-permute-start.4 = (f32[1120]{0:T(1024)S(1)}, f32[1120]{0:T(1024)S(1)}, u32[]{:S(2)}, u32[]{:S(2)}) collective-permute-start(f32[1120]{0:T(1024)S(1)} %slice_select_fusion.6), channel_id=1, source_target_pairs={{0,1},{1,0},{2,3},{3,2},{4,5},{5,4},{6,7},{7,6},{8,9},{9,8},{10,11... | collective-permute-start | bytes 13448 | tf_op jit(solution)/shard_map/ppermute | solution.py:85
  31.7 8.3 %collective-permute-start.5 = (f32[1120]{0:T(1024)S(1)}, f32[1120]{0:T(1024)S(1)}, u32[]{:S(2)}, u32[]{:S(2)}) collective-permute-start(f32[1120]{0:T(1024)S(1)} %select_add_fusion.2), channel_id=1, source_target_pairs={{0,8},{1,9},{2,10},{3,11},{4,12},{5,13},{6,14},{7,15},{8,0},{9,1},... | collective-permute-start | bytes 13448 | tf_op jit(solution)/shard_map/ppermute | solution.py:85
  40.1 4.6 %collective-permute-start.6 = (f32[2240]{0:T(1024)S(1)}, f32[2240]{0:T(1024)S(1)}, u32[]{:S(2)}, u32[]{:S(2)}) collective-permute-start(f32[2240]{0:T(1024)S(1)} %maximum_select_fusion.22), channel_id=1, source_target_pairs={{0,16},{1,17},{2,18},{3,19},{4,20},{5,21},{6,22},{7,23},{8,24},{9,... | collective-permute-start | bytes 26888 | tf_op jit(solution)/shard_map/ppermute | solution.py:85
  43.6 38.8 %copy-start.26 = (f32[108]{0:T(128)}, f32[108]{0:T(128)S(1)}, u32[]{:S(2)}) copy-start(f32[108]{0:T(128)S(1)} %broadcast_multiply_fusion) | copy-start | bytes 1300
  44.7 9.6 %collective-permute-start.7 = (f32[4480]{0:T(1024)S(1)}, f32[4480]{0:T(1024)S(1)}, u32[]{:S(2)}, u32[]{:S(2)}) collective-permute-start(f32[4480]{0:T(1024)S(1)} %maximum_select_fusion.18), channel_id=1, source_target_pairs={{0,32},{1,33},{2,34},{3,35},{4,36},{5,37},{6,38},{7,39},{8,40},{9,... | collective-permute-start | bytes 53768 | tf_op jit(solution)/shard_map/ppermute | solution.py:85
  51.2 24.6 %copy-start.3 = (f32[3,256]{1,0:T(4,128)S(1)}, f32[3,256]{1,0:T(4,128)}, u32[]{:S(2)}) copy-start(f32[3,256]{1,0:T(4,128)} %param.11) | copy-start | bytes 9220
  54.6 4.7 %collective-permute-start.8 = (f32[8960]{0:T(1024)S(1)}, f32[8960]{0:T(1024)S(1)}, u32[]{:S(2)}, u32[]{:S(2)}) collective-permute-start(f32[8960]{0:T(1024)S(1)} %maximum_select_fusion.14), channel_id=1, source_target_pairs={{0,64},{1,65},{2,66},{3,67},{4,68},{5,69},{6,70},{7,71},{8,72},{9,... | collective-permute-start | bytes 107528 | tf_op jit(solution)/shard_map/ppermute | solution.py:85
  59.6 17.1 %copy-start.14 = (s32[108]{0:T(128)S(1)}, s32[108]{0:T(128)}, u32[]{:S(2)}) copy-start(s32[108]{0:T(128)} %param.19) | copy-start | bytes 1300
  59.7 6.0 %collective-permute-start.9 = (f32[17920]{0:T(1024)S(1)}, f32[17920]{0:T(1024)S(1)}, u32[]{:S(2)}, u32[]{:S(2)}) collective-permute-start(f32[17920]{0:T(1024)S(1)} %maximum_select_fusion.9), channel_id=1, source_target_pairs={{0,128},{1,129},{2,130},{3,131},{4,132},{5,133},{6,134},{7,135},{8... | collective-permute-start | bytes 215048 | tf_op jit(solution)/shard_map/ppermute | solution.py:85
  67.5 22.9 %collective-permute-start.10 = (f32[35840]{0:T(1024)}, f32[35840]{0:T(1024)}, u32[]{:S(2)}, u32[]{:S(2)}) collective-permute-start(f32[35840]{0:T(1024)} %maximum_select_fusion.5), channel_id=1, source_target_pairs={{0,256},{1,257},{2,258},{3,259},{4,260},{5,261},{6,262},{7,263},{8... | collective-permute-start | bytes 430088 | tf_op jit(solution)/shard_map/ppermute | solution.py:85
  78.4 12.0 %copy-start.1 = (bf16[108,64,128]{2,0,1:T(8,128)(2,1)}, bf16[108,64,128]{2,0,1:T(8,128)(2,1)S(1)}, u32[]{:S(2)}) copy-start(bf16[108,64,128]{2,0,1:T(8,128)(2,1)S(1)} %convert_bitcast_fusion) | copy-start | bytes 5308420
  90.4 4.6 %copy-start.4 = (f32[35,35]{1,0:T(8,128)S(1)}, f32[35,35]{1,0:T(8,128)}, u32[]{:S(2)}) copy-start(f32[35,35]{1,0:T(8,128)} %param.16) | copy-start | bytes 14704
  90.4 12.2 %copy-start.15 = (s32[108]{0:T(128)S(1)}, s32[108]{0:T(128)}, u32[]{:S(2)}) copy-start(s32[108]{0:T(128)} %param.18) | copy-start | bytes 1300
  92.7 25.2 %copy-start.20 = (f32[128]{0:T(128)S(1)}, f32[128]{0:T(128)}, u32[]{:S(2)}) copy-start(f32[128]{0:T(128)} %param.17) | copy-start | bytes 1540
  95.3 11.9 %collective-permute-start.11 = (f32[1120]{0:T(1024)S(1)}, f32[1120]{0:T(1024)S(1)}, u32[]{:S(2)}, u32[]{:S(2)}) collective-permute-start(f32[1120]{0:T(1024)S(1)} %reshape.251), channel_id=1, source_target_pairs={{0,1},{1,0},{2,3},{3,2},{4,5},{5,4},{6,7},{7,6},{8,9},{9,8},{10,11... | collective-permute-start | bytes 13448 | tf_op jit(solution)/shard_map/ppermute | solution.py:85
  107.1 13.6 %copy-start.5 = (f32[108,64]{1,0:T(8,128)S(1)}, f32[108,64]{1,0:T(8,128)}, u32[]{:S(2)}) copy-start(f32[108,64]{1,0:T(8,128)} %copy.217) | copy-start | bytes 82948
  107.1 13.6 %copy-start.6 = (f32[108,64]{1,0:T(8,128)S(1)}, f32[108,64]{1,0:T(8,128)}, u32[]{:S(2)}) copy-start(f32[108,64]{1,0:T(8,128)} %copy.215) | copy-start | bytes 82948
  107.1 13.6 %copy-start.7 = (f32[108,64]{1,0:T(8,128)S(1)}, f32[108,64]{1,0:T(8,128)}, u32[]{:S(2)}) copy-start(f32[108,64]{1,0:T(8,128)} %copy.212) | copy-start | bytes 82948
  107.1 13.6 %copy-start.8 = (f32[108,64]{1,0:T(8,128)S(1)}, f32[108,64]{1,0:T(8,128)}, u32[]{:S(2)}) copy-start(f32[108,64]{1,0:T(8,128)} %copy.218) | copy-start | bytes 82948
  107.1 13.6 %copy-start.10 = (f32[108,64]{1,0:T(8,128)S(1)}, f32[108,64]{1,0:T(8,128)}, u32[]{:S(2)}) copy-start(f32[108,64]{1,0:T(8,128)} %copy.216) | copy-start | bytes 82948
  107.1 13.6 %copy-start.27 = (f32[108]{0:T(128)S(1)}, f32[108]{0:T(128)}, u32[]{:S(2)}) copy-start(f32[108]{0:T(128)} %copy-done.26) | copy-start | bytes 1300
  107.5 4.4 %collective-permute-start.12 = (f32[2240]{0:T(1024)S(1)}, f32[2240]{0:T(1024)S(1)}, u32[]{:S(2)}, u32[]{:S(2)}) collective-permute-start(f32[2240]{0:T(1024)S(1)} %maximum_select_fusion.23), channel_id=1, source_target_pairs={{0,2},{1,3},{2,0},{3,1},{4,6},{5,7},{6,4},{7,5},{8,10},{9,11},{10,... | collective-permute-start | bytes 26888 | tf_op jit(solution)/shard_map/ppermute | solution.py:85
  112.2 5.4 %collective-permute-start.13 = (f32[4480]{0:T(1024)S(1)}, f32[4480]{0:T(1024)S(1)}, u32[]{:S(2)}, u32[]{:S(2)}) collective-permute-start(f32[4480]{0:T(1024)S(1)} %maximum_select_fusion.19), channel_id=1, source_target_pairs={{0,4},{1,5},{2,6},{3,7},{4,0},{5,1},{6,2},{7,3},{8,12},{9,13},{10,... | collective-permute-start | bytes 53768 | tf_op jit(solution)/shard_map/ppermute | solution.py:85
  120.7 7.1 %copy-start.2 = (bf16[108,64,128]{2,0,1:T(8,128)(2,1)S(1)}, bf16[108,64,128]{2,0,1:T(8,128)(2,1)}, u32[]{:S(2)}) copy-start(bf16[108,64,128]{2,0,1:T(8,128)(2,1)} %copy-done.1) | copy-start | bytes 5308420
  120.7 7.1 %copy-start.9 = (f32[108,64]{1,0:T(8,128)S(1)}, f32[108,64]{1,0:T(8,128)}, u32[]{:S(2)}) copy-start(f32[108,64]{1,0:T(8,128)} %copy.218) | copy-start | bytes 82948
  120.7 7.1 %copy-start.11 = (f32[108,64]{1,0:T(8,128)S(1)}, f32[108,64]{1,0:T(8,128)}, u32[]{:S(2)}) copy-start(f32[108,64]{1,0:T(8,128)} %copy.216) | copy-start | bytes 82948
  120.7 7.1 %copy-start.12 = (f32[108,64]{1,0:T(8,128)S(1)}, f32[108,64]{1,0:T(8,128)}, u32[]{:S(2)}) copy-start(f32[108,64]{1,0:T(8,128)} %copy.214) | copy-start | bytes 82948
  120.8 7.1 %copy-start.28 = (f32[108]{0:T(128)S(1)}, f32[108]{0:T(128)}, u32[]{:S(2)}) copy-start(f32[108]{0:T(128)} %convert_element_type.56) | copy-start | bytes 1300
  136.2 9.7 %copy-start.21 = (f32[128]{0:T(128)S(1)}, f32[128]{0:T(128)}, u32[]{:S(2)}) copy-start(f32[128]{0:T(128)} %param.17) | copy-start | bytes 1540
  136.2 16.7 %copy-start.25 = (pred[256,1]{0,1:T(4,128)(4,1)S(1)}, pred[256,1]{0,1:T(4,128)(4,1)}, u32[]{:S(2)}) copy-start(pred[256,1]{0,1:T(4,128)(4,1)} %reshape.270) | copy-start | bytes 772
  136.4 6.0 %collective-permute-start.16 = (f32[2240]{0:T(1024)S(1)}, f32[2240]{0:T(1024)S(1)}, u32[]{:S(2)}, u32[]{:S(2)}) collective-permute-start(f32[2240]{0:T(1024)S(1)} %select_n.320), channel_id=1, source_target_pairs={{0,4},{1,5},{2,6},{3,7},{4,0},{5,1},{6,2},{7,3},{8,12},{9,13},{10,... | collective-permute-start | bytes 26888 | tf_op jit(solution)/shard_map/ppermute | solution.py:85
  141.3 38.5 %copy-start.18 = (pred[256]{0:T(512)(128)(4,1)S(1)}, pred[256]{0:T(512)(128)(4,1)}, u32[]{:S(2)}) copy-start(pred[256]{0:T(512)(128)(4,1)} %copy-done.17) | copy-start | bytes 772
  142.6 4.5 %collective-permute-start.17 = (f32[1120]{0:T(1024)S(1)}, f32[1120]{0:T(1024)S(1)}, u32[]{:S(2)}, u32[]{:S(2)}) collective-permute-start(f32[1120]{0:T(1024)S(1)} %slice_select_fusion.5), channel_id=1, source_target_pairs={{0,2},{1,3},{2,0},{3,1},{4,6},{5,7},{6,4},{7,5},{8,10},{9,11},{10,... | collective-permute-start | bytes 13448 | tf_op jit(solution)/shard_map/ppermute | solution.py:85
  147.2 6.8 %collective-permute-start.18 = (f32[560]{0:T(1024)S(1)}, f32[560]{0:T(1024)S(1)}, u32[]{:S(2)}, u32[]{:S(2)}) collective-permute-start(f32[560]{0:T(1024)S(1)} %slice_select_fusion.7), channel_id=1, source_target_pairs={{0,1},{1,0},{2,3},{3,2},{4,5},{5,4},{6,7},{7,6},{8,9},{9,8},{10,11... | collective-permute-start | bytes 6728 | tf_op jit(solution)/shard_map/ppermute | solution.py:85
  155.3 9.6 %collective-permute-start.19 = (f32[18297]{0:T(1024)S(1)}, f32[18297]{0:T(1024)S(1)}, u32[]{:S(2)}, u32[]{:S(2)}) collective-permute-start(f32[18297]{0:T(1024)S(1)} %concatenate.289), channel_id=1, source_target_pairs={{0,8},{1,9},{2,10},{3,11},{4,12},{5,13},{6,14},{7,15},{8,0},{9,1},... | collective-permute-start | bytes 219572 | tf_op jit(solution)/shard_map/ppermute | solution.py:85
  165.2 5.1 %collective-permute-start.20 = (f32[18857]{0:T(1024)S(1)}, f32[18857]{0:T(1024)S(1)}, u32[]{:S(2)}, u32[]{:S(2)}) collective-permute-start(f32[18857]{0:T(1024)S(1)} %pad_maximum_fusion.15), channel_id=1, source_target_pairs={{0,16},{1,17},{2,18},{3,19},{4,20},{5,21},{6,22},{7,23},{8,24},{9,... | collective-permute-start | bytes 226292 | tf_op jit(solution)/shard_map/ppermute | solution.py:85
  170.6 6.7 %collective-permute-start.21 = (f32[19977]{0:T(1024)S(1)}, f32[19977]{0:T(1024)S(1)}, u32[]{:S(2)}, u32[]{:S(2)}) collective-permute-start(f32[19977]{0:T(1024)S(1)} %pad_maximum_fusion.13), channel_id=1, source_target_pairs={{0,32},{1,33},{2,34},{3,35},{4,36},{5,37},{6,38},{7,39},{8,40},{9,... | collective-permute-start | bytes 239732 | tf_op jit(solution)/shard_map/ppermute | solution.py:85
  177.5 11.1 %collective-permute-start.22 = (f32[22217]{0:T(1024)S(1)}, f32[22217]{0:T(1024)S(1)}, u32[]{:S(2)}, u32[]{:S(2)}) collective-permute-start(f32[22217]{0:T(1024)S(1)} %pad_maximum_fusion.12), channel_id=1, source_target_pairs={{0,64},{1,65},{2,66},{3,67},{4,68},{5,69},{6,70},{7,71},{8,72},{9,... | collective-permute-start | bytes 266612 | tf_op jit(solution)/shard_map/ppermute | solution.py:85
  180.4 53.3 %collective-permute-start.15 = (f32[3,256]{1,0:T(4,128)S(1)}, f32[3,256]{1,0:T(4,128)S(1)}, u32[]{:S(2)}, u32[]{:S(2)}) collective-permute-start(f32[3,256]{1,0:T(4,128)S(1)} %get-tuple-element.32), channel_id=1, source_target_pairs={{0,1},{1,2},{2,3},{3,4},{4,5},{5,6},{6,7},{7,8},{8,9},{9,10},{10,1... | collective-permute-start | bytes 9224 | tf_op jit(solution)/shard_map/ppermute | solution.py:38
  186.2 19.5 %copy-start.16 = (f32[64]{0:T(128)S(1)}, f32[64]{0:T(128)}, u32[]{:S(2)}) copy-start(f32[64]{0:T(128)} %dynamic-slice_reduce_fusion) | copy-start | bytes 772
  186.2 47.4 %collective-permute-start.14 = (f32[3,256]{1,0:T(4,128)S(1)}, f32[3,256]{1,0:T(4,128)S(1)}, u32[]{:S(2)}, u32[]{:S(2)}) collective-permute-start(f32[3,256]{1,0:T(4,128)S(1)} %get-tuple-element.31), channel_id=1, source_target_pairs={{1,0},{2,1},{3,2},{4,3},{5,4},{6,5},{7,6},{8,7},{9,8},{10,9},{11,1... | collective-permute-start | bytes 9224 | tf_op jit(solution)/shard_map/ppermute | solution.py:38
  188.6 25.2 %copy-start.22 = (f32[108,64]{1,0:T(8,128)S(1)}, f32[108,64]{1,0:T(8,128)}, u32[]{:S(2)}) copy-start(f32[108,64]{1,0:T(8,128)} %get-tuple-element.5) | copy-start | bytes 82948
  188.6 25.2 %copy-start.23 = (f32[108,64]{1,0:T(8,128)S(1)}, f32[108,64]{1,0:T(8,128)}, u32[]{:S(2)}) copy-start(f32[108,64]{1,0:T(8,128)} %get-tuple-element.12) | copy-start | bytes 82948
  188.6 25.2 %copy-start.24 = (f32[108,64]{1,0:T(8,128)S(1)}, f32[108,64]{1,0:T(8,128)}, u32[]{:S(2)}) copy-start(f32[108,64]{1,0:T(8,128)} %get-tuple-element.14) | copy-start | bytes 82948
  188.7 6.5 %collective-permute-start.23 = (f32[26697]{0:T(1024)S(1)}, f32[26697]{0:T(1024)S(1)}, u32[]{:S(2)}, u32[]{:S(2)}) collective-permute-start(f32[26697]{0:T(1024)S(1)} %pad_maximum_fusion.11), channel_id=1, source_target_pairs={{0,128},{1,129},{2,130},{3,131},{4,132},{5,133},{6,134},{7,135},{8... | collective-permute-start | bytes 320372 | tf_op jit(solution)/shard_map/ppermute | solution.py:85
  195.2 9.8 %collective-permute-start.24 = (f32[35657]{0:T(1024)S(1)}, f32[35657]{0:T(1024)S(1)}, u32[]{:S(2)}, u32[]{:S(2)}) collective-permute-start(f32[35657]{0:T(1024)S(1)} %pad_maximum_fusion.10), channel_id=1, source_target_pairs={{0,256},{1,257},{2,258},{3,259},{4,260},{5,261},{6,262},{7,263},{8... | collective-permute-start | bytes 427892 | tf_op jit(solution)/shard_map/ppermute | solution.py:85
  206.2 8.5 %collective-permute-start.25 = (f32[18297]{0:T(1024)S(1)}, f32[18297]{0:T(1024)S(1)}, u32[]{:S(2)}, u32[]{:S(2)}) collective-permute-start(f32[18297]{0:T(1024)S(1)} %pad_maximum_fusion.17), channel_id=1, source_target_pairs={{0,1},{1,0},{2,3},{3,2},{4,5},{5,4},{6,7},{7,6},{8,9},{9,8},{10,11... | collective-permute-start | bytes 219572 | tf_op jit(solution)/shard_map/ppermute | solution.py:85
  215.1 9.3 %collective-permute-start.26 = (f32[18857]{0:T(1024)S(1)}, f32[18857]{0:T(1024)S(1)}, u32[]{:S(2)}, u32[]{:S(2)}) collective-permute-start(f32[18857]{0:T(1024)S(1)} %pad_maximum_fusion.16), channel_id=1, source_target_pairs={{0,2},{1,3},{2,0},{3,1},{4,6},{5,7},{6,4},{7,5},{8,10},{9,11},{10,... | collective-permute-start | bytes 226292 | tf_op jit(solution)/shard_map/ppermute | solution.py:85
  224.9 6.1 %collective-permute-start.27 = (f32[19977]{0:T(1024)S(1)}, f32[19977]{0:T(1024)S(1)}, u32[]{:S(2)}, u32[]{:S(2)}) collective-permute-start(f32[19977]{0:T(1024)S(1)} %pad_maximum_fusion.14), channel_id=1, source_target_pairs={{0,4},{1,5},{2,6},{3,7},{4,0},{5,1},{6,2},{7,3},{8,12},{9,13},{10,... | collective-permute-start | bytes 239732 | tf_op jit(solution)/shard_map/ppermute | solution.py:85

commit v9 on v7

--- a/solution.py
+++ b/solution.py
@@ -207,7 +207,9 @@
     d_own, d_ext, d_feat_ext = near_back(d_pre)
     d_pack = jnp.concatenate([d_ext, d_feat_ext], axis=0)
     low_pack = passed_along(d_pack[:, :atom_num], "box", -1)
-    high_pack = passed_along(d_pack[:, 2 * atom_num :], "box", 1)
+    high_pack = passed_along(d_pack[:, 2 * atom_num :].astype(jnp.bfloat16), "box", 1).astype(
+        jnp.float32
+    )
     low_pos, low_feat = low_pack[:3], low_pack[3:]
     high_pos, high_feat = high_pack[:3], high_pack[3:]
     d_hidden_near = d_feat_ext[:, atom_num : 2 * atom_num] + low_feat + high_feat

time: 227 us -> 223 us (0.982)
  starting transfers between devices: 127 us -> 119 us
  waiting for transfers between devices: 37.8 us -> 41.2 us
    ppermute x24, starting transfers between devices: 111 us -> 104 us  [xor_swap(): return lax.ppermute(block, 'box', [(i, i ^ 1 << bit) for i in range(count)])]
    ppermute x24, waiting for transfers between devices: 37.7 us -> 40.8 us  [xor_swap(): return lax.ppermute(block, 'box', [(i, i ^ 1 << bit) for i in range(count)])]
  transfers between devices with their start and end apart: 28 -> 28, of which waited for: 16 -> 17; matrix products, arithmetic and copies ran while one was open for 18% -> 19% of each run, Pallas kernels for 0% -> 0%
where the time goes in v9:
time: 223 us; the launch traced here: 221 us
  starting transfers between devices  119 us (53%)
  waiting for transfers between devices  41.2 us (18%)
  matrix products  37.1 us (17%)
  local copies, waits for them, and re-layouts  13.7 us (6%)
  other arithmetic  8.51 us (4%)
    ppermute x24, starting transfers between devices, xor_swap(): return lax.ppermute(block, 'box', [(i, i ^ 1 << bit) for i in range(count)])  104 us
    ppermute x24, waiting for transfers between devices, xor_swap(): return lax.ppermute(block, 'box', [(i, i ^ 1 << bit) for i in range(count)])  40.8 us
    dot_general x3, matrix products, near_field(): jnp.einsum('pij,pjc->pic', kernel, source_feat, preferred_element_type=jn...  20.2 us
    ppermute x2, starting transfers between devices, passed_along(): return lax.ppermute(block, axis, route)  6.32 us
    dot_general x2, matrix products, near_field(): jnp.einsum('pt,pic->tic', tgt_hot, contrib, precision=lax.Precision.HIGH)  5.65 us
    ppermute x1, starting transfers between devices, extended(): lax.ppermute(lax.slice_in_dim(block, 0, width, axis=dim), axis, backward)  5.46 us
  transfers between devices with their start and end apart: 28, of which 17 were waited for; matrix products, arithmetic and copies ran while one was open for 19% of the time, Pallas kernels for 0%

profile of v9, /device:TPU:1, one launch (start us, length us, event | category | flops | bytes accessed | tf_op | source)
XLA Modules:
  0.0 221.3 jit_solution(13361709005956764137)
XLA Ops:
  0.7 0.8 broadcast_in_dim.8
  1.5 0.7 subtract_multiply_fusion.3
  2.2 0.7 iota_compare_fusion.3
  3.2 1.3 fusion.53
  4.5 1.0 convert_convert_fusion
  6.1 6.6 %collective-permute-start.2 = (f32[4480]{0:T(1024)S(1)}, f32[4480]{0:T(1024)S(1)}, u32[]{:S(2)}, u32[]{:S(2)}) collective-permute-start(f32[4480]{0:T(1024)S(1)} %select_n.283), channel_id=1, source_target_pairs={{0,4},{1,5},{2,6},{3,7},{4,0},{5,1},{6,2},{7,3},{8,12},{9,13},{10,... | collective-permute-start | bytes 53768 | tf_op jit(solution)/shard_map/ppermute | solution.py:85
  13.0 0.9 collective-permute-done.2
  14.0 4.0 %collective-permute-start.3 = (f32[2240]{0:T(1024)S(1)}, f32[2240]{0:T(1024)S(1)}, u32[]{:S(2)}, u32[]{:S(2)}) collective-permute-start(f32[2240]{0:T(1024)S(1)} %slice_select_fusion.4), channel_id=1, source_target_pairs={{0,2},{1,3},{2,0},{3,1},{4,6},{5,7},{6,4},{7,5},{8,10},{9,11},{10,... | collective-permute-start | bytes 26888 | tf_op jit(solution)/shard_map/ppermute | solution.py:85
  18.0 0.7 pad_maximum_fusion.5
  18.7 5.5 %collective-permute-start.1 = (f32[131,256]{1,0:T(8,128)S(1)}, f32[131,256]{1,0:T(8,128)S(1)}, u32[]{:S(2)}, u32[]{:S(2)}) collective-permute-start(f32[131,256]{1,0:T(8,128)S(1)} %pad_maximum_fusion.5), channel_id=1, source_target_pairs={{1,0},{2,1},{3,2},{4,3},{5,4},{6,5},{7,6},{8,7},{9,8},{10,9},{11,1... | collective-permute-start | bytes 402440 | tf_op jit(solution)/shard_map/ppermute | solution.py:30
  24.2 3.5 %collective-permute-start = (f32[131,256]{1,0:T(8,128)S(1)}, f32[131,256]{1,0:T(8,128)S(1)}, u32[]{:S(2)}, u32[]{:S(2)}) collective-permute-start(f32[131,256]{1,0:T(8,128)S(1)} %pad_maximum_fusion.5), channel_id=1, source_target_pairs={{0,1},{1,2},{2,3},{3,4},{4,5},{5,6},{6,7},{7,8},{8,9},{9,10},{10,1... | collective-permute-start | bytes 402440 | tf_op jit(solution)/shard_map/ppermute | solution.py:27
  27.7 0.8 reshape.246
  28.6 1.9 collective-permute-start.4
  30.5 0.9 convolution_bitcast_fusion.1
  31.8 5.4 %collective-permute-start.5 = (f32[1120]{0:T(1024)S(1)}, f32[1120]{0:T(1024)S(1)}, u32[]{:S(2)}, u32[]{:S(2)}) collective-permute-start(f32[1120]{0:T(1024)S(1)} %select_add_fusion.2), channel_id=1, source_target_pairs={{0,8},{1,9},{2,10},{3,11},{4,12},{5,13},{6,14},{7,15},{8,0},{9,1},... | collective-permute-start | bytes 13448 | tf_op jit(solution)/shard_map/ppermute | solution.py:85
  37.2 2.9 %collective-permute-done.5 = f32[1120]{0:T(1024)S(1)} collective-permute-done((f32[1120]{0:T(1024)S(1)}, f32[1120]{0:T(1024)S(1)}, u32[]{:S(2)}, u32[]{:S(2)}) %collective-permute-start.5) | collective-permute-done | bytes 4512 | tf_op jit(solution)/shard_map/ppermute | solution.py:85
  40.1 3.5 %collective-permute-start.6 = (f32[2240]{0:T(1024)S(1)}, f32[2240]{0:T(1024)S(1)}, u32[]{:S(2)}, u32[]{:S(2)}) collective-permute-start(f32[2240]{0:T(1024)S(1)} %maximum_select_fusion.22), channel_id=1, source_target_pairs={{0,16},{1,17},{2,18},{3,19},{4,20},{5,21},{6,22},{7,23},{8,24},{9,... | collective-permute-start | bytes 26888 | tf_op jit(solution)/shard_map/ppermute | solution.py:85
  43.7 0.7 broadcast_multiply_fusion
  44.3 0.8 copy.214
  45.2 4.6 %collective-permute-start.7 = (f32[4480]{0:T(1024)S(1)}, f32[4480]{0:T(1024)S(1)}, u32[]{:S(2)}, u32[]{:S(2)}) collective-permute-start(f32[4480]{0:T(1024)S(1)} %maximum_select_fusion.18), channel_id=1, source_target_pairs={{0,32},{1,33},{2,34},{3,35},{4,36},{5,37},{6,38},{7,39},{8,40},{9,... | collective-permute-start | bytes 53768 | tf_op jit(solution)/shard_map/ppermute | solution.py:85
  50.3 0.7 convert_element_type.59
  51.6 4.8 %collective-permute-start.8 = (f32[8960]{0:T(1024)S(1)}, f32[8960]{0:T(1024)S(1)}, u32[]{:S(2)}, u32[]{:S(2)}) collective-permute-start(f32[8960]{0:T(1024)S(1)} %maximum_select_fusion.14), channel_id=1, source_target_pairs={{0,64},{1,65},{2,66},{3,67},{4,68},{5,69},{6,70},{7,71},{8,72},{9,... | collective-permute-start | bytes 107528 | tf_op jit(solution)/shard_map/ppermute | solution.py:85
  56.7 1.1 collective-permute-done.8
  57.7 4.4 %collective-permute-start.9 = (f32[17920]{0:T(1024)S(1)}, f32[17920]{0:T(1024)S(1)}, u32[]{:S(2)}, u32[]{:S(2)}) collective-permute-start(f32[17920]{0:T(1024)S(1)} %maximum_select_fusion.9), channel_id=1, source_target_pairs={{0,128},{1,129},{2,130},{3,131},{4,132},{5,133},{6,134},{7,135},{8... | collective-permute-start | bytes 215048 | tf_op jit(solution)/shard_map/ppermute | solution.py:85
  63.1 0.7 convert_bitcast_fusion
  64.2 7.2 %collective-permute-start.10 = (f32[35840]{0:T(1024)S(1)}, f32[35840]{0:T(1024)S(1)}, u32[]{:S(2)}, u32[]{:S(2)}) collective-permute-start(f32[35840]{0:T(1024)S(1)} %maximum_select_fusion.5), channel_id=1, source_target_pairs={{0,256},{1,257},{2,258},{3,259},{4,260},{5,261},{6,262},{7,263},{8... | collective-permute-start | bytes 430088 | tf_op jit(solution)/shard_map/ppermute | solution.py:85
  71.4 6.5 %fusion.26 = f32[108,64,128]{2,1,0:T(8,128)} fusion(bf16[108,64,128]{2,0,1:T(8,128)(2,1)S(1)} %convert_bitcast_fusion, f32[108]{0:T(128)S(1)} %broadcast_multiply_fusion, f32[108,64]{1,0:T(8,128)S(1)} %copy.208, f32[108,64]{1,0:T(8,128)S(1)} %copy.207, f32[108,64]{1,0:T(8,128)S(1)} %copy.206, f32[108,64]{1,0:T(8,128)S(1)} %copy.205, ...), kind=kOutput, calls=%fused_computation.32 | convolution fusion | flops 118112256 | bytes 5474736 | tf_op jit(solution)/shard_map/jvp(pij,pjc->pic)/dot_general | solution.py:78
  80.4 2.2 %fusion.31 = f32[1,2,35,16]{2,0,3,1:T(1,128)S(1)} fusion(f32[64,2,35,16]{0,3,2,1:T(8,128)S(1)} %maximum_select_fusion, f32[64,64]{1,0:T(8,128)S(1)} %convert_reduce_fusion, s32[]{:T(128)S(6)} %select_n.270), kind=kOutput, calls=%fused_computation.47 | convolution fusion | flops 860160 | bytes 578436 | tf_op jit(solution)/shard_map/j,jnkc->nkc/dot_general | solution.py:180
  83.1 8.2 %collective-permute-start.11 = (f32[1120]{0:T(1024)S(1)}, f32[1120]{0:T(1024)S(1)}, u32[]{:S(2)}, u32[]{:S(2)}) collective-permute-start(f32[1120]{0:T(1024)S(1)} %reshape.251), channel_id=1, source_target_pairs={{0,1},{1,0},{2,3},{3,2},{4,5},{5,4},{6,7},{7,6},{8,9},{9,8},{10,11... | collective-permute-start | bytes 13448 | tf_op jit(solution)/shard_map/ppermute | solution.py:85
  91.3 4.4 %fusion = f32[4,64,128]{2,0,1:T(4,128)S(1)} fusion(f32[108,64,128]{2,1,0:T(8,128)} %fusion.26, s32[108]{0:T(128)S(1)} %copy-done.7), kind=kOutput, calls=%fused_computation.6 | convolution fusion | flops 21234096 | bytes 3670448 | tf_op jit(solution)/shard_map/jvp(pt,pic->tic)/dot_general | solution.py:79
  95.9 1.9 collective-permute-start.12
  98.0 2.3 %collective-permute-done.12 = f32[2240]{0:T(1024)S(1)} collective-permute-done((f32[2240]{0:T(1024)S(1)}, f32[2240]{0:T(1024)S(1)}, u32[]{:S(2)}, u32[]{:S(2)}) %collective-permute-start.12) | collective-permute-done | bytes 8992 | tf_op jit(solution)/shard_map/ppermute | solution.py:85
  100.4 2.6 %collective-permute-start.13 = (f32[4480]{0:T(1024)S(1)}, f32[4480]{0:T(1024)S(1)}, u32[]{:S(2)}, u32[]{:S(2)}) collective-permute-start(f32[4480]{0:T(1024)S(1)} %maximum_select_fusion.19), channel_id=1, source_target_pairs={{0,4},{1,5},{2,6},{3,7},{4,0},{5,1},{6,2},{7,3},{8,12},{9,13},{10,... | collective-permute-start | bytes 53768 | tf_op jit(solution)/shard_map/ppermute | solution.py:85
  103.2 2.6 %collective-permute-done.13 = f32[4480]{0:T(1024)S(1)} collective-permute-done((f32[4480]{0:T(1024)S(1)}, f32[4480]{0:T(1024)S(1)}, u32[]{:S(2)}, u32[]{:S(2)}) %collective-permute-start.13) | collective-permute-done | bytes 17952 | tf_op jit(solution)/shard_map/ppermute | solution.py:85
  107.1 2.4 %collective-permute-start.16 = (f32[2240]{0:T(1024)S(1)}, f32[2240]{0:T(1024)S(1)}, u32[]{:S(2)}, u32[]{:S(2)}) collective-permute-start(f32[2240]{0:T(1024)S(1)} %select_n.320), channel_id=1, source_target_pairs={{0,4},{1,5},{2,6},{3,7},{4,0},{5,1},{6,2},{7,3},{8,12},{9,13},{10,... | collective-permute-start | bytes 26888 | tf_op jit(solution)/shard_map/ppermute | solution.py:85
  109.5 1.2 fusion.51
  110.7 6.0 %convert_bitcast_fusion.1 = bf16[128,64,108]{0,1,2:T(8,128)(2,1)S(1)} fusion(bf16[108,64,128]{2,0,1:T(8,128)(2,1)S(1)} %fusion.51, f32[108]{0:T(128)S(1)} %broadcast_multiply_fusion, f32[108,64]{1,0:T(8,128)S(1)} %copy.208, f32[108,64]{1,0:T(8,128)S(1)} %copy.207, f32[108,64]{1,0:T(8,128)S(1)} %copy.206, f32[108,64]{1,0:T(8,128)S(1)} %copy.205, ...), kind=kOutput, calls=%fused_computation.30 | convolution fusion | flops 118112256 | bytes 3705264 | tf_op jit(solution)/shard_map/transpose(jvp(pij,pjc->pic))/dot_general | solution.py:78
  116.7 7.7 %fusion.14 = (f32[108,64]{1,0:T(8,128)S(1)}, f32[108,64]{1,0:T(8,128)S(1)}, f32[108,64]{1,0:T(8,128)S(1)}, f32[108,64]{1,0:T(8,128)S(1)}, f32[108,64]{1,0:T(8,128)S(1)}, /*index=5*/f32[108,64]{1,0:T(8,128)S(1)}) fusion(f32[108,64]{1,0:T(8,128)S(1)} %copy.208, f32[108,64]{1,0:T(8,128)S(1)} %copy.207, f32[108,64]{1,0:T(8,128)S(1)} %copy.204, ...), kind=kOutput, calls=%fused_computation.22 | convolution fusion | flops 124706304 | bytes 3871152 | tf_op jit(solution)/shard_map/transpose(jvp(pij,pjc->pic))/dot_general | solution.py:78
  124.5 1.0 fusion.28
  126.5 3.4 %collective-permute-start.17 = (f32[1120]{0:T(1024)S(1)}, f32[1120]{0:T(1024)S(1)}, u32[]{:S(2)}, u32[]{:S(2)}) collective-permute-start(f32[1120]{0:T(1024)S(1)} %slice_select_fusion.5), channel_id=1, source_target_pairs={{0,2},{1,3},{2,0},{3,1},{4,6},{5,7},{6,4},{7,5},{8,10},{9,11},{10,... | collective-permute-start | bytes 13448 | tf_op jit(solution)/shard_map/ppermute | solution.py:85
  129.9 4.4 %collective-permute-start.15 = (bf16[131,256]{1,0:T(8,128)(2,1)S(1)}, bf16[131,256]{1,0:T(8,128)(2,1)S(1)}, u32[]{:S(2)}, u32[]{:S(2)}) collective-permute-start(bf16[131,256]{1,0:T(8,128)(2,1)S(1)} %fusion.47), channel_id=1, source_target_pairs={{0,1},{1,2},{2,3},{3,4},{4,5},{5,6},{6,7},{7,8},{8,9},{9,10},{10,1... | collective-permute-start | bytes 201224 | tf_op jit(solution)/shard_map/ppermute | solution.py:38
  134.3 1.9 collective-permute-start.14
  136.4 1.9 collective-permute-start.18
  138.5 0.9 collective-permute-done.18
  141.4 9.0 %collective-permute-start.19 = (f32[18297]{0:T(1024)S(1)}, f32[18297]{0:T(1024)S(1)}, u32[]{:S(2)}, u32[]{:S(2)}) collective-permute-start(f32[18297]{0:T(1024)S(1)} %concatenate.293), channel_id=1, source_target_pairs={{0,8},{1,9},{2,10},{3,11},{4,12},{5,13},{6,14},{7,15},{8,0},{9,1},... | collective-permute-start | bytes 219572 | tf_op jit(solution)/shard_map/ppermute | solution.py:85
  150.7 2.0 collective-permute-done.19
  153.0 6.9 %collective-permute-start.20 = (f32[18857]{0:T(1024)S(1)}, f32[18857]{0:T(1024)S(1)}, u32[]{:S(2)}, u32[]{:S(2)}) collective-permute-start(f32[18857]{0:T(1024)S(1)} %pad_maximum_fusion.10), channel_id=1, source_target_pairs={{0,16},{1,17},{2,18},{3,19},{4,20},{5,21},{6,22},{7,23},{8,24},{9,... | collective-permute-start | bytes 226292 | tf_op jit(solution)/shard_map/ppermute | solution.py:85
  160.2 2.0 collective-permute-done.20
  162.4 4.2 %collective-permute-start.21 = (f32[19977]{0:T(1024)S(1)}, f32[19977]{0:T(1024)S(1)}, u32[]{:S(2)}, u32[]{:S(2)}) collective-permute-start(f32[19977]{0:T(1024)S(1)} %pad_maximum_fusion.8), channel_id=1, source_target_pairs={{0,32},{1,33},{2,34},{3,35},{4,36},{5,37},{6,38},{7,39},{8,40},{9,... | collective-permute-start | bytes 239732 | tf_op jit(solution)/shard_map/ppermute | solution.py:85
  166.9 2.2 %collective-permute-done.21 = f32[19977]{0:T(1024)S(1)} collective-permute-done((f32[19977]{0:T(1024)S(1)}, f32[19977]{0:T(1024)S(1)}, u32[]{:S(2)}, u32[]{:S(2)}) %collective-permute-start.21) | collective-permute-done | bytes 79940 | tf_op jit(solution)/shard_map/ppermute | solution.py:85
  169.3 1.9 collective-permute-start.22
  171.8 2.8 %collective-permute-done.22 = f32[22217]{0:T(1024)S(1)} collective-permute-done((f32[22217]{0:T(1024)S(1)}, f32[22217]{0:T(1024)S(1)}, u32[]{:S(2)}, u32[]{:S(2)}) %collective-permute-start.22) | collective-permute-done | bytes 88900 | tf_op jit(solution)/shard_map/ppermute | solution.py:85
  174.7 1.9 collective-permute-start.23
  176.8 5.1 %collective-permute-done.23 = f32[26697]{0:T(1024)S(1)} collective-permute-done((f32[26697]{0:T(1024)S(1)}, f32[26697]{0:T(1024)S(1)}, u32[]{:S(2)}, u32[]{:S(2)}) %collective-permute-start.23) | collective-permute-done | bytes 106820 | tf_op jit(solution)/shard_map/ppermute | solution.py:85
  182.0 4.5 %collective-permute-start.24 = (f32[35657]{0:T(1024)S(1)}, f32[35657]{0:T(1024)S(1)}, u32[]{:S(2)}, u32[]{:S(2)}) collective-permute-start(f32[35657]{0:T(1024)S(1)} %pad_maximum_fusion.3), channel_id=1, source_target_pairs={{0,256},{1,257},{2,258},{3,259},{4,260},{5,261},{6,262},{7,263},{8... | collective-permute-start | bytes 427892 | tf_op jit(solution)/shard_map/ppermute | solution.py:85
  187.1 6.0 %collective-permute-done.24 = f32[35657]{0:T(1024)S(1)} collective-permute-done((f32[35657]{0:T(1024)S(1)}, f32[35657]{0:T(1024)S(1)}, u32[]{:S(2)}, u32[]{:S(2)}) %collective-permute-start.24) | collective-permute-done | bytes 142660 | tf_op jit(solution)/shard_map/ppermute | solution.py:85
  194.3 8.1 %collective-permute-start.25 = (f32[18297]{0:T(1024)S(1)}, f32[18297]{0:T(1024)S(1)}, u32[]{:S(2)}, u32[]{:S(2)}) collective-permute-start(f32[18297]{0:T(1024)S(1)} %pad_maximum_fusion.12), channel_id=1, source_target_pairs={{0,1},{1,0},{2,3},{3,2},{4,5},{5,4},{6,7},{7,6},{8,9},{9,8},{10,11... | collective-permute-start | bytes 219572 | tf_op jit(solution)/shard_map/ppermute | solution.py:85
  203.7 1.9 collective-permute-start.26
  205.6 3.5 %collective-permute-done.26 = f32[18857]{0:T(1024)S(1)} collective-permute-done((f32[18857]{0:T(1024)S(1)}, f32[18857]{0:T(1024)S(1)}, u32[]{:S(2)}, u32[]{:S(2)}) %collective-permute-start.26) | collective-permute-done | bytes 75460 | tf_op jit(solution)/shard_map/ppermute | solution.py:85
  209.6 2.3 %collective-permute-start.27 = (f32[19977]{0:T(1024)S(1)}, f32[19977]{0:T(1024)S(1)}, u32[]{:S(2)}, u32[]{:S(2)}) collective-permute-start(f32[19977]{0:T(1024)S(1)} %pad_maximum_fusion.9), channel_id=1, source_target_pairs={{0,4},{1,5},{2,6},{3,7},{4,0},{5,1},{6,2},{7,3},{8,12},{9,13},{10,... | collective-permute-start | bytes 239732 | tf_op jit(solution)/shard_map/ppermute | solution.py:85
  211.9 6.1 %collective-permute-done.27 = f32[19977]{0:T(1024)S(1)} collective-permute-done((f32[19977]{0:T(1024)S(1)}, f32[19977]{0:T(1024)S(1)}, u32[]{:S(2)}, u32[]{:S(2)}) %collective-permute-start.27) | collective-permute-done | bytes 79940 | tf_op jit(solution)/shard_map/ppermute | solution.py:85
  218.7 0.6 slice_bitcast_fusion
  220.0 0.7 reshape.263
  220.7 0.6 fusion.64
  (210 shorter events, 19.2 us)
Async XLA Ops:
  0.6 3.9 %copy-start = (bf16[128,128]{1,0:T(8,128)(2,1)S(1)}, bf16[128,128]{1,0:T(8,128)(2,1)}, u32[]{:S(2)}) copy-start(bf16[128,128]{1,0:T(8,128)(2,1)} %param.15) | copy-start | bytes 98308
  0.6 61.9 %copy-start.4 = (f32[3,256]{1,0:T(4,128)S(1)}, f32[3,256]{1,0:T(4,128)}, u32[]{:S(2)}) copy-start(f32[3,256]{1,0:T(4,128)} %param.11) | copy-start | bytes 9220
  5.6 57.3 %copy-start.6 = (s32[108]{0:T(128)S(1)}, s32[108]{0:T(128)}, u32[]{:S(2)}) copy-start(s32[108]{0:T(128)} %param.19) | copy-start | bytes 1300
  6.1 7.8 %collective-permute-start.2 = (f32[4480]{0:T(1024)S(1)}, f32[4480]{0:T(1024)S(1)}, u32[]{:S(2)}, u32[]{:S(2)}) collective-permute-start(f32[4480]{0:T(1024)S(1)} %select_n.283), channel_id=1, source_target_pairs={{0,4},{1,5},{2,6},{3,7},{4,0},{5,1},{6,2},{7,3},{8,12},{9,13},{10,... | collective-permute-start | bytes 53768 | tf_op jit(solution)/shard_map/ppermute | solution.py:85
  14.0 14.5 %collective-permute-start.3 = (f32[2240]{0:T(1024)S(1)}, f32[2240]{0:T(1024)S(1)}, u32[]{:S(2)}, u32[]{:S(2)}) collective-permute-start(f32[2240]{0:T(1024)S(1)} %slice_select_fusion.4), channel_id=1, source_target_pairs={{0,2},{1,3},{2,0},{3,1},{4,6},{5,7},{6,4},{7,5},{8,10},{9,11},{10,... | collective-permute-start | bytes 26888 | tf_op jit(solution)/shard_map/ppermute | solution.py:85
  18.7 43.8 %collective-permute-start.1 = (f32[131,256]{1,0:T(8,128)S(1)}, f32[131,256]{1,0:T(8,128)S(1)}, u32[]{:S(2)}, u32[]{:S(2)}) collective-permute-start(f32[131,256]{1,0:T(8,128)S(1)} %pad_maximum_fusion.5), channel_id=1, source_target_pairs={{1,0},{2,1},{3,2},{4,3},{5,4},{6,5},{7,6},{8,7},{9,8},{10,9},{11,1... | collective-permute-start | bytes 402440 | tf_op jit(solution)/shard_map/ppermute | solution.py:30
  24.2 38.3 %collective-permute-start = (f32[131,256]{1,0:T(8,128)S(1)}, f32[131,256]{1,0:T(8,128)S(1)}, u32[]{:S(2)}, u32[]{:S(2)}) collective-permute-start(f32[131,256]{1,0:T(8,128)S(1)} %pad_maximum_fusion.5), channel_id=1, source_target_pairs={{0,1},{1,2},{2,3},{3,4},{4,5},{5,6},{6,7},{7,8},{8,9},{9,10},{10,1... | collective-permute-start | bytes 402440 | tf_op jit(solution)/shard_map/ppermute | solution.py:27
  28.6 3.1 %collective-permute-start.4 = (f32[1120]{0:T(1024)S(1)}, f32[1120]{0:T(1024)S(1)}, u32[]{:S(2)}, u32[]{:S(2)}) collective-permute-start(f32[1120]{0:T(1024)S(1)} %slice_select_fusion.6), channel_id=1, source_target_pairs={{0,1},{1,0},{2,3},{3,2},{4,5},{5,4},{6,7},{7,6},{8,9},{9,8},{10,11... | collective-permute-start | bytes 13448 | tf_op jit(solution)/shard_map/ppermute | solution.py:85
  31.8 8.3 %collective-permute-start.5 = (f32[1120]{0:T(1024)S(1)}, f32[1120]{0:T(1024)S(1)}, u32[]{:S(2)}, u32[]{:S(2)}) collective-permute-start(f32[1120]{0:T(1024)S(1)} %select_add_fusion.2), channel_id=1, source_target_pairs={{0,8},{1,9},{2,10},{3,11},{4,12},{5,13},{6,14},{7,15},{8,0},{9,1},... | collective-permute-start | bytes 13448 | tf_op jit(solution)/shard_map/ppermute | solution.py:85
  40.1 5.0 %collective-permute-start.6 = (f32[2240]{0:T(1024)S(1)}, f32[2240]{0:T(1024)S(1)}, u32[]{:S(2)}, u32[]{:S(2)}) collective-permute-start(f32[2240]{0:T(1024)S(1)} %maximum_select_fusion.22), channel_id=1, source_target_pairs={{0,16},{1,17},{2,18},{3,19},{4,20},{5,21},{6,22},{7,23},{8,24},{9,... | collective-permute-start | bytes 26888 | tf_op jit(solution)/shard_map/ppermute | solution.py:85
  45.2 6.3 %collective-permute-start.7 = (f32[4480]{0:T(1024)S(1)}, f32[4480]{0:T(1024)S(1)}, u32[]{:S(2)}, u32[]{:S(2)}) collective-permute-start(f32[4480]{0:T(1024)S(1)} %maximum_select_fusion.18), channel_id=1, source_target_pairs={{0,32},{1,33},{2,34},{3,35},{4,36},{5,37},{6,38},{7,39},{8,40},{9,... | collective-permute-start | bytes 53768 | tf_op jit(solution)/shard_map/ppermute | solution.py:85
  51.6 6.2 %collective-permute-start.8 = (f32[8960]{0:T(1024)S(1)}, f32[8960]{0:T(1024)S(1)}, u32[]{:S(2)}, u32[]{:S(2)}) collective-permute-start(f32[8960]{0:T(1024)S(1)} %maximum_select_fusion.14), channel_id=1, source_target_pairs={{0,64},{1,65},{2,66},{3,67},{4,68},{5,69},{6,70},{7,71},{8,72},{9,... | collective-permute-start | bytes 107528 | tf_op jit(solution)/shard_map/ppermute | solution.py:85
  57.7 6.4 %collective-permute-start.9 = (f32[17920]{0:T(1024)S(1)}, f32[17920]{0:T(1024)S(1)}, u32[]{:S(2)}, u32[]{:S(2)}) collective-permute-start(f32[17920]{0:T(1024)S(1)} %maximum_select_fusion.9), channel_id=1, source_target_pairs={{0,128},{1,129},{2,130},{3,131},{4,132},{5,133},{6,134},{7,135},{8... | collective-permute-start | bytes 215048 | tf_op jit(solution)/shard_map/ppermute | solution.py:85
  63.8 7.6 %copy-start.1 = (bf16[108,64,128]{2,0,1:T(8,128)(2,1)}, bf16[108,64,128]{2,0,1:T(8,128)(2,1)S(1)}, u32[]{:S(2)}) copy-start(bf16[108,64,128]{2,0,1:T(8,128)(2,1)S(1)} %convert_bitcast_fusion) | copy-start | bytes 5308420
  64.2 14.9 %collective-permute-start.10 = (f32[35840]{0:T(1024)S(1)}, f32[35840]{0:T(1024)S(1)}, u32[]{:S(2)}, u32[]{:S(2)}) collective-permute-start(f32[35840]{0:T(1024)S(1)} %maximum_select_fusion.5), channel_id=1, source_target_pairs={{0,256},{1,257},{2,258},{3,259},{4,260},{5,261},{6,262},{7,263},{8... | collective-permute-start | bytes 430088 | tf_op jit(solution)/shard_map/ppermute | solution.py:85
  78.5 4.2 %copy-start.5 = (f32[35,35]{1,0:T(8,128)S(1)}, f32[35,35]{1,0:T(8,128)}, u32[]{:S(2)}) copy-start(f32[35,35]{1,0:T(8,128)} %param.16) | copy-start | bytes 14704
  78.5 12.8 %copy-start.7 = (s32[108]{0:T(128)S(1)}, s32[108]{0:T(128)}, u32[]{:S(2)}) copy-start(s32[108]{0:T(128)} %param.18) | copy-start | bytes 1300
  80.4 25.6 %copy-start.8 = (f32[128]{0:T(128)S(1)}, f32[128]{0:T(128)}, u32[]{:S(2)}) copy-start(f32[128]{0:T(128)} %param.17) | copy-start | bytes 1540
  83.1 12.7 %collective-permute-start.11 = (f32[1120]{0:T(1024)S(1)}, f32[1120]{0:T(1024)S(1)}, u32[]{:S(2)}, u32[]{:S(2)}) collective-permute-start(f32[1120]{0:T(1024)S(1)} %reshape.251), channel_id=1, source_target_pairs={{0,1},{1,0},{2,3},{3,2},{4,5},{5,4},{6,7},{7,6},{8,9},{9,8},{10,11... | collective-permute-start | bytes 13448 | tf_op jit(solution)/shard_map/ppermute | solution.py:85
  95.9 4.4 %collective-permute-start.12 = (f32[2240]{0:T(1024)S(1)}, f32[2240]{0:T(1024)S(1)}, u32[]{:S(2)}, u32[]{:S(2)}) collective-permute-start(f32[2240]{0:T(1024)S(1)} %maximum_select_fusion.23), channel_id=1, source_target_pairs={{0,2},{1,3},{2,0},{3,1},{4,6},{5,7},{6,4},{7,5},{8,10},{9,11},{10,... | collective-permute-start | bytes 26888 | tf_op jit(solution)/shard_map/ppermute | solution.py:85
  100.4 5.4 %collective-permute-start.13 = (f32[4480]{0:T(1024)S(1)}, f32[4480]{0:T(1024)S(1)}, u32[]{:S(2)}, u32[]{:S(2)}) collective-permute-start(f32[4480]{0:T(1024)S(1)} %maximum_select_fusion.19), channel_id=1, source_target_pairs={{0,4},{1,5},{2,6},{3,7},{4,0},{5,1},{6,2},{7,3},{8,12},{9,13},{10,... | collective-permute-start | bytes 53768 | tf_op jit(solution)/shard_map/ppermute | solution.py:85
  107.1 19.3 %collective-permute-start.16 = (f32[2240]{0:T(1024)S(1)}, f32[2240]{0:T(1024)S(1)}, u32[]{:S(2)}, u32[]{:S(2)}) collective-permute-start(f32[2240]{0:T(1024)S(1)} %select_n.320), channel_id=1, source_target_pairs={{0,4},{1,5},{2,6},{3,7},{4,0},{5,1},{6,2},{7,3},{8,12},{9,13},{10,... | collective-permute-start | bytes 26888 | tf_op jit(solution)/shard_map/ppermute | solution.py:85
  110.7 6.0 %copy-start.2 = (bf16[108,64,128]{2,0,1:T(8,128)(2,1)S(1)}, bf16[108,64,128]{2,0,1:T(8,128)(2,1)}, u32[]{:S(2)}) copy-start(bf16[108,64,128]{2,0,1:T(8,128)(2,1)} %copy-done.1) | copy-start | bytes 5308420
  124.5 16.2 %copy-start.3 = (bf16[256,128]{1,0:T(8,128)(2,1)S(1)}, bf16[256,128]{1,0:T(8,128)(2,1)}, u32[]{:S(2)}) copy-start(bf16[256,128]{1,0:T(8,128)(2,1)} %param.14) | copy-start | bytes 196612
  126.5 9.7 %collective-permute-start.17 = (f32[1120]{0:T(1024)S(1)}, f32[1120]{0:T(1024)S(1)}, u32[]{:S(2)}, u32[]{:S(2)}) collective-permute-start(f32[1120]{0:T(1024)S(1)} %slice_select_fusion.5), channel_id=1, source_target_pairs={{0,2},{1,3},{2,0},{3,1},{4,6},{5,7},{6,4},{7,5},{8,10},{9,11},{10,... | collective-permute-start | bytes 13448 | tf_op jit(solution)/shard_map/ppermute | solution.py:85
  129.9 10.4 %collective-permute-start.15 = (bf16[131,256]{1,0:T(8,128)(2,1)S(1)}, bf16[131,256]{1,0:T(8,128)(2,1)S(1)}, u32[]{:S(2)}, u32[]{:S(2)}) collective-permute-start(bf16[131,256]{1,0:T(8,128)(2,1)S(1)} %fusion.47), channel_id=1, source_target_pairs={{0,1},{1,2},{2,3},{3,4},{4,5},{5,6},{6,7},{7,8},{8,9},{9,10},{10,1... | collective-permute-start | bytes 201224 | tf_op jit(solution)/shard_map/ppermute | solution.py:38
  134.3 6.4 %collective-permute-start.14 = (f32[131,256]{1,0:T(8,128)S(1)}, f32[131,256]{1,0:T(8,128)S(1)}, u32[]{:S(2)}, u32[]{:S(2)}) collective-permute-start(f32[131,256]{1,0:T(8,128)S(1)} %fusion.46), channel_id=1, source_target_pairs={{1,0},{2,1},{3,2},{4,3},{5,4},{6,5},{7,6},{8,7},{9,8},{10,9},{11,1... | collective-permute-start | bytes 402440 | tf_op jit(solution)/shard_map/ppermute | solution.py:38
  136.4 3.1 %collective-permute-start.18 = (f32[560]{0:T(1024)S(1)}, f32[560]{0:T(1024)S(1)}, u32[]{:S(2)}, u32[]{:S(2)}) collective-permute-start(f32[560]{0:T(1024)S(1)} %slice_select_fusion.7), channel_id=1, source_target_pairs={{0,1},{1,0},{2,3},{3,2},{4,5},{5,4},{6,7},{7,6},{8,9},{9,8},{10,11... | collective-permute-start | bytes 6728 | tf_op jit(solution)/shard_map/ppermute | solution.py:85
  141.4 11.3 %collective-permute-start.19 = (f32[18297]{0:T(1024)S(1)}, f32[18297]{0:T(1024)S(1)}, u32[]{:S(2)}, u32[]{:S(2)}) collective-permute-start(f32[18297]{0:T(1024)S(1)} %concatenate.293), channel_id=1, source_target_pairs={{0,8},{1,9},{2,10},{3,11},{4,12},{5,13},{6,14},{7,15},{8,0},{9,1},... | collective-permute-start | bytes 219572 | tf_op jit(solution)/shard_map/ppermute | solution.py:85
  153.0 9.2 %collective-permute-start.20 = (f32[18857]{0:T(1024)S(1)}, f32[18857]{0:T(1024)S(1)}, u32[]{:S(2)}, u32[]{:S(2)}) collective-permute-start(f32[18857]{0:T(1024)S(1)} %pad_maximum_fusion.10), channel_id=1, source_target_pairs={{0,16},{1,17},{2,18},{3,19},{4,20},{5,21},{6,22},{7,23},{8,24},{9,... | collective-permute-start | bytes 226292 | tf_op jit(solution)/shard_map/ppermute | solution.py:85
  162.4 6.7 %collective-permute-start.21 = (f32[19977]{0:T(1024)S(1)}, f32[19977]{0:T(1024)S(1)}, u32[]{:S(2)}, u32[]{:S(2)}) collective-permute-start(f32[19977]{0:T(1024)S(1)} %pad_maximum_fusion.8), channel_id=1, source_target_pairs={{0,32},{1,33},{2,34},{3,35},{4,36},{5,37},{6,38},{7,39},{8,40},{9,... | collective-permute-start | bytes 239732 | tf_op jit(solution)/shard_map/ppermute | solution.py:85
  169.3 5.3 %collective-permute-start.22 = (f32[22217]{0:T(1024)S(1)}, f32[22217]{0:T(1024)S(1)}, u32[]{:S(2)}, u32[]{:S(2)}) collective-permute-start(f32[22217]{0:T(1024)S(1)} %pad_maximum_fusion.7), channel_id=1, source_target_pairs={{0,64},{1,65},{2,66},{3,67},{4,68},{5,69},{6,70},{7,71},{8,72},{9,... | collective-permute-start | bytes 266612 | tf_op jit(solution)/shard_map/ppermute | solution.py:85
  174.7 7.3 %collective-permute-start.23 = (f32[26697]{0:T(1024)S(1)}, f32[26697]{0:T(1024)S(1)}, u32[]{:S(2)}, u32[]{:S(2)}) collective-permute-start(f32[26697]{0:T(1024)S(1)} %pad_maximum_fusion.6), channel_id=1, source_target_pairs={{0,128},{1,129},{2,130},{3,131},{4,132},{5,133},{6,134},{7,135},{8... | collective-permute-start | bytes 320372 | tf_op jit(solution)/shard_map/ppermute | solution.py:85
  182.0 11.0 %collective-permute-start.24 = (f32[35657]{0:T(1024)S(1)}, f32[35657]{0:T(1024)S(1)}, u32[]{:S(2)}, u32[]{:S(2)}) collective-permute-start(f32[35657]{0:T(1024)S(1)} %pad_maximum_fusion.3), channel_id=1, source_target_pairs={{0,256},{1,257},{2,258},{3,259},{4,260},{5,261},{6,262},{7,263},{8... | collective-permute-start | bytes 427892 | tf_op jit(solution)/shard_map/ppermute | solution.py:85
  194.3 9.0 %collective-permute-start.25 = (f32[18297]{0:T(1024)S(1)}, f32[18297]{0:T(1024)S(1)}, u32[]{:S(2)}, u32[]{:S(2)}) collective-permute-start(f32[18297]{0:T(1024)S(1)} %pad_maximum_fusion.12), channel_id=1, source_target_pairs={{0,1},{1,0},{2,3},{3,2},{4,5},{5,4},{6,7},{7,6},{8,9},{9,8},{10,11... | collective-permute-start | bytes 219572 | tf_op jit(solution)/shard_map/ppermute | solution.py:85
  203.7 5.5 %collective-permute-start.26 = (f32[18857]{0:T(1024)S(1)}, f32[18857]{0:T(1024)S(1)}, u32[]{:S(2)}, u32[]{:S(2)}) collective-permute-start(f32[18857]{0:T(1024)S(1)} %pad_maximum_fusion.11), channel_id=1, source_target_pairs={{0,2},{1,3},{2,0},{3,1},{4,6},{5,7},{6,4},{7,5},{8,10},{9,11},{10,... | collective-permute-start | bytes 226292 | tf_op jit(solution)/shard_map/ppermute | solution.py:85
  209.6 8.5 %collective-permute-start.27 = (f32[19977]{0:T(1024)S(1)}, f32[19977]{0:T(1024)S(1)}, u32[]{:S(2)}, u32[]{:S(2)}) collective-permute-start(f32[19977]{0:T(1024)S(1)} %pad_maximum_fusion.9), channel_id=1, source_target_pairs={{0,4},{1,5},{2,6},{3,7},{4,0},{5,1},{6,2},{7,3},{8,12},{9,13},{10,... | collective-permute-start | bytes 239732 | tf_op jit(solution)/shard_map/ppermute | solution.py:85

commit v10 on v9

--- a/solution.py
+++ b/solution.py
@@ -206,7 +206,9 @@
     )
     d_own, d_ext, d_feat_ext = near_back(d_pre)
     d_pack = jnp.concatenate([d_ext, d_feat_ext], axis=0)
-    low_pack = passed_along(d_pack[:, :atom_num], "box", -1)
+    low_pack = passed_along(d_pack[:, :atom_num].astype(jnp.bfloat16), "box", -1).astype(
+        jnp.float32
+    )
     high_pack = passed_along(d_pack[:, 2 * atom_num :].astype(jnp.bfloat16), "box", 1).astype(
         jnp.float32
     )

time: 223 us -> 226 us (1.013)
  starting transfers between devices: 119 us -> 126 us
  waiting for transfers between devices: 41.2 us -> 37.1 us
    ppermute x24, starting transfers between devices: 104 us -> 110 us  [xor_swap(): return lax.ppermute(block, 'box', [(i, i ^ 1 << bit) for i in range(count)])]
    ppermute x24, waiting for transfers between devices: 40.8 us -> 37.1 us  [xor_swap(): return lax.ppermute(block, 'box', [(i, i ^ 1 << bit) for i in range(count)])]
  transfers between devices with their start and end apart: 28 -> 28, of which waited for: 17 -> 16; matrix products, arithmetic and copies ran while one was open for 19% -> 19% of each run, Pallas kernels for 0% -> 0%
where the time goes in v10:
time: 226 us; the launch traced here: 224 us
  starting transfers between devices  126 us (56%)
  matrix products  37.2 us (16%)
  waiting for transfers between devices  37.1 us (16%)
  local copies, waits for them, and re-layouts  13.7 us (6%)
  other arithmetic  8.52 us (4%)
    ppermute x24, starting transfers between devices, xor_swap(): return lax.ppermute(block, 'box', [(i, i ^ 1 << bit) for i in range(count)])  110 us
    ppermute x24, waiting for transfers between devices, xor_swap(): return lax.ppermute(block, 'box', [(i, i ^ 1 << bit) for i in range(count)])  37.1 us
    dot_general x3, matrix products, near_field(): jnp.einsum('pij,pjc->pic', kernel, source_feat, preferred_element_type=jn...  20.2 us
    ppermute x2, starting transfers between devices, passed_along(): return lax.ppermute(block, axis, route)  6.7 us
    dot_general x2, matrix products, near_field(): jnp.einsum('pt,pic->tic', tgt_hot, contrib, precision=lax.Precision.HIGH)  5.65 us
    ppermute x1, starting transfers between devices, extended(): lax.ppermute(lax.slice_in_dim(block, 0, width, axis=dim), axis, backward)  5.46 us
  transfers between devices with their start and end apart: 28, of which 16 were waited for; matrix products, arithmetic and copies ran while one was open for 19% of the time, Pallas kernels for 0%

profile of v10, /device:TPU:1, one launch (start us, length us, event | category | flops | bytes accessed | tf_op | source)
XLA Modules:
  0.0 224.4 jit_solution(647784119060707484)
XLA Ops:
  0.7 0.8 broadcast_in_dim.8
  1.5 0.7 subtract_multiply_fusion.3
  2.2 0.7 iota_compare_fusion.3
  3.2 1.3 fusion.52
  4.5 1.0 convert_convert_fusion
  6.1 6.6 %collective-permute-start.2 = (f32[4480]{0:T(1024)S(1)}, f32[4480]{0:T(1024)S(1)}, u32[]{:S(2)}, u32[]{:S(2)}) collective-permute-start(f32[4480]{0:T(1024)S(1)} %select_n.283), channel_id=1, source_target_pairs={{0,4},{1,5},{2,6},{3,7},{4,0},{5,1},{6,2},{7,3},{8,12},{9,13},{10,... | collective-permute-start | bytes 53768 | tf_op jit(solution)/shard_map/ppermute | solution.py:85
  13.0 0.9 collective-permute-done.2
  14.0 4.0 %collective-permute-start.3 = (f32[2240]{0:T(1024)S(1)}, f32[2240]{0:T(1024)S(1)}, u32[]{:S(2)}, u32[]{:S(2)}) collective-permute-start(f32[2240]{0:T(1024)S(1)} %slice_select_fusion.4), channel_id=1, source_target_pairs={{0,2},{1,3},{2,0},{3,1},{4,6},{5,7},{6,4},{7,5},{8,10},{9,11},{10,... | collective-permute-start | bytes 26888 | tf_op jit(solution)/shard_map/ppermute | solution.py:85
  18.0 0.7 pad_maximum_fusion.5
  18.7 5.5 %collective-permute-start.1 = (f32[131,256]{1,0:T(8,128)S(1)}, f32[131,256]{1,0:T(8,128)S(1)}, u32[]{:S(2)}, u32[]{:S(2)}) collective-permute-start(f32[131,256]{1,0:T(8,128)S(1)} %pad_maximum_fusion.5), channel_id=1, source_target_pairs={{1,0},{2,1},{3,2},{4,3},{5,4},{6,5},{7,6},{8,7},{9,8},{10,9},{11,1... | collective-permute-start | bytes 402440 | tf_op jit(solution)/shard_map/ppermute | solution.py:30
  24.2 3.5 %collective-permute-start = (f32[131,256]{1,0:T(8,128)S(1)}, f32[131,256]{1,0:T(8,128)S(1)}, u32[]{:S(2)}, u32[]{:S(2)}) collective-permute-start(f32[131,256]{1,0:T(8,128)S(1)} %pad_maximum_fusion.5), channel_id=1, source_target_pairs={{0,1},{1,2},{2,3},{3,4},{4,5},{5,6},{6,7},{7,8},{8,9},{9,10},{10,1... | collective-permute-start | bytes 402440 | tf_op jit(solution)/shard_map/ppermute | solution.py:27
  27.7 0.8 reshape.246
  28.6 1.9 collective-permute-start.4
  30.5 0.9 convolution_bitcast_fusion.1
  31.8 5.4 %collective-permute-start.5 = (f32[1120]{0:T(1024)S(1)}, f32[1120]{0:T(1024)S(1)}, u32[]{:S(2)}, u32[]{:S(2)}) collective-permute-start(f32[1120]{0:T(1024)S(1)} %select_add_fusion.2), channel_id=1, source_target_pairs={{0,8},{1,9},{2,10},{3,11},{4,12},{5,13},{6,14},{7,15},{8,0},{9,1},... | collective-permute-start | bytes 13448 | tf_op jit(solution)/shard_map/ppermute | solution.py:85
  37.2 2.9 %collective-permute-done.5 = f32[1120]{0:T(1024)S(1)} collective-permute-done((f32[1120]{0:T(1024)S(1)}, f32[1120]{0:T(1024)S(1)}, u32[]{:S(2)}, u32[]{:S(2)}) %collective-permute-start.5) | collective-permute-done | bytes 4512 | tf_op jit(solution)/shard_map/ppermute | solution.py:85
  40.1 3.5 %collective-permute-start.6 = (f32[2240]{0:T(1024)S(1)}, f32[2240]{0:T(1024)S(1)}, u32[]{:S(2)}, u32[]{:S(2)}) collective-permute-start(f32[2240]{0:T(1024)S(1)} %maximum_select_fusion.22), channel_id=1, source_target_pairs={{0,16},{1,17},{2,18},{3,19},{4,20},{5,21},{6,22},{7,23},{8,24},{9,... | collective-permute-start | bytes 26888 | tf_op jit(solution)/shard_map/ppermute | solution.py:85
  43.7 0.7 broadcast_multiply_fusion
  44.3 0.8 copy.214
  45.2 4.6 %collective-permute-start.7 = (f32[4480]{0:T(1024)S(1)}, f32[4480]{0:T(1024)S(1)}, u32[]{:S(2)}, u32[]{:S(2)}) collective-permute-start(f32[4480]{0:T(1024)S(1)} %maximum_select_fusion.18), channel_id=1, source_target_pairs={{0,32},{1,33},{2,34},{3,35},{4,36},{5,37},{6,38},{7,39},{8,40},{9,... | collective-permute-start | bytes 53768 | tf_op jit(solution)/shard_map/ppermute | solution.py:85
  50.3 0.7 convert_element_type.63
  51.6 4.8 %collective-permute-start.8 = (f32[8960]{0:T(1024)S(1)}, f32[8960]{0:T(1024)S(1)}, u32[]{:S(2)}, u32[]{:S(2)}) collective-permute-start(f32[8960]{0:T(1024)S(1)} %maximum_select_fusion.14), channel_id=1, source_target_pairs={{0,64},{1,65},{2,66},{3,67},{4,68},{5,69},{6,70},{7,71},{8,72},{9,... | collective-permute-start | bytes 107528 | tf_op jit(solution)/shard_map/ppermute | solution.py:85
  56.7 1.1 collective-permute-done.8
  57.7 4.4 %collective-permute-start.9 = (f32[17920]{0:T(1024)S(1)}, f32[17920]{0:T(1024)S(1)}, u32[]{:S(2)}, u32[]{:S(2)}) collective-permute-start(f32[17920]{0:T(1024)S(1)} %maximum_select_fusion.9), channel_id=1, source_target_pairs={{0,128},{1,129},{2,130},{3,131},{4,132},{5,133},{6,134},{7,135},{8... | collective-permute-start | bytes 215048 | tf_op jit(solution)/shard_map/ppermute | solution.py:85
  63.1 0.7 convert_bitcast_fusion
  64.2 7.2 %collective-permute-start.10 = (f32[35840]{0:T(1024)S(1)}, f32[35840]{0:T(1024)S(1)}, u32[]{:S(2)}, u32[]{:S(2)}) collective-permute-start(f32[35840]{0:T(1024)S(1)} %maximum_select_fusion.5), channel_id=1, source_target_pairs={{0,256},{1,257},{2,258},{3,259},{4,260},{5,261},{6,262},{7,263},{8... | collective-permute-start | bytes 430088 | tf_op jit(solution)/shard_map/ppermute | solution.py:85
  71.4 6.5 %fusion.26 = f32[108,64,128]{2,1,0:T(8,128)} fusion(bf16[108,64,128]{2,0,1:T(8,128)(2,1)S(1)} %convert_bitcast_fusion, f32[108]{0:T(128)S(1)} %broadcast_multiply_fusion, f32[108,64]{1,0:T(8,128)S(1)} %copy.208, f32[108,64]{1,0:T(8,128)S(1)} %copy.207, f32[108,64]{1,0:T(8,128)S(1)} %copy.206, f32[108,64]{1,0:T(8,128)S(1)} %copy.205, ...), kind=kOutput, calls=%fused_computation.32 | convolution fusion | flops 118112256 | bytes 5474736 | tf_op jit(solution)/shard_map/jvp(pij,pjc->pic)/dot_general | solution.py:78
  80.5 2.2 %fusion.31 = f32[1,2,35,16]{2,0,3,1:T(1,128)S(1)} fusion(f32[64,2,35,16]{0,3,2,1:T(8,128)S(1)} %maximum_select_fusion, f32[64,64]{1,0:T(8,128)S(1)} %convert_reduce_fusion, s32[]{:T(128)S(6)} %select_n.270), kind=kOutput, calls=%fused_computation.47 | convolution fusion | flops 860160 | bytes 578436 | tf_op jit(solution)/shard_map/j,jnkc->nkc/dot_general | solution.py:180
  83.1 8.2 %collective-permute-start.11 = (f32[1120]{0:T(1024)S(1)}, f32[1120]{0:T(1024)S(1)}, u32[]{:S(2)}, u32[]{:S(2)}) collective-permute-start(f32[1120]{0:T(1024)S(1)} %reshape.251), channel_id=1, source_target_pairs={{0,1},{1,0},{2,3},{3,2},{4,5},{5,4},{6,7},{7,6},{8,9},{9,8},{10,11... | collective-permute-start | bytes 13448 | tf_op jit(solution)/shard_map/ppermute | solution.py:85
  91.4 4.4 %fusion = f32[4,64,128]{2,0,1:T(4,128)S(1)} fusion(f32[108,64,128]{2,1,0:T(8,128)} %fusion.26, s32[108]{0:T(128)S(1)} %copy-done.7), kind=kOutput, calls=%fused_computation.6 | convolution fusion | flops 21234096 | bytes 3670448 | tf_op jit(solution)/shard_map/jvp(pt,pic->tic)/dot_general | solution.py:79
  95.9 1.9 collective-permute-start.12
  98.0 2.3 %collective-permute-done.12 = f32[2240]{0:T(1024)S(1)} collective-permute-done((f32[2240]{0:T(1024)S(1)}, f32[2240]{0:T(1024)S(1)}, u32[]{:S(2)}, u32[]{:S(2)}) %collective-permute-start.12) | collective-permute-done | bytes 8992 | tf_op jit(solution)/shard_map/ppermute | solution.py:85
  100.4 2.6 %collective-permute-start.13 = (f32[4480]{0:T(1024)S(1)}, f32[4480]{0:T(1024)S(1)}, u32[]{:S(2)}, u32[]{:S(2)}) collective-permute-start(f32[4480]{0:T(1024)S(1)} %maximum_select_fusion.19), channel_id=1, source_target_pairs={{0,4},{1,5},{2,6},{3,7},{4,0},{5,1},{6,2},{7,3},{8,12},{9,13},{10,... | collective-permute-start | bytes 53768 | tf_op jit(solution)/shard_map/ppermute | solution.py:85
  103.2 2.6 %collective-permute-done.13 = f32[4480]{0:T(1024)S(1)} collective-permute-done((f32[4480]{0:T(1024)S(1)}, f32[4480]{0:T(1024)S(1)}, u32[]{:S(2)}, u32[]{:S(2)}) %collective-permute-start.13) | collective-permute-done | bytes 17952 | tf_op jit(solution)/shard_map/ppermute | solution.py:85
  107.1 2.4 %collective-permute-start.16 = (f32[2240]{0:T(1024)S(1)}, f32[2240]{0:T(1024)S(1)}, u32[]{:S(2)}, u32[]{:S(2)}) collective-permute-start(f32[2240]{0:T(1024)S(1)} %select_n.320), channel_id=1, source_target_pairs={{0,4},{1,5},{2,6},{3,7},{4,0},{5,1},{6,2},{7,3},{8,12},{9,13},{10,... | collective-permute-start | bytes 26888 | tf_op jit(solution)/shard_map/ppermute | solution.py:85
  109.5 1.2 fusion.50
  110.8 6.0 %convert_bitcast_fusion.1 = bf16[128,64,108]{0,1,2:T(8,128)(2,1)S(1)} fusion(bf16[108,64,128]{2,0,1:T(8,128)(2,1)S(1)} %fusion.50, f32[108]{0:T(128)S(1)} %broadcast_multiply_fusion, f32[108,64]{1,0:T(8,128)S(1)} %copy.208, f32[108,64]{1,0:T(8,128)S(1)} %copy.207, f32[108,64]{1,0:T(8,128)S(1)} %copy.206, f32[108,64]{1,0:T(8,128)S(1)} %copy.205, ...), kind=kOutput, calls=%fused_computation.30 | convolution fusion | flops 118112256 | bytes 3705264 | tf_op jit(solution)/shard_map/transpose(jvp(pij,pjc->pic))/dot_general | solution.py:78
  116.8 7.7 %fusion.14 = (f32[108,64]{1,0:T(8,128)S(1)}, f32[108,64]{1,0:T(8,128)S(1)}, f32[108,64]{1,0:T(8,128)S(1)}, f32[108,64]{1,0:T(8,128)S(1)}, f32[108,64]{1,0:T(8,128)S(1)}, /*index=5*/f32[108,64]{1,0:T(8,128)S(1)}) fusion(f32[108,64]{1,0:T(8,128)S(1)} %copy.208, f32[108,64]{1,0:T(8,128)S(1)} %copy.207, f32[108,64]{1,0:T(8,128)S(1)} %copy.204, ...), kind=kOutput, calls=%fused_computation.22 | convolution fusion | flops 124706304 | bytes 3871152 | tf_op jit(solution)/shard_map/transpose(jvp(pij,pjc->pic))/dot_general | solution.py:78
  124.5 1.0 fusion.28
  126.5 3.4 %collective-permute-start.17 = (f32[1120]{0:T(1024)S(1)}, f32[1120]{0:T(1024)S(1)}, u32[]{:S(2)}, u32[]{:S(2)}) collective-permute-start(f32[1120]{0:T(1024)S(1)} %slice_select_fusion.5), channel_id=1, source_target_pairs={{0,2},{1,3},{2,0},{3,1},{4,6},{5,7},{6,4},{7,5},{8,10},{9,11},{10,... | collective-permute-start | bytes 13448 | tf_op jit(solution)/shard_map/ppermute | solution.py:85
  129.9 4.8 %collective-permute-start.14 = (bf16[131,256]{1,0:T(8,128)(2,1)S(1)}, bf16[131,256]{1,0:T(8,128)(2,1)S(1)}, u32[]{:S(2)}, u32[]{:S(2)}) collective-permute-start(bf16[131,256]{1,0:T(8,128)(2,1)S(1)} %get-tuple-element.17), channel_id=1, source_target_pairs={{1,0},{2,1},{3,2},{4,3},{5,4},{6,5},{7,6},{8,7},{9,8},{10,9},{11,1... | collective-permute-start | bytes 201224 | tf_op jit(solution)/shard_map/ppermute | solution.py:38
  134.7 1.9 collective-permute-start.15
  136.8 2.4 %collective-permute-start.18 = (f32[560]{0:T(1024)S(1)}, f32[560]{0:T(1024)S(1)}, u32[]{:S(2)}, u32[]{:S(2)}) collective-permute-start(f32[560]{0:T(1024)S(1)} %slice_select_fusion.7), channel_id=1, source_target_pairs={{0,1},{1,0},{2,3},{3,2},{4,5},{5,4},{6,7},{7,6},{8,9},{9,8},{10,11... | collective-permute-start | bytes 6728 | tf_op jit(solution)/shard_map/ppermute | solution.py:85
  139.4 0.6 collective-permute-done.18
  141.6 6.4 %collective-permute-start.19 = (f32[18297]{0:T(1024)S(1)}, f32[18297]{0:T(1024)S(1)}, u32[]{:S(2)}, u32[]{:S(2)}) collective-permute-start(f32[18297]{0:T(1024)S(1)} %concatenate.293), channel_id=1, source_target_pairs={{0,8},{1,9},{2,10},{3,11},{4,12},{5,13},{6,14},{7,15},{8,0},{9,1},... | collective-permute-start | bytes 219572 | tf_op jit(solution)/shard_map/ppermute | solution.py:85
  148.3 2.5 %collective-permute-done.19 = f32[18297]{0:T(1024)S(1)} collective-permute-done((f32[18297]{0:T(1024)S(1)}, f32[18297]{0:T(1024)S(1)}, u32[]{:S(2)}, u32[]{:S(2)}) %collective-permute-start.19) | collective-permute-done | bytes 73220 | tf_op jit(solution)/shard_map/ppermute | solution.py:85
  151.0 3.1 %collective-permute-start.20 = (f32[18857]{0:T(1024)S(1)}, f32[18857]{0:T(1024)S(1)}, u32[]{:S(2)}, u32[]{:S(2)}) collective-permute-start(f32[18857]{0:T(1024)S(1)} %pad_maximum_fusion.10), channel_id=1, source_target_pairs={{0,16},{1,17},{2,18},{3,19},{4,20},{5,21},{6,22},{7,23},{8,24},{9,... | collective-permute-start | bytes 226292 | tf_op jit(solution)/shard_map/ppermute | solution.py:85
  154.4 1.7 collective-permute-done.20
  156.4 4.6 %collective-permute-start.21 = (f32[19977]{0:T(1024)S(1)}, f32[19977]{0:T(1024)S(1)}, u32[]{:S(2)}, u32[]{:S(2)}) collective-permute-start(f32[19977]{0:T(1024)S(1)} %pad_maximum_fusion.8), channel_id=1, source_target_pairs={{0,32},{1,33},{2,34},{3,35},{4,36},{5,37},{6,38},{7,39},{8,40},{9,... | collective-permute-start | bytes 239732 | tf_op jit(solution)/shard_map/ppermute | solution.py:85
  161.2 1.9 collective-permute-done.21
  163.3 5.1 %collective-permute-start.22 = (f32[22217]{0:T(1024)S(1)}, f32[22217]{0:T(1024)S(1)}, u32[]{:S(2)}, u32[]{:S(2)}) collective-permute-start(f32[22217]{0:T(1024)S(1)} %pad_maximum_fusion.7), channel_id=1, source_target_pairs={{0,64},{1,65},{2,66},{3,67},{4,68},{5,69},{6,70},{7,71},{8,72},{9,... | collective-permute-start | bytes 266612 | tf_op jit(solution)/shard_map/ppermute | solution.py:85
  169.0 1.3 collective-permute-done.22
  170.4 3.7 %collective-permute-start.23 = (f32[26697]{0:T(1024)S(1)}, f32[26697]{0:T(1024)S(1)}, u32[]{:S(2)}, u32[]{:S(2)}) collective-permute-start(f32[26697]{0:T(1024)S(1)} %pad_maximum_fusion.6), channel_id=1, source_target_pairs={{0,128},{1,129},{2,130},{3,131},{4,132},{5,133},{6,134},{7,135},{8... | collective-permute-start | bytes 320372 | tf_op jit(solution)/shard_map/ppermute | solution.py:85
  174.3 2.5 %collective-permute-done.23 = f32[26697]{0:T(1024)S(1)} collective-permute-done((f32[26697]{0:T(1024)S(1)}, f32[26697]{0:T(1024)S(1)}, u32[]{:S(2)}, u32[]{:S(2)}) %collective-permute-start.23) | collective-permute-done | bytes 106820 | tf_op jit(solution)/shard_map/ppermute | solution.py:85
  176.9 4.3 %collective-permute-start.24 = (f32[35657]{0:T(1024)S(1)}, f32[35657]{0:T(1024)S(1)}, u32[]{:S(2)}, u32[]{:S(2)}) collective-permute-start(f32[35657]{0:T(1024)S(1)} %pad_maximum_fusion.3), channel_id=1, source_target_pairs={{0,256},{1,257},{2,258},{3,259},{4,260},{5,261},{6,262},{7,263},{8... | collective-permute-start | bytes 427892 | tf_op jit(solution)/shard_map/ppermute | solution.py:85
  181.7 6.4 %collective-permute-done.24 = f32[35657]{0:T(1024)S(1)} collective-permute-done((f32[35657]{0:T(1024)S(1)}, f32[35657]{0:T(1024)S(1)}, u32[]{:S(2)}, u32[]{:S(2)}) %collective-permute-start.24) | collective-permute-done | bytes 142660 | tf_op jit(solution)/shard_map/ppermute | solution.py:85
  189.4 16.0 %collective-permute-start.25 = (f32[18297]{0:T(1024)S(1)}, f32[18297]{0:T(1024)S(1)}, u32[]{:S(2)}, u32[]{:S(2)}) collective-permute-start(f32[18297]{0:T(1024)S(1)} %pad_maximum_fusion.12), channel_id=1, source_target_pairs={{0,1},{1,0},{2,3},{3,2},{4,5},{5,4},{6,7},{7,6},{8,9},{9,8},{10,11... | collective-permute-start | bytes 219572 | tf_op jit(solution)/shard_map/ppermute | solution.py:85
  206.8 1.9 collective-permute-start.26
  208.7 3.5 %collective-permute-done.26 = f32[18857]{0:T(1024)S(1)} collective-permute-done((f32[18857]{0:T(1024)S(1)}, f32[18857]{0:T(1024)S(1)}, u32[]{:S(2)}, u32[]{:S(2)}) %collective-permute-start.26) | collective-permute-done | bytes 75460 | tf_op jit(solution)/shard_map/ppermute | solution.py:85
  212.7 1.9 collective-permute-start.27
  214.6 6.5 %collective-permute-done.27 = f32[19977]{0:T(1024)S(1)} collective-permute-done((f32[19977]{0:T(1024)S(1)}, f32[19977]{0:T(1024)S(1)}, u32[]{:S(2)}, u32[]{:S(2)}) %collective-permute-start.27) | collective-permute-done | bytes 79940 | tf_op jit(solution)/shard_map/ppermute | solution.py:85
  221.8 0.6 slice_bitcast_fusion
  223.1 0.7 reshape.263
  223.8 0.6 fusion.63
  (210 shorter events, 18.9 us)
Async XLA Ops:
  0.6 3.9 %copy-start = (bf16[128,128]{1,0:T(8,128)(2,1)S(1)}, bf16[128,128]{1,0:T(8,128)(2,1)}, u32[]{:S(2)}) copy-start(bf16[128,128]{1,0:T(8,128)(2,1)} %param.15) | copy-start | bytes 98308
  0.6 61.9 %copy-start.4 = (f32[3,256]{1,0:T(4,128)S(1)}, f32[3,256]{1,0:T(4,128)}, u32[]{:S(2)}) copy-start(f32[3,256]{1,0:T(4,128)} %param.11) | copy-start | bytes 9220
  5.6 57.3 %copy-start.6 = (s32[108]{0:T(128)S(1)}, s32[108]{0:T(128)}, u32[]{:S(2)}) copy-start(s32[108]{0:T(128)} %param.19) | copy-start | bytes 1300
  6.1 7.8 %collective-permute-start.2 = (f32[4480]{0:T(1024)S(1)}, f32[4480]{0:T(1024)S(1)}, u32[]{:S(2)}, u32[]{:S(2)}) collective-permute-start(f32[4480]{0:T(1024)S(1)} %select_n.283), channel_id=1, source_target_pairs={{0,4},{1,5},{2,6},{3,7},{4,0},{5,1},{6,2},{7,3},{8,12},{9,13},{10,... | collective-permute-start | bytes 53768 | tf_op jit(solution)/shard_map/ppermute | solution.py:85
  14.0 14.5 %collective-permute-start.3 = (f32[2240]{0:T(1024)S(1)}, f32[2240]{0:T(1024)S(1)}, u32[]{:S(2)}, u32[]{:S(2)}) collective-permute-start(f32[2240]{0:T(1024)S(1)} %slice_select_fusion.4), channel_id=1, source_target_pairs={{0,2},{1,3},{2,0},{3,1},{4,6},{5,7},{6,4},{7,5},{8,10},{9,11},{10,... | collective-permute-start | bytes 26888 | tf_op jit(solution)/shard_map/ppermute | solution.py:85
  18.7 43.8 %collective-permute-start.1 = (f32[131,256]{1,0:T(8,128)S(1)}, f32[131,256]{1,0:T(8,128)S(1)}, u32[]{:S(2)}, u32[]{:S(2)}) collective-permute-start(f32[131,256]{1,0:T(8,128)S(1)} %pad_maximum_fusion.5), channel_id=1, source_target_pairs={{1,0},{2,1},{3,2},{4,3},{5,4},{6,5},{7,6},{8,7},{9,8},{10,9},{11,1... | collective-permute-start | bytes 402440 | tf_op jit(solution)/shard_map/ppermute | solution.py:30
  24.2 38.3 %collective-permute-start = (f32[131,256]{1,0:T(8,128)S(1)}, f32[131,256]{1,0:T(8,128)S(1)}, u32[]{:S(2)}, u32[]{:S(2)}) collective-permute-start(f32[131,256]{1,0:T(8,128)S(1)} %pad_maximum_fusion.5), channel_id=1, source_target_pairs={{0,1},{1,2},{2,3},{3,4},{4,5},{5,6},{6,7},{7,8},{8,9},{9,10},{10,1... | collective-permute-start | bytes 402440 | tf_op jit(solution)/shard_map/ppermute | solution.py:27
  28.6 3.1 %collective-permute-start.4 = (f32[1120]{0:T(1024)S(1)}, f32[1120]{0:T(1024)S(1)}, u32[]{:S(2)}, u32[]{:S(2)}) collective-permute-start(f32[1120]{0:T(1024)S(1)} %slice_select_fusion.6), channel_id=1, source_target_pairs={{0,1},{1,0},{2,3},{3,2},{4,5},{5,4},{6,7},{7,6},{8,9},{9,8},{10,11... | collective-permute-start | bytes 13448 | tf_op jit(solution)/shard_map/ppermute | solution.py:85
  31.8 8.3 %collective-permute-start.5 = (f32[1120]{0:T(1024)S(1)}, f32[1120]{0:T(1024)S(1)}, u32[]{:S(2)}, u32[]{:S(2)}) collective-permute-start(f32[1120]{0:T(1024)S(1)} %select_add_fusion.2), channel_id=1, source_target_pairs={{0,8},{1,9},{2,10},{3,11},{4,12},{5,13},{6,14},{7,15},{8,0},{9,1},... | collective-permute-start | bytes 13448 | tf_op jit(solution)/shard_map/ppermute | solution.py:85
  40.1 5.0 %collective-permute-start.6 = (f32[2240]{0:T(1024)S(1)}, f32[2240]{0:T(1024)S(1)}, u32[]{:S(2)}, u32[]{:S(2)}) collective-permute-start(f32[2240]{0:T(1024)S(1)} %maximum_select_fusion.22), channel_id=1, source_target_pairs={{0,16},{1,17},{2,18},{3,19},{4,20},{5,21},{6,22},{7,23},{8,24},{9,... | collective-permute-start | bytes 26888 | tf_op jit(solution)/shard_map/ppermute | solution.py:85
  45.2 6.3 %collective-permute-start.7 = (f32[4480]{0:T(1024)S(1)}, f32[4480]{0:T(1024)S(1)}, u32[]{:S(2)}, u32[]{:S(2)}) collective-permute-start(f32[4480]{0:T(1024)S(1)} %maximum_select_fusion.18), channel_id=1, source_target_pairs={{0,32},{1,33},{2,34},{3,35},{4,36},{5,37},{6,38},{7,39},{8,40},{9,... | collective-permute-start | bytes 53768 | tf_op jit(solution)/shard_map/ppermute | solution.py:85
  51.6 6.2 %collective-permute-start.8 = (f32[8960]{0:T(1024)S(1)}, f32[8960]{0:T(1024)S(1)}, u32[]{:S(2)}, u32[]{:S(2)}) collective-permute-start(f32[8960]{0:T(1024)S(1)} %maximum_select_fusion.14), channel_id=1, source_target_pairs={{0,64},{1,65},{2,66},{3,67},{4,68},{5,69},{6,70},{7,71},{8,72},{9,... | collective-permute-start | bytes 107528 | tf_op jit(solution)/shard_map/ppermute | solution.py:85
  57.7 6.4 %collective-permute-start.9 = (f32[17920]{0:T(1024)S(1)}, f32[17920]{0:T(1024)S(1)}, u32[]{:S(2)}, u32[]{:S(2)}) collective-permute-start(f32[17920]{0:T(1024)S(1)} %maximum_select_fusion.9), channel_id=1, source_target_pairs={{0,128},{1,129},{2,130},{3,131},{4,132},{5,133},{6,134},{7,135},{8... | collective-permute-start | bytes 215048 | tf_op jit(solution)/shard_map/ppermute | solution.py:85
  63.8 7.6 %copy-start.1 = (bf16[108,64,128]{2,0,1:T(8,128)(2,1)}, bf16[108,64,128]{2,0,1:T(8,128)(2,1)S(1)}, u32[]{:S(2)}) copy-start(bf16[108,64,128]{2,0,1:T(8,128)(2,1)S(1)} %convert_bitcast_fusion) | copy-start | bytes 5308420
  64.2 14.9 %collective-permute-start.10 = (f32[35840]{0:T(1024)S(1)}, f32[35840]{0:T(1024)S(1)}, u32[]{:S(2)}, u32[]{:S(2)}) collective-permute-start(f32[35840]{0:T(1024)S(1)} %maximum_select_fusion.5), channel_id=1, source_target_pairs={{0,256},{1,257},{2,258},{3,259},{4,260},{5,261},{6,262},{7,263},{8... | collective-permute-start | bytes 430088 | tf_op jit(solution)/shard_map/ppermute | solution.py:85
  78.5 4.2 %copy-start.5 = (f32[35,35]{1,0:T(8,128)S(1)}, f32[35,35]{1,0:T(8,128)}, u32[]{:S(2)}) copy-start(f32[35,35]{1,0:T(8,128)} %param.16) | copy-start | bytes 14704
  78.5 12.8 %copy-start.7 = (s32[108]{0:T(128)S(1)}, s32[108]{0:T(128)}, u32[]{:S(2)}) copy-start(s32[108]{0:T(128)} %param.18) | copy-start | bytes 1300
  80.5 25.6 %copy-start.8 = (f32[128]{0:T(128)S(1)}, f32[128]{0:T(128)}, u32[]{:S(2)}) copy-start(f32[128]{0:T(128)} %param.17) | copy-start | bytes 1540
  83.1 12.7 %collective-permute-start.11 = (f32[1120]{0:T(1024)S(1)}, f32[1120]{0:T(1024)S(1)}, u32[]{:S(2)}, u32[]{:S(2)}) collective-permute-start(f32[1120]{0:T(1024)S(1)} %reshape.251), channel_id=1, source_target_pairs={{0,1},{1,0},{2,3},{3,2},{4,5},{5,4},{6,7},{7,6},{8,9},{9,8},{10,11... | collective-permute-start | bytes 13448 | tf_op jit(solution)/shard_map/ppermute | solution.py:85
  95.9 4.4 %collective-permute-start.12 = (f32[2240]{0:T(1024)S(1)}, f32[2240]{0:T(1024)S(1)}, u32[]{:S(2)}, u32[]{:S(2)}) collective-permute-start(f32[2240]{0:T(1024)S(1)} %maximum_select_fusion.23), channel_id=1, source_target_pairs={{0,2},{1,3},{2,0},{3,1},{4,6},{5,7},{6,4},{7,5},{8,10},{9,11},{10,... | collective-permute-start | bytes 26888 | tf_op jit(solution)/shard_map/ppermute | solution.py:85
  100.4 5.4 %collective-permute-start.13 = (f32[4480]{0:T(1024)S(1)}, f32[4480]{0:T(1024)S(1)}, u32[]{:S(2)}, u32[]{:S(2)}) collective-permute-start(f32[4480]{0:T(1024)S(1)} %maximum_select_fusion.19), channel_id=1, source_target_pairs={{0,4},{1,5},{2,6},{3,7},{4,0},{5,1},{6,2},{7,3},{8,12},{9,13},{10,... | collective-permute-start | bytes 53768 | tf_op jit(solution)/shard_map/ppermute | solution.py:85
  107.1 19.3 %collective-permute-start.16 = (f32[2240]{0:T(1024)S(1)}, f32[2240]{0:T(1024)S(1)}, u32[]{:S(2)}, u32[]{:S(2)}) collective-permute-start(f32[2240]{0:T(1024)S(1)} %select_n.320), channel_id=1, source_target_pairs={{0,4},{1,5},{2,6},{3,7},{4,0},{5,1},{6,2},{7,3},{8,12},{9,13},{10,... | collective-permute-start | bytes 26888 | tf_op jit(solution)/shard_map/ppermute | solution.py:85
  110.8 6.0 %copy-start.2 = (bf16[108,64,128]{2,0,1:T(8,128)(2,1)S(1)}, bf16[108,64,128]{2,0,1:T(8,128)(2,1)}, u32[]{:S(2)}) copy-start(bf16[108,64,128]{2,0,1:T(8,128)(2,1)} %copy-done.1) | copy-start | bytes 5308420
  124.5 16.3 %copy-start.3 = (bf16[256,128]{1,0:T(8,128)(2,1)S(1)}, bf16[256,128]{1,0:T(8,128)(2,1)}, u32[]{:S(2)}) copy-start(bf16[256,128]{1,0:T(8,128)(2,1)} %param.14) | copy-start | bytes 196612
  126.5 10.1 %collective-permute-start.17 = (f32[1120]{0:T(1024)S(1)}, f32[1120]{0:T(1024)S(1)}, u32[]{:S(2)}, u32[]{:S(2)}) collective-permute-start(f32[1120]{0:T(1024)S(1)} %slice_select_fusion.5), channel_id=1, source_target_pairs={{0,2},{1,3},{2,0},{3,1},{4,6},{5,7},{6,4},{7,5},{8,10},{9,11},{10,... | collective-permute-start | bytes 13448 | tf_op jit(solution)/shard_map/ppermute | solution.py:85
  129.9 10.9 %collective-permute-start.14 = (bf16[131,256]{1,0:T(8,128)(2,1)S(1)}, bf16[131,256]{1,0:T(8,128)(2,1)S(1)}, u32[]{:S(2)}, u32[]{:S(2)}) collective-permute-start(bf16[131,256]{1,0:T(8,128)(2,1)S(1)} %get-tuple-element.17), channel_id=1, source_target_pairs={{1,0},{2,1},{3,2},{4,3},{5,4},{6,5},{7,6},{8,7},{9,8},{10,9},{11,1... | collective-permute-start | bytes 201224 | tf_op jit(solution)/shard_map/ppermute | solution.py:38
  134.7 6.1 %collective-permute-start.15 = (bf16[131,256]{1,0:T(8,128)(2,1)S(1)}, bf16[131,256]{1,0:T(8,128)(2,1)S(1)}, u32[]{:S(2)}, u32[]{:S(2)}) collective-permute-start(bf16[131,256]{1,0:T(8,128)(2,1)S(1)} %get-tuple-element.18), channel_id=1, source_target_pairs={{0,1},{1,2},{2,3},{3,4},{4,5},{5,6},{6,7},{7,8},{8,9},{9,10},{10,1... | collective-permute-start | bytes 201224 | tf_op jit(solution)/shard_map/ppermute | solution.py:38
  136.8 3.2 %collective-permute-start.18 = (f32[560]{0:T(1024)S(1)}, f32[560]{0:T(1024)S(1)}, u32[]{:S(2)}, u32[]{:S(2)}) collective-permute-start(f32[560]{0:T(1024)S(1)} %slice_select_fusion.7), channel_id=1, source_target_pairs={{0,1},{1,0},{2,3},{3,2},{4,5},{5,4},{6,7},{7,6},{8,9},{9,8},{10,11... | collective-permute-start | bytes 6728 | tf_op jit(solution)/shard_map/ppermute | solution.py:85
  141.6 9.1 %collective-permute-start.19 = (f32[18297]{0:T(1024)S(1)}, f32[18297]{0:T(1024)S(1)}, u32[]{:S(2)}, u32[]{:S(2)}) collective-permute-start(f32[18297]{0:T(1024)S(1)} %concatenate.293), channel_id=1, source_target_pairs={{0,8},{1,9},{2,10},{3,11},{4,12},{5,13},{6,14},{7,15},{8,0},{9,1},... | collective-permute-start | bytes 219572 | tf_op jit(solution)/shard_map/ppermute | solution.py:85
  151.0 5.1 %collective-permute-start.20 = (f32[18857]{0:T(1024)S(1)}, f32[18857]{0:T(1024)S(1)}, u32[]{:S(2)}, u32[]{:S(2)}) collective-permute-start(f32[18857]{0:T(1024)S(1)} %pad_maximum_fusion.10), channel_id=1, source_target_pairs={{0,16},{1,17},{2,18},{3,19},{4,20},{5,21},{6,22},{7,23},{8,24},{9,... | collective-permute-start | bytes 226292 | tf_op jit(solution)/shard_map/ppermute | solution.py:85
  156.4 6.7 %collective-permute-start.21 = (f32[19977]{0:T(1024)S(1)}, f32[19977]{0:T(1024)S(1)}, u32[]{:S(2)}, u32[]{:S(2)}) collective-permute-start(f32[19977]{0:T(1024)S(1)} %pad_maximum_fusion.8), channel_id=1, source_target_pairs={{0,32},{1,33},{2,34},{3,35},{4,36},{5,37},{6,38},{7,39},{8,40},{9,... | collective-permute-start | bytes 239732 | tf_op jit(solution)/shard_map/ppermute | solution.py:85
  163.3 7.0 %collective-permute-start.22 = (f32[22217]{0:T(1024)S(1)}, f32[22217]{0:T(1024)S(1)}, u32[]{:S(2)}, u32[]{:S(2)}) collective-permute-start(f32[22217]{0:T(1024)S(1)} %pad_maximum_fusion.7), channel_id=1, source_target_pairs={{0,64},{1,65},{2,66},{3,67},{4,68},{5,69},{6,70},{7,71},{8,72},{9,... | collective-permute-start | bytes 266612 | tf_op jit(solution)/shard_map/ppermute | solution.py:85
  170.4 6.4 %collective-permute-start.23 = (f32[26697]{0:T(1024)S(1)}, f32[26697]{0:T(1024)S(1)}, u32[]{:S(2)}, u32[]{:S(2)}) collective-permute-start(f32[26697]{0:T(1024)S(1)} %pad_maximum_fusion.6), channel_id=1, source_target_pairs={{0,128},{1,129},{2,130},{3,131},{4,132},{5,133},{6,134},{7,135},{8... | collective-permute-start | bytes 320372 | tf_op jit(solution)/shard_map/ppermute | solution.py:85
  176.9 11.3 %collective-permute-start.24 = (f32[35657]{0:T(1024)S(1)}, f32[35657]{0:T(1024)S(1)}, u32[]{:S(2)}, u32[]{:S(2)}) collective-permute-start(f32[35657]{0:T(1024)S(1)} %pad_maximum_fusion.3), channel_id=1, source_target_pairs={{0,256},{1,257},{2,258},{3,259},{4,260},{5,261},{6,262},{7,263},{8... | collective-permute-start | bytes 427892 | tf_op jit(solution)/shard_map/ppermute | solution.py:85
  189.4 16.9 %collective-permute-start.25 = (f32[18297]{0:T(1024)S(1)}, f32[18297]{0:T(1024)S(1)}, u32[]{:S(2)}, u32[]{:S(2)}) collective-permute-start(f32[18297]{0:T(1024)S(1)} %pad_maximum_fusion.12), channel_id=1, source_target_pairs={{0,1},{1,0},{2,3},{3,2},{4,5},{5,4},{6,7},{7,6},{8,9},{9,8},{10,11... | collective-permute-start | bytes 219572 | tf_op jit(solution)/shard_map/ppermute | solution.py:85
  206.8 5.5 %collective-permute-start.26 = (f32[18857]{0:T(1024)S(1)}, f32[18857]{0:T(1024)S(1)}, u32[]{:S(2)}, u32[]{:S(2)}) collective-permute-start(f32[18857]{0:T(1024)S(1)} %pad_maximum_fusion.11), channel_id=1, source_target_pairs={{0,2},{1,3},{2,0},{3,1},{4,6},{5,7},{6,4},{7,5},{8,10},{9,11},{10,... | collective-permute-start | bytes 226292 | tf_op jit(solution)/shard_map/ppermute | solution.py:85
  212.7 8.5 %collective-permute-start.27 = (f32[19977]{0:T(1024)S(1)}, f32[19977]{0:T(1024)S(1)}, u32[]{:S(2)}, u32[]{:S(2)}) collective-permute-start(f32[19977]{0:T(1024)S(1)} %pad_maximum_fusion.9), channel_id=1, source_target_pairs={{0,4},{1,5},{2,6},{3,7},{4,0},{5,1},{6,2},{7,3},{8,12},{9,13},{10,... | collective-permute-start | bytes 239732 | tf_op jit(solution)/shard_map/ppermute | solution.py:85
